TPU v7x, 256 devices: a whole 4x4x8 slice. The times are simulated.
256 devices in a mesh: chord: 4 (over y), span: 16 (over z, x_lo), wall: 4 (over x_hi, core).
Axes of the slice: x: 4 (x_hi: 2, x_lo: 2; x = x_hi * 2 + x_lo), y: 4, z: 8, core: 2. Of those that a mesh axis runs over, the one named last changes fastest.
Arguments:
- sensitivity: float32 [6, 32, 256, 512], P(None, 'chord', 'span', 'wall'), may hold values from -6 to 6
- diagonal: float32 [6, 32, 256, 512], P(None, 'chord', 'span', 'wall'), may hold values from 10 to 20
- face_coef: float32 [3, 32, 256, 512], P(None, 'chord', 'span', 'wall'), may hold values from 0.3 to 1.5
- upper_blocks: float32 [3, 6, 6], replicated, may hold values from -2.5 to 2.5
- lower_blocks: float32 [3, 6, 6], replicated, may hold values from -2.5 to 2.5
- iface_blocks: float32 [2, 6, 6], replicated, may hold values from -2.5 to 2.5
- production: float32 [32, 256, 512], P('chord', 'span', 'wall'), may hold values from -6 to 6
- send_cell: int32 [4, 16, 4, 16, 64], P('chord', 'span', 'wall'), may hold values from 0 to 16383
- target_cell: int32 [4, 16, 4, 16, 64], P('chord', 'span', 'wall'), may hold values from 0 to 16383
- orient: int32 [4, 16, 4, 16, 64], P('chord', 'span', 'wall'), may hold values from 0 to 1
- iface_weight: float32 [4, 16, 4, 16, 64], P('chord', 'span', 'wall'), may hold values from 0.5 to 2
Outputs:
- adjoint: float32 [6, 32, 256, 512], P(None, 'chord', 'span', 'wall')
- gradient: float32 [32, 256, 512], P('chord', 'span', 'wall')
All inputs are finite; a program needn't handle non-finite values.
Results may differ from a plain program's by a relative error of at most 0.0001.
Values sent between devices are 32-bit elements; how exact they have to be, the bound alone decides.
No kernel may reach another device: no remote copies, remote signals or barrier semaphores. Data moves between devices by JAX's collectives and lax.ppermute only.
A program may use at most 64 MiB of HBM per device.

v0:
```python
import jax
import jax.numpy as jnp
from jax import lax
from jax.experimental import pallas as pl
from jax.experimental.pallas import tpu as pltpu
from jax.sharding import PartitionSpec as P

SWEEPS = 3
F32 = jnp.float32
BF16 = jnp.bfloat16


def split3(x):
    p1 = x.astype(BF16)
    r1 = x - p1.astype(F32)
    p2 = r1.astype(BF16)
    p3 = (r1 - p2.astype(F32)).astype(BF16)
    return p1, p2, p3


def gather_rows(adj, send_ref, orient_ref, weight_ref, blk, n_var, lanes):
    rows = adj.shape[1] * adj.shape[2]
    n_rows = send_ref.shape[1]
    cell = send_ref[...]
    row_of = cell // lanes
    lane_of = cell % lanes
    lane_hot = (lax.broadcasted_iota(jnp.int32, (lanes, n_rows), 0) == lane_of).astype(BF16)
    row_hot = (lax.broadcasted_iota(jnp.int32, (rows, n_rows), 0) == row_of).astype(F32)
    flat = adj.reshape(n_var * rows, lanes)
    picked = None
    for part in split3(flat):
        term = jnp.dot(part, lane_hot, preferred_element_type=F32)
        picked = term if picked is None else picked + term
    src = jnp.sum(picked.reshape(n_var, rows, n_rows) * row_hot[None], axis=1)
    orient = orient_ref[...]
    weight = weight_ref[...]
    out = []
    for i in range(n_var):
        first = None
        second = None
        for j in range(n_var):
            a = blk[216 + j * n_var + i] * src[j:j + 1]
            b = blk[216 + 36 + j * n_var + i] * src[j:j + 1]
            first = a if first is None else first + a
            second = b if second is None else second + b
        out.append(jnp.where(orient == 1, second, first) * weight)
    return jnp.concatenate(out, axis=0)


def write_faces(adj, faces):
    c_lo, c_hi, s_lo, s_hi, w_lo, w_hi = faces
    nx, ny, nz = adj.shape[1], adj.shape[2], adj.shape[3]
    c_lo[...] = adj[:, 0:1]
    c_hi[...] = adj[:, nx - 1:nx]
    s_lo[...] = adj[:, :, 0:1]
    s_hi[...] = adj[:, :, ny - 1:ny]
    w_lo[...] = adj[:, :, :, 0:1]
    w_hi[...] = adj[:, :, :, nz - 1:nz]


def init_kernel(blk_ref, sens_ref, diag_ref, send_ref, orient_ref, weight_ref,
                adj_ref, rows_ref, c_lo, c_hi, s_lo, s_hi, w_lo, w_hi):
    n_var = sens_ref.shape[0]
    lanes = sens_ref.shape[3]
    adj = sens_ref[...] / diag_ref[...]
    adj_ref[...] = adj
    write_faces(adj, (c_lo, c_hi, s_lo, s_hi, w_lo, w_hi))
    rows_ref[...] = gather_rows(adj, send_ref, orient_ref, weight_ref, blk_ref, n_var, lanes)


def sweep_body(blk, adj, sens, diag, face, halos, incoming, target_ref):
    n_var, nx, ny, nz = adj.shape
    rows = nx * ny
    h_c_lo, h_c_hi, h_s_lo, h_s_hi, h_w_lo, h_w_hi = halos
    j_idx = lax.broadcasted_iota(jnp.int32, adj.shape, 2)
    k_idx = lax.broadcasted_iota(jnp.int32, adj.shape, 3)
    up = [
        jnp.concatenate([adj[:, 1:], h_c_hi], axis=1),
        jnp.where(j_idx == ny - 1, h_s_hi, pltpu.roll(adj, ny - 1, 2)),
        jnp.where(k_idx == nz - 1, h_w_hi, pltpu.roll(adj, nz - 1, 3)),
    ]
    lo = [
        jnp.concatenate([h_c_lo, adj[:, :-1]], axis=1),
        jnp.where(j_idx == 0, h_s_lo, pltpu.roll(adj, 1, 2)),
        jnp.where(k_idx == 0, h_w_lo, pltpu.roll(adj, 1, 3)),
    ]
    n_rows = incoming.shape[1]
    cell = target_ref[...]
    row_of = cell // nz
    lane_of = cell % nz
    row_hot = (lax.broadcasted_iota(jnp.int32, (rows, n_rows), 0) == row_of).astype(F32)
    lane_hot = (lax.broadcasted_iota(jnp.int32, (nz, n_rows), 0) == lane_of).astype(BF16)
    coupled = None
    for part in split3(incoming):
        lhs = (row_hot[None] * part.astype(F32)[:, None, :]).astype(BF16).reshape(n_var * rows, n_rows)
        term = lax.dot_general(lhs, lane_hot, (((1,), (1,)), ((), ())), preferred_element_type=F32)
        coupled = term if coupled is None else coupled + term
    coupled = coupled.reshape(n_var, nx, ny, nz)
    new = []
    for i in range(n_var):
        applied = diag[i] * adj[i] + coupled[i]
        for d in range(3):
            acc = None
            for j in range(n_var):
                t = blk[d * 36 + j * n_var + i] * up[d][j] + blk[108 + d * 36 + j * n_var + i] * lo[d][j]
                acc = t if acc is None else acc + t
            applied = applied + face[d] * acc
        new.append(adj[i] + (sens[i] - applied) / diag[i])
    return jnp.stack(new, axis=0)


def sweep_kernel(blk_ref, adj_ref, sens_ref, diag_ref, face_ref, hcl, hch, hsl, hsh, hwl, hwh,
                 inc_ref, tgt_ref, send_ref, orient_ref, weight_ref,
                 out_ref, rows_ref, c_lo, c_hi, s_lo, s_hi, w_lo, w_hi):
    n_var = adj_ref.shape[0]
    lanes = adj_ref.shape[3]
    halos = (hcl[...], hch[...], hsl[...], hsh[...], hwl[...], hwh[...])
    new = sweep_body(blk_ref, adj_ref[...], sens_ref[...], diag_ref[...], face_ref[...], halos,
                     inc_ref[...], tgt_ref)
    out_ref[...] = new
    write_faces(new, (c_lo, c_hi, s_lo, s_hi, w_lo, w_hi))
    rows_ref[...] = gather_rows(new, send_ref, orient_ref, weight_ref, blk_ref, n_var, lanes)


def last_kernel(blk_ref, adj_ref, sens_ref, diag_ref, face_ref, hcl, hch, hsl, hsh, hwl, hwh,
                inc_ref, tgt_ref, prod_ref, out_ref, grad_ref):
    n_var = adj_ref.shape[0]
    halos = (hcl[...], hch[...], hsl[...], hsh[...], hwl[...], hwh[...])
    new = sweep_body(blk_ref, adj_ref[...], sens_ref[...], diag_ref[...], face_ref[...], halos,
                     inc_ref[...], tgt_ref)
    out_ref[...] = new
    grad_ref[...] = prod_ref[...] * new[n_var - 1]


def face_shapes(shape):
    n_var, nx, ny, nz = shape
    c = jax.ShapeDtypeStruct((n_var, 1, ny, nz), F32)
    s = jax.ShapeDtypeStruct((n_var, nx, 1, nz), F32)
    w = jax.ShapeDtypeStruct((n_var, nx, ny, 1), F32)
    return [c, c, s, s, w, w]


def exchange(faces):
    c_lo, c_hi, s_lo, s_hi, w_lo, w_hi = faces
    out = []
    for axis, lo_face, hi_face in (("chord", c_lo, c_hi), ("span", s_lo, s_hi), ("wall", w_lo, w_hi)):
        count = lax.axis_size(axis)
        forward = [(i, i + 1) for i in range(count - 1)]
        backward = [(i + 1, i) for i in range(count - 1)]
        out.append(lax.ppermute(hi_face, axis, forward))
        out.append(lax.ppermute(lo_face, axis, backward))
    return out


def local(sensitivity, diagonal, face_coef, upper_blocks, lower_blocks, iface_blocks, production,
          send_cell, target_cell, orient, iface_weight):
    n_span = lax.axis_size("span")
    n_var = sensitivity.shape[0]
    slots = send_cell.shape[-1]
    n_rows = n_span * slots
    shape = sensitivity.shape
    blk = jnp.concatenate([upper_blocks.reshape(-1), lower_blocks.reshape(-1), iface_blocks.reshape(-1)])
    send_row = send_cell.reshape(1, n_rows)
    orient_row = orient.reshape(1, n_rows)
    weight_row = iface_weight.reshape(1, n_rows)
    target_row = lax.all_to_all(
        target_cell.reshape(n_span, slots), "span", split_axis=0, concat_axis=0, tiled=True
    ).reshape(1, n_rows)

    vmem = pl.BlockSpec(memory_space=pltpu.VMEM)
    smem = pl.BlockSpec(memory_space=pltpu.SMEM)
    adj_sds = jax.ShapeDtypeStruct(shape, F32)
    rows_sds = jax.ShapeDtypeStruct((n_var, n_rows), F32)

    init = pl.pallas_call(
        init_kernel,
        out_shape=[adj_sds, rows_sds] + face_shapes(shape),
        in_specs=[smem] + [vmem] * 5,
        out_specs=[vmem] * 8,
    )
    adj, rows, *faces = init(blk, sensitivity, diagonal, send_row, orient_row, weight_row)

    step = pl.pallas_call(
        sweep_kernel,
        out_shape=[adj_sds, rows_sds] + face_shapes(shape),
        in_specs=[smem] + [vmem] * 15,
        out_specs=[vmem] * 8,
    )
    last = pl.pallas_call(
        last_kernel,
        out_shape=[adj_sds, jax.ShapeDtypeStruct(production.shape, F32)],
        in_specs=[smem] + [vmem] * 13,
        out_specs=[vmem] * 2,
    )
    for sweep in range(SWEEPS):
        halos = exchange(faces)
        incoming = lax.all_to_all(
            rows.reshape(n_var, n_span, slots), "span", split_axis=1, concat_axis=1, tiled=True
        ).reshape(n_var, n_rows)
        if sweep < SWEEPS - 1:
            adj, rows, *faces = step(blk, adj, sensitivity, diagonal, face_coef, *halos, incoming,
                                     target_row, send_row, orient_row, weight_row)
        else:
            adj, gradient = last(blk, adj, sensitivity, diagonal, face_coef, *halos, incoming,
                                 target_row, production)
    return (adj, gradient)


def solution(mesh):
    placed = (
        P(None, "chord", "span", "wall"),
        P(None, "chord", "span", "wall"),
        P(None, "chord", "span", "wall"),
        P(),
        P(),
        P(),
        P("chord", "span", "wall"),
        P("chord", "span", "wall", None, None),
        P("chord", "span", "wall", None, None),
        P("chord", "span", "wall", None, None),
        P("chord", "span", "wall", None, None),
    )
    return jax.shard_map(
        local,
        mesh=mesh,
        in_specs=placed,
        out_specs=(P(None, "chord", "span", "wall"), P("chord", "span", "wall")),
        check_vma=False,
    )
```

profile of v0, /device:TPU:49, one launch (start us, length us, event | category | flops | bytes accessed | tf_op | source)
XLA Modules:
  0.0 163.3 jit_solution(9088400505223845041)
XLA Ops:
  0.6 9.1 %all-to-all-start.1 = ((s32[16,1,64]{2,1,0:T(1,128)}), s32[16,1,64]{2,1,0:T(1,128)S(1)}, u32[]{:S(2)}, u32[]{:S(2)}) async-start(s32[16,1,64]{2,1,0:T(1,128)} %bitcast.25), calls=%async_computation.1 | async-start | bytes 16384 | tf_op jit(solution)/shard_map/all_to_all | solution.py:166
  13.3 3.4 %shard_map.122 = (f32[6,8,16,128]{3,2,1,0:T(8,128)}, f32[6,1024]{1,0:T(8,128)}, f32[6,1,16,128]{3,2,1,0:T(8,128)}, f32[6,1,16,128]{3,2,1,0:T(8,128)}, f32[6,8,1,...) custom-call(f32[288]{0:T(512)} %pad_maximum_fusion.blk_ref, ...), custom_call_target="tpu_custom_call" | custom-call | tf_op jit(solution)/shard_map/pallas_call | solution.py:181
  23.5 7.7 %all-to-all-start = ((f32[16,1,384]{2,1,0:T(1,128)}), f32[16,1,384]{2,1,0:T(1,128)S(1)}, u32[]{:S(2)}, u32[]{:S(2)}) async-start(f32[16,1,384]{2,1,0:T(1,128)} %reshape.70), calls=%async_computation | async-start | bytes 49152 | tf_op jit(solution)/shard_map/all_to_all | solution.py:197
  31.2 3.1 %collective-permute-start.2 = (f32[6,8,1,128]{3,2,1,0:T(1,128)S(1)}, f32[6,8,1,128]{3,2,1,0:T(1,128)S(1)}, u32[]{:S(2)}, u32[]{:S(2)}) collective-permute-start(f32[6,8,1,128]{3,2,1,0:T(1,128)S(1)} %copy-done.26), channel_id=1, source_target_pairs={{0,4},{4,8},{8,12},{12,16},{16,20},{20,24},{24,28},{28,32},{32,36}... | collective-permute-start | bytes 73736 | tf_op jit(solution)/shard_map/ppermute | solution.py:150
  34.4 3.1 %collective-permute-start.3 = (f32[6,8,1,128]{3,2,1,0:T(1,128)S(1)}, f32[6,8,1,128]{3,2,1,0:T(1,128)S(1)}, u32[]{:S(2)}, u32[]{:S(2)}) collective-permute-start(f32[6,8,1,128]{3,2,1,0:T(1,128)S(1)} %copy-done.24), channel_id=1, source_target_pairs={{4,0},{8,4},{12,8},{16,12},{20,16},{24,20},{28,24},{32,28},{36,32}... | collective-permute-start | bytes 73736 | tf_op jit(solution)/shard_map/ppermute | solution.py:151
  37.5 7.2 %collective-permute-start.4 = (f32[6,8,16,1]{3,2,1,0:T(8,128)}, f32[6,8,16,1]{3,2,1,0:T(8,128)S(1)}, u32[]{:S(2)}, u32[]{:S(2)}) collective-permute-start(f32[6,8,16,1]{3,2,1,0:T(8,128)} %get-tuple-element.31), channel_id=1, source_target_pairs={{0,1},{1,2},{2,3},{4,5},{5,6},{6,7},{8,9},{9,10},{10,11},{12,13},{... | collective-permute-start | bytes 9224 | tf_op jit(solution)/shard_map/ppermute | solution.py:150
  44.6 5.0 %collective-permute-done.4.hwl = f32[6,8,16,1]{3,2,1,0:T(8,128)S(1)} collective-permute-done((f32[6,8,16,1]{3,2,1,0:T(8,128)}, f32[6,8,16,1]{3,2,1,0:T(8,128)S(1)}, u32[]{:S(2)}, u32[]{:S(2)}) %collective-permute-start.4) | collective-permute-done | bytes 3104 | tf_op jit(solution)/shard_map/ppermute | solution.py:150
  55.6 5.5 %collective-permute-done.5.hwh = f32[6,8,16,1]{3,2,1,0:T(8,128)S(1)} collective-permute-done((f32[6,8,16,1]{3,2,1,0:T(8,128)}, f32[6,8,16,1]{3,2,1,0:T(8,128)S(1)}, u32[]{:S(2)}, u32[]{:S(2)}) %collective-permute-start.5) | collective-permute-done | bytes 3104 | tf_op jit(solution)/shard_map/ppermute | solution.py:151
  61.9 6.4 %shard_map.123 = (f32[6,8,16,128]{3,2,1,0:T(8,128)}, f32[6,1024]{1,0:T(8,128)}, f32[6,1,16,128]{3,2,1,0:T(8,128)}, f32[6,1,16,128]{3,2,1,0:T(8,128)}, f32[6,8,1,...) custom-call(f32[288]{0:T(512)} %pad_maximum_fusion.blk_ref, ...), custom_call_target="tpu_custom_call" | custom-call | tf_op jit(solution)/shard_map/pallas_call | solution.py:201
  75.1 8.0 %all-to-all-start.2 = ((f32[16,1,384]{2,1,0:T(1,128)}), f32[16,1,384]{2,1,0:T(1,128)S(1)}, u32[]{:S(2)}, u32[]{:S(2)}) async-start(f32[16,1,384]{2,1,0:T(1,128)} %reshape.72), calls=%async_computation.2 | async-start | bytes 49152 | tf_op jit(solution)/shard_map/all_to_all | solution.py:197
  83.2 3.1 %collective-permute-start.8 = (f32[6,8,1,128]{3,2,1,0:T(1,128)S(1)}, f32[6,8,1,128]{3,2,1,0:T(1,128)S(1)}, u32[]{:S(2)}, u32[]{:S(2)}) collective-permute-start(f32[6,8,1,128]{3,2,1,0:T(1,128)S(1)} %copy-done.29), channel_id=1, source_target_pairs={{0,4},{4,8},{8,12},{12,16},{16,20},{20,24},{24,28},{28,32},{32,36}... | collective-permute-start | bytes 73736 | tf_op jit(solution)/shard_map/ppermute | solution.py:150
  86.3 3.1 %collective-permute-start.9 = (f32[6,8,1,128]{3,2,1,0:T(1,128)S(1)}, f32[6,8,1,128]{3,2,1,0:T(1,128)S(1)}, u32[]{:S(2)}, u32[]{:S(2)}) collective-permute-start(f32[6,8,1,128]{3,2,1,0:T(1,128)S(1)} %copy-done.28), channel_id=1, source_target_pairs={{4,0},{8,4},{12,8},{16,12},{20,16},{24,20},{28,24},{32,28},{36,32}... | collective-permute-start | bytes 73736 | tf_op jit(solution)/shard_map/ppermute | solution.py:151
  89.4 3.5 %collective-permute-start.10 = (f32[6,8,16,1]{3,2,1,0:T(8,128)}, f32[6,8,16,1]{3,2,1,0:T(8,128)S(1)}, u32[]{:S(2)}, u32[]{:S(2)}) collective-permute-start(f32[6,8,16,1]{3,2,1,0:T(8,128)} %get-tuple-element.39), channel_id=1, source_target_pairs={{0,1},{1,2},{2,3},{4,5},{5,6},{6,7},{8,9},{9,10},{10,11},{12,13},{... | collective-permute-start | bytes 9224 | tf_op jit(solution)/shard_map/ppermute | solution.py:150
  92.9 5.0 %collective-permute-done.10.hwl = f32[6,8,16,1]{3,2,1,0:T(8,128)S(1)} collective-permute-done((f32[6,8,16,1]{3,2,1,0:T(8,128)}, f32[6,8,16,1]{3,2,1,0:T(8,128)S(1)}, u32[]{:S(2)}, u32[]{:S(2)}) %collective-permute-start.10) | collective-permute-done | bytes 3104 | tf_op jit(solution)/shard_map/ppermute | solution.py:150
  101.4 8.0 %collective-permute-done.11.hwh = f32[6,8,16,1]{3,2,1,0:T(8,128)S(1)} collective-permute-done((f32[6,8,16,1]{3,2,1,0:T(8,128)}, f32[6,8,16,1]{3,2,1,0:T(8,128)S(1)}, u32[]{:S(2)}, u32[]{:S(2)}) %collective-permute-start.11) | collective-permute-done | bytes 3104 | tf_op jit(solution)/shard_map/ppermute | solution.py:151
  110.1 6.4 %shard_map.124 = (f32[6,8,16,128]{3,2,1,0:T(8,128)}, f32[6,1024]{1,0:T(8,128)}, f32[6,1,16,128]{3,2,1,0:T(8,128)}, f32[6,1,16,128]{3,2,1,0:T(8,128)}, f32[6,8,1,...) custom-call(f32[288]{0:T(512)} %pad_maximum_fusion.blk_ref, ...), custom_call_target="tpu_custom_call" | custom-call | tf_op jit(solution)/shard_map/pallas_call | solution.py:201
  116.6 2.9 %collective-permute-start.12 = (f32[6,1,16,128]{3,2,1,0:T(8,128)}, f32[6,1,16,128]{3,2,1,0:T(8,128)S(1)}, u32[]{:S(2)}, u32[]{:S(2)}) collective-permute-start(f32[6,1,16,128]{3,2,1,0:T(8,128)} %get-tuple-element.43), channel_id=1, source_target_pairs={{0,64},{64,128},{128,192},{1,65},{65,129},{129,193},{2,66},{66,130... | collective-permute-start | bytes 147464 | tf_op jit(solution)/shard_map/ppermute | solution.py:150
  123.4 8.0 %all-to-all-start.3 = ((f32[16,1,384]{2,1,0:T(1,128)}), f32[16,1,384]{2,1,0:T(1,128)S(1)}, u32[]{:S(2)}, u32[]{:S(2)}) async-start(f32[16,1,384]{2,1,0:T(1,128)} %reshape.74), calls=%async_computation.3 | async-start | bytes 49152 | tf_op jit(solution)/shard_map/all_to_all | solution.py:197
  131.4 3.1 %collective-permute-start.14 = (f32[6,8,1,128]{3,2,1,0:T(1,128)S(1)}, f32[6,8,1,128]{3,2,1,0:T(1,128)S(1)}, u32[]{:S(2)}, u32[]{:S(2)}) collective-permute-start(f32[6,8,1,128]{3,2,1,0:T(1,128)S(1)} %copy-done.27), channel_id=1, source_target_pairs={{0,4},{4,8},{8,12},{12,16},{16,20},{20,24},{24,28},{28,32},{32,36}... | collective-permute-start | bytes 73736 | tf_op jit(solution)/shard_map/ppermute | solution.py:150
  134.5 3.1 %collective-permute-start.15 = (f32[6,8,1,128]{3,2,1,0:T(1,128)S(1)}, f32[6,8,1,128]{3,2,1,0:T(1,128)S(1)}, u32[]{:S(2)}, u32[]{:S(2)}) collective-permute-start(f32[6,8,1,128]{3,2,1,0:T(1,128)S(1)} %copy-done.25), channel_id=1, source_target_pairs={{4,0},{8,4},{12,8},{16,12},{20,16},{24,20},{28,24},{32,28},{36,32}... | collective-permute-start | bytes 73736 | tf_op jit(solution)/shard_map/ppermute | solution.py:151
  137.6 3.5 %collective-permute-start.16 = (f32[6,8,16,1]{3,2,1,0:T(8,128)}, f32[6,8,16,1]{3,2,1,0:T(8,128)S(1)}, u32[]{:S(2)}, u32[]{:S(2)}) collective-permute-start(f32[6,8,16,1]{3,2,1,0:T(8,128)} %get-tuple-element.47), channel_id=1, source_target_pairs={{0,1},{1,2},{2,3},{4,5},{5,6},{6,7},{8,9},{9,10},{10,11},{12,13},{... | collective-permute-start | bytes 9224 | tf_op jit(solution)/shard_map/ppermute | solution.py:150
  141.2 5.0 %collective-permute-done.16.hwl = f32[6,8,16,1]{3,2,1,0:T(8,128)S(1)} collective-permute-done((f32[6,8,16,1]{3,2,1,0:T(8,128)}, f32[6,8,16,1]{3,2,1,0:T(8,128)S(1)}, u32[]{:S(2)}, u32[]{:S(2)}) %collective-permute-start.16) | collective-permute-done | bytes 3104 | tf_op jit(solution)/shard_map/ppermute | solution.py:150
  149.7 8.0 %collective-permute-done.17.hwh = f32[6,8,16,1]{3,2,1,0:T(8,128)S(1)} collective-permute-done((f32[6,8,16,1]{3,2,1,0:T(8,128)}, f32[6,8,16,1]{3,2,1,0:T(8,128)S(1)}, u32[]{:S(2)}, u32[]{:S(2)}) %collective-permute-start.17) | collective-permute-done | bytes 3104 | tf_op jit(solution)/shard_map/ppermute | solution.py:151
  158.4 4.9 %shard_map.125 = (f32[6,8,16,128]{3,2,1,0:T(8,128)}, f32[8,16,128]{2,1,0:T(8,128)}) custom-call(f32[288]{0:T(512)} %pad_maximum_fusion.blk_ref, f32[6,8,16,128]{3,2,1,0:T(8,128)} %get-tuple-element.42.adj_ref, f32[6,8,16,128]{3,2,1,0:T(8,128)} %sens_ref.7, f32[6,8,16,128]{3,2,1,0:T(8,128)} %diag_ref.7, f32[3,8,16,128]{3,2,1,0:T(8,128)} %face_ref.5, ...), custom_call_target="tpu_custom_call" | custom-call | tf_op jit(solution)/shard_map/pallas_call | solution.py:204
  (117 shorter events, 36.1 us)
Async XLA Ops:
  0.6 22.9 %all-to-all-start.1 = ((s32[16,1,64]{2,1,0:T(1,128)}), s32[16,1,64]{2,1,0:T(1,128)S(1)}, u32[]{:S(2)}, u32[]{:S(2)}) async-start(s32[16,1,64]{2,1,0:T(1,128)} %bitcast.25), calls=%async_computation.1 | async-start | bytes 16384 | tf_op jit(solution)/shard_map/all_to_all | solution.py:166
  16.7 44.4 %collective-permute-start = (f32[6,1,16,128]{3,2,1,0:T(8,128)}, f32[6,1,16,128]{3,2,1,0:T(8,128)S(1)}, u32[]{:S(2)}, u32[]{:S(2)}) collective-permute-start(f32[6,1,16,128]{3,2,1,0:T(8,128)} %get-tuple-element.27), channel_id=1, source_target_pairs={{0,64},{64,128},{128,192},{1,65},{65,129},{129,193},{2,66},{66,130... | collective-permute-start | bytes 147464 | tf_op jit(solution)/shard_map/ppermute | solution.py:150
  19.6 41.5 %collective-permute-start.1 = (f32[6,1,16,128]{3,2,1,0:T(8,128)}, f32[6,1,16,128]{3,2,1,0:T(8,128)S(1)}, u32[]{:S(2)}, u32[]{:S(2)}) collective-permute-start(f32[6,1,16,128]{3,2,1,0:T(8,128)} %get-tuple-element.28), channel_id=1, source_target_pairs={{64,0},{128,64},{192,128},{65,1},{129,65},{193,129},{66,2},{130,66... | collective-permute-start | bytes 147464 | tf_op jit(solution)/shard_map/ppermute | solution.py:151
  23.5 29.9 %all-to-all-start = ((f32[16,1,384]{2,1,0:T(1,128)}), f32[16,1,384]{2,1,0:T(1,128)S(1)}, u32[]{:S(2)}, u32[]{:S(2)}) async-start(f32[16,1,384]{2,1,0:T(1,128)} %reshape.70), calls=%async_computation | async-start | bytes 49152 | tf_op jit(solution)/shard_map/all_to_all | solution.py:197
  31.2 29.9 %collective-permute-start.2 = (f32[6,8,1,128]{3,2,1,0:T(1,128)S(1)}, f32[6,8,1,128]{3,2,1,0:T(1,128)S(1)}, u32[]{:S(2)}, u32[]{:S(2)}) collective-permute-start(f32[6,8,1,128]{3,2,1,0:T(1,128)S(1)} %copy-done.26), channel_id=1, source_target_pairs={{0,4},{4,8},{8,12},{12,16},{16,20},{20,24},{24,28},{28,32},{32,36}... | collective-permute-start | bytes 73736 | tf_op jit(solution)/shard_map/ppermute | solution.py:150
  34.4 26.7 %collective-permute-start.3 = (f32[6,8,1,128]{3,2,1,0:T(1,128)S(1)}, f32[6,8,1,128]{3,2,1,0:T(1,128)S(1)}, u32[]{:S(2)}, u32[]{:S(2)}) collective-permute-start(f32[6,8,1,128]{3,2,1,0:T(1,128)S(1)} %copy-done.24), channel_id=1, source_target_pairs={{4,0},{8,4},{12,8},{16,12},{20,16},{24,20},{28,24},{32,28},{36,32}... | collective-permute-start | bytes 73736 | tf_op jit(solution)/shard_map/ppermute | solution.py:151
  37.5 12.2 %collective-permute-start.4 = (f32[6,8,16,1]{3,2,1,0:T(8,128)}, f32[6,8,16,1]{3,2,1,0:T(8,128)S(1)}, u32[]{:S(2)}, u32[]{:S(2)}) collective-permute-start(f32[6,8,16,1]{3,2,1,0:T(8,128)} %get-tuple-element.31), channel_id=1, source_target_pairs={{0,1},{1,2},{2,3},{4,5},{5,6},{6,7},{8,9},{9,10},{10,11},{12,13},{... | collective-permute-start | bytes 9224 | tf_op jit(solution)/shard_map/ppermute | solution.py:150
  49.7 11.5 %copy-start = (f32[6,8,16,1]{3,2,1,0:T(8,128)}, f32[6,8,16,1]{3,2,1,0:T(8,128)S(1)}, u32[]{:S(2)}) copy-start(f32[6,8,16,1]{3,2,1,0:T(8,128)S(1)} %collective-permute-done.4.hwl) | copy-start | bytes 9220
  49.7 11.4 %collective-permute-start.5 = (f32[6,8,16,1]{3,2,1,0:T(8,128)}, f32[6,8,16,1]{3,2,1,0:T(8,128)S(1)}, u32[]{:S(2)}, u32[]{:S(2)}) collective-permute-start(f32[6,8,16,1]{3,2,1,0:T(8,128)} %get-tuple-element.32), channel_id=1, source_target_pairs={{1,0},{2,1},{3,2},{5,4},{6,5},{7,6},{9,8},{10,9},{11,10},{13,12},{... | collective-permute-start | bytes 9224 | tf_op jit(solution)/shard_map/ppermute | solution.py:151
  68.3 41.1 %collective-permute-start.6 = (f32[6,1,16,128]{3,2,1,0:T(8,128)}, f32[6,1,16,128]{3,2,1,0:T(8,128)S(1)}, u32[]{:S(2)}, u32[]{:S(2)}) collective-permute-start(f32[6,1,16,128]{3,2,1,0:T(8,128)} %get-tuple-element.35), channel_id=1, source_target_pairs={{0,64},{64,128},{128,192},{1,65},{65,129},{129,193},{2,66},{66,130... | collective-permute-start | bytes 147464 | tf_op jit(solution)/shard_map/ppermute | solution.py:150
  71.2 38.2 %collective-permute-start.7 = (f32[6,1,16,128]{3,2,1,0:T(8,128)}, f32[6,1,16,128]{3,2,1,0:T(8,128)S(1)}, u32[]{:S(2)}, u32[]{:S(2)}) collective-permute-start(f32[6,1,16,128]{3,2,1,0:T(8,128)} %get-tuple-element.36), channel_id=1, source_target_pairs={{64,0},{128,64},{192,128},{65,1},{129,65},{193,129},{66,2},{130,66... | collective-permute-start | bytes 147464 | tf_op jit(solution)/shard_map/ppermute | solution.py:151
  75.1 24.7 %all-to-all-start.2 = ((f32[16,1,384]{2,1,0:T(1,128)}), f32[16,1,384]{2,1,0:T(1,128)S(1)}, u32[]{:S(2)}, u32[]{:S(2)}) async-start(f32[16,1,384]{2,1,0:T(1,128)} %reshape.72), calls=%async_computation.2 | async-start | bytes 49152 | tf_op jit(solution)/shard_map/all_to_all | solution.py:197
  83.2 26.2 %collective-permute-start.8 = (f32[6,8,1,128]{3,2,1,0:T(1,128)S(1)}, f32[6,8,1,128]{3,2,1,0:T(1,128)S(1)}, u32[]{:S(2)}, u32[]{:S(2)}) collective-permute-start(f32[6,8,1,128]{3,2,1,0:T(1,128)S(1)} %copy-done.29), channel_id=1, source_target_pairs={{0,4},{4,8},{8,12},{12,16},{16,20},{20,24},{24,28},{28,32},{32,36}... | collective-permute-start | bytes 73736 | tf_op jit(solution)/shard_map/ppermute | solution.py:150
  86.3 23.1 %collective-permute-start.9 = (f32[6,8,1,128]{3,2,1,0:T(1,128)S(1)}, f32[6,8,1,128]{3,2,1,0:T(1,128)S(1)}, u32[]{:S(2)}, u32[]{:S(2)}) collective-permute-start(f32[6,8,1,128]{3,2,1,0:T(1,128)S(1)} %copy-done.28), channel_id=1, source_target_pairs={{4,0},{8,4},{12,8},{16,12},{20,16},{24,20},{28,24},{32,28},{36,32}... | collective-permute-start | bytes 73736 | tf_op jit(solution)/shard_map/ppermute | solution.py:151
  89.4 8.6 %collective-permute-start.10 = (f32[6,8,16,1]{3,2,1,0:T(8,128)}, f32[6,8,16,1]{3,2,1,0:T(8,128)S(1)}, u32[]{:S(2)}, u32[]{:S(2)}) collective-permute-start(f32[6,8,16,1]{3,2,1,0:T(8,128)} %get-tuple-element.39), channel_id=1, source_target_pairs={{0,1},{1,2},{2,3},{4,5},{5,6},{6,7},{8,9},{9,10},{10,11},{12,13},{... | collective-permute-start | bytes 9224 | tf_op jit(solution)/shard_map/ppermute | solution.py:150
  97.9 11.5 %copy-start.1 = (f32[6,8,16,1]{3,2,1,0:T(8,128)}, f32[6,8,16,1]{3,2,1,0:T(8,128)S(1)}, u32[]{:S(2)}) copy-start(f32[6,8,16,1]{3,2,1,0:T(8,128)S(1)} %collective-permute-done.10.hwl) | copy-start | bytes 9220
  97.9 11.4 %collective-permute-start.11 = (f32[6,8,16,1]{3,2,1,0:T(8,128)}, f32[6,8,16,1]{3,2,1,0:T(8,128)S(1)}, u32[]{:S(2)}, u32[]{:S(2)}) collective-permute-start(f32[6,8,16,1]{3,2,1,0:T(8,128)} %get-tuple-element.40), channel_id=1, source_target_pairs={{1,0},{2,1},{3,2},{5,4},{6,5},{7,6},{9,8},{10,9},{11,10},{13,12},{... | collective-permute-start | bytes 9224 | tf_op jit(solution)/shard_map/ppermute | solution.py:151
  116.6 41.1 %collective-permute-start.12 = (f32[6,1,16,128]{3,2,1,0:T(8,128)}, f32[6,1,16,128]{3,2,1,0:T(8,128)S(1)}, u32[]{:S(2)}, u32[]{:S(2)}) collective-permute-start(f32[6,1,16,128]{3,2,1,0:T(8,128)} %get-tuple-element.43), channel_id=1, source_target_pairs={{0,64},{64,128},{128,192},{1,65},{65,129},{129,193},{2,66},{66,130... | collective-permute-start | bytes 147464 | tf_op jit(solution)/shard_map/ppermute | solution.py:150
  119.5 38.2 %collective-permute-start.13 = (f32[6,1,16,128]{3,2,1,0:T(8,128)}, f32[6,1,16,128]{3,2,1,0:T(8,128)S(1)}, u32[]{:S(2)}, u32[]{:S(2)}) collective-permute-start(f32[6,1,16,128]{3,2,1,0:T(8,128)} %get-tuple-element.44), channel_id=1, source_target_pairs={{64,0},{128,64},{192,128},{65,1},{129,65},{193,129},{66,2},{130,66... | collective-permute-start | bytes 147464 | tf_op jit(solution)/shard_map/ppermute | solution.py:151
  123.4 24.7 %all-to-all-start.3 = ((f32[16,1,384]{2,1,0:T(1,128)}), f32[16,1,384]{2,1,0:T(1,128)S(1)}, u32[]{:S(2)}, u32[]{:S(2)}) async-start(f32[16,1,384]{2,1,0:T(1,128)} %reshape.74), calls=%async_computation.3 | async-start | bytes 49152 | tf_op jit(solution)/shard_map/all_to_all | solution.py:197
  131.4 26.2 %collective-permute-start.14 = (f32[6,8,1,128]{3,2,1,0:T(1,128)S(1)}, f32[6,8,1,128]{3,2,1,0:T(1,128)S(1)}, u32[]{:S(2)}, u32[]{:S(2)}) collective-permute-start(f32[6,8,1,128]{3,2,1,0:T(1,128)S(1)} %copy-done.27), channel_id=1, source_target_pairs={{0,4},{4,8},{8,12},{12,16},{16,20},{20,24},{24,28},{28,32},{32,36}... | collective-permute-start | bytes 73736 | tf_op jit(solution)/shard_map/ppermute | solution.py:150
  134.5 23.1 %collective-permute-start.15 = (f32[6,8,1,128]{3,2,1,0:T(1,128)S(1)}, f32[6,8,1,128]{3,2,1,0:T(1,128)S(1)}, u32[]{:S(2)}, u32[]{:S(2)}) collective-permute-start(f32[6,8,1,128]{3,2,1,0:T(1,128)S(1)} %copy-done.25), channel_id=1, source_target_pairs={{4,0},{8,4},{12,8},{16,12},{20,16},{24,20},{28,24},{32,28},{36,32}... | collective-permute-start | bytes 73736 | tf_op jit(solution)/shard_map/ppermute | solution.py:151
  137.6 8.5 %collective-permute-start.16 = (f32[6,8,16,1]{3,2,1,0:T(8,128)}, f32[6,8,16,1]{3,2,1,0:T(8,128)S(1)}, u32[]{:S(2)}, u32[]{:S(2)}) collective-permute-start(f32[6,8,16,1]{3,2,1,0:T(8,128)} %get-tuple-element.47), channel_id=1, source_target_pairs={{0,1},{1,2},{2,3},{4,5},{5,6},{6,7},{8,9},{9,10},{10,11},{12,13},{... | collective-permute-start | bytes 9224 | tf_op jit(solution)/shard_map/ppermute | solution.py:150
  146.2 11.4 %collective-permute-start.17 = (f32[6,8,16,1]{3,2,1,0:T(8,128)}, f32[6,8,16,1]{3,2,1,0:T(8,128)S(1)}, u32[]{:S(2)}, u32[]{:S(2)}) collective-permute-start(f32[6,8,16,1]{3,2,1,0:T(8,128)} %get-tuple-element.48), channel_id=1, source_target_pairs={{1,0},{2,1},{3,2},{5,4},{6,5},{7,6},{9,8},{10,9},{11,10},{13,12},{... | collective-permute-start | bytes 9224 | tf_op jit(solution)/shard_map/ppermute | solution.py:151
  (28 other events, 101.3 us)
where the time goes:
time: 165 us; the launch traced here: 163 us
  starting transfers between devices  87.1 us (53%)
  waiting for transfers between devices  36.6 us (22%)
  Pallas kernels  21.1 us (13%)
  local copies, waits for them, and re-layouts  13.9 us (8%)
  other arithmetic  3.55 us (2%)
    ppermute x9, starting transfers between devices, exchange(): out.append(lax.ppermute(hi_face, axis, forward))  32.2 us
    all_to_all x3, starting transfers between devices, local(): lax.all_to_all(rows.reshape(n_var, n_span, slots), 'span', split_axis=1,...  23.7 us
    ppermute x9, starting transfers between devices, exchange(): out.append(lax.ppermute(lo_face, axis, backward))  22.1 us
    ppermute x9, waiting for transfers between devices, exchange(): out.append(lax.ppermute(lo_face, axis, backward))  21.5 us
    ppermute x9, waiting for transfers between devices, exchange(): out.append(lax.ppermute(hi_face, axis, forward))  15.1 us
    pallas_call x2, Pallas kernels, local(): step(blk, adj, sensitivity, diagonal, face_coef, *halos, incoming, target...  12.8 us
    all_to_all x1, starting transfers between devices, local(): lax.all_to_all(target_cell.reshape(n_span, slots), 'span', split_axis=0,...  9.1 us
    unnamed x67, local copies, waits for them, and re-layouts  5.16 us
  transfers between devices with their start and end apart: 22, of which 6 were waited for; matrix products, arithmetic and copies ran while one was open for 9% of the time, Pallas kernels for 2%

commit v1 on v0

--- a/solution.py
+++ b/solution.py
@@ -47,15 +47,27 @@
     return jnp.concatenate(out, axis=0)
 
 
+def wall_columns(adj):
+    n_var, nx, ny, nz = adj.shape
+    lo, hi = [], []
+    for v in range(n_var):
+        t = adj[v].reshape(nx * ny, nz).T
+        lo.append(t[0:1])
+        hi.append(t[nz - 1:nz])
+    return jnp.concatenate(lo, axis=0), jnp.concatenate(hi, axis=0)
+
+
 def write_faces(adj, faces):
     c_lo, c_hi, s_lo, s_hi, w_lo, w_hi = faces
     nx, ny, nz = adj.shape[1], adj.shape[2], adj.shape[3]
+    j_idx = lax.broadcasted_iota(jnp.int32, adj.shape, 2)
     c_lo[...] = adj[:, 0:1]
     c_hi[...] = adj[:, nx - 1:nx]
-    s_lo[...] = adj[:, :, 0:1]
-    s_hi[...] = adj[:, :, ny - 1:ny]
-    w_lo[...] = adj[:, :, :, 0:1]
-    w_hi[...] = adj[:, :, :, nz - 1:nz]
+    s_lo[...] = jnp.sum(jnp.where(j_idx == 0, adj, 0.0), axis=2)
+    s_hi[...] = jnp.sum(jnp.where(j_idx == ny - 1, adj, 0.0), axis=2)
+    lo, hi = wall_columns(adj)
+    w_lo[...] = lo
+    w_hi[...] = hi
 
 
 def init_kernel(blk_ref, sens_ref, diag_ref, send_ref, orient_ref, weight_ref,
@@ -74,15 +86,21 @@
     h_c_lo, h_c_hi, h_s_lo, h_s_hi, h_w_lo, h_w_hi = halos
     j_idx = lax.broadcasted_iota(jnp.int32, adj.shape, 2)
     k_idx = lax.broadcasted_iota(jnp.int32, adj.shape, 3)
+    kk = lax.broadcasted_iota(jnp.int32, (nz, rows), 0)
+    wall = []
+    for v in range(n_var):
+        z = jnp.where(kk == 0, h_w_lo[v:v + 1], jnp.where(kk == nz - 1, h_w_hi[v:v + 1], 0.0))
+        wall.append(z.T.reshape(nx, ny, nz))
+    wall = jnp.stack(wall, axis=0)
     up = [
         jnp.concatenate([adj[:, 1:], h_c_hi], axis=1),
-        jnp.where(j_idx == ny - 1, h_s_hi, pltpu.roll(adj, ny - 1, 2)),
-        jnp.where(k_idx == nz - 1, h_w_hi, pltpu.roll(adj, nz - 1, 3)),
+        jnp.where(j_idx == ny - 1, h_s_hi[:, :, None, :], pltpu.roll(adj, ny - 1, 2)),
+        jnp.where(k_idx == nz - 1, wall, pltpu.roll(adj, nz - 1, 3)),
     ]
     lo = [
         jnp.concatenate([h_c_lo, adj[:, :-1]], axis=1),
-        jnp.where(j_idx == 0, h_s_lo, pltpu.roll(adj, 1, 2)),
-        jnp.where(k_idx == 0, h_w_lo, pltpu.roll(adj, 1, 3)),
+        jnp.where(j_idx == 0, h_s_lo[:, :, None, :], pltpu.roll(adj, 1, 2)),
+        jnp.where(k_idx == 0, wall, pltpu.roll(adj, 1, 3)),
     ]
     n_rows = incoming.shape[1]
     cell = target_ref[...]
@@ -135,8 +153,8 @@
 def face_shapes(shape):
     n_var, nx, ny, nz = shape
     c = jax.ShapeDtypeStruct((n_var, 1, ny, nz), F32)
-    s = jax.ShapeDtypeStruct((n_var, nx, 1, nz), F32)
-    w = jax.ShapeDtypeStruct((n_var, nx, ny, 1), F32)
+    s = jax.ShapeDtypeStruct((n_var, nx, nz), F32)
+    w = jax.ShapeDtypeStruct((n_var, nx * ny), F32)
     return [c, c, s, s, w, w]
 
 

time: 165 us -> 140 us (0.85)
  the two profiles are of different devices: /device:TPU:49 before, /device:TPU:41 now
where the time goes in v1:
time: 140 us; the launch traced here: 139 us
  starting transfers between devices  90.2 us (64%)
  Pallas kernels  20 us (14%)
  local copies, waits for them, and re-layouts  13.6 us (10%)
  waiting for transfers between devices  10.5 us (8%)
  other arithmetic  3.35 us (2%)
    ppermute x9, starting transfers between devices, exchange(): out.append(lax.ppermute(hi_face, axis, forward))  36.1 us
    all_to_all x3, starting transfers between devices, local(): lax.all_to_all(rows.reshape(n_var, n_span, slots), 'span', split_axis=1,...  23.7 us
    ppermute x9, starting transfers between devices, exchange(): out.append(lax.ppermute(lo_face, axis, backward))  21.3 us
    pallas_call x2, Pallas kernels, local(): step(blk, adj, sensitivity, diagonal, face_coef, *halos, incoming, target...  11.9 us
    all_to_all x1, starting transfers between devices, local(): lax.all_to_all(target_cell.reshape(n_span, slots), 'span', split_axis=0,...  9.1 us
    ppermute x9, waiting for transfers between devices, exchange(): out.append(lax.ppermute(lo_face, axis, backward))  8.26 us
    unnamed x79, local copies, waits for them, and re-layouts  4.91 us
    pallas_call x1, Pallas kernels, local(): last(blk, adj, sensitivity, diagonal, face_coef, *halos, incoming, target...  4.65 us
  transfers between devices with their start and end apart: 22, of which 6 were waited for; matrix products, arithmetic and copies ran while one was open for 10% of the time, Pallas kernels for 2%

profile of v1, /device:TPU:41, one launch (start us, length us, event | category | flops | bytes accessed | tf_op | source)
XLA Modules:
  0.0 138.8 jit_solution(13423571062174644046)
XLA Ops:
  0.6 9.1 %all-to-all-start.1 = ((s32[16,1,64]{2,1,0:T(1,128)}), s32[16,1,64]{2,1,0:T(1,128)S(1)}, u32[]{:S(2)}, u32[]{:S(2)}) async-start(s32[16,1,64]{2,1,0:T(1,128)} %bitcast.25), calls=%async_computation.1 | async-start | bytes 16384 | tf_op jit(solution)/shard_map/all_to_all | solution.py:184
  13.3 3.4 %shard_map.122 = (f32[6,8,16,128]{3,2,1,0:T(8,128)}, f32[6,1024]{1,0:T(8,128)}, f32[6,1,16,128]{3,2,1,0:T(8,128)}, f32[6,1,16,128]{3,2,1,0:T(8,128)}, f32[6,8,12...) custom-call(f32[288]{0:T(512)} %pad_maximum_fusion.blk_ref, ...), custom_call_target="tpu_custom_call" | custom-call | tf_op jit(solution)/shard_map/pallas_call | solution.py:199
  16.8 3.2 %collective-permute-start = (f32[6,1,16,128]{3,2,1,0:T(8,128)}, f32[6,1,16,128]{3,2,1,0:T(8,128)S(1)}, u32[]{:S(2)}, u32[]{:S(2)}) collective-permute-start(f32[6,1,16,128]{3,2,1,0:T(8,128)} %get-tuple-element.27), channel_id=1, source_target_pairs={{0,64},{64,128},{128,192},{1,65},{65,129},{129,193},{2,66},{66,130... | collective-permute-start | bytes 147464 | tf_op jit(solution)/shard_map/ppermute | solution.py:168
  23.7 7.7 %all-to-all-start = ((f32[16,1,384]{2,1,0:T(1,128)}), f32[16,1,384]{2,1,0:T(1,128)S(1)}, u32[]{:S(2)}, u32[]{:S(2)}) async-start(f32[16,1,384]{2,1,0:T(1,128)} %reshape.70), calls=%async_computation | async-start | bytes 49152 | tf_op jit(solution)/shard_map/all_to_all | solution.py:215
  31.4 3.1 %collective-permute-start.2 = (f32[6,8,128]{2,1,0:T(8,128)S(1)}, f32[6,8,128]{2,1,0:T(8,128)S(1)}, u32[]{:S(2)}, u32[]{:S(2)}) collective-permute-start(f32[6,8,128]{2,1,0:T(8,128)S(1)} %copy-done.26), channel_id=1, source_target_pairs={{0,4},{4,8},{8,12},{12,16},{16,20},{20,24},{24,28},{28,32},{32,36}... | collective-permute-start | bytes 73736 | tf_op jit(solution)/shard_map/ppermute | solution.py:168
  34.5 3.1 %collective-permute-start.3 = (f32[6,8,128]{2,1,0:T(8,128)S(1)}, f32[6,8,128]{2,1,0:T(8,128)S(1)}, u32[]{:S(2)}, u32[]{:S(2)}) collective-permute-start(f32[6,8,128]{2,1,0:T(8,128)S(1)} %copy-done.24), channel_id=1, source_target_pairs={{4,0},{8,4},{12,8},{16,12},{20,16},{24,20},{28,24},{32,28},{36,32}... | collective-permute-start | bytes 73736 | tf_op jit(solution)/shard_map/ppermute | solution.py:169
  37.6 7.2 %collective-permute-start.4 = (f32[6,128]{1,0:T(8,128)S(1)}, f32[6,128]{1,0:T(8,128)S(1)}, u32[]{:S(2)}, u32[]{:S(2)}) collective-permute-start(f32[6,128]{1,0:T(8,128)S(1)} %copy-done.35), channel_id=1, source_target_pairs={{0,1},{1,2},{2,3},{4,5},{5,6},{6,7},{8,9},{9,10},{10,11},{12,13},{... | collective-permute-start | bytes 9224 | tf_op jit(solution)/shard_map/ppermute | solution.py:168
  53.1 6.0 %shard_map.123 = (f32[6,8,16,128]{3,2,1,0:T(8,128)}, f32[6,1024]{1,0:T(8,128)}, f32[6,1,16,128]{3,2,1,0:T(8,128)}, f32[6,1,16,128]{3,2,1,0:T(8,128)}, f32[6,8,12...) custom-call(f32[288]{0:T(512)} %pad_maximum_fusion.blk_ref, ...), custom_call_target="tpu_custom_call" | custom-call | tf_op jit(solution)/shard_map/pallas_call | solution.py:219
  59.1 3.2 %collective-permute-start.6 = (f32[6,1,16,128]{3,2,1,0:T(8,128)}, f32[6,1,16,128]{3,2,1,0:T(8,128)S(1)}, u32[]{:S(2)}, u32[]{:S(2)}) collective-permute-start(f32[6,1,16,128]{3,2,1,0:T(8,128)} %get-tuple-element.35), channel_id=1, source_target_pairs={{0,64},{64,128},{128,192},{1,65},{65,129},{129,193},{2,66},{66,130... | collective-permute-start | bytes 147464 | tf_op jit(solution)/shard_map/ppermute | solution.py:168
  62.3 2.1 %collective-permute-start.7 = (f32[6,1,16,128]{3,2,1,0:T(8,128)}, f32[6,1,16,128]{3,2,1,0:T(8,128)S(1)}, u32[]{:S(2)}, u32[]{:S(2)}) collective-permute-start(f32[6,1,16,128]{3,2,1,0:T(8,128)} %get-tuple-element.36), channel_id=1, source_target_pairs={{64,0},{128,64},{192,128},{65,1},{129,65},{193,129},{66,2},{130,66... | collective-permute-start | bytes 147464 | tf_op jit(solution)/shard_map/ppermute | solution.py:169
  66.0 8.0 %all-to-all-start.2 = ((f32[16,1,384]{2,1,0:T(1,128)}), f32[16,1,384]{2,1,0:T(1,128)S(1)}, u32[]{:S(2)}, u32[]{:S(2)}) async-start(f32[16,1,384]{2,1,0:T(1,128)} %reshape.72), calls=%async_computation.2 | async-start | bytes 49152 | tf_op jit(solution)/shard_map/all_to_all | solution.py:215
  74.0 3.1 %collective-permute-start.8 = (f32[6,8,128]{2,1,0:T(8,128)S(1)}, f32[6,8,128]{2,1,0:T(8,128)S(1)}, u32[]{:S(2)}, u32[]{:S(2)}) collective-permute-start(f32[6,8,128]{2,1,0:T(8,128)S(1)} %copy-done.29), channel_id=1, source_target_pairs={{0,4},{4,8},{8,12},{12,16},{16,20},{20,24},{24,28},{28,32},{32,36}... | collective-permute-start | bytes 73736 | tf_op jit(solution)/shard_map/ppermute | solution.py:168
  77.1 3.1 %collective-permute-start.9 = (f32[6,8,128]{2,1,0:T(8,128)S(1)}, f32[6,8,128]{2,1,0:T(8,128)S(1)}, u32[]{:S(2)}, u32[]{:S(2)}) collective-permute-start(f32[6,8,128]{2,1,0:T(8,128)S(1)} %copy-done.28), channel_id=1, source_target_pairs={{4,0},{8,4},{12,8},{16,12},{20,16},{24,20},{28,24},{32,28},{36,32}... | collective-permute-start | bytes 73736 | tf_op jit(solution)/shard_map/ppermute | solution.py:169
  80.2 6.3 %collective-permute-start.10 = (f32[6,128]{1,0:T(8,128)S(1)}, f32[6,128]{1,0:T(8,128)S(1)}, u32[]{:S(2)}, u32[]{:S(2)}) collective-permute-start(f32[6,128]{1,0:T(8,128)S(1)} %copy-done.34), channel_id=1, source_target_pairs={{0,1},{1,2},{2,3},{4,5},{5,6},{6,7},{8,9},{9,10},{10,11},{12,13},{... | collective-permute-start | bytes 9224 | tf_op jit(solution)/shard_map/ppermute | solution.py:168
  90.6 3.6 %collective-permute-done.11.hwh = f32[6,128]{1,0:T(8,128)S(1)} collective-permute-done((f32[6,128]{1,0:T(8,128)S(1)}, f32[6,128]{1,0:T(8,128)S(1)}, u32[]{:S(2)}, u32[]{:S(2)}) %collective-permute-start.11) | collective-permute-done | bytes 3104 | tf_op jit(solution)/shard_map/ppermute | solution.py:169
  94.9 6.0 %shard_map.124 = (f32[6,8,16,128]{3,2,1,0:T(8,128)}, f32[6,1024]{1,0:T(8,128)}, f32[6,1,16,128]{3,2,1,0:T(8,128)}, f32[6,1,16,128]{3,2,1,0:T(8,128)}, f32[6,8,12...) custom-call(f32[288]{0:T(512)} %pad_maximum_fusion.blk_ref, ...), custom_call_target="tpu_custom_call" | custom-call | tf_op jit(solution)/shard_map/pallas_call | solution.py:219
  100.8 3.2 %collective-permute-start.12 = (f32[6,1,16,128]{3,2,1,0:T(8,128)}, f32[6,1,16,128]{3,2,1,0:T(8,128)S(1)}, u32[]{:S(2)}, u32[]{:S(2)}) collective-permute-start(f32[6,1,16,128]{3,2,1,0:T(8,128)} %get-tuple-element.43), channel_id=1, source_target_pairs={{0,64},{64,128},{128,192},{1,65},{65,129},{129,193},{2,66},{66,130... | collective-permute-start | bytes 147464 | tf_op jit(solution)/shard_map/ppermute | solution.py:168
  104.1 2.1 %collective-permute-start.13 = (f32[6,1,16,128]{3,2,1,0:T(8,128)}, f32[6,1,16,128]{3,2,1,0:T(8,128)S(1)}, u32[]{:S(2)}, u32[]{:S(2)}) collective-permute-start(f32[6,1,16,128]{3,2,1,0:T(8,128)} %get-tuple-element.44), channel_id=1, source_target_pairs={{64,0},{128,64},{192,128},{65,1},{129,65},{193,129},{66,2},{130,66... | collective-permute-start | bytes 147464 | tf_op jit(solution)/shard_map/ppermute | solution.py:169
  107.7 8.0 %all-to-all-start.3 = ((f32[16,1,384]{2,1,0:T(1,128)}), f32[16,1,384]{2,1,0:T(1,128)S(1)}, u32[]{:S(2)}, u32[]{:S(2)}) async-start(f32[16,1,384]{2,1,0:T(1,128)} %reshape.74), calls=%async_computation.3 | async-start | bytes 49152 | tf_op jit(solution)/shard_map/all_to_all | solution.py:215
  115.8 3.1 %collective-permute-start.14 = (f32[6,8,128]{2,1,0:T(8,128)S(1)}, f32[6,8,128]{2,1,0:T(8,128)S(1)}, u32[]{:S(2)}, u32[]{:S(2)}) collective-permute-start(f32[6,8,128]{2,1,0:T(8,128)S(1)} %copy-done.27), channel_id=1, source_target_pairs={{0,4},{4,8},{8,12},{12,16},{16,20},{20,24},{24,28},{28,32},{32,36}... | collective-permute-start | bytes 73736 | tf_op jit(solution)/shard_map/ppermute | solution.py:168
  118.9 3.1 %collective-permute-start.15 = (f32[6,8,128]{2,1,0:T(8,128)S(1)}, f32[6,8,128]{2,1,0:T(8,128)S(1)}, u32[]{:S(2)}, u32[]{:S(2)}) collective-permute-start(f32[6,8,128]{2,1,0:T(8,128)S(1)} %copy-done.25), channel_id=1, source_target_pairs={{4,0},{8,4},{12,8},{16,12},{20,16},{24,20},{28,24},{32,28},{36,32}... | collective-permute-start | bytes 73736 | tf_op jit(solution)/shard_map/ppermute | solution.py:169
  122.0 3.8 %collective-permute-start.16 = (f32[6,128]{1,0:T(8,128)S(1)}, f32[6,128]{1,0:T(8,128)S(1)}, u32[]{:S(2)}, u32[]{:S(2)}) collective-permute-start(f32[6,128]{1,0:T(8,128)S(1)} %copy-done.33), channel_id=1, source_target_pairs={{0,1},{1,2},{2,3},{4,5},{5,6},{6,7},{8,9},{9,10},{10,11},{12,13},{... | collective-permute-start | bytes 9224 | tf_op jit(solution)/shard_map/ppermute | solution.py:168
  129.9 3.6 %collective-permute-done.17.hwh = f32[6,128]{1,0:T(8,128)S(1)} collective-permute-done((f32[6,128]{1,0:T(8,128)S(1)}, f32[6,128]{1,0:T(8,128)S(1)}, u32[]{:S(2)}, u32[]{:S(2)}) %collective-permute-start.17) | collective-permute-done | bytes 3104 | tf_op jit(solution)/shard_map/ppermute | solution.py:169
  134.1 4.7 %shard_map.125 = (f32[6,8,16,128]{3,2,1,0:T(8,128)}, f32[8,16,128]{2,1,0:T(8,128)}) custom-call(f32[288]{0:T(512)} %pad_maximum_fusion.blk_ref, f32[6,8,16,128]{3,2,1,0:T(8,128)} %get-tuple-element.42.adj_ref, f32[6,8,16,128]{3,2,1,0:T(8,128)} %sens_ref.7, f32[6,8,16,128]{3,2,1,0:T(8,128)} %diag_ref.7, f32[3,8,16,128]{3,2,1,0:T(8,128)} %face_ref.5, ...), custom_call_target="tpu_custom_call" | custom-call | tf_op jit(solution)/shard_map/pallas_call | solution.py:222
  (129 shorter events, 28.1 us)
Async XLA Ops:
  0.6 23.0 %all-to-all-start.1 = ((s32[16,1,64]{2,1,0:T(1,128)}), s32[16,1,64]{2,1,0:T(1,128)S(1)}, u32[]{:S(2)}, u32[]{:S(2)}) async-start(s32[16,1,64]{2,1,0:T(1,128)} %bitcast.25), calls=%async_computation.1 | async-start | bytes 16384 | tf_op jit(solution)/shard_map/all_to_all | solution.py:184
  16.8 35.7 %collective-permute-start = (f32[6,1,16,128]{3,2,1,0:T(8,128)}, f32[6,1,16,128]{3,2,1,0:T(8,128)S(1)}, u32[]{:S(2)}, u32[]{:S(2)}) collective-permute-start(f32[6,1,16,128]{3,2,1,0:T(8,128)} %get-tuple-element.27), channel_id=1, source_target_pairs={{0,64},{64,128},{128,192},{1,65},{65,129},{129,193},{2,66},{66,130... | collective-permute-start | bytes 147464 | tf_op jit(solution)/shard_map/ppermute | solution.py:168
  20.0 32.5 %collective-permute-start.1 = (f32[6,1,16,128]{3,2,1,0:T(8,128)}, f32[6,1,16,128]{3,2,1,0:T(8,128)S(1)}, u32[]{:S(2)}, u32[]{:S(2)}) collective-permute-start(f32[6,1,16,128]{3,2,1,0:T(8,128)} %get-tuple-element.28), channel_id=1, source_target_pairs={{64,0},{128,64},{192,128},{65,1},{129,65},{193,129},{66,2},{130,66... | collective-permute-start | bytes 147464 | tf_op jit(solution)/shard_map/ppermute | solution.py:169
  23.7 25.7 %all-to-all-start = ((f32[16,1,384]{2,1,0:T(1,128)}), f32[16,1,384]{2,1,0:T(1,128)S(1)}, u32[]{:S(2)}, u32[]{:S(2)}) async-start(f32[16,1,384]{2,1,0:T(1,128)} %reshape.70), calls=%async_computation | async-start | bytes 49152 | tf_op jit(solution)/shard_map/all_to_all | solution.py:215
  31.4 21.1 %collective-permute-start.2 = (f32[6,8,128]{2,1,0:T(8,128)S(1)}, f32[6,8,128]{2,1,0:T(8,128)S(1)}, u32[]{:S(2)}, u32[]{:S(2)}) collective-permute-start(f32[6,8,128]{2,1,0:T(8,128)S(1)} %copy-done.26), channel_id=1, source_target_pairs={{0,4},{4,8},{8,12},{12,16},{16,20},{20,24},{24,28},{28,32},{32,36}... | collective-permute-start | bytes 73736 | tf_op jit(solution)/shard_map/ppermute | solution.py:168
  34.5 18.0 %collective-permute-start.3 = (f32[6,8,128]{2,1,0:T(8,128)S(1)}, f32[6,8,128]{2,1,0:T(8,128)S(1)}, u32[]{:S(2)}, u32[]{:S(2)}) collective-permute-start(f32[6,8,128]{2,1,0:T(8,128)S(1)} %copy-done.24), channel_id=1, source_target_pairs={{4,0},{8,4},{12,8},{16,12},{20,16},{24,20},{28,24},{32,28},{36,32}... | collective-permute-start | bytes 73736 | tf_op jit(solution)/shard_map/ppermute | solution.py:169
  37.6 7.9 %collective-permute-start.4 = (f32[6,128]{1,0:T(8,128)S(1)}, f32[6,128]{1,0:T(8,128)S(1)}, u32[]{:S(2)}, u32[]{:S(2)}) collective-permute-start(f32[6,128]{1,0:T(8,128)S(1)} %copy-done.35), channel_id=1, source_target_pairs={{0,1},{1,2},{2,3},{4,5},{5,6},{6,7},{8,9},{9,10},{10,11},{12,13},{... | collective-permute-start | bytes 9224 | tf_op jit(solution)/shard_map/ppermute | solution.py:168
  45.5 7.0 %collective-permute-start.5 = (f32[6,128]{1,0:T(8,128)S(1)}, f32[6,128]{1,0:T(8,128)S(1)}, u32[]{:S(2)}, u32[]{:S(2)}) collective-permute-start(f32[6,128]{1,0:T(8,128)S(1)} %copy-done.30), channel_id=1, source_target_pairs={{1,0},{2,1},{3,2},{5,4},{6,5},{7,6},{9,8},{10,9},{11,10},{13,12},{... | collective-permute-start | bytes 9224 | tf_op jit(solution)/shard_map/ppermute | solution.py:169
  59.1 35.1 %collective-permute-start.6 = (f32[6,1,16,128]{3,2,1,0:T(8,128)}, f32[6,1,16,128]{3,2,1,0:T(8,128)S(1)}, u32[]{:S(2)}, u32[]{:S(2)}) collective-permute-start(f32[6,1,16,128]{3,2,1,0:T(8,128)} %get-tuple-element.35), channel_id=1, source_target_pairs={{0,64},{64,128},{128,192},{1,65},{65,129},{129,193},{2,66},{66,130... | collective-permute-start | bytes 147464 | tf_op jit(solution)/shard_map/ppermute | solution.py:168
  62.3 32.0 %collective-permute-start.7 = (f32[6,1,16,128]{3,2,1,0:T(8,128)}, f32[6,1,16,128]{3,2,1,0:T(8,128)S(1)}, u32[]{:S(2)}, u32[]{:S(2)}) collective-permute-start(f32[6,1,16,128]{3,2,1,0:T(8,128)} %get-tuple-element.36), channel_id=1, source_target_pairs={{64,0},{128,64},{192,128},{65,1},{129,65},{193,129},{66,2},{130,66... | collective-permute-start | bytes 147464 | tf_op jit(solution)/shard_map/ppermute | solution.py:169
  65.3 14.9 %copy-start.34 = (f32[6,128]{1,0:T(8,128)S(1)}, f32[6,128]{1,0:T(8,128)}, u32[]{:S(2)}) copy-start(f32[6,128]{1,0:T(8,128)} %get-tuple-element.39) | copy-start | bytes 9220
  66.0 23.2 %all-to-all-start.2 = ((f32[16,1,384]{2,1,0:T(1,128)}), f32[16,1,384]{2,1,0:T(1,128)S(1)}, u32[]{:S(2)}, u32[]{:S(2)}) async-start(f32[16,1,384]{2,1,0:T(1,128)} %reshape.72), calls=%async_computation.2 | async-start | bytes 49152 | tf_op jit(solution)/shard_map/all_to_all | solution.py:215
  74.0 20.2 %collective-permute-start.8 = (f32[6,8,128]{2,1,0:T(8,128)S(1)}, f32[6,8,128]{2,1,0:T(8,128)S(1)}, u32[]{:S(2)}, u32[]{:S(2)}) collective-permute-start(f32[6,8,128]{2,1,0:T(8,128)S(1)} %copy-done.29), channel_id=1, source_target_pairs={{0,4},{4,8},{8,12},{12,16},{16,20},{20,24},{24,28},{28,32},{32,36}... | collective-permute-start | bytes 73736 | tf_op jit(solution)/shard_map/ppermute | solution.py:168
  77.1 17.1 %collective-permute-start.9 = (f32[6,8,128]{2,1,0:T(8,128)S(1)}, f32[6,8,128]{2,1,0:T(8,128)S(1)}, u32[]{:S(2)}, u32[]{:S(2)}) collective-permute-start(f32[6,8,128]{2,1,0:T(8,128)S(1)} %copy-done.28), channel_id=1, source_target_pairs={{4,0},{8,4},{12,8},{16,12},{20,16},{24,20},{28,24},{32,28},{36,32}... | collective-permute-start | bytes 73736 | tf_op jit(solution)/shard_map/ppermute | solution.py:169
  80.2 7.0 %collective-permute-start.10 = (f32[6,128]{1,0:T(8,128)S(1)}, f32[6,128]{1,0:T(8,128)S(1)}, u32[]{:S(2)}, u32[]{:S(2)}) collective-permute-start(f32[6,128]{1,0:T(8,128)S(1)} %copy-done.34), channel_id=1, source_target_pairs={{0,1},{1,2},{2,3},{4,5},{5,6},{6,7},{8,9},{9,10},{10,11},{12,13},{... | collective-permute-start | bytes 9224 | tf_op jit(solution)/shard_map/ppermute | solution.py:168
  87.2 7.0 %collective-permute-start.11 = (f32[6,128]{1,0:T(8,128)S(1)}, f32[6,128]{1,0:T(8,128)S(1)}, u32[]{:S(2)}, u32[]{:S(2)}) collective-permute-start(f32[6,128]{1,0:T(8,128)S(1)} %copy-done.32), channel_id=1, source_target_pairs={{1,0},{2,1},{3,2},{5,4},{6,5},{7,6},{9,8},{10,9},{11,10},{13,12},{... | collective-permute-start | bytes 9224 | tf_op jit(solution)/shard_map/ppermute | solution.py:169
  100.8 32.6 %collective-permute-start.12 = (f32[6,1,16,128]{3,2,1,0:T(8,128)}, f32[6,1,16,128]{3,2,1,0:T(8,128)S(1)}, u32[]{:S(2)}, u32[]{:S(2)}) collective-permute-start(f32[6,1,16,128]{3,2,1,0:T(8,128)} %get-tuple-element.43), channel_id=1, source_target_pairs={{0,64},{64,128},{128,192},{1,65},{65,129},{129,193},{2,66},{66,130... | collective-permute-start | bytes 147464 | tf_op jit(solution)/shard_map/ppermute | solution.py:168
  104.1 29.5 %collective-permute-start.13 = (f32[6,1,16,128]{3,2,1,0:T(8,128)}, f32[6,1,16,128]{3,2,1,0:T(8,128)S(1)}, u32[]{:S(2)}, u32[]{:S(2)}) collective-permute-start(f32[6,1,16,128]{3,2,1,0:T(8,128)} %get-tuple-element.44), channel_id=1, source_target_pairs={{64,0},{128,64},{192,128},{65,1},{129,65},{193,129},{66,2},{130,66... | collective-permute-start | bytes 147464 | tf_op jit(solution)/shard_map/ppermute | solution.py:169
  107.0 14.9 %copy-start.33 = (f32[6,128]{1,0:T(8,128)S(1)}, f32[6,128]{1,0:T(8,128)}, u32[]{:S(2)}) copy-start(f32[6,128]{1,0:T(8,128)} %get-tuple-element.47) | copy-start | bytes 9220
  107.7 20.7 %all-to-all-start.3 = ((f32[16,1,384]{2,1,0:T(1,128)}), f32[16,1,384]{2,1,0:T(1,128)S(1)}, u32[]{:S(2)}, u32[]{:S(2)}) async-start(f32[16,1,384]{2,1,0:T(1,128)} %reshape.74), calls=%async_computation.3 | async-start | bytes 49152 | tf_op jit(solution)/shard_map/all_to_all | solution.py:215
  115.8 17.7 %collective-permute-start.14 = (f32[6,8,128]{2,1,0:T(8,128)S(1)}, f32[6,8,128]{2,1,0:T(8,128)S(1)}, u32[]{:S(2)}, u32[]{:S(2)}) collective-permute-start(f32[6,8,128]{2,1,0:T(8,128)S(1)} %copy-done.27), channel_id=1, source_target_pairs={{0,4},{4,8},{8,12},{12,16},{16,20},{20,24},{24,28},{28,32},{32,36}... | collective-permute-start | bytes 73736 | tf_op jit(solution)/shard_map/ppermute | solution.py:168
  118.9 14.6 %collective-permute-start.15 = (f32[6,8,128]{2,1,0:T(8,128)S(1)}, f32[6,8,128]{2,1,0:T(8,128)S(1)}, u32[]{:S(2)}, u32[]{:S(2)}) collective-permute-start(f32[6,8,128]{2,1,0:T(8,128)S(1)} %copy-done.25), channel_id=1, source_target_pairs={{4,0},{8,4},{12,8},{16,12},{20,16},{24,20},{28,24},{32,28},{36,32}... | collective-permute-start | bytes 73736 | tf_op jit(solution)/shard_map/ppermute | solution.py:169
  122.0 4.5 %collective-permute-start.16 = (f32[6,128]{1,0:T(8,128)S(1)}, f32[6,128]{1,0:T(8,128)S(1)}, u32[]{:S(2)}, u32[]{:S(2)}) collective-permute-start(f32[6,128]{1,0:T(8,128)S(1)} %copy-done.33), channel_id=1, source_target_pairs={{0,1},{1,2},{2,3},{4,5},{5,6},{6,7},{8,9},{9,10},{10,11},{12,13},{... | collective-permute-start | bytes 9224 | tf_op jit(solution)/shard_map/ppermute | solution.py:168
  126.5 7.0 %collective-permute-start.17 = (f32[6,128]{1,0:T(8,128)S(1)}, f32[6,128]{1,0:T(8,128)S(1)}, u32[]{:S(2)}, u32[]{:S(2)}) collective-permute-start(f32[6,128]{1,0:T(8,128)S(1)} %copy-done.31), channel_id=1, source_target_pairs={{1,0},{2,1},{3,2},{5,4},{6,5},{7,6},{9,8},{10,9},{11,10},{13,12},{... | collective-permute-start | bytes 9224 | tf_op jit(solution)/shard_map/ppermute | solution.py:169
  (34 other events, 149.0 us)

commit v2 on v1

--- a/solution.py
+++ b/solution.py
@@ -44,7 +44,19 @@
             first = a if first is None else first + a
             second = b if second is None else second + b
         out.append(jnp.where(orient == 1, second, first) * weight)
-    return jnp.concatenate(out, axis=0)
+    return out
+
+
+def to_chunks(rows_ref, pieces, slots):
+    n_dest = rows_ref.shape[0]
+    for t in range(n_dest):
+        rows_ref[t] = jnp.concatenate([p[:, t * slots:(t + 1) * slots] for p in pieces], axis=1)
+
+
+def from_chunks(inc, count, slots):
+    n_src = inc.shape[0]
+    return [jnp.concatenate([inc[s][:, v * slots:(v + 1) * slots] for s in range(n_src)], axis=1)
+            for v in range(count)]
 
 
 def wall_columns(adj):
@@ -70,17 +82,19 @@
     w_hi[...] = hi
 
 
-def init_kernel(blk_ref, sens_ref, diag_ref, send_ref, orient_ref, weight_ref,
+def init_kernel(blk_ref, sens_ref, diag_ref, send_ref, orient_ref, weight_ref, tgt_ref,
                 adj_ref, rows_ref, c_lo, c_hi, s_lo, s_hi, w_lo, w_hi):
     n_var = sens_ref.shape[0]
     lanes = sens_ref.shape[3]
+    slots = send_ref.shape[1] // rows_ref.shape[0]
     adj = sens_ref[...] / diag_ref[...]
     adj_ref[...] = adj
     write_faces(adj, (c_lo, c_hi, s_lo, s_hi, w_lo, w_hi))
-    rows_ref[...] = gather_rows(adj, send_ref, orient_ref, weight_ref, blk_ref, n_var, lanes)
-
-
-def sweep_body(blk, adj, sens, diag, face, halos, incoming, target_ref):
+    pieces = gather_rows(adj, send_ref, orient_ref, weight_ref, blk_ref, n_var, lanes)
+    to_chunks(rows_ref, pieces + [tgt_ref[...].astype(F32)], slots)
+
+
+def sweep_body(blk, adj, sens, diag, face, halos, incoming, cell):
     n_var, nx, ny, nz = adj.shape
     rows = nx * ny
     h_c_lo, h_c_hi, h_s_lo, h_s_hi, h_w_lo, h_w_hi = halos
@@ -103,7 +117,6 @@
         jnp.where(k_idx == 0, wall, pltpu.roll(adj, 1, 3)),
     ]
     n_rows = incoming.shape[1]
-    cell = target_ref[...]
     row_of = cell // nz
     lane_of = cell % nz
     row_hot = (lax.broadcasted_iota(jnp.int32, (rows, n_rows), 0) == row_of).astype(F32)
@@ -129,23 +142,40 @@
 
 def sweep_kernel(blk_ref, adj_ref, sens_ref, diag_ref, face_ref, hcl, hch, hsl, hsh, hwl, hwh,
                  inc_ref, tgt_ref, send_ref, orient_ref, weight_ref,
-                 out_ref, rows_ref, c_lo, c_hi, s_lo, s_hi, w_lo, w_hi):
+                 out_ref, rows_ref, tgt_out, c_lo, c_hi, s_lo, s_hi, w_lo, w_hi):
     n_var = adj_ref.shape[0]
     lanes = adj_ref.shape[3]
+    slots = send_ref.shape[1] // rows_ref.shape[0]
     halos = (hcl[...], hch[...], hsl[...], hsh[...], hwl[...], hwh[...])
+    inc = inc_ref[...]
+    if tgt_ref is None:
+        got = from_chunks(inc, n_var + 1, slots)
+        cell = got[n_var].astype(jnp.int32)
+    else:
+        got = from_chunks(inc, n_var, slots)
+        cell = tgt_ref[...]
+    tgt_out[...] = cell
     new = sweep_body(blk_ref, adj_ref[...], sens_ref[...], diag_ref[...], face_ref[...], halos,
-                     inc_ref[...], tgt_ref)
+                     jnp.concatenate(got[:n_var], axis=0), cell)
     out_ref[...] = new
     write_faces(new, (c_lo, c_hi, s_lo, s_hi, w_lo, w_hi))
-    rows_ref[...] = gather_rows(new, send_ref, orient_ref, weight_ref, blk_ref, n_var, lanes)
+    to_chunks(rows_ref, gather_rows(new, send_ref, orient_ref, weight_ref, blk_ref, n_var, lanes), slots)
+
+
+def first_sweep_kernel(blk_ref, adj_ref, sens_ref, diag_ref, face_ref, hcl, hch, hsl, hsh, hwl, hwh,
+                       inc_ref, send_ref, orient_ref, weight_ref, *outs):
+    sweep_kernel(blk_ref, adj_ref, sens_ref, diag_ref, face_ref, hcl, hch, hsl, hsh, hwl, hwh,
+                 inc_ref, None, send_ref, orient_ref, weight_ref, *outs)
 
 
 def last_kernel(blk_ref, adj_ref, sens_ref, diag_ref, face_ref, hcl, hch, hsl, hsh, hwl, hwh,
                 inc_ref, tgt_ref, prod_ref, out_ref, grad_ref):
     n_var = adj_ref.shape[0]
+    slots = inc_ref.shape[2] // n_var
     halos = (hcl[...], hch[...], hsl[...], hsh[...], hwl[...], hwh[...])
+    got = from_chunks(inc_ref[...], n_var, slots)
     new = sweep_body(blk_ref, adj_ref[...], sens_ref[...], diag_ref[...], face_ref[...], halos,
-                     inc_ref[...], tgt_ref)
+                     jnp.concatenate(got, axis=0), tgt_ref[...])
     out_ref[...] = new
     grad_ref[...] = prod_ref[...] * new[n_var - 1]
 
@@ -181,28 +211,34 @@
     send_row = send_cell.reshape(1, n_rows)
     orient_row = orient.reshape(1, n_rows)
     weight_row = iface_weight.reshape(1, n_rows)
-    target_row = lax.all_to_all(
-        target_cell.reshape(n_span, slots), "span", split_axis=0, concat_axis=0, tiled=True
-    ).reshape(1, n_rows)
+    target_row = target_cell.reshape(1, n_rows)
 
     vmem = pl.BlockSpec(memory_space=pltpu.VMEM)
     smem = pl.BlockSpec(memory_space=pltpu.SMEM)
     adj_sds = jax.ShapeDtypeStruct(shape, F32)
-    rows_sds = jax.ShapeDtypeStruct((n_var, n_rows), F32)
+    tgt_sds = jax.ShapeDtypeStruct((1, n_rows), jnp.int32)
+    first_rows = jax.ShapeDtypeStruct((n_span, 1, (n_var + 1) * slots), F32)
+    rows_sds = jax.ShapeDtypeStruct((n_span, 1, n_var * slots), F32)
 
     init = pl.pallas_call(
         init_kernel,
-        out_shape=[adj_sds, rows_sds] + face_shapes(shape),
-        in_specs=[smem] + [vmem] * 5,
+        out_shape=[adj_sds, first_rows] + face_shapes(shape),
+        in_specs=[smem] + [vmem] * 6,
         out_specs=[vmem] * 8,
     )
-    adj, rows, *faces = init(blk, sensitivity, diagonal, send_row, orient_row, weight_row)
-
+    adj, rows, *faces = init(blk, sensitivity, diagonal, send_row, orient_row, weight_row, target_row)
+
+    first = pl.pallas_call(
+        first_sweep_kernel,
+        out_shape=[adj_sds, rows_sds, tgt_sds] + face_shapes(shape),
+        in_specs=[smem] + [vmem] * 14,
+        out_specs=[vmem] * 9,
+    )
     step = pl.pallas_call(
         sweep_kernel,
-        out_shape=[adj_sds, rows_sds] + face_shapes(shape),
+        out_shape=[adj_sds, rows_sds, tgt_sds] + face_shapes(shape),
         in_specs=[smem] + [vmem] * 15,
-        out_specs=[vmem] * 8,
+        out_specs=[vmem] * 9,
     )
     last = pl.pallas_call(
         last_kernel,
@@ -210,17 +246,19 @@
         in_specs=[smem] + [vmem] * 13,
         out_specs=[vmem] * 2,
     )
+    received = None
     for sweep in range(SWEEPS):
         halos = exchange(faces)
-        incoming = lax.all_to_all(
-            rows.reshape(n_var, n_span, slots), "span", split_axis=1, concat_axis=1, tiled=True
-        ).reshape(n_var, n_rows)
-        if sweep < SWEEPS - 1:
-            adj, rows, *faces = step(blk, adj, sensitivity, diagonal, face_coef, *halos, incoming,
-                                     target_row, send_row, orient_row, weight_row)
+        incoming = lax.all_to_all(rows, "span", split_axis=0, concat_axis=0, tiled=True)
+        if sweep == 0:
+            adj, rows, received, *faces = first(blk, adj, sensitivity, diagonal, face_coef, *halos,
+                                                incoming, send_row, orient_row, weight_row)
+        elif sweep < SWEEPS - 1:
+            adj, rows, received, *faces = step(blk, adj, sensitivity, diagonal, face_coef, *halos,
+                                               incoming, received, send_row, orient_row, weight_row)
         else:
             adj, gradient = last(blk, adj, sensitivity, diagonal, face_coef, *halos, incoming,
-                                 target_row, production)
+                                 received, production)
     return (adj, gradient)
 
 

time: 140 us -> 127 us (0.907)
  the two profiles are of different devices: /device:TPU:41 before, /device:TPU:49 now
where the time goes in v2:
time: 127 us; the launch traced here: 125 us
  starting transfers between devices  79.1 us (62%)
  Pallas kernels  20.7 us (16%)
  waiting for transfers between devices  17.6 us (14%)
  local copies, waits for them, and re-layouts  6.23 us (5%)
    ppermute x9, starting transfers between devices, exchange(): out.append(lax.ppermute(hi_face, axis, forward))  31.9 us
    all_to_all x3, starting transfers between devices, local(): lax.all_to_all(rows, 'span', split_axis=0, concat_axis=0, tiled=True)  25.1 us
    ppermute x9, starting transfers between devices, exchange(): out.append(lax.ppermute(lo_face, axis, backward))  22.1 us
    ppermute x9, waiting for transfers between devices, exchange(): out.append(lax.ppermute(lo_face, axis, backward))  15.2 us
    pallas_call x1, Pallas kernels, local(): first(blk, adj, sensitivity, diagonal, face_coef, *halos, incoming, send_...  6.29 us
    pallas_call x1, Pallas kernels, local(): step(blk, adj, sensitivity, diagonal, face_coef, *halos, incoming, receiv...  6.22 us
    pallas_call x1, Pallas kernels, local(): last(blk, adj, sensitivity, diagonal, face_coef, *halos, incoming, receiv...  4.72 us
    pallas_call x1, Pallas kernels, local(): init(blk, sensitivity, diagonal, send_row, orient_row, weight_row, target...  3.49 us
  transfers between devices with their start and end apart: 21, of which 6 were waited for; matrix products, arithmetic and copies ran while one was open for 0% of the time, Pallas kernels for 0%

profile of v2, /device:TPU:49, one launch (start us, length us, event | category | flops | bytes accessed | tf_op | source)
XLA Modules:
  0.0 125.5 jit_solution(4512074470337179360)
XLA Ops:
  5.7 3.5 %shard_map.122 = (f32[6,8,16,128]{3,2,1,0:T(8,128)}, f32[16,1,448]{2,1,0:T(1,128)}, f32[6,1,16,128]{3,2,1,0:T(8,128)}, f32[6,1,16,128]{3,2,1,0:T(8,128)}, f32[6,...) custom-call(f32[288]{0:T(512)} %pad_maximum_fusion.blk_ref, ...), custom_call_target="tpu_custom_call" | custom-call | tf_op jit(solution)/shard_map/pallas_call | solution.py:229
  9.2 9.1 %all-to-all-start = ((f32[16,1,448]{2,1,0:T(1,128)}), f32[16,1,448]{2,1,0:T(1,128)S(1)}, u32[]{:S(2)}, u32[]{:S(2)}) async-start(f32[16,1,448]{2,1,0:T(1,128)} %get-tuple-element.35), calls=%async_computation | async-start | bytes 65536 | tf_op jit(solution)/shard_map/all_to_all | solution.py:252
  18.3 2.9 %collective-permute-start = (f32[6,1,16,128]{3,2,1,0:T(8,128)}, f32[6,1,16,128]{3,2,1,0:T(8,128)S(1)}, u32[]{:S(2)}, u32[]{:S(2)}) collective-permute-start(f32[6,1,16,128]{3,2,1,0:T(8,128)} %get-tuple-element.29), channel_id=1, source_target_pairs={{0,64},{64,128},{128,192},{1,65},{65,129},{129,193},{2,66},{66,130... | collective-permute-start | bytes 147464 | tf_op jit(solution)/shard_map/ppermute | solution.py:198
  21.2 2.4 %collective-permute-start.1 = (f32[6,1,16,128]{3,2,1,0:T(8,128)S(1)}, f32[6,1,16,128]{3,2,1,0:T(8,128)S(1)}, u32[]{:S(2)}, u32[]{:S(2)}) collective-permute-start(f32[6,1,16,128]{3,2,1,0:T(8,128)S(1)} %copy-done.27), channel_id=1, source_target_pairs={{64,0},{128,64},{192,128},{65,1},{129,65},{193,129},{66,2},{130,66... | collective-permute-start | bytes 147464 | tf_op jit(solution)/shard_map/ppermute | solution.py:199
  23.6 3.1 %collective-permute-start.2 = (f32[6,8,128]{2,1,0:T(8,128)}, f32[6,8,128]{2,1,0:T(8,128)S(1)}, u32[]{:S(2)}, u32[]{:S(2)}) collective-permute-start(f32[6,8,128]{2,1,0:T(8,128)} %get-tuple-element.31), channel_id=1, source_target_pairs={{0,4},{4,8},{8,12},{12,16},{16,20},{20,24},{24,28},{28,32},{32,36}... | collective-permute-start | bytes 73736 | tf_op jit(solution)/shard_map/ppermute | solution.py:198
  26.7 3.1 %collective-permute-start.3 = (f32[6,8,128]{2,1,0:T(8,128)S(1)}, f32[6,8,128]{2,1,0:T(8,128)S(1)}, u32[]{:S(2)}, u32[]{:S(2)}) collective-permute-start(f32[6,8,128]{2,1,0:T(8,128)S(1)} %copy-done.32), channel_id=1, source_target_pairs={{4,0},{8,4},{12,8},{16,12},{20,16},{24,20},{28,24},{32,28},{36,32}... | collective-permute-start | bytes 73736 | tf_op jit(solution)/shard_map/ppermute | solution.py:199
  29.8 6.6 %collective-permute-start.4 = (f32[6,128]{1,0:T(8,128)}, f32[6,128]{1,0:T(8,128)S(1)}, u32[]{:S(2)}, u32[]{:S(2)}) collective-permute-start(f32[6,128]{1,0:T(8,128)} %get-tuple-element.33), channel_id=1, source_target_pairs={{0,1},{1,2},{2,3},{4,5},{5,6},{6,7},{8,9},{9,10},{10,11},{12,13},{... | collective-permute-start | bytes 9224 | tf_op jit(solution)/shard_map/ppermute | solution.py:198
  39.3 5.0 %collective-permute-done.5.hwh = f32[6,128]{1,0:T(8,128)S(1)} collective-permute-done((f32[6,128]{1,0:T(8,128)S(1)}, f32[6,128]{1,0:T(8,128)S(1)}, u32[]{:S(2)}, u32[]{:S(2)}) %collective-permute-start.5) | collective-permute-done | bytes 3104 | tf_op jit(solution)/shard_map/ppermute | solution.py:199
  45.0 6.3 %shard_map.123 = (f32[6,8,16,128]{3,2,1,0:T(8,128)}, f32[16,1,384]{2,1,0:T(1,128)}, s32[1,1024]{1,0:T(1,128)}, f32[6,1,16,128]{3,2,1,0:T(8,128)}, f32[6,1,16,128...) custom-call(f32[288]{0:T(512)} %pad_maximum_fusion.blk_ref, ...), custom_call_target="tpu_custom_call" | custom-call | tf_op jit(solution)/shard_map/pallas_call | solution.py:254
  51.3 2.9 %collective-permute-start.6 = (f32[6,1,16,128]{3,2,1,0:T(8,128)}, f32[6,1,16,128]{3,2,1,0:T(8,128)S(1)}, u32[]{:S(2)}, u32[]{:S(2)}) collective-permute-start(f32[6,1,16,128]{3,2,1,0:T(8,128)} %get-tuple-element.37), channel_id=1, source_target_pairs={{0,64},{64,128},{128,192},{1,65},{65,129},{129,193},{2,66},{66,130... | collective-permute-start | bytes 147464 | tf_op jit(solution)/shard_map/ppermute | solution.py:198
  56.6 8.0 %all-to-all-start.1 = ((f32[16,1,384]{2,1,0:T(1,128)}), f32[16,1,384]{2,1,0:T(1,128)S(1)}, u32[]{:S(2)}, u32[]{:S(2)}) async-start(f32[16,1,384]{2,1,0:T(1,128)} %get-tuple-element.43), calls=%async_computation.1 | async-start | bytes 49152 | tf_op jit(solution)/shard_map/all_to_all | solution.py:252
  64.7 3.1 %collective-permute-start.8 = (f32[6,8,128]{2,1,0:T(8,128)S(1)}, f32[6,8,128]{2,1,0:T(8,128)S(1)}, u32[]{:S(2)}, u32[]{:S(2)}) collective-permute-start(f32[6,8,128]{2,1,0:T(8,128)S(1)} %copy-done.31), channel_id=1, source_target_pairs={{0,4},{4,8},{8,12},{12,16},{16,20},{20,24},{24,28},{28,32},{32,36}... | collective-permute-start | bytes 73736 | tf_op jit(solution)/shard_map/ppermute | solution.py:198
  67.8 3.1 %collective-permute-start.9 = (f32[6,8,128]{2,1,0:T(8,128)S(1)}, f32[6,8,128]{2,1,0:T(8,128)S(1)}, u32[]{:S(2)}, u32[]{:S(2)}) collective-permute-start(f32[6,8,128]{2,1,0:T(8,128)S(1)} %copy-done.30), channel_id=1, source_target_pairs={{4,0},{8,4},{12,8},{16,12},{20,16},{24,20},{28,24},{32,28},{36,32}... | collective-permute-start | bytes 73736 | tf_op jit(solution)/shard_map/ppermute | solution.py:199
  70.9 3.6 %collective-permute-start.10 = (f32[6,128]{1,0:T(8,128)S(1)}, f32[6,128]{1,0:T(8,128)S(1)}, u32[]{:S(2)}, u32[]{:S(2)}) collective-permute-start(f32[6,128]{1,0:T(8,128)S(1)} %copy-done.36), channel_id=1, source_target_pairs={{0,1},{1,2},{2,3},{4,5},{5,6},{6,7},{8,9},{9,10},{10,11},{12,13},{... | collective-permute-start | bytes 9224 | tf_op jit(solution)/shard_map/ppermute | solution.py:198
  77.2 5.0 %collective-permute-done.11.hwh = f32[6,128]{1,0:T(8,128)S(1)} collective-permute-done((f32[6,128]{1,0:T(8,128)S(1)}, f32[6,128]{1,0:T(8,128)S(1)}, u32[]{:S(2)}, u32[]{:S(2)}) %collective-permute-start.11) | collective-permute-done | bytes 3104 | tf_op jit(solution)/shard_map/ppermute | solution.py:199
  82.9 6.2 %shard_map.124 = (f32[6,8,16,128]{3,2,1,0:T(8,128)}, f32[16,1,384]{2,1,0:T(1,128)}, s32[1,1024]{1,0:T(1,128)}, f32[6,1,16,128]{3,2,1,0:T(8,128)}, f32[6,1,16,128...) custom-call(f32[288]{0:T(512)} %pad_maximum_fusion.blk_ref, ...), custom_call_target="tpu_custom_call" | custom-call | tf_op jit(solution)/shard_map/pallas_call | solution.py:257
  89.1 2.9 %collective-permute-start.12 = (f32[6,1,16,128]{3,2,1,0:T(8,128)}, f32[6,1,16,128]{3,2,1,0:T(8,128)S(1)}, u32[]{:S(2)}, u32[]{:S(2)}) collective-permute-start(f32[6,1,16,128]{3,2,1,0:T(8,128)} %get-tuple-element.46), channel_id=1, source_target_pairs={{0,64},{64,128},{128,192},{1,65},{65,129},{129,193},{2,66},{66,130... | collective-permute-start | bytes 147464 | tf_op jit(solution)/shard_map/ppermute | solution.py:198
  92.1 2.4 %collective-permute-start.13 = (f32[6,1,16,128]{3,2,1,0:T(8,128)}, f32[6,1,16,128]{3,2,1,0:T(8,128)S(1)}, u32[]{:S(2)}, u32[]{:S(2)}) collective-permute-start(f32[6,1,16,128]{3,2,1,0:T(8,128)} %get-tuple-element.47), channel_id=1, source_target_pairs={{64,0},{128,64},{192,128},{65,1},{129,65},{193,129},{66,2},{130,66... | collective-permute-start | bytes 147464 | tf_op jit(solution)/shard_map/ppermute | solution.py:199
  94.5 8.0 %all-to-all-start.2 = ((f32[16,1,384]{2,1,0:T(1,128)}), f32[16,1,384]{2,1,0:T(1,128)S(1)}, u32[]{:S(2)}, u32[]{:S(2)}) async-start(f32[16,1,384]{2,1,0:T(1,128)} %get-tuple-element.52), calls=%async_computation.2 | async-start | bytes 49152 | tf_op jit(solution)/shard_map/all_to_all | solution.py:252
  102.5 3.1 %collective-permute-start.14 = (f32[6,8,128]{2,1,0:T(8,128)S(1)}, f32[6,8,128]{2,1,0:T(8,128)S(1)}, u32[]{:S(2)}, u32[]{:S(2)}) collective-permute-start(f32[6,8,128]{2,1,0:T(8,128)S(1)} %copy-done.29), channel_id=1, source_target_pairs={{0,4},{4,8},{8,12},{12,16},{16,20},{20,24},{24,28},{28,32},{32,36}... | collective-permute-start | bytes 73736 | tf_op jit(solution)/shard_map/ppermute | solution.py:198
  105.6 3.1 %collective-permute-start.15 = (f32[6,8,128]{2,1,0:T(8,128)S(1)}, f32[6,8,128]{2,1,0:T(8,128)S(1)}, u32[]{:S(2)}, u32[]{:S(2)}) collective-permute-start(f32[6,8,128]{2,1,0:T(8,128)S(1)} %copy-done.28), channel_id=1, source_target_pairs={{4,0},{8,4},{12,8},{16,12},{20,16},{24,20},{28,24},{32,28},{36,32}... | collective-permute-start | bytes 73736 | tf_op jit(solution)/shard_map/ppermute | solution.py:199
  108.7 3.6 %collective-permute-start.16 = (f32[6,128]{1,0:T(8,128)S(1)}, f32[6,128]{1,0:T(8,128)S(1)}, u32[]{:S(2)}, u32[]{:S(2)}) collective-permute-start(f32[6,128]{1,0:T(8,128)S(1)} %copy-done.35), channel_id=1, source_target_pairs={{0,1},{1,2},{2,3},{4,5},{5,6},{6,7},{8,9},{9,10},{10,11},{12,13},{... | collective-permute-start | bytes 9224 | tf_op jit(solution)/shard_map/ppermute | solution.py:198
  115.0 5.0 %collective-permute-done.17.hwh = f32[6,128]{1,0:T(8,128)S(1)} collective-permute-done((f32[6,128]{1,0:T(8,128)S(1)}, f32[6,128]{1,0:T(8,128)S(1)}, u32[]{:S(2)}, u32[]{:S(2)}) %collective-permute-start.17) | collective-permute-done | bytes 3104 | tf_op jit(solution)/shard_map/ppermute | solution.py:199
  120.8 4.7 %shard_map.125 = (f32[6,8,16,128]{3,2,1,0:T(8,128)}, f32[8,16,128]{2,1,0:T(8,128)}) custom-call(f32[288]{0:T(512)} %pad_maximum_fusion.blk_ref, f32[6,8,16,128]{3,2,1,0:T(8,128)} %get-tuple-element.45.adj_ref, f32[6,8,16,128]{3,2,1,0:T(8,128)} %sens_ref.7, f32[6,8,16,128]{3,2,1,0:T(8,128)} %diag_ref.7, f32[3,8,16,128]{3,2,1,0:T(8,128)} %face_ref.5, ...), custom_call_target="tpu_custom_call" | custom-call | tf_op jit(solution)/shard_map/pallas_call | solution.py:260
  (107 shorter events, 17.4 us)
Async XLA Ops:
  9.2 17.5 %copy-start.32 = (f32[6,8,128]{2,1,0:T(8,128)S(1)}, f32[6,8,128]{2,1,0:T(8,128)}, u32[]{:S(2)}) copy-start(f32[6,8,128]{2,1,0:T(8,128)} %get-tuple-element.32) | copy-start | bytes 73732
  9.2 35.2 %all-to-all-start = ((f32[16,1,448]{2,1,0:T(1,128)}), f32[16,1,448]{2,1,0:T(1,128)S(1)}, u32[]{:S(2)}, u32[]{:S(2)}) async-start(f32[16,1,448]{2,1,0:T(1,128)} %get-tuple-element.35), calls=%async_computation | async-start | bytes 65536 | tf_op jit(solution)/shard_map/all_to_all | solution.py:252
  18.3 26.1 %collective-permute-start = (f32[6,1,16,128]{3,2,1,0:T(8,128)}, f32[6,1,16,128]{3,2,1,0:T(8,128)S(1)}, u32[]{:S(2)}, u32[]{:S(2)}) collective-permute-start(f32[6,1,16,128]{3,2,1,0:T(8,128)} %get-tuple-element.29), channel_id=1, source_target_pairs={{0,64},{64,128},{128,192},{1,65},{65,129},{129,193},{2,66},{66,130... | collective-permute-start | bytes 147464 | tf_op jit(solution)/shard_map/ppermute | solution.py:198
  21.2 23.2 %collective-permute-start.1 = (f32[6,1,16,128]{3,2,1,0:T(8,128)S(1)}, f32[6,1,16,128]{3,2,1,0:T(8,128)S(1)}, u32[]{:S(2)}, u32[]{:S(2)}) collective-permute-start(f32[6,1,16,128]{3,2,1,0:T(8,128)S(1)} %copy-done.27), channel_id=1, source_target_pairs={{64,0},{128,64},{192,128},{65,1},{129,65},{193,129},{66,2},{130,66... | collective-permute-start | bytes 147464 | tf_op jit(solution)/shard_map/ppermute | solution.py:199
  23.6 20.7 %collective-permute-start.2 = (f32[6,8,128]{2,1,0:T(8,128)}, f32[6,8,128]{2,1,0:T(8,128)S(1)}, u32[]{:S(2)}, u32[]{:S(2)}) collective-permute-start(f32[6,8,128]{2,1,0:T(8,128)} %get-tuple-element.31), channel_id=1, source_target_pairs={{0,4},{4,8},{8,12},{12,16},{16,20},{20,24},{24,28},{28,32},{32,36}... | collective-permute-start | bytes 73736 | tf_op jit(solution)/shard_map/ppermute | solution.py:198
  26.7 17.6 %collective-permute-start.3 = (f32[6,8,128]{2,1,0:T(8,128)S(1)}, f32[6,8,128]{2,1,0:T(8,128)S(1)}, u32[]{:S(2)}, u32[]{:S(2)}) collective-permute-start(f32[6,8,128]{2,1,0:T(8,128)S(1)} %copy-done.32), channel_id=1, source_target_pairs={{4,0},{8,4},{12,8},{16,12},{20,16},{24,20},{28,24},{32,28},{36,32}... | collective-permute-start | bytes 73736 | tf_op jit(solution)/shard_map/ppermute | solution.py:199
  29.8 7.6 %collective-permute-start.4 = (f32[6,128]{1,0:T(8,128)}, f32[6,128]{1,0:T(8,128)S(1)}, u32[]{:S(2)}, u32[]{:S(2)}) collective-permute-start(f32[6,128]{1,0:T(8,128)} %get-tuple-element.33), channel_id=1, source_target_pairs={{0,1},{1,2},{2,3},{4,5},{5,6},{6,7},{8,9},{9,10},{10,11},{12,13},{... | collective-permute-start | bytes 9224 | tf_op jit(solution)/shard_map/ppermute | solution.py:198
  37.4 7.0 %collective-permute-start.5 = (f32[6,128]{1,0:T(8,128)S(1)}, f32[6,128]{1,0:T(8,128)S(1)}, u32[]{:S(2)}, u32[]{:S(2)}) collective-permute-start(f32[6,128]{1,0:T(8,128)S(1)} %copy-done.37), channel_id=1, source_target_pairs={{1,0},{2,1},{3,2},{5,4},{6,5},{7,6},{9,8},{10,9},{11,10},{13,12},{... | collective-permute-start | bytes 9224 | tf_op jit(solution)/shard_map/ppermute | solution.py:199
  51.3 31.0 %collective-permute-start.6 = (f32[6,1,16,128]{3,2,1,0:T(8,128)}, f32[6,1,16,128]{3,2,1,0:T(8,128)S(1)}, u32[]{:S(2)}, u32[]{:S(2)}) collective-permute-start(f32[6,1,16,128]{3,2,1,0:T(8,128)} %get-tuple-element.37), channel_id=1, source_target_pairs={{0,64},{64,128},{128,192},{1,65},{65,129},{129,193},{2,66},{66,130... | collective-permute-start | bytes 147464 | tf_op jit(solution)/shard_map/ppermute | solution.py:198
  54.2 16.7 %copy-start.36 = (f32[6,128]{1,0:T(8,128)S(1)}, f32[6,128]{1,0:T(8,128)}, u32[]{:S(2)}) copy-start(f32[6,128]{1,0:T(8,128)} %get-tuple-element.41) | copy-start | bytes 9220
  54.2 28.1 %collective-permute-start.7 = (f32[6,1,16,128]{3,2,1,0:T(8,128)}, f32[6,1,16,128]{3,2,1,0:T(8,128)S(1)}, u32[]{:S(2)}, u32[]{:S(2)}) collective-permute-start(f32[6,1,16,128]{3,2,1,0:T(8,128)} %get-tuple-element.38), channel_id=1, source_target_pairs={{64,0},{128,64},{192,128},{65,1},{129,65},{193,129},{66,2},{130,66... | collective-permute-start | bytes 147464 | tf_op jit(solution)/shard_map/ppermute | solution.py:199
  56.6 25.6 %all-to-all-start.1 = ((f32[16,1,384]{2,1,0:T(1,128)}), f32[16,1,384]{2,1,0:T(1,128)S(1)}, u32[]{:S(2)}, u32[]{:S(2)}) async-start(f32[16,1,384]{2,1,0:T(1,128)} %get-tuple-element.43), calls=%async_computation.1 | async-start | bytes 49152 | tf_op jit(solution)/shard_map/all_to_all | solution.py:252
  64.7 17.6 %collective-permute-start.8 = (f32[6,8,128]{2,1,0:T(8,128)S(1)}, f32[6,8,128]{2,1,0:T(8,128)S(1)}, u32[]{:S(2)}, u32[]{:S(2)}) collective-permute-start(f32[6,8,128]{2,1,0:T(8,128)S(1)} %copy-done.31), channel_id=1, source_target_pairs={{0,4},{4,8},{8,12},{12,16},{16,20},{20,24},{24,28},{28,32},{32,36}... | collective-permute-start | bytes 73736 | tf_op jit(solution)/shard_map/ppermute | solution.py:198
  67.8 14.5 %collective-permute-start.9 = (f32[6,8,128]{2,1,0:T(8,128)S(1)}, f32[6,8,128]{2,1,0:T(8,128)S(1)}, u32[]{:S(2)}, u32[]{:S(2)}) collective-permute-start(f32[6,8,128]{2,1,0:T(8,128)S(1)} %copy-done.30), channel_id=1, source_target_pairs={{4,0},{8,4},{12,8},{16,12},{20,16},{24,20},{28,24},{32,28},{36,32}... | collective-permute-start | bytes 73736 | tf_op jit(solution)/shard_map/ppermute | solution.py:199
  70.9 4.4 %collective-permute-start.10 = (f32[6,128]{1,0:T(8,128)S(1)}, f32[6,128]{1,0:T(8,128)S(1)}, u32[]{:S(2)}, u32[]{:S(2)}) collective-permute-start(f32[6,128]{1,0:T(8,128)S(1)} %copy-done.36), channel_id=1, source_target_pairs={{0,1},{1,2},{2,3},{4,5},{5,6},{6,7},{8,9},{9,10},{10,11},{12,13},{... | collective-permute-start | bytes 9224 | tf_op jit(solution)/shard_map/ppermute | solution.py:198
  75.2 7.0 %collective-permute-start.11 = (f32[6,128]{1,0:T(8,128)S(1)}, f32[6,128]{1,0:T(8,128)S(1)}, u32[]{:S(2)}, u32[]{:S(2)}) collective-permute-start(f32[6,128]{1,0:T(8,128)S(1)} %copy-done.34), channel_id=1, source_target_pairs={{1,0},{2,1},{3,2},{5,4},{6,5},{7,6},{9,8},{10,9},{11,10},{13,12},{... | collective-permute-start | bytes 9224 | tf_op jit(solution)/shard_map/ppermute | solution.py:199
  89.1 31.0 %collective-permute-start.12 = (f32[6,1,16,128]{3,2,1,0:T(8,128)}, f32[6,1,16,128]{3,2,1,0:T(8,128)S(1)}, u32[]{:S(2)}, u32[]{:S(2)}) collective-permute-start(f32[6,1,16,128]{3,2,1,0:T(8,128)} %get-tuple-element.46), channel_id=1, source_target_pairs={{0,64},{64,128},{128,192},{1,65},{65,129},{129,193},{2,66},{66,130... | collective-permute-start | bytes 147464 | tf_op jit(solution)/shard_map/ppermute | solution.py:198
  92.1 16.7 %copy-start.35 = (f32[6,128]{1,0:T(8,128)S(1)}, f32[6,128]{1,0:T(8,128)}, u32[]{:S(2)}) copy-start(f32[6,128]{1,0:T(8,128)} %get-tuple-element.50) | copy-start | bytes 9220
  92.1 28.1 %collective-permute-start.13 = (f32[6,1,16,128]{3,2,1,0:T(8,128)}, f32[6,1,16,128]{3,2,1,0:T(8,128)S(1)}, u32[]{:S(2)}, u32[]{:S(2)}) collective-permute-start(f32[6,1,16,128]{3,2,1,0:T(8,128)} %get-tuple-element.47), channel_id=1, source_target_pairs={{64,0},{128,64},{192,128},{65,1},{129,65},{193,129},{66,2},{130,66... | collective-permute-start | bytes 147464 | tf_op jit(solution)/shard_map/ppermute | solution.py:199
  94.5 25.6 %all-to-all-start.2 = ((f32[16,1,384]{2,1,0:T(1,128)}), f32[16,1,384]{2,1,0:T(1,128)S(1)}, u32[]{:S(2)}, u32[]{:S(2)}) async-start(f32[16,1,384]{2,1,0:T(1,128)} %get-tuple-element.52), calls=%async_computation.2 | async-start | bytes 49152 | tf_op jit(solution)/shard_map/all_to_all | solution.py:252
  102.5 17.6 %collective-permute-start.14 = (f32[6,8,128]{2,1,0:T(8,128)S(1)}, f32[6,8,128]{2,1,0:T(8,128)S(1)}, u32[]{:S(2)}, u32[]{:S(2)}) collective-permute-start(f32[6,8,128]{2,1,0:T(8,128)S(1)} %copy-done.29), channel_id=1, source_target_pairs={{0,4},{4,8},{8,12},{12,16},{16,20},{20,24},{24,28},{28,32},{32,36}... | collective-permute-start | bytes 73736 | tf_op jit(solution)/shard_map/ppermute | solution.py:198
  105.6 14.5 %collective-permute-start.15 = (f32[6,8,128]{2,1,0:T(8,128)S(1)}, f32[6,8,128]{2,1,0:T(8,128)S(1)}, u32[]{:S(2)}, u32[]{:S(2)}) collective-permute-start(f32[6,8,128]{2,1,0:T(8,128)S(1)} %copy-done.28), channel_id=1, source_target_pairs={{4,0},{8,4},{12,8},{16,12},{20,16},{24,20},{28,24},{32,28},{36,32}... | collective-permute-start | bytes 73736 | tf_op jit(solution)/shard_map/ppermute | solution.py:199
  108.7 4.4 %collective-permute-start.16 = (f32[6,128]{1,0:T(8,128)S(1)}, f32[6,128]{1,0:T(8,128)S(1)}, u32[]{:S(2)}, u32[]{:S(2)}) collective-permute-start(f32[6,128]{1,0:T(8,128)S(1)} %copy-done.35), channel_id=1, source_target_pairs={{0,1},{1,2},{2,3},{4,5},{5,6},{6,7},{8,9},{9,10},{10,11},{12,13},{... | collective-permute-start | bytes 9224 | tf_op jit(solution)/shard_map/ppermute | solution.py:198
  113.1 7.0 %collective-permute-start.17 = (f32[6,128]{1,0:T(8,128)S(1)}, f32[6,128]{1,0:T(8,128)S(1)}, u32[]{:S(2)}, u32[]{:S(2)}) collective-permute-start(f32[6,128]{1,0:T(8,128)S(1)} %copy-done.33), channel_id=1, source_target_pairs={{1,0},{2,1},{3,2},{5,4},{6,5},{7,6},{9,8},{10,9},{11,10},{13,12},{... | collective-permute-start | bytes 9224 | tf_op jit(solution)/shard_map/ppermute | solution.py:199
  (35 other events, 124.3 us)

commit v3 on v2

--- a/solution.py
+++ b/solution.py
@@ -20,8 +20,8 @@
 
 def gather_rows(adj, send_ref, orient_ref, weight_ref, blk, n_var, lanes):
     rows = adj.shape[1] * adj.shape[2]
-    n_rows = send_ref.shape[1]
-    cell = send_ref[...]
+    cell = flat_row(send_ref[...])
+    n_rows = cell.shape[1]
     row_of = cell // lanes
     lane_of = cell % lanes
     lane_hot = (lax.broadcasted_iota(jnp.int32, (lanes, n_rows), 0) == lane_of).astype(BF16)
@@ -32,19 +32,23 @@
         term = jnp.dot(part, lane_hot, preferred_element_type=F32)
         picked = term if picked is None else picked + term
     src = jnp.sum(picked.reshape(n_var, rows, n_rows) * row_hot[None], axis=1)
-    orient = orient_ref[...]
-    weight = weight_ref[...]
+    orient = flat_row(orient_ref[...])
+    weight = flat_row(weight_ref[...])
     out = []
     for i in range(n_var):
         first = None
         second = None
         for j in range(n_var):
-            a = blk[216 + j * n_var + i] * src[j:j + 1]
-            b = blk[216 + 36 + j * n_var + i] * src[j:j + 1]
+            a = blk[2][0, j, i] * src[j:j + 1]
+            b = blk[2][1, j, i] * src[j:j + 1]
             first = a if first is None else first + a
             second = b if second is None else second + b
         out.append(jnp.where(orient == 1, second, first) * weight)
     return out
+
+
+def flat_row(x):
+    return jnp.concatenate([x[t:t + 1] for t in range(x.shape[0])], axis=1)
 
 
 def to_chunks(rows_ref, pieces, slots):
@@ -82,16 +86,17 @@
     w_hi[...] = hi
 
 
-def init_kernel(blk_ref, sens_ref, diag_ref, send_ref, orient_ref, weight_ref, tgt_ref,
+def init_kernel(ub_ref, lb_ref, ib_ref, sens_ref, diag_ref, send_ref, orient_ref, weight_ref, tgt_ref,
                 adj_ref, rows_ref, c_lo, c_hi, s_lo, s_hi, w_lo, w_hi):
     n_var = sens_ref.shape[0]
     lanes = sens_ref.shape[3]
-    slots = send_ref.shape[1] // rows_ref.shape[0]
+    slots = send_ref.shape[1]
+    blk_ref = (ub_ref, lb_ref, ib_ref)
     adj = sens_ref[...] / diag_ref[...]
     adj_ref[...] = adj
     write_faces(adj, (c_lo, c_hi, s_lo, s_hi, w_lo, w_hi))
     pieces = gather_rows(adj, send_ref, orient_ref, weight_ref, blk_ref, n_var, lanes)
-    to_chunks(rows_ref, pieces + [tgt_ref[...].astype(F32)], slots)
+    to_chunks(rows_ref, pieces + [flat_row(tgt_ref[...]).astype(F32)], slots)
 
 
 def sweep_body(blk, adj, sens, diag, face, halos, incoming, cell):
@@ -119,11 +124,11 @@
     n_rows = incoming.shape[1]
     row_of = cell // nz
     lane_of = cell % nz
-    row_hot = (lax.broadcasted_iota(jnp.int32, (rows, n_rows), 0) == row_of).astype(F32)
+    row_hot = (lax.broadcasted_iota(jnp.int32, (rows, n_rows), 0) == row_of).astype(BF16)
     lane_hot = (lax.broadcasted_iota(jnp.int32, (nz, n_rows), 0) == lane_of).astype(BF16)
     coupled = None
     for part in split3(incoming):
-        lhs = (row_hot[None] * part.astype(F32)[:, None, :]).astype(BF16).reshape(n_var * rows, n_rows)
+        lhs = (row_hot[None] * part[:, None, :]).reshape(n_var * rows, n_rows)
         term = lax.dot_general(lhs, lane_hot, (((1,), (1,)), ((), ())), preferred_element_type=F32)
         coupled = term if coupled is None else coupled + term
     coupled = coupled.reshape(n_var, nx, ny, nz)
@@ -133,19 +138,20 @@
         for d in range(3):
             acc = None
             for j in range(n_var):
-                t = blk[d * 36 + j * n_var + i] * up[d][j] + blk[108 + d * 36 + j * n_var + i] * lo[d][j]
+                t = blk[0][d, j, i] * up[d][j] + blk[1][d, j, i] * lo[d][j]
                 acc = t if acc is None else acc + t
             applied = applied + face[d] * acc
         new.append(adj[i] + (sens[i] - applied) / diag[i])
     return jnp.stack(new, axis=0)
 
 
-def sweep_kernel(blk_ref, adj_ref, sens_ref, diag_ref, face_ref, hcl, hch, hsl, hsh, hwl, hwh,
+def sweep_kernel(ub_ref, lb_ref, ib_ref, adj_ref, sens_ref, diag_ref, face_ref, hcl, hch, hsl, hsh, hwl, hwh,
                  inc_ref, tgt_ref, send_ref, orient_ref, weight_ref,
                  out_ref, rows_ref, tgt_out, c_lo, c_hi, s_lo, s_hi, w_lo, w_hi):
     n_var = adj_ref.shape[0]
     lanes = adj_ref.shape[3]
-    slots = send_ref.shape[1] // rows_ref.shape[0]
+    slots = send_ref.shape[1]
+    blk_ref = (ub_ref, lb_ref, ib_ref)
     halos = (hcl[...], hch[...], hsl[...], hsh[...], hwl[...], hwh[...])
     inc = inc_ref[...]
     if tgt_ref is None:
@@ -162,16 +168,17 @@
     to_chunks(rows_ref, gather_rows(new, send_ref, orient_ref, weight_ref, blk_ref, n_var, lanes), slots)
 
 
-def first_sweep_kernel(blk_ref, adj_ref, sens_ref, diag_ref, face_ref, hcl, hch, hsl, hsh, hwl, hwh,
+def first_sweep_kernel(ub_ref, lb_ref, ib_ref, adj_ref, sens_ref, diag_ref, face_ref, hcl, hch, hsl, hsh, hwl, hwh,
                        inc_ref, send_ref, orient_ref, weight_ref, *outs):
-    sweep_kernel(blk_ref, adj_ref, sens_ref, diag_ref, face_ref, hcl, hch, hsl, hsh, hwl, hwh,
+    sweep_kernel(ub_ref, lb_ref, ib_ref, adj_ref, sens_ref, diag_ref, face_ref, hcl, hch, hsl, hsh, hwl, hwh,
                  inc_ref, None, send_ref, orient_ref, weight_ref, *outs)
 
 
-def last_kernel(blk_ref, adj_ref, sens_ref, diag_ref, face_ref, hcl, hch, hsl, hsh, hwl, hwh,
+def last_kernel(ub_ref, lb_ref, ib_ref, adj_ref, sens_ref, diag_ref, face_ref, hcl, hch, hsl, hsh, hwl, hwh,
                 inc_ref, tgt_ref, prod_ref, out_ref, grad_ref):
     n_var = adj_ref.shape[0]
     slots = inc_ref.shape[2] // n_var
+    blk_ref = (ub_ref, lb_ref, ib_ref)
     halos = (hcl[...], hch[...], hsl[...], hsh[...], hwl[...], hwh[...])
     got = from_chunks(inc_ref[...], n_var, slots)
     new = sweep_body(blk_ref, adj_ref[...], sens_ref[...], diag_ref[...], face_ref[...], halos,
@@ -207,11 +214,11 @@
     slots = send_cell.shape[-1]
     n_rows = n_span * slots
     shape = sensitivity.shape
-    blk = jnp.concatenate([upper_blocks.reshape(-1), lower_blocks.reshape(-1), iface_blocks.reshape(-1)])
-    send_row = send_cell.reshape(1, n_rows)
-    orient_row = orient.reshape(1, n_rows)
-    weight_row = iface_weight.reshape(1, n_rows)
-    target_row = target_cell.reshape(1, n_rows)
+    blk = (upper_blocks, lower_blocks, iface_blocks)
+    send_row = send_cell.reshape(n_span, slots)
+    orient_row = orient.reshape(n_span, slots)
+    weight_row = iface_weight.reshape(n_span, slots)
+    target_row = target_cell.reshape(n_span, slots)
 
     vmem = pl.BlockSpec(memory_space=pltpu.VMEM)
     smem = pl.BlockSpec(memory_space=pltpu.SMEM)
@@ -223,27 +230,27 @@
     init = pl.pallas_call(
         init_kernel,
         out_shape=[adj_sds, first_rows] + face_shapes(shape),
-        in_specs=[smem] + [vmem] * 6,
+        in_specs=[smem] * 3 + [vmem] * 6,
         out_specs=[vmem] * 8,
     )
-    adj, rows, *faces = init(blk, sensitivity, diagonal, send_row, orient_row, weight_row, target_row)
+    adj, rows, *faces = init(*blk, sensitivity, diagonal, send_row, orient_row, weight_row, target_row)
 
     first = pl.pallas_call(
         first_sweep_kernel,
         out_shape=[adj_sds, rows_sds, tgt_sds] + face_shapes(shape),
-        in_specs=[smem] + [vmem] * 14,
+        in_specs=[smem] * 3 + [vmem] * 14,
         out_specs=[vmem] * 9,
     )
     step = pl.pallas_call(
         sweep_kernel,
         out_shape=[adj_sds, rows_sds, tgt_sds] + face_shapes(shape),
-        in_specs=[smem] + [vmem] * 15,
+        in_specs=[smem] * 3 + [vmem] * 15,
         out_specs=[vmem] * 9,
     )
     last = pl.pallas_call(
         last_kernel,
         out_shape=[adj_sds, jax.ShapeDtypeStruct(production.shape, F32)],
-        in_specs=[smem] + [vmem] * 13,
+        in_specs=[smem] * 3 + [vmem] * 13,
         out_specs=[vmem] * 2,
     )
     received = None
@@ -251,13 +258,13 @@
         halos = exchange(faces)
         incoming = lax.all_to_all(rows, "span", split_axis=0, concat_axis=0, tiled=True)
         if sweep == 0:
-            adj, rows, received, *faces = first(blk, adj, sensitivity, diagonal, face_coef, *halos,
+            adj, rows, received, *faces = first(*blk, adj, sensitivity, diagonal, face_coef, *halos,
                                                 incoming, send_row, orient_row, weight_row)
         elif sweep < SWEEPS - 1:
-            adj, rows, received, *faces = step(blk, adj, sensitivity, diagonal, face_coef, *halos,
+            adj, rows, received, *faces = step(*blk, adj, sensitivity, diagonal, face_coef, *halos,
                                                incoming, received, send_row, orient_row, weight_row)
         else:
-            adj, gradient = last(blk, adj, sensitivity, diagonal, face_coef, *halos, incoming,
+            adj, gradient = last(*blk, adj, sensitivity, diagonal, face_coef, *halos, incoming,
                                  received, production)
     return (adj, gradient)
 

time: 127 us -> 123 us (0.969)
  local copies, waits for them, and re-layouts: 6.23 us -> 3.17 us
    reshape x7 -> x0, local copies, waits for them, and re-layouts: 3.63 us -> none  [the longest x1 0.8 us: local(): upper_blocks.reshape(-1)]
    unnamed x77 -> x65, local copies, waits for them, and re-layouts: 2.6 us -> 3.17 us
where the time goes in v3:
time: 123 us; the launch traced here: 121 us
  starting transfers between devices  79.3 us (64%)
  Pallas kernels  20.5 us (17%)
  waiting for transfers between devices  17.4 us (14%)
  local copies, waits for them, and re-layouts  3.17 us (3%)
    ppermute x9, starting transfers between devices, exchange(): out.append(lax.ppermute(hi_face, axis, forward))  31.8 us
    all_to_all x3, starting transfers between devices, local(): lax.all_to_all(rows, 'span', split_axis=0, concat_axis=0, tiled=True)  25.1 us
    ppermute x9, starting transfers between devices, exchange(): out.append(lax.ppermute(lo_face, axis, backward))  22.3 us
    ppermute x9, waiting for transfers between devices, exchange(): out.append(lax.ppermute(lo_face, axis, backward))  15 us
    pallas_call x1, Pallas kernels, local(): step(*blk, adj, sensitivity, diagonal, face_coef, *halos, incoming, recei...  6.1 us
    pallas_call x1, Pallas kernels, local(): first(*blk, adj, sensitivity, diagonal, face_coef, *halos, incoming, send...  6.09 us
    pallas_call x1, Pallas kernels, local(): last(*blk, adj, sensitivity, diagonal, face_coef, *halos, incoming, recei...  4.58 us
    pallas_call x1, Pallas kernels, local(): init(*blk, sensitivity, diagonal, send_row, orient_row, weight_row, targe...  3.72 us
  transfers between devices with their start and end apart: 21, of which 6 were waited for; matrix products, arithmetic and copies ran while one was open for 0% of the time, Pallas kernels for 0%

profile of v3, /device:TPU:49, one launch (start us, length us, event | category | flops | bytes accessed | tf_op | source)
XLA Modules:
  0.0 121.5 jit_solution(3808351722528476919)
XLA Ops:
  1.9 3.7 %shard_map.122 = (f32[6,8,16,128]{3,2,1,0:T(8,128)}, f32[16,1,448]{2,1,0:T(1,128)}, f32[6,1,16,128]{3,2,1,0:T(8,128)}, f32[6,1,16,128]{3,2,1,0:T(8,128)}, f32[6,...) custom-call(f32[3,6,6]{2,1,0:T(8,128)} %ub_ref.7, f32[3,6,6]{2,1,0:T(8,128)} %lb_ref.7, ...), custom_call_target="tpu_custom_call" | custom-call | tf_op jit(solution)/shard_map/pallas_call | solution.py:236
  5.7 9.1 %all-to-all-start = ((f32[16,1,448]{2,1,0:T(1,128)}), f32[16,1,448]{2,1,0:T(1,128)S(1)}, u32[]{:S(2)}, u32[]{:S(2)}) async-start(f32[16,1,448]{2,1,0:T(1,128)} %get-tuple-element.35), calls=%async_computation | async-start | bytes 65536 | tf_op jit(solution)/shard_map/all_to_all | solution.py:259
  14.8 2.9 %collective-permute-start = (f32[6,1,16,128]{3,2,1,0:T(8,128)}, f32[6,1,16,128]{3,2,1,0:T(8,128)S(1)}, u32[]{:S(2)}, u32[]{:S(2)}) collective-permute-start(f32[6,1,16,128]{3,2,1,0:T(8,128)} %get-tuple-element.29), channel_id=1, source_target_pairs={{0,64},{64,128},{128,192},{1,65},{65,129},{129,193},{2,66},{66,130... | collective-permute-start | bytes 147464 | tf_op jit(solution)/shard_map/ppermute | solution.py:205
  17.7 2.4 %collective-permute-start.1 = (f32[6,1,16,128]{3,2,1,0:T(8,128)S(1)}, f32[6,1,16,128]{3,2,1,0:T(8,128)S(1)}, u32[]{:S(2)}, u32[]{:S(2)}) collective-permute-start(f32[6,1,16,128]{3,2,1,0:T(8,128)S(1)} %copy-done.21), channel_id=1, source_target_pairs={{64,0},{128,64},{192,128},{65,1},{129,65},{193,129},{66,2},{130,66... | collective-permute-start | bytes 147464 | tf_op jit(solution)/shard_map/ppermute | solution.py:206
  20.1 3.1 %collective-permute-start.2 = (f32[6,8,128]{2,1,0:T(8,128)}, f32[6,8,128]{2,1,0:T(8,128)S(1)}, u32[]{:S(2)}, u32[]{:S(2)}) collective-permute-start(f32[6,8,128]{2,1,0:T(8,128)} %get-tuple-element.31), channel_id=1, source_target_pairs={{0,4},{4,8},{8,12},{12,16},{16,20},{20,24},{24,28},{28,32},{32,36}... | collective-permute-start | bytes 73736 | tf_op jit(solution)/shard_map/ppermute | solution.py:205
  23.2 3.1 %collective-permute-start.3 = (f32[6,8,128]{2,1,0:T(8,128)S(1)}, f32[6,8,128]{2,1,0:T(8,128)S(1)}, u32[]{:S(2)}, u32[]{:S(2)}) collective-permute-start(f32[6,8,128]{2,1,0:T(8,128)S(1)} %copy-done.26), channel_id=1, source_target_pairs={{4,0},{8,4},{12,8},{16,12},{20,16},{24,20},{28,24},{32,28},{36,32}... | collective-permute-start | bytes 73736 | tf_op jit(solution)/shard_map/ppermute | solution.py:206
  26.3 6.6 %collective-permute-start.4 = (f32[6,128]{1,0:T(8,128)}, f32[6,128]{1,0:T(8,128)S(1)}, u32[]{:S(2)}, u32[]{:S(2)}) collective-permute-start(f32[6,128]{1,0:T(8,128)} %get-tuple-element.33), channel_id=1, source_target_pairs={{0,1},{1,2},{2,3},{4,5},{5,6},{6,7},{8,9},{9,10},{10,11},{12,13},{... | collective-permute-start | bytes 9224 | tf_op jit(solution)/shard_map/ppermute | solution.py:205
  35.7 5.0 %collective-permute-done.5.hwh = f32[6,128]{1,0:T(8,128)S(1)} collective-permute-done((f32[6,128]{1,0:T(8,128)S(1)}, f32[6,128]{1,0:T(8,128)S(1)}, u32[]{:S(2)}, u32[]{:S(2)}) %collective-permute-start.5) | collective-permute-done | bytes 3104 | tf_op jit(solution)/shard_map/ppermute | solution.py:206
  41.5 6.1 %shard_map.123 = (f32[6,8,16,128]{3,2,1,0:T(8,128)}, f32[16,1,384]{2,1,0:T(1,128)}, s32[1,1024]{1,0:T(1,128)}, f32[6,1,16,128]{3,2,1,0:T(8,128)}, f32[6,1,16,128...) custom-call(f32[3,6,6]{2,1,0:T(8,128)} %ub_ref.7, ...), custom_call_target="tpu_custom_call" | custom-call | tf_op jit(solution)/shard_map/pallas_call | solution.py:261
  47.6 2.9 %collective-permute-start.6 = (f32[6,1,16,128]{3,2,1,0:T(8,128)}, f32[6,1,16,128]{3,2,1,0:T(8,128)S(1)}, u32[]{:S(2)}, u32[]{:S(2)}) collective-permute-start(f32[6,1,16,128]{3,2,1,0:T(8,128)} %get-tuple-element.37), channel_id=1, source_target_pairs={{0,64},{64,128},{128,192},{1,65},{65,129},{129,193},{2,66},{66,130... | collective-permute-start | bytes 147464 | tf_op jit(solution)/shard_map/ppermute | solution.py:205
  50.5 2.4 %collective-permute-start.7 = (f32[6,1,16,128]{3,2,1,0:T(8,128)}, f32[6,1,16,128]{3,2,1,0:T(8,128)S(1)}, u32[]{:S(2)}, u32[]{:S(2)}) collective-permute-start(f32[6,1,16,128]{3,2,1,0:T(8,128)} %get-tuple-element.38), channel_id=1, source_target_pairs={{64,0},{128,64},{192,128},{65,1},{129,65},{193,129},{66,2},{130,66... | collective-permute-start | bytes 147464 | tf_op jit(solution)/shard_map/ppermute | solution.py:206
  52.9 8.0 %all-to-all-start.1 = ((f32[16,1,384]{2,1,0:T(1,128)}), f32[16,1,384]{2,1,0:T(1,128)S(1)}, u32[]{:S(2)}, u32[]{:S(2)}) async-start(f32[16,1,384]{2,1,0:T(1,128)} %get-tuple-element.43), calls=%async_computation.1 | async-start | bytes 49152 | tf_op jit(solution)/shard_map/all_to_all | solution.py:259
  60.9 3.1 %collective-permute-start.8 = (f32[6,8,128]{2,1,0:T(8,128)S(1)}, f32[6,8,128]{2,1,0:T(8,128)S(1)}, u32[]{:S(2)}, u32[]{:S(2)}) collective-permute-start(f32[6,8,128]{2,1,0:T(8,128)S(1)} %copy-done.25), channel_id=1, source_target_pairs={{0,4},{4,8},{8,12},{12,16},{16,20},{20,24},{24,28},{28,32},{32,36}... | collective-permute-start | bytes 73736 | tf_op jit(solution)/shard_map/ppermute | solution.py:205
  64.0 3.1 %collective-permute-start.9 = (f32[6,8,128]{2,1,0:T(8,128)S(1)}, f32[6,8,128]{2,1,0:T(8,128)S(1)}, u32[]{:S(2)}, u32[]{:S(2)}) collective-permute-start(f32[6,8,128]{2,1,0:T(8,128)S(1)} %copy-done.23), channel_id=1, source_target_pairs={{4,0},{8,4},{12,8},{16,12},{20,16},{24,20},{28,24},{32,28},{36,32}... | collective-permute-start | bytes 73736 | tf_op jit(solution)/shard_map/ppermute | solution.py:206
  67.1 3.6 %collective-permute-start.10 = (f32[6,128]{1,0:T(8,128)S(1)}, f32[6,128]{1,0:T(8,128)S(1)}, u32[]{:S(2)}, u32[]{:S(2)}) collective-permute-start(f32[6,128]{1,0:T(8,128)S(1)} %copy-done.30), channel_id=1, source_target_pairs={{0,1},{1,2},{2,3},{4,5},{5,6},{6,7},{8,9},{9,10},{10,11},{12,13},{... | collective-permute-start | bytes 9224 | tf_op jit(solution)/shard_map/ppermute | solution.py:205
  73.4 5.0 %collective-permute-done.11.hwh = f32[6,128]{1,0:T(8,128)S(1)} collective-permute-done((f32[6,128]{1,0:T(8,128)S(1)}, f32[6,128]{1,0:T(8,128)S(1)}, u32[]{:S(2)}, u32[]{:S(2)}) %collective-permute-start.11) | collective-permute-done | bytes 3104 | tf_op jit(solution)/shard_map/ppermute | solution.py:206
  79.2 6.1 %shard_map.124 = (f32[6,8,16,128]{3,2,1,0:T(8,128)}, f32[16,1,384]{2,1,0:T(1,128)}, s32[1,1024]{1,0:T(1,128)}, f32[6,1,16,128]{3,2,1,0:T(8,128)}, f32[6,1,16,128...) custom-call(f32[3,6,6]{2,1,0:T(8,128)} %ub_ref.7, ...), custom_call_target="tpu_custom_call" | custom-call | tf_op jit(solution)/shard_map/pallas_call | solution.py:264
  85.3 2.9 %collective-permute-start.12 = (f32[6,1,16,128]{3,2,1,0:T(8,128)}, f32[6,1,16,128]{3,2,1,0:T(8,128)S(1)}, u32[]{:S(2)}, u32[]{:S(2)}) collective-permute-start(f32[6,1,16,128]{3,2,1,0:T(8,128)} %get-tuple-element.46), channel_id=1, source_target_pairs={{0,64},{64,128},{128,192},{1,65},{65,129},{129,193},{2,66},{66,130... | collective-permute-start | bytes 147464 | tf_op jit(solution)/shard_map/ppermute | solution.py:205
  90.6 8.0 %all-to-all-start.2 = ((f32[16,1,384]{2,1,0:T(1,128)}), f32[16,1,384]{2,1,0:T(1,128)S(1)}, u32[]{:S(2)}, u32[]{:S(2)}) async-start(f32[16,1,384]{2,1,0:T(1,128)} %get-tuple-element.52), calls=%async_computation.2 | async-start | bytes 49152 | tf_op jit(solution)/shard_map/all_to_all | solution.py:259
  98.6 3.1 %collective-permute-start.14 = (f32[6,8,128]{2,1,0:T(8,128)S(1)}, f32[6,8,128]{2,1,0:T(8,128)S(1)}, u32[]{:S(2)}, u32[]{:S(2)}) collective-permute-start(f32[6,8,128]{2,1,0:T(8,128)S(1)} %copy-done.24), channel_id=1, source_target_pairs={{0,4},{4,8},{8,12},{12,16},{16,20},{20,24},{24,28},{28,32},{32,36}... | collective-permute-start | bytes 73736 | tf_op jit(solution)/shard_map/ppermute | solution.py:205
  101.7 3.1 %collective-permute-start.15 = (f32[6,8,128]{2,1,0:T(8,128)S(1)}, f32[6,8,128]{2,1,0:T(8,128)S(1)}, u32[]{:S(2)}, u32[]{:S(2)}) collective-permute-start(f32[6,8,128]{2,1,0:T(8,128)S(1)} %copy-done.22), channel_id=1, source_target_pairs={{4,0},{8,4},{12,8},{16,12},{20,16},{24,20},{28,24},{32,28},{36,32}... | collective-permute-start | bytes 73736 | tf_op jit(solution)/shard_map/ppermute | solution.py:206
  104.8 3.6 %collective-permute-start.16 = (f32[6,128]{1,0:T(8,128)S(1)}, f32[6,128]{1,0:T(8,128)S(1)}, u32[]{:S(2)}, u32[]{:S(2)}) collective-permute-start(f32[6,128]{1,0:T(8,128)S(1)} %copy-done.29), channel_id=1, source_target_pairs={{0,1},{1,2},{2,3},{4,5},{5,6},{6,7},{8,9},{9,10},{10,11},{12,13},{... | collective-permute-start | bytes 9224 | tf_op jit(solution)/shard_map/ppermute | solution.py:205
  111.3 4.9 %collective-permute-done.17.hwh = f32[6,128]{1,0:T(8,128)S(1)} collective-permute-done((f32[6,128]{1,0:T(8,128)S(1)}, f32[6,128]{1,0:T(8,128)S(1)}, u32[]{:S(2)}, u32[]{:S(2)}) %collective-permute-start.17) | collective-permute-done | bytes 3104 | tf_op jit(solution)/shard_map/ppermute | solution.py:206
  116.9 4.6 %shard_map.125 = (f32[6,8,16,128]{3,2,1,0:T(8,128)}, f32[8,16,128]{2,1,0:T(8,128)}) custom-call(f32[3,6,6]{2,1,0:T(8,128)} %ub_ref.7, f32[3,6,6]{2,1,0:T(8,128)} %lb_ref.7, f32[2,6,6]{2,1,0:T(8,128)} %copy.16.ib_ref, f32[6,8,16,128]{3,2,1,0:T(8,128)} %get-tuple-element.45.adj_ref, f32[6,8,16,128]{3,2,1,0:T(8,128)} %sens_ref.7, f32[6,8,16,128]{3,2,1,0:T(8,128)} %diag_ref.7, ...), custom_call_target="tpu_custom_call" | custom-call | tf_op jit(solution)/shard_map/pallas_call | solution.py:267
  (87 shorter events, 13.9 us)
Async XLA Ops:
  5.7 17.5 %copy-start.26 = (f32[6,8,128]{2,1,0:T(8,128)S(1)}, f32[6,8,128]{2,1,0:T(8,128)}, u32[]{:S(2)}) copy-start(f32[6,8,128]{2,1,0:T(8,128)} %get-tuple-element.32) | copy-start | bytes 73732
  5.7 35.2 %all-to-all-start = ((f32[16,1,448]{2,1,0:T(1,128)}), f32[16,1,448]{2,1,0:T(1,128)S(1)}, u32[]{:S(2)}, u32[]{:S(2)}) async-start(f32[16,1,448]{2,1,0:T(1,128)} %get-tuple-element.35), calls=%async_computation | async-start | bytes 65536 | tf_op jit(solution)/shard_map/all_to_all | solution.py:259
  14.8 26.1 %collective-permute-start = (f32[6,1,16,128]{3,2,1,0:T(8,128)}, f32[6,1,16,128]{3,2,1,0:T(8,128)S(1)}, u32[]{:S(2)}, u32[]{:S(2)}) collective-permute-start(f32[6,1,16,128]{3,2,1,0:T(8,128)} %get-tuple-element.29), channel_id=1, source_target_pairs={{0,64},{64,128},{128,192},{1,65},{65,129},{129,193},{2,66},{66,130... | collective-permute-start | bytes 147464 | tf_op jit(solution)/shard_map/ppermute | solution.py:205
  17.7 23.2 %collective-permute-start.1 = (f32[6,1,16,128]{3,2,1,0:T(8,128)S(1)}, f32[6,1,16,128]{3,2,1,0:T(8,128)S(1)}, u32[]{:S(2)}, u32[]{:S(2)}) collective-permute-start(f32[6,1,16,128]{3,2,1,0:T(8,128)S(1)} %copy-done.21), channel_id=1, source_target_pairs={{64,0},{128,64},{192,128},{65,1},{129,65},{193,129},{66,2},{130,66... | collective-permute-start | bytes 147464 | tf_op jit(solution)/shard_map/ppermute | solution.py:206
  20.1 20.7 %collective-permute-start.2 = (f32[6,8,128]{2,1,0:T(8,128)}, f32[6,8,128]{2,1,0:T(8,128)S(1)}, u32[]{:S(2)}, u32[]{:S(2)}) collective-permute-start(f32[6,8,128]{2,1,0:T(8,128)} %get-tuple-element.31), channel_id=1, source_target_pairs={{0,4},{4,8},{8,12},{12,16},{16,20},{20,24},{24,28},{28,32},{32,36}... | collective-permute-start | bytes 73736 | tf_op jit(solution)/shard_map/ppermute | solution.py:205
  23.2 17.6 %collective-permute-start.3 = (f32[6,8,128]{2,1,0:T(8,128)S(1)}, f32[6,8,128]{2,1,0:T(8,128)S(1)}, u32[]{:S(2)}, u32[]{:S(2)}) collective-permute-start(f32[6,8,128]{2,1,0:T(8,128)S(1)} %copy-done.26), channel_id=1, source_target_pairs={{4,0},{8,4},{12,8},{16,12},{20,16},{24,20},{28,24},{32,28},{36,32}... | collective-permute-start | bytes 73736 | tf_op jit(solution)/shard_map/ppermute | solution.py:206
  26.3 7.5 %collective-permute-start.4 = (f32[6,128]{1,0:T(8,128)}, f32[6,128]{1,0:T(8,128)S(1)}, u32[]{:S(2)}, u32[]{:S(2)}) collective-permute-start(f32[6,128]{1,0:T(8,128)} %get-tuple-element.33), channel_id=1, source_target_pairs={{0,1},{1,2},{2,3},{4,5},{5,6},{6,7},{8,9},{9,10},{10,11},{12,13},{... | collective-permute-start | bytes 9224 | tf_op jit(solution)/shard_map/ppermute | solution.py:205
  33.8 7.0 %collective-permute-start.5 = (f32[6,128]{1,0:T(8,128)S(1)}, f32[6,128]{1,0:T(8,128)S(1)}, u32[]{:S(2)}, u32[]{:S(2)}) collective-permute-start(f32[6,128]{1,0:T(8,128)S(1)} %copy-done.31), channel_id=1, source_target_pairs={{1,0},{2,1},{3,2},{5,4},{6,5},{7,6},{9,8},{10,9},{11,10},{13,12},{... | collective-permute-start | bytes 9224 | tf_op jit(solution)/shard_map/ppermute | solution.py:206
  47.6 31.0 %collective-permute-start.6 = (f32[6,1,16,128]{3,2,1,0:T(8,128)}, f32[6,1,16,128]{3,2,1,0:T(8,128)S(1)}, u32[]{:S(2)}, u32[]{:S(2)}) collective-permute-start(f32[6,1,16,128]{3,2,1,0:T(8,128)} %get-tuple-element.37), channel_id=1, source_target_pairs={{0,64},{64,128},{128,192},{1,65},{65,129},{129,193},{2,66},{66,130... | collective-permute-start | bytes 147464 | tf_op jit(solution)/shard_map/ppermute | solution.py:205
  50.5 16.7 %copy-start.30 = (f32[6,128]{1,0:T(8,128)S(1)}, f32[6,128]{1,0:T(8,128)}, u32[]{:S(2)}) copy-start(f32[6,128]{1,0:T(8,128)} %get-tuple-element.41) | copy-start | bytes 9220
  50.5 28.1 %collective-permute-start.7 = (f32[6,1,16,128]{3,2,1,0:T(8,128)}, f32[6,1,16,128]{3,2,1,0:T(8,128)S(1)}, u32[]{:S(2)}, u32[]{:S(2)}) collective-permute-start(f32[6,1,16,128]{3,2,1,0:T(8,128)} %get-tuple-element.38), channel_id=1, source_target_pairs={{64,0},{128,64},{192,128},{65,1},{129,65},{193,129},{66,2},{130,66... | collective-permute-start | bytes 147464 | tf_op jit(solution)/shard_map/ppermute | solution.py:206
  52.9 25.6 %all-to-all-start.1 = ((f32[16,1,384]{2,1,0:T(1,128)}), f32[16,1,384]{2,1,0:T(1,128)S(1)}, u32[]{:S(2)}, u32[]{:S(2)}) async-start(f32[16,1,384]{2,1,0:T(1,128)} %get-tuple-element.43), calls=%async_computation.1 | async-start | bytes 49152 | tf_op jit(solution)/shard_map/all_to_all | solution.py:259
  60.9 17.6 %collective-permute-start.8 = (f32[6,8,128]{2,1,0:T(8,128)S(1)}, f32[6,8,128]{2,1,0:T(8,128)S(1)}, u32[]{:S(2)}, u32[]{:S(2)}) collective-permute-start(f32[6,8,128]{2,1,0:T(8,128)S(1)} %copy-done.25), channel_id=1, source_target_pairs={{0,4},{4,8},{8,12},{12,16},{16,20},{20,24},{24,28},{28,32},{32,36}... | collective-permute-start | bytes 73736 | tf_op jit(solution)/shard_map/ppermute | solution.py:205
  64.0 14.5 %collective-permute-start.9 = (f32[6,8,128]{2,1,0:T(8,128)S(1)}, f32[6,8,128]{2,1,0:T(8,128)S(1)}, u32[]{:S(2)}, u32[]{:S(2)}) collective-permute-start(f32[6,8,128]{2,1,0:T(8,128)S(1)} %copy-done.23), channel_id=1, source_target_pairs={{4,0},{8,4},{12,8},{16,12},{20,16},{24,20},{28,24},{32,28},{36,32}... | collective-permute-start | bytes 73736 | tf_op jit(solution)/shard_map/ppermute | solution.py:206
  67.1 4.4 %collective-permute-start.10 = (f32[6,128]{1,0:T(8,128)S(1)}, f32[6,128]{1,0:T(8,128)S(1)}, u32[]{:S(2)}, u32[]{:S(2)}) collective-permute-start(f32[6,128]{1,0:T(8,128)S(1)} %copy-done.30), channel_id=1, source_target_pairs={{0,1},{1,2},{2,3},{4,5},{5,6},{6,7},{8,9},{9,10},{10,11},{12,13},{... | collective-permute-start | bytes 9224 | tf_op jit(solution)/shard_map/ppermute | solution.py:205
  71.5 7.0 %collective-permute-start.11 = (f32[6,128]{1,0:T(8,128)S(1)}, f32[6,128]{1,0:T(8,128)S(1)}, u32[]{:S(2)}, u32[]{:S(2)}) collective-permute-start(f32[6,128]{1,0:T(8,128)S(1)} %copy-done.28), channel_id=1, source_target_pairs={{1,0},{2,1},{3,2},{5,4},{6,5},{7,6},{9,8},{10,9},{11,10},{13,12},{... | collective-permute-start | bytes 9224 | tf_op jit(solution)/shard_map/ppermute | solution.py:206
  85.3 31.0 %collective-permute-start.12 = (f32[6,1,16,128]{3,2,1,0:T(8,128)}, f32[6,1,16,128]{3,2,1,0:T(8,128)S(1)}, u32[]{:S(2)}, u32[]{:S(2)}) collective-permute-start(f32[6,1,16,128]{3,2,1,0:T(8,128)} %get-tuple-element.46), channel_id=1, source_target_pairs={{0,64},{64,128},{128,192},{1,65},{65,129},{129,193},{2,66},{66,130... | collective-permute-start | bytes 147464 | tf_op jit(solution)/shard_map/ppermute | solution.py:205
  88.2 16.7 %copy-start.29 = (f32[6,128]{1,0:T(8,128)S(1)}, f32[6,128]{1,0:T(8,128)}, u32[]{:S(2)}) copy-start(f32[6,128]{1,0:T(8,128)} %get-tuple-element.50) | copy-start | bytes 9220
  88.2 28.1 %collective-permute-start.13 = (f32[6,1,16,128]{3,2,1,0:T(8,128)}, f32[6,1,16,128]{3,2,1,0:T(8,128)S(1)}, u32[]{:S(2)}, u32[]{:S(2)}) collective-permute-start(f32[6,1,16,128]{3,2,1,0:T(8,128)} %get-tuple-element.47), channel_id=1, source_target_pairs={{64,0},{128,64},{192,128},{65,1},{129,65},{193,129},{66,2},{130,66... | collective-permute-start | bytes 147464 | tf_op jit(solution)/shard_map/ppermute | solution.py:206
  90.6 25.6 %all-to-all-start.2 = ((f32[16,1,384]{2,1,0:T(1,128)}), f32[16,1,384]{2,1,0:T(1,128)S(1)}, u32[]{:S(2)}, u32[]{:S(2)}) async-start(f32[16,1,384]{2,1,0:T(1,128)} %get-tuple-element.52), calls=%async_computation.2 | async-start | bytes 49152 | tf_op jit(solution)/shard_map/all_to_all | solution.py:259
  98.6 17.6 %collective-permute-start.14 = (f32[6,8,128]{2,1,0:T(8,128)S(1)}, f32[6,8,128]{2,1,0:T(8,128)S(1)}, u32[]{:S(2)}, u32[]{:S(2)}) collective-permute-start(f32[6,8,128]{2,1,0:T(8,128)S(1)} %copy-done.24), channel_id=1, source_target_pairs={{0,4},{4,8},{8,12},{12,16},{16,20},{20,24},{24,28},{28,32},{32,36}... | collective-permute-start | bytes 73736 | tf_op jit(solution)/shard_map/ppermute | solution.py:205
  101.7 14.5 %collective-permute-start.15 = (f32[6,8,128]{2,1,0:T(8,128)S(1)}, f32[6,8,128]{2,1,0:T(8,128)S(1)}, u32[]{:S(2)}, u32[]{:S(2)}) collective-permute-start(f32[6,8,128]{2,1,0:T(8,128)S(1)} %copy-done.22), channel_id=1, source_target_pairs={{4,0},{8,4},{12,8},{16,12},{20,16},{24,20},{28,24},{32,28},{36,32}... | collective-permute-start | bytes 73736 | tf_op jit(solution)/shard_map/ppermute | solution.py:206
  104.8 4.4 %collective-permute-start.16 = (f32[6,128]{1,0:T(8,128)S(1)}, f32[6,128]{1,0:T(8,128)S(1)}, u32[]{:S(2)}, u32[]{:S(2)}) collective-permute-start(f32[6,128]{1,0:T(8,128)S(1)} %copy-done.29), channel_id=1, source_target_pairs={{0,1},{1,2},{2,3},{4,5},{5,6},{6,7},{8,9},{9,10},{10,11},{12,13},{... | collective-permute-start | bytes 9224 | tf_op jit(solution)/shard_map/ppermute | solution.py:205
  109.2 7.0 %collective-permute-start.17 = (f32[6,128]{1,0:T(8,128)S(1)}, f32[6,128]{1,0:T(8,128)S(1)}, u32[]{:S(2)}, u32[]{:S(2)}) collective-permute-start(f32[6,128]{1,0:T(8,128)S(1)} %copy-done.27), channel_id=1, source_target_pairs={{1,0},{2,1},{3,2},{5,4},{6,5},{7,6},{9,8},{10,9},{11,10},{13,12},{... | collective-permute-start | bytes 9224 | tf_op jit(solution)/shard_map/ppermute | solution.py:206
  (29 other events, 120.0 us)

commit v4 on v3

--- a/solution.py
+++ b/solution.py
@@ -255,8 +255,9 @@
     )
     received = None
     for sweep in range(SWEEPS):
+        incoming = lax.all_to_all(rows, "span", split_axis=0, concat_axis=0, tiled=True)
+        incoming, faces = lax.optimization_barrier((incoming, faces))
         halos = exchange(faces)
-        incoming = lax.all_to_all(rows, "span", split_axis=0, concat_axis=0, tiled=True)
         if sweep == 0:
             adj, rows, received, *faces = first(*blk, adj, sensitivity, diagonal, face_coef, *halos,
                                                 incoming, send_row, orient_row, weight_row)

time: 123 us -> 137 us (1.11)
  blocking collectives: 0 us -> 37.1 us
  starting transfers between devices: 79.3 us -> 57.2 us
    all_to_all x0 -> x3, blocking collectives: none -> 37.1 us  [local(): lax.all_to_all(rows, 'span', split_axis=0, concat_axis=0, tiled=True)]
    all_to_all x3 -> x0, starting transfers between devices: 25.1 us -> none  [local(): lax.all_to_all(rows, 'span', split_axis=0, concat_axis=0, tiled=True)]
    ppermute x9, starting transfers between devices: 22.3 us -> 24.9 us  [exchange(): out.append(lax.ppermute(lo_face, axis, backward))]
    unnamed x65 -> x55, local copies, waits for them, and re-layouts: 3.17 us -> 3.16 us
  transfers between devices with their start and end apart: 21 -> 18, of which waited for: 6 -> 6; matrix products, arithmetic and copies ran while one was open for 0% -> 0% of each run, Pallas kernels for 0% -> 0%
where the time goes in v4:
time: 137 us; the launch traced here: 136 us
  starting transfers between devices  57.2 us (42%)
  blocking collectives  37.1 us (27%)
  Pallas kernels  20.5 us (15%)
  waiting for transfers between devices  17.4 us (13%)
  local copies, waits for them, and re-layouts  3.16 us (2%)
    all_to_all x3, blocking collectives, local(): lax.all_to_all(rows, 'span', split_axis=0, concat_axis=0, tiled=True)  37.1 us
    ppermute x9, starting transfers between devices, exchange(): out.append(lax.ppermute(hi_face, axis, forward))  32.2 us
    ppermute x9, starting transfers between devices, exchange(): out.append(lax.ppermute(lo_face, axis, backward))  24.9 us
    ppermute x9, waiting for transfers between devices, exchange(): out.append(lax.ppermute(lo_face, axis, backward))  15 us
    pallas_call x1, Pallas kernels, local(): step(*blk, adj, sensitivity, diagonal, face_coef, *halos, incoming, recei...  6.09 us
    pallas_call x1, Pallas kernels, local(): first(*blk, adj, sensitivity, diagonal, face_coef, *halos, incoming, send...  6.09 us
    pallas_call x1, Pallas kernels, local(): last(*blk, adj, sensitivity, diagonal, face_coef, *halos, incoming, recei...  4.58 us
    pallas_call x1, Pallas kernels, local(): init(*blk, sensitivity, diagonal, send_row, orient_row, weight_row, targe...  3.73 us
  transfers between devices with their start and end apart: 18, of which 6 were waited for; matrix products, arithmetic and copies ran while one was open for 0% of the time, Pallas kernels for 0%

profile of v4, /device:TPU:49, one launch (start us, length us, event | category | flops | bytes accessed | tf_op | source)
XLA Modules:
  0.0 136.4 jit_solution(3289420113912529611)
XLA Ops:
  1.9 3.7 %shard_map.122 = (f32[6,8,16,128]{3,2,1,0:T(8,128)}, f32[16,1,448]{2,1,0:T(1,128)}, f32[6,1,16,128]{3,2,1,0:T(8,128)}, f32[6,1,16,128]{3,2,1,0:T(8,128)}, f32[6,...) custom-call(f32[3,6,6]{2,1,0:T(8,128)} %ub_ref.7, f32[3,6,6]{2,1,0:T(8,128)} %lb_ref.7, ...), custom_call_target="tpu_custom_call" | custom-call | tf_op jit(solution)/shard_map/pallas_call | solution.py:236
  5.7 15.7 %all_to_all.15.inc_ref = f32[16,1,448]{2,1,0:T(1,128)} all-to-all(f32[16,1,448]{2,1,0:T(1,128)} %get-tuple-element.50), channel_id=1, replica_groups=mesh['chord'=4,'span'=16,'wall'=4] {'span'}, dimensions={0} | all-to-all | bytes 57344 | tf_op jit(solution)/shard_map/all_to_all | solution.py:258
  21.3 3.0 %collective-permute-start = (f32[6,1,16,128]{3,2,1,0:T(8,128)}, f32[6,1,16,128]{3,2,1,0:T(8,128)S(1)}, u32[]{:S(2)}, u32[]{:S(2)}) collective-permute-start(f32[6,1,16,128]{3,2,1,0:T(8,128)} %get-tuple-element.57), channel_id=1, source_target_pairs={{0,64},{64,128},{128,192},{1,65},{65,129},{129,193},{2,66},{66,130... | collective-permute-start | bytes 147464 | tf_op jit(solution)/shard_map/ppermute | solution.py:205
  24.4 2.4 %collective-permute-start.1 = (f32[6,1,16,128]{3,2,1,0:T(8,128)S(1)}, f32[6,1,16,128]{3,2,1,0:T(8,128)S(1)}, u32[]{:S(2)}, u32[]{:S(2)}) collective-permute-start(f32[6,1,16,128]{3,2,1,0:T(8,128)S(1)} %copy-done.20), channel_id=1, source_target_pairs={{64,0},{128,64},{192,128},{65,1},{129,65},{193,129},{66,2},{130,66... | collective-permute-start | bytes 147464 | tf_op jit(solution)/shard_map/ppermute | solution.py:206
  26.8 2.2 %collective-permute-start.2 = (f32[6,8,128]{2,1,0:T(8,128)}, f32[6,8,128]{2,1,0:T(8,128)S(1)}, u32[]{:S(2)}, u32[]{:S(2)}) collective-permute-start(f32[6,8,128]{2,1,0:T(8,128)} %get-tuple-element.59), channel_id=1, source_target_pairs={{0,4},{4,8},{8,12},{12,16},{16,20},{20,24},{24,28},{28,32},{32,36}... | collective-permute-start | bytes 73736 | tf_op jit(solution)/shard_map/ppermute | solution.py:205
  29.0 3.9 %collective-permute-start.3 = (f32[6,8,128]{2,1,0:T(8,128)S(1)}, f32[6,8,128]{2,1,0:T(8,128)S(1)}, u32[]{:S(2)}, u32[]{:S(2)}) collective-permute-start(f32[6,8,128]{2,1,0:T(8,128)S(1)} %copy-done.21), channel_id=1, source_target_pairs={{4,0},{8,4},{12,8},{16,12},{20,16},{24,20},{28,24},{32,28},{36,32}... | collective-permute-start | bytes 73736 | tf_op jit(solution)/shard_map/ppermute | solution.py:206
  33.0 7.5 %collective-permute-start.4 = (f32[6,128]{1,0:T(8,128)}, f32[6,128]{1,0:T(8,128)S(1)}, u32[]{:S(2)}, u32[]{:S(2)}) collective-permute-start(f32[6,128]{1,0:T(8,128)} %get-tuple-element.61), channel_id=1, source_target_pairs={{0,1},{1,2},{2,3},{4,5},{5,6},{6,7},{8,9},{9,10},{10,11},{12,13},{... | collective-permute-start | bytes 9224 | tf_op jit(solution)/shard_map/ppermute | solution.py:205
  43.3 5.0 %collective-permute-done.5.hwh = f32[6,128]{1,0:T(8,128)S(1)} collective-permute-done((f32[6,128]{1,0:T(8,128)S(1)}, f32[6,128]{1,0:T(8,128)S(1)}, u32[]{:S(2)}, u32[]{:S(2)}) %collective-permute-start.5) | collective-permute-done | bytes 3104 | tf_op jit(solution)/shard_map/ppermute | solution.py:206
  49.0 6.1 %shard_map.123 = (f32[6,8,16,128]{3,2,1,0:T(8,128)}, f32[16,1,384]{2,1,0:T(1,128)}, s32[1,1024]{1,0:T(1,128)}, f32[6,1,16,128]{3,2,1,0:T(8,128)}, f32[6,1,16,128...) custom-call(f32[3,6,6]{2,1,0:T(8,128)} %ub_ref.7, ...), custom_call_target="tpu_custom_call" | custom-call | tf_op jit(solution)/shard_map/pallas_call | solution.py:262
  55.1 10.8 %all_to_all.16.inc_ref = f32[16,1,384]{2,1,0:T(1,128)} all-to-all(f32[16,1,384]{2,1,0:T(1,128)} %get-tuple-element.65), channel_id=1, replica_groups=mesh['chord'=4,'span'=16,'wall'=4] {'span'}, dimensions={0} | all-to-all | bytes 49152 | tf_op jit(solution)/shard_map/all_to_all | solution.py:258
  65.9 3.0 %collective-permute-start.6 = (f32[6,1,16,128]{3,2,1,0:T(8,128)}, f32[6,1,16,128]{3,2,1,0:T(8,128)S(1)}, u32[]{:S(2)}, u32[]{:S(2)}) collective-permute-start(f32[6,1,16,128]{3,2,1,0:T(8,128)} %get-tuple-element.72), channel_id=1, source_target_pairs={{0,64},{64,128},{128,192},{1,65},{65,129},{129,193},{2,66},{66,130... | collective-permute-start | bytes 147464 | tf_op jit(solution)/shard_map/ppermute | solution.py:205
  69.0 2.4 %collective-permute-start.7 = (f32[6,1,16,128]{3,2,1,0:T(8,128)S(1)}, f32[6,1,16,128]{3,2,1,0:T(8,128)S(1)}, u32[]{:S(2)}, u32[]{:S(2)}) collective-permute-start(f32[6,1,16,128]{3,2,1,0:T(8,128)S(1)} %copy-done.19), channel_id=1, source_target_pairs={{64,0},{128,64},{192,128},{65,1},{129,65},{193,129},{66,2},{130,66... | collective-permute-start | bytes 147464 | tf_op jit(solution)/shard_map/ppermute | solution.py:206
  73.5 4.0 %collective-permute-start.9 = (f32[6,8,128]{2,1,0:T(8,128)}, f32[6,8,128]{2,1,0:T(8,128)S(1)}, u32[]{:S(2)}, u32[]{:S(2)}) collective-permute-start(f32[6,8,128]{2,1,0:T(8,128)} %get-tuple-element.75), channel_id=1, source_target_pairs={{4,0},{8,4},{12,8},{16,12},{20,16},{24,20},{28,24},{32,28},{36,32}... | collective-permute-start | bytes 73736 | tf_op jit(solution)/shard_map/ppermute | solution.py:206
  77.5 4.5 %collective-permute-start.10 = (f32[6,128]{1,0:T(8,128)S(1)}, f32[6,128]{1,0:T(8,128)S(1)}, u32[]{:S(2)}, u32[]{:S(2)}) collective-permute-start(f32[6,128]{1,0:T(8,128)S(1)} %copy-done.25), channel_id=1, source_target_pairs={{0,1},{1,2},{2,3},{4,5},{5,6},{6,7},{8,9},{9,10},{10,11},{12,13},{... | collective-permute-start | bytes 9224 | tf_op jit(solution)/shard_map/ppermute | solution.py:205
  84.7 5.0 %collective-permute-done.11.hwh = f32[6,128]{1,0:T(8,128)S(1)} collective-permute-done((f32[6,128]{1,0:T(8,128)S(1)}, f32[6,128]{1,0:T(8,128)S(1)}, u32[]{:S(2)}, u32[]{:S(2)}) %collective-permute-start.11) | collective-permute-done | bytes 3104 | tf_op jit(solution)/shard_map/ppermute | solution.py:206
  90.5 6.1 %shard_map.124 = (f32[6,8,16,128]{3,2,1,0:T(8,128)}, f32[16,1,384]{2,1,0:T(1,128)}, s32[1,1024]{1,0:T(1,128)}, f32[6,1,16,128]{3,2,1,0:T(8,128)}, f32[6,1,16,128...) custom-call(f32[3,6,6]{2,1,0:T(8,128)} %ub_ref.7, ...), custom_call_target="tpu_custom_call" | custom-call | tf_op jit(solution)/shard_map/pallas_call | solution.py:265
  96.6 10.7 %all_to_all.17.inc_ref = f32[16,1,384]{2,1,0:T(1,128)} all-to-all(f32[16,1,384]{2,1,0:T(1,128)} %get-tuple-element.81), channel_id=1, replica_groups=mesh['chord'=4,'span'=16,'wall'=4] {'span'}, dimensions={0} | all-to-all | bytes 49152 | tf_op jit(solution)/shard_map/all_to_all | solution.py:258
  107.3 3.0 %collective-permute-start.12 = (f32[6,1,16,128]{3,2,1,0:T(8,128)}, f32[6,1,16,128]{3,2,1,0:T(8,128)S(1)}, u32[]{:S(2)}, u32[]{:S(2)}) collective-permute-start(f32[6,1,16,128]{3,2,1,0:T(8,128)} %get-tuple-element.88), channel_id=1, source_target_pairs={{0,64},{64,128},{128,192},{1,65},{65,129},{129,193},{2,66},{66,130... | collective-permute-start | bytes 147464 | tf_op jit(solution)/shard_map/ppermute | solution.py:205
  110.3 2.4 %collective-permute-start.13 = (f32[6,1,16,128]{3,2,1,0:T(8,128)S(1)}, f32[6,1,16,128]{3,2,1,0:T(8,128)S(1)}, u32[]{:S(2)}, u32[]{:S(2)}) collective-permute-start(f32[6,1,16,128]{3,2,1,0:T(8,128)S(1)} %copy-done.18), channel_id=1, source_target_pairs={{64,0},{128,64},{192,128},{65,1},{129,65},{193,129},{66,2},{130,66... | collective-permute-start | bytes 147464 | tf_op jit(solution)/shard_map/ppermute | solution.py:206
  112.7 2.2 %collective-permute-start.14 = (f32[6,8,128]{2,1,0:T(8,128)}, f32[6,8,128]{2,1,0:T(8,128)S(1)}, u32[]{:S(2)}, u32[]{:S(2)}) collective-permute-start(f32[6,8,128]{2,1,0:T(8,128)} %get-tuple-element.90), channel_id=1, source_target_pairs={{0,4},{4,8},{8,12},{12,16},{16,20},{20,24},{24,28},{28,32},{32,36}... | collective-permute-start | bytes 73736 | tf_op jit(solution)/shard_map/ppermute | solution.py:205
  114.9 4.0 %collective-permute-start.15 = (f32[6,8,128]{2,1,0:T(8,128)}, f32[6,8,128]{2,1,0:T(8,128)S(1)}, u32[]{:S(2)}, u32[]{:S(2)}) collective-permute-start(f32[6,8,128]{2,1,0:T(8,128)} %get-tuple-element.91), channel_id=1, source_target_pairs={{4,0},{8,4},{12,8},{16,12},{20,16},{24,20},{28,24},{32,28},{36,32}... | collective-permute-start | bytes 73736 | tf_op jit(solution)/shard_map/ppermute | solution.py:206
  118.9 4.5 %collective-permute-start.16 = (f32[6,128]{1,0:T(8,128)S(1)}, f32[6,128]{1,0:T(8,128)S(1)}, u32[]{:S(2)}, u32[]{:S(2)}) collective-permute-start(f32[6,128]{1,0:T(8,128)S(1)} %copy-done.24), channel_id=1, source_target_pairs={{0,1},{1,2},{2,3},{4,5},{5,6},{6,7},{8,9},{9,10},{10,11},{12,13},{... | collective-permute-start | bytes 9224 | tf_op jit(solution)/shard_map/ppermute | solution.py:205
  126.3 4.9 %collective-permute-done.17.hwh = f32[6,128]{1,0:T(8,128)S(1)} collective-permute-done((f32[6,128]{1,0:T(8,128)S(1)}, f32[6,128]{1,0:T(8,128)S(1)}, u32[]{:S(2)}, u32[]{:S(2)}) %collective-permute-start.17) | collective-permute-done | bytes 3104 | tf_op jit(solution)/shard_map/ppermute | solution.py:206
  131.8 4.6 %shard_map.125 = (f32[6,8,16,128]{3,2,1,0:T(8,128)}, f32[8,16,128]{2,1,0:T(8,128)}) custom-call(f32[3,6,6]{2,1,0:T(8,128)} %ub_ref.7, f32[3,6,6]{2,1,0:T(8,128)} %lb_ref.7, f32[2,6,6]{2,1,0:T(8,128)} %copy.16.ib_ref, f32[6,8,16,128]{3,2,1,0:T(8,128)} %get-tuple-element.80.adj_ref, f32[6,8,16,128]{3,2,1,0:T(8,128)} %sens_ref.7, f32[6,8,16,128]{3,2,1,0:T(8,128)} %diag_ref.7, ...), custom_call_target="tpu_custom_call" | custom-call | tf_op jit(solution)/shard_map/pallas_call | solution.py:268
  (74 shorter events, 13.7 us)
Async XLA Ops:
  5.6 18.7 %copy-start.20 = (f32[6,1,16,128]{3,2,1,0:T(8,128)S(1)}, f32[6,1,16,128]{3,2,1,0:T(8,128)}, u32[]{:S(2)}) copy-start(f32[6,1,16,128]{3,2,1,0:T(8,128)} %get-tuple-element.58) | copy-start | bytes 147460
  5.7 23.4 %copy-start.21 = (f32[6,8,128]{2,1,0:T(8,128)S(1)}, f32[6,8,128]{2,1,0:T(8,128)}, u32[]{:S(2)}) copy-start(f32[6,8,128]{2,1,0:T(8,128)} %get-tuple-element.60) | copy-start | bytes 73732
  21.3 20.1 %copy-start.26 = (f32[6,128]{1,0:T(8,128)S(1)}, f32[6,128]{1,0:T(8,128)}, u32[]{:S(2)}) copy-start(f32[6,128]{1,0:T(8,128)} %get-tuple-element.62) | copy-start | bytes 9220
  21.3 27.0 %collective-permute-start = (f32[6,1,16,128]{3,2,1,0:T(8,128)}, f32[6,1,16,128]{3,2,1,0:T(8,128)S(1)}, u32[]{:S(2)}, u32[]{:S(2)}) collective-permute-start(f32[6,1,16,128]{3,2,1,0:T(8,128)} %get-tuple-element.57), channel_id=1, source_target_pairs={{0,64},{64,128},{128,192},{1,65},{65,129},{129,193},{2,66},{66,130... | collective-permute-start | bytes 147464 | tf_op jit(solution)/shard_map/ppermute | solution.py:205
  24.4 24.0 %collective-permute-start.1 = (f32[6,1,16,128]{3,2,1,0:T(8,128)S(1)}, f32[6,1,16,128]{3,2,1,0:T(8,128)S(1)}, u32[]{:S(2)}, u32[]{:S(2)}) collective-permute-start(f32[6,1,16,128]{3,2,1,0:T(8,128)S(1)} %copy-done.20), channel_id=1, source_target_pairs={{64,0},{128,64},{192,128},{65,1},{129,65},{193,129},{66,2},{130,66... | collective-permute-start | bytes 147464 | tf_op jit(solution)/shard_map/ppermute | solution.py:206
  26.8 21.6 %collective-permute-start.2 = (f32[6,8,128]{2,1,0:T(8,128)}, f32[6,8,128]{2,1,0:T(8,128)S(1)}, u32[]{:S(2)}, u32[]{:S(2)}) collective-permute-start(f32[6,8,128]{2,1,0:T(8,128)} %get-tuple-element.59), channel_id=1, source_target_pairs={{0,4},{4,8},{8,12},{12,16},{16,20},{20,24},{24,28},{28,32},{32,36}... | collective-permute-start | bytes 73736 | tf_op jit(solution)/shard_map/ppermute | solution.py:205
  29.0 19.3 %collective-permute-start.3 = (f32[6,8,128]{2,1,0:T(8,128)S(1)}, f32[6,8,128]{2,1,0:T(8,128)S(1)}, u32[]{:S(2)}, u32[]{:S(2)}) collective-permute-start(f32[6,8,128]{2,1,0:T(8,128)S(1)} %copy-done.21), channel_id=1, source_target_pairs={{4,0},{8,4},{12,8},{16,12},{20,16},{24,20},{28,24},{32,28},{36,32}... | collective-permute-start | bytes 73736 | tf_op jit(solution)/shard_map/ppermute | solution.py:206
  33.0 8.4 %collective-permute-start.4 = (f32[6,128]{1,0:T(8,128)}, f32[6,128]{1,0:T(8,128)S(1)}, u32[]{:S(2)}, u32[]{:S(2)}) collective-permute-start(f32[6,128]{1,0:T(8,128)} %get-tuple-element.61), channel_id=1, source_target_pairs={{0,1},{1,2},{2,3},{4,5},{5,6},{6,7},{8,9},{9,10},{10,11},{12,13},{... | collective-permute-start | bytes 9224 | tf_op jit(solution)/shard_map/ppermute | solution.py:205
  41.4 7.0 %collective-permute-start.5 = (f32[6,128]{1,0:T(8,128)S(1)}, f32[6,128]{1,0:T(8,128)S(1)}, u32[]{:S(2)}, u32[]{:S(2)}) collective-permute-start(f32[6,128]{1,0:T(8,128)S(1)} %copy-done.26), channel_id=1, source_target_pairs={{1,0},{2,1},{3,2},{5,4},{6,5},{7,6},{9,8},{10,9},{11,10},{13,12},{... | collective-permute-start | bytes 9224 | tf_op jit(solution)/shard_map/ppermute | solution.py:206
  55.1 13.8 %copy-start.19 = (f32[6,1,16,128]{3,2,1,0:T(8,128)S(1)}, f32[6,1,16,128]{3,2,1,0:T(8,128)}, u32[]{:S(2)}) copy-start(f32[6,1,16,128]{3,2,1,0:T(8,128)} %get-tuple-element.73) | copy-start | bytes 147460
  65.9 16.9 %copy-start.23 = (f32[6,128]{1,0:T(8,128)S(1)}, f32[6,128]{1,0:T(8,128)}, u32[]{:S(2)}) copy-start(f32[6,128]{1,0:T(8,128)} %get-tuple-element.77) | copy-start | bytes 9220
  65.9 23.9 %collective-permute-start.6 = (f32[6,1,16,128]{3,2,1,0:T(8,128)}, f32[6,1,16,128]{3,2,1,0:T(8,128)S(1)}, u32[]{:S(2)}, u32[]{:S(2)}) collective-permute-start(f32[6,1,16,128]{3,2,1,0:T(8,128)} %get-tuple-element.72), channel_id=1, source_target_pairs={{0,64},{64,128},{128,192},{1,65},{65,129},{129,193},{2,66},{66,130... | collective-permute-start | bytes 147464 | tf_op jit(solution)/shard_map/ppermute | solution.py:205
  69.0 20.9 %collective-permute-start.7 = (f32[6,1,16,128]{3,2,1,0:T(8,128)S(1)}, f32[6,1,16,128]{3,2,1,0:T(8,128)S(1)}, u32[]{:S(2)}, u32[]{:S(2)}) collective-permute-start(f32[6,1,16,128]{3,2,1,0:T(8,128)S(1)} %copy-done.19), channel_id=1, source_target_pairs={{64,0},{128,64},{192,128},{65,1},{129,65},{193,129},{66,2},{130,66... | collective-permute-start | bytes 147464 | tf_op jit(solution)/shard_map/ppermute | solution.py:206
  71.3 18.4 %collective-permute-start.8 = (f32[6,8,128]{2,1,0:T(8,128)}, f32[6,8,128]{2,1,0:T(8,128)S(1)}, u32[]{:S(2)}, u32[]{:S(2)}) collective-permute-start(f32[6,8,128]{2,1,0:T(8,128)} %get-tuple-element.74), channel_id=1, source_target_pairs={{0,4},{4,8},{8,12},{12,16},{16,20},{20,24},{24,28},{28,32},{32,36}... | collective-permute-start | bytes 73736 | tf_op jit(solution)/shard_map/ppermute | solution.py:205
  73.5 16.3 %collective-permute-start.9 = (f32[6,8,128]{2,1,0:T(8,128)}, f32[6,8,128]{2,1,0:T(8,128)S(1)}, u32[]{:S(2)}, u32[]{:S(2)}) collective-permute-start(f32[6,8,128]{2,1,0:T(8,128)} %get-tuple-element.75), channel_id=1, source_target_pairs={{4,0},{8,4},{12,8},{16,12},{20,16},{24,20},{28,24},{32,28},{36,32}... | collective-permute-start | bytes 73736 | tf_op jit(solution)/shard_map/ppermute | solution.py:206
  77.5 5.3 %collective-permute-start.10 = (f32[6,128]{1,0:T(8,128)S(1)}, f32[6,128]{1,0:T(8,128)S(1)}, u32[]{:S(2)}, u32[]{:S(2)}) collective-permute-start(f32[6,128]{1,0:T(8,128)S(1)} %copy-done.25), channel_id=1, source_target_pairs={{0,1},{1,2},{2,3},{4,5},{5,6},{6,7},{8,9},{9,10},{10,11},{12,13},{... | collective-permute-start | bytes 9224 | tf_op jit(solution)/shard_map/ppermute | solution.py:205
  82.8 7.0 %collective-permute-start.11 = (f32[6,128]{1,0:T(8,128)S(1)}, f32[6,128]{1,0:T(8,128)S(1)}, u32[]{:S(2)}, u32[]{:S(2)}) collective-permute-start(f32[6,128]{1,0:T(8,128)S(1)} %copy-done.23), channel_id=1, source_target_pairs={{1,0},{2,1},{3,2},{5,4},{6,5},{7,6},{9,8},{10,9},{11,10},{13,12},{... | collective-permute-start | bytes 9224 | tf_op jit(solution)/shard_map/ppermute | solution.py:206
  107.3 16.9 %copy-start.22 = (f32[6,128]{1,0:T(8,128)S(1)}, f32[6,128]{1,0:T(8,128)}, u32[]{:S(2)}) copy-start(f32[6,128]{1,0:T(8,128)} %get-tuple-element.93) | copy-start | bytes 9220
  107.3 23.9 %collective-permute-start.12 = (f32[6,1,16,128]{3,2,1,0:T(8,128)}, f32[6,1,16,128]{3,2,1,0:T(8,128)S(1)}, u32[]{:S(2)}, u32[]{:S(2)}) collective-permute-start(f32[6,1,16,128]{3,2,1,0:T(8,128)} %get-tuple-element.88), channel_id=1, source_target_pairs={{0,64},{64,128},{128,192},{1,65},{65,129},{129,193},{2,66},{66,130... | collective-permute-start | bytes 147464 | tf_op jit(solution)/shard_map/ppermute | solution.py:205
  110.3 20.9 %collective-permute-start.13 = (f32[6,1,16,128]{3,2,1,0:T(8,128)S(1)}, f32[6,1,16,128]{3,2,1,0:T(8,128)S(1)}, u32[]{:S(2)}, u32[]{:S(2)}) collective-permute-start(f32[6,1,16,128]{3,2,1,0:T(8,128)S(1)} %copy-done.18), channel_id=1, source_target_pairs={{64,0},{128,64},{192,128},{65,1},{129,65},{193,129},{66,2},{130,66... | collective-permute-start | bytes 147464 | tf_op jit(solution)/shard_map/ppermute | solution.py:206
  112.7 18.4 %collective-permute-start.14 = (f32[6,8,128]{2,1,0:T(8,128)}, f32[6,8,128]{2,1,0:T(8,128)S(1)}, u32[]{:S(2)}, u32[]{:S(2)}) collective-permute-start(f32[6,8,128]{2,1,0:T(8,128)} %get-tuple-element.90), channel_id=1, source_target_pairs={{0,4},{4,8},{8,12},{12,16},{16,20},{20,24},{24,28},{28,32},{32,36}... | collective-permute-start | bytes 73736 | tf_op jit(solution)/shard_map/ppermute | solution.py:205
  114.9 16.3 %collective-permute-start.15 = (f32[6,8,128]{2,1,0:T(8,128)}, f32[6,8,128]{2,1,0:T(8,128)S(1)}, u32[]{:S(2)}, u32[]{:S(2)}) collective-permute-start(f32[6,8,128]{2,1,0:T(8,128)} %get-tuple-element.91), channel_id=1, source_target_pairs={{4,0},{8,4},{12,8},{16,12},{20,16},{24,20},{28,24},{32,28},{36,32}... | collective-permute-start | bytes 73736 | tf_op jit(solution)/shard_map/ppermute | solution.py:206
  118.9 5.3 %collective-permute-start.16 = (f32[6,128]{1,0:T(8,128)S(1)}, f32[6,128]{1,0:T(8,128)S(1)}, u32[]{:S(2)}, u32[]{:S(2)}) collective-permute-start(f32[6,128]{1,0:T(8,128)S(1)} %copy-done.24), channel_id=1, source_target_pairs={{0,1},{1,2},{2,3},{4,5},{5,6},{6,7},{8,9},{9,10},{10,11},{12,13},{... | collective-permute-start | bytes 9224 | tf_op jit(solution)/shard_map/ppermute | solution.py:205
  124.2 7.0 %collective-permute-start.17 = (f32[6,128]{1,0:T(8,128)S(1)}, f32[6,128]{1,0:T(8,128)S(1)}, u32[]{:S(2)}, u32[]{:S(2)}) collective-permute-start(f32[6,128]{1,0:T(8,128)S(1)} %copy-done.22), channel_id=1, source_target_pairs={{1,0},{2,1},{3,2},{5,4},{6,5},{7,6},{9,8},{10,9},{11,10},{13,12},{... | collective-permute-start | bytes 9224 | tf_op jit(solution)/shard_map/ppermute | solution.py:206
  (21 other events, 67.2 us)

commit v5 on v3

--- a/solution.py
+++ b/solution.py
@@ -27,10 +27,8 @@
     lane_hot = (lax.broadcasted_iota(jnp.int32, (lanes, n_rows), 0) == lane_of).astype(BF16)
     row_hot = (lax.broadcasted_iota(jnp.int32, (rows, n_rows), 0) == row_of).astype(F32)
     flat = adj.reshape(n_var * rows, lanes)
-    picked = None
-    for part in split3(flat):
-        term = jnp.dot(part, lane_hot, preferred_element_type=F32)
-        picked = term if picked is None else picked + term
+    picked = jnp.dot(jnp.concatenate(split3(flat), axis=1),
+                     jnp.concatenate([lane_hot] * 3, axis=0), preferred_element_type=F32)
     src = jnp.sum(picked.reshape(n_var, rows, n_rows) * row_hot[None], axis=1)
     orient = flat_row(orient_ref[...])
     weight = flat_row(weight_ref[...])
@@ -126,11 +124,10 @@
     lane_of = cell % nz
     row_hot = (lax.broadcasted_iota(jnp.int32, (rows, n_rows), 0) == row_of).astype(BF16)
     lane_hot = (lax.broadcasted_iota(jnp.int32, (nz, n_rows), 0) == lane_of).astype(BF16)
-    coupled = None
-    for part in split3(incoming):
-        lhs = (row_hot[None] * part[:, None, :]).reshape(n_var * rows, n_rows)
-        term = lax.dot_general(lhs, lane_hot, (((1,), (1,)), ((), ())), preferred_element_type=F32)
-        coupled = term if coupled is None else coupled + term
+    lhs = jnp.concatenate([(row_hot[None] * part[:, None, :]).reshape(n_var * rows, n_rows)
+                           for part in split3(incoming)], axis=1)
+    coupled = lax.dot_general(lhs, jnp.concatenate([lane_hot] * 3, axis=1), (((1,), (1,)), ((), ())),
+                              preferred_element_type=F32)
     coupled = coupled.reshape(n_var, nx, ny, nz)
     new = []
     for i in range(n_var):

time: 123 us -> 121 us (0.984)
  Pallas kernels: 20.5 us -> 19 us
where the time goes in v5:
time: 121 us; the launch traced here: 120 us
  starting transfers between devices  79.3 us (66%)
  Pallas kernels  19 us (16%)
  waiting for transfers between devices  17.4 us (14%)
  local copies, waits for them, and re-layouts  3.17 us (3%)
    ppermute x9, starting transfers between devices, exchange(): out.append(lax.ppermute(hi_face, axis, forward))  31.8 us
    all_to_all x3, starting transfers between devices, local(): lax.all_to_all(rows, 'span', split_axis=0, concat_axis=0, tiled=True)  25.1 us
    ppermute x9, starting transfers between devices, exchange(): out.append(lax.ppermute(lo_face, axis, backward))  22.3 us
    ppermute x9, waiting for transfers between devices, exchange(): out.append(lax.ppermute(lo_face, axis, backward))  15 us
    pallas_call x1, Pallas kernels, local(): step(*blk, adj, sensitivity, diagonal, face_coef, *halos, incoming, recei...  5.55 us
    pallas_call x1, Pallas kernels, local(): first(*blk, adj, sensitivity, diagonal, face_coef, *halos, incoming, send...  5.53 us
    pallas_call x1, Pallas kernels, local(): last(*blk, adj, sensitivity, diagonal, face_coef, *halos, incoming, recei...  4.67 us
    pallas_call x1, Pallas kernels, local(): init(*blk, sensitivity, diagonal, send_row, orient_row, weight_row, targe...  3.22 us
  transfers between devices with their start and end apart: 21, of which 6 were waited for; matrix products, arithmetic and copies ran while one was open for 0% of the time, Pallas kernels for 0%

profile of v5, /device:TPU:49, one launch (start us, length us, event | category | flops | bytes accessed | tf_op | source)
XLA Modules:
  0.0 119.9 jit_solution(7934250052592990906)
XLA Ops:
  1.9 3.2 %shard_map.122 = (f32[6,8,16,128]{3,2,1,0:T(8,128)}, f32[16,1,448]{2,1,0:T(1,128)}, f32[6,1,16,128]{3,2,1,0:T(8,128)}, f32[6,1,16,128]{3,2,1,0:T(8,128)}, f32[6,...) custom-call(f32[3,6,6]{2,1,0:T(8,128)} %ub_ref.7, f32[3,6,6]{2,1,0:T(8,128)} %lb_ref.7, ...), custom_call_target="tpu_custom_call" | custom-call | tf_op jit(solution)/shard_map/pallas_call | solution.py:233
  5.2 9.1 %all-to-all-start = ((f32[16,1,448]{2,1,0:T(1,128)}), f32[16,1,448]{2,1,0:T(1,128)S(1)}, u32[]{:S(2)}, u32[]{:S(2)}) async-start(f32[16,1,448]{2,1,0:T(1,128)} %get-tuple-element.35), calls=%async_computation | async-start | bytes 65536 | tf_op jit(solution)/shard_map/all_to_all | solution.py:256
  14.3 2.9 %collective-permute-start = (f32[6,1,16,128]{3,2,1,0:T(8,128)}, f32[6,1,16,128]{3,2,1,0:T(8,128)S(1)}, u32[]{:S(2)}, u32[]{:S(2)}) collective-permute-start(f32[6,1,16,128]{3,2,1,0:T(8,128)} %get-tuple-element.29), channel_id=1, source_target_pairs={{0,64},{64,128},{128,192},{1,65},{65,129},{129,193},{2,66},{66,130... | collective-permute-start | bytes 147464 | tf_op jit(solution)/shard_map/ppermute | solution.py:202
  19.6 3.1 %collective-permute-start.2 = (f32[6,8,128]{2,1,0:T(8,128)}, f32[6,8,128]{2,1,0:T(8,128)S(1)}, u32[]{:S(2)}, u32[]{:S(2)}) collective-permute-start(f32[6,8,128]{2,1,0:T(8,128)} %get-tuple-element.31), channel_id=1, source_target_pairs={{0,4},{4,8},{8,12},{12,16},{16,20},{20,24},{24,28},{28,32},{32,36}... | collective-permute-start | bytes 73736 | tf_op jit(solution)/shard_map/ppermute | solution.py:202
  22.7 3.1 %collective-permute-start.3 = (f32[6,8,128]{2,1,0:T(8,128)S(1)}, f32[6,8,128]{2,1,0:T(8,128)S(1)}, u32[]{:S(2)}, u32[]{:S(2)}) collective-permute-start(f32[6,8,128]{2,1,0:T(8,128)S(1)} %copy-done.26), channel_id=1, source_target_pairs={{4,0},{8,4},{12,8},{16,12},{20,16},{24,20},{28,24},{32,28},{36,32}... | collective-permute-start | bytes 73736 | tf_op jit(solution)/shard_map/ppermute | solution.py:203
  25.8 6.6 %collective-permute-start.4 = (f32[6,128]{1,0:T(8,128)}, f32[6,128]{1,0:T(8,128)S(1)}, u32[]{:S(2)}, u32[]{:S(2)}) collective-permute-start(f32[6,128]{1,0:T(8,128)} %get-tuple-element.33), channel_id=1, source_target_pairs={{0,1},{1,2},{2,3},{4,5},{5,6},{6,7},{8,9},{9,10},{10,11},{12,13},{... | collective-permute-start | bytes 9224 | tf_op jit(solution)/shard_map/ppermute | solution.py:202
  35.2 5.0 %collective-permute-done.5.hwh = f32[6,128]{1,0:T(8,128)S(1)} collective-permute-done((f32[6,128]{1,0:T(8,128)S(1)}, f32[6,128]{1,0:T(8,128)S(1)}, u32[]{:S(2)}, u32[]{:S(2)}) %collective-permute-start.5) | collective-permute-done | bytes 3104 | tf_op jit(solution)/shard_map/ppermute | solution.py:203
  41.0 5.5 %shard_map.123 = (f32[6,8,16,128]{3,2,1,0:T(8,128)}, f32[16,1,384]{2,1,0:T(1,128)}, s32[1,1024]{1,0:T(1,128)}, f32[6,1,16,128]{3,2,1,0:T(8,128)}, f32[6,1,16,128...) custom-call(f32[3,6,6]{2,1,0:T(8,128)} %ub_ref.7, ...), custom_call_target="tpu_custom_call" | custom-call | tf_op jit(solution)/shard_map/pallas_call | solution.py:258
  46.5 2.9 %collective-permute-start.6 = (f32[6,1,16,128]{3,2,1,0:T(8,128)}, f32[6,1,16,128]{3,2,1,0:T(8,128)S(1)}, u32[]{:S(2)}, u32[]{:S(2)}) collective-permute-start(f32[6,1,16,128]{3,2,1,0:T(8,128)} %get-tuple-element.37), channel_id=1, source_target_pairs={{0,64},{64,128},{128,192},{1,65},{65,129},{129,193},{2,66},{66,130... | collective-permute-start | bytes 147464 | tf_op jit(solution)/shard_map/ppermute | solution.py:202
  49.4 2.4 %collective-permute-start.7 = (f32[6,1,16,128]{3,2,1,0:T(8,128)}, f32[6,1,16,128]{3,2,1,0:T(8,128)S(1)}, u32[]{:S(2)}, u32[]{:S(2)}) collective-permute-start(f32[6,1,16,128]{3,2,1,0:T(8,128)} %get-tuple-element.38), channel_id=1, source_target_pairs={{64,0},{128,64},{192,128},{65,1},{129,65},{193,129},{66,2},{130,66... | collective-permute-start | bytes 147464 | tf_op jit(solution)/shard_map/ppermute | solution.py:203
  51.8 8.0 %all-to-all-start.1 = ((f32[16,1,384]{2,1,0:T(1,128)}), f32[16,1,384]{2,1,0:T(1,128)S(1)}, u32[]{:S(2)}, u32[]{:S(2)}) async-start(f32[16,1,384]{2,1,0:T(1,128)} %get-tuple-element.43), calls=%async_computation.1 | async-start | bytes 49152 | tf_op jit(solution)/shard_map/all_to_all | solution.py:256
  59.8 3.1 %collective-permute-start.8 = (f32[6,8,128]{2,1,0:T(8,128)S(1)}, f32[6,8,128]{2,1,0:T(8,128)S(1)}, u32[]{:S(2)}, u32[]{:S(2)}) collective-permute-start(f32[6,8,128]{2,1,0:T(8,128)S(1)} %copy-done.25), channel_id=1, source_target_pairs={{0,4},{4,8},{8,12},{12,16},{16,20},{20,24},{24,28},{28,32},{32,36}... | collective-permute-start | bytes 73736 | tf_op jit(solution)/shard_map/ppermute | solution.py:202
  62.9 3.1 %collective-permute-start.9 = (f32[6,8,128]{2,1,0:T(8,128)S(1)}, f32[6,8,128]{2,1,0:T(8,128)S(1)}, u32[]{:S(2)}, u32[]{:S(2)}) collective-permute-start(f32[6,8,128]{2,1,0:T(8,128)S(1)} %copy-done.23), channel_id=1, source_target_pairs={{4,0},{8,4},{12,8},{16,12},{20,16},{24,20},{28,24},{32,28},{36,32}... | collective-permute-start | bytes 73736 | tf_op jit(solution)/shard_map/ppermute | solution.py:203
  66.1 3.6 %collective-permute-start.10 = (f32[6,128]{1,0:T(8,128)S(1)}, f32[6,128]{1,0:T(8,128)S(1)}, u32[]{:S(2)}, u32[]{:S(2)}) collective-permute-start(f32[6,128]{1,0:T(8,128)S(1)} %copy-done.30), channel_id=1, source_target_pairs={{0,1},{1,2},{2,3},{4,5},{5,6},{6,7},{8,9},{9,10},{10,11},{12,13},{... | collective-permute-start | bytes 9224 | tf_op jit(solution)/shard_map/ppermute | solution.py:202
  72.3 5.0 %collective-permute-done.11.hwh = f32[6,128]{1,0:T(8,128)S(1)} collective-permute-done((f32[6,128]{1,0:T(8,128)S(1)}, f32[6,128]{1,0:T(8,128)S(1)}, u32[]{:S(2)}, u32[]{:S(2)}) %collective-permute-start.11) | collective-permute-done | bytes 3104 | tf_op jit(solution)/shard_map/ppermute | solution.py:203
  78.1 5.5 %shard_map.124 = (f32[6,8,16,128]{3,2,1,0:T(8,128)}, f32[16,1,384]{2,1,0:T(1,128)}, s32[1,1024]{1,0:T(1,128)}, f32[6,1,16,128]{3,2,1,0:T(8,128)}, f32[6,1,16,128...) custom-call(f32[3,6,6]{2,1,0:T(8,128)} %ub_ref.7, ...), custom_call_target="tpu_custom_call" | custom-call | tf_op jit(solution)/shard_map/pallas_call | solution.py:261
  83.6 2.9 %collective-permute-start.12 = (f32[6,1,16,128]{3,2,1,0:T(8,128)}, f32[6,1,16,128]{3,2,1,0:T(8,128)S(1)}, u32[]{:S(2)}, u32[]{:S(2)}) collective-permute-start(f32[6,1,16,128]{3,2,1,0:T(8,128)} %get-tuple-element.46), channel_id=1, source_target_pairs={{0,64},{64,128},{128,192},{1,65},{65,129},{129,193},{2,66},{66,130... | collective-permute-start | bytes 147464 | tf_op jit(solution)/shard_map/ppermute | solution.py:202
  86.6 2.4 %collective-permute-start.13 = (f32[6,1,16,128]{3,2,1,0:T(8,128)}, f32[6,1,16,128]{3,2,1,0:T(8,128)S(1)}, u32[]{:S(2)}, u32[]{:S(2)}) collective-permute-start(f32[6,1,16,128]{3,2,1,0:T(8,128)} %get-tuple-element.47), channel_id=1, source_target_pairs={{64,0},{128,64},{192,128},{65,1},{129,65},{193,129},{66,2},{130,66... | collective-permute-start | bytes 147464 | tf_op jit(solution)/shard_map/ppermute | solution.py:203
  89.0 8.0 %all-to-all-start.2 = ((f32[16,1,384]{2,1,0:T(1,128)}), f32[16,1,384]{2,1,0:T(1,128)S(1)}, u32[]{:S(2)}, u32[]{:S(2)}) async-start(f32[16,1,384]{2,1,0:T(1,128)} %get-tuple-element.52), calls=%async_computation.2 | async-start | bytes 49152 | tf_op jit(solution)/shard_map/all_to_all | solution.py:256
  97.0 3.1 %collective-permute-start.14 = (f32[6,8,128]{2,1,0:T(8,128)S(1)}, f32[6,8,128]{2,1,0:T(8,128)S(1)}, u32[]{:S(2)}, u32[]{:S(2)}) collective-permute-start(f32[6,8,128]{2,1,0:T(8,128)S(1)} %copy-done.24), channel_id=1, source_target_pairs={{0,4},{4,8},{8,12},{12,16},{16,20},{20,24},{24,28},{28,32},{32,36}... | collective-permute-start | bytes 73736 | tf_op jit(solution)/shard_map/ppermute | solution.py:202
  100.1 3.1 %collective-permute-start.15 = (f32[6,8,128]{2,1,0:T(8,128)S(1)}, f32[6,8,128]{2,1,0:T(8,128)S(1)}, u32[]{:S(2)}, u32[]{:S(2)}) collective-permute-start(f32[6,8,128]{2,1,0:T(8,128)S(1)} %copy-done.22), channel_id=1, source_target_pairs={{4,0},{8,4},{12,8},{16,12},{20,16},{24,20},{28,24},{32,28},{36,32}... | collective-permute-start | bytes 73736 | tf_op jit(solution)/shard_map/ppermute | solution.py:203
  103.2 3.6 %collective-permute-start.16 = (f32[6,128]{1,0:T(8,128)S(1)}, f32[6,128]{1,0:T(8,128)S(1)}, u32[]{:S(2)}, u32[]{:S(2)}) collective-permute-start(f32[6,128]{1,0:T(8,128)S(1)} %copy-done.29), channel_id=1, source_target_pairs={{0,1},{1,2},{2,3},{4,5},{5,6},{6,7},{8,9},{9,10},{10,11},{12,13},{... | collective-permute-start | bytes 9224 | tf_op jit(solution)/shard_map/ppermute | solution.py:202
  109.7 4.9 %collective-permute-done.17.hwh = f32[6,128]{1,0:T(8,128)S(1)} collective-permute-done((f32[6,128]{1,0:T(8,128)S(1)}, f32[6,128]{1,0:T(8,128)S(1)}, u32[]{:S(2)}, u32[]{:S(2)}) %collective-permute-start.17) | collective-permute-done | bytes 3104 | tf_op jit(solution)/shard_map/ppermute | solution.py:203
  115.3 4.7 %shard_map.125 = (f32[6,8,16,128]{3,2,1,0:T(8,128)}, f32[8,16,128]{2,1,0:T(8,128)}) custom-call(f32[3,6,6]{2,1,0:T(8,128)} %ub_ref.7, f32[3,6,6]{2,1,0:T(8,128)} %lb_ref.7, f32[2,6,6]{2,1,0:T(8,128)} %copy.16.ib_ref, f32[6,8,16,128]{3,2,1,0:T(8,128)} %get-tuple-element.45.adj_ref, f32[6,8,16,128]{3,2,1,0:T(8,128)} %sens_ref.7, f32[6,8,16,128]{3,2,1,0:T(8,128)} %diag_ref.7, ...), custom_call_target="tpu_custom_call" | custom-call | tf_op jit(solution)/shard_map/pallas_call | solution.py:264
  (87 shorter events, 13.9 us)
Async XLA Ops:
  5.1 17.5 %copy-start.26 = (f32[6,8,128]{2,1,0:T(8,128)S(1)}, f32[6,8,128]{2,1,0:T(8,128)}, u32[]{:S(2)}) copy-start(f32[6,8,128]{2,1,0:T(8,128)} %get-tuple-element.32) | copy-start | bytes 73732
  5.2 35.2 %all-to-all-start = ((f32[16,1,448]{2,1,0:T(1,128)}), f32[16,1,448]{2,1,0:T(1,128)S(1)}, u32[]{:S(2)}, u32[]{:S(2)}) async-start(f32[16,1,448]{2,1,0:T(1,128)} %get-tuple-element.35), calls=%async_computation | async-start | bytes 65536 | tf_op jit(solution)/shard_map/all_to_all | solution.py:256
  14.3 26.1 %collective-permute-start = (f32[6,1,16,128]{3,2,1,0:T(8,128)}, f32[6,1,16,128]{3,2,1,0:T(8,128)S(1)}, u32[]{:S(2)}, u32[]{:S(2)}) collective-permute-start(f32[6,1,16,128]{3,2,1,0:T(8,128)} %get-tuple-element.29), channel_id=1, source_target_pairs={{0,64},{64,128},{128,192},{1,65},{65,129},{129,193},{2,66},{66,130... | collective-permute-start | bytes 147464 | tf_op jit(solution)/shard_map/ppermute | solution.py:202
  17.2 23.2 %collective-permute-start.1 = (f32[6,1,16,128]{3,2,1,0:T(8,128)S(1)}, f32[6,1,16,128]{3,2,1,0:T(8,128)S(1)}, u32[]{:S(2)}, u32[]{:S(2)}) collective-permute-start(f32[6,1,16,128]{3,2,1,0:T(8,128)S(1)} %copy-done.21), channel_id=1, source_target_pairs={{64,0},{128,64},{192,128},{65,1},{129,65},{193,129},{66,2},{130,66... | collective-permute-start | bytes 147464 | tf_op jit(solution)/shard_map/ppermute | solution.py:203
  19.6 20.7 %collective-permute-start.2 = (f32[6,8,128]{2,1,0:T(8,128)}, f32[6,8,128]{2,1,0:T(8,128)S(1)}, u32[]{:S(2)}, u32[]{:S(2)}) collective-permute-start(f32[6,8,128]{2,1,0:T(8,128)} %get-tuple-element.31), channel_id=1, source_target_pairs={{0,4},{4,8},{8,12},{12,16},{16,20},{20,24},{24,28},{28,32},{32,36}... | collective-permute-start | bytes 73736 | tf_op jit(solution)/shard_map/ppermute | solution.py:202
  22.7 17.6 %collective-permute-start.3 = (f32[6,8,128]{2,1,0:T(8,128)S(1)}, f32[6,8,128]{2,1,0:T(8,128)S(1)}, u32[]{:S(2)}, u32[]{:S(2)}) collective-permute-start(f32[6,8,128]{2,1,0:T(8,128)S(1)} %copy-done.26), channel_id=1, source_target_pairs={{4,0},{8,4},{12,8},{16,12},{20,16},{24,20},{28,24},{32,28},{36,32}... | collective-permute-start | bytes 73736 | tf_op jit(solution)/shard_map/ppermute | solution.py:203
  25.8 7.5 %collective-permute-start.4 = (f32[6,128]{1,0:T(8,128)}, f32[6,128]{1,0:T(8,128)S(1)}, u32[]{:S(2)}, u32[]{:S(2)}) collective-permute-start(f32[6,128]{1,0:T(8,128)} %get-tuple-element.33), channel_id=1, source_target_pairs={{0,1},{1,2},{2,3},{4,5},{5,6},{6,7},{8,9},{9,10},{10,11},{12,13},{... | collective-permute-start | bytes 9224 | tf_op jit(solution)/shard_map/ppermute | solution.py:202
  33.3 7.0 %collective-permute-start.5 = (f32[6,128]{1,0:T(8,128)S(1)}, f32[6,128]{1,0:T(8,128)S(1)}, u32[]{:S(2)}, u32[]{:S(2)}) collective-permute-start(f32[6,128]{1,0:T(8,128)S(1)} %copy-done.31), channel_id=1, source_target_pairs={{1,0},{2,1},{3,2},{5,4},{6,5},{7,6},{9,8},{10,9},{11,10},{13,12},{... | collective-permute-start | bytes 9224 | tf_op jit(solution)/shard_map/ppermute | solution.py:203
  46.5 31.0 %collective-permute-start.6 = (f32[6,1,16,128]{3,2,1,0:T(8,128)}, f32[6,1,16,128]{3,2,1,0:T(8,128)S(1)}, u32[]{:S(2)}, u32[]{:S(2)}) collective-permute-start(f32[6,1,16,128]{3,2,1,0:T(8,128)} %get-tuple-element.37), channel_id=1, source_target_pairs={{0,64},{64,128},{128,192},{1,65},{65,129},{129,193},{2,66},{66,130... | collective-permute-start | bytes 147464 | tf_op jit(solution)/shard_map/ppermute | solution.py:202
  49.4 16.7 %copy-start.30 = (f32[6,128]{1,0:T(8,128)S(1)}, f32[6,128]{1,0:T(8,128)}, u32[]{:S(2)}) copy-start(f32[6,128]{1,0:T(8,128)} %get-tuple-element.41) | copy-start | bytes 9220
  49.4 28.1 %collective-permute-start.7 = (f32[6,1,16,128]{3,2,1,0:T(8,128)}, f32[6,1,16,128]{3,2,1,0:T(8,128)S(1)}, u32[]{:S(2)}, u32[]{:S(2)}) collective-permute-start(f32[6,1,16,128]{3,2,1,0:T(8,128)} %get-tuple-element.38), channel_id=1, source_target_pairs={{64,0},{128,64},{192,128},{65,1},{129,65},{193,129},{66,2},{130,66... | collective-permute-start | bytes 147464 | tf_op jit(solution)/shard_map/ppermute | solution.py:203
  51.8 25.6 %all-to-all-start.1 = ((f32[16,1,384]{2,1,0:T(1,128)}), f32[16,1,384]{2,1,0:T(1,128)S(1)}, u32[]{:S(2)}, u32[]{:S(2)}) async-start(f32[16,1,384]{2,1,0:T(1,128)} %get-tuple-element.43), calls=%async_computation.1 | async-start | bytes 49152 | tf_op jit(solution)/shard_map/all_to_all | solution.py:256
  59.8 17.6 %collective-permute-start.8 = (f32[6,8,128]{2,1,0:T(8,128)S(1)}, f32[6,8,128]{2,1,0:T(8,128)S(1)}, u32[]{:S(2)}, u32[]{:S(2)}) collective-permute-start(f32[6,8,128]{2,1,0:T(8,128)S(1)} %copy-done.25), channel_id=1, source_target_pairs={{0,4},{4,8},{8,12},{12,16},{16,20},{20,24},{24,28},{28,32},{32,36}... | collective-permute-start | bytes 73736 | tf_op jit(solution)/shard_map/ppermute | solution.py:202
  62.9 14.5 %collective-permute-start.9 = (f32[6,8,128]{2,1,0:T(8,128)S(1)}, f32[6,8,128]{2,1,0:T(8,128)S(1)}, u32[]{:S(2)}, u32[]{:S(2)}) collective-permute-start(f32[6,8,128]{2,1,0:T(8,128)S(1)} %copy-done.23), channel_id=1, source_target_pairs={{4,0},{8,4},{12,8},{16,12},{20,16},{24,20},{28,24},{32,28},{36,32}... | collective-permute-start | bytes 73736 | tf_op jit(solution)/shard_map/ppermute | solution.py:203
  66.1 4.4 %collective-permute-start.10 = (f32[6,128]{1,0:T(8,128)S(1)}, f32[6,128]{1,0:T(8,128)S(1)}, u32[]{:S(2)}, u32[]{:S(2)}) collective-permute-start(f32[6,128]{1,0:T(8,128)S(1)} %copy-done.30), channel_id=1, source_target_pairs={{0,1},{1,2},{2,3},{4,5},{5,6},{6,7},{8,9},{9,10},{10,11},{12,13},{... | collective-permute-start | bytes 9224 | tf_op jit(solution)/shard_map/ppermute | solution.py:202
  70.4 7.0 %collective-permute-start.11 = (f32[6,128]{1,0:T(8,128)S(1)}, f32[6,128]{1,0:T(8,128)S(1)}, u32[]{:S(2)}, u32[]{:S(2)}) collective-permute-start(f32[6,128]{1,0:T(8,128)S(1)} %copy-done.28), channel_id=1, source_target_pairs={{1,0},{2,1},{3,2},{5,4},{6,5},{7,6},{9,8},{10,9},{11,10},{13,12},{... | collective-permute-start | bytes 9224 | tf_op jit(solution)/shard_map/ppermute | solution.py:203
  83.6 31.0 %collective-permute-start.12 = (f32[6,1,16,128]{3,2,1,0:T(8,128)}, f32[6,1,16,128]{3,2,1,0:T(8,128)S(1)}, u32[]{:S(2)}, u32[]{:S(2)}) collective-permute-start(f32[6,1,16,128]{3,2,1,0:T(8,128)} %get-tuple-element.46), channel_id=1, source_target_pairs={{0,64},{64,128},{128,192},{1,65},{65,129},{129,193},{2,66},{66,130... | collective-permute-start | bytes 147464 | tf_op jit(solution)/shard_map/ppermute | solution.py:202
  86.5 16.7 %copy-start.29 = (f32[6,128]{1,0:T(8,128)S(1)}, f32[6,128]{1,0:T(8,128)}, u32[]{:S(2)}) copy-start(f32[6,128]{1,0:T(8,128)} %get-tuple-element.50) | copy-start | bytes 9220
  86.6 28.1 %collective-permute-start.13 = (f32[6,1,16,128]{3,2,1,0:T(8,128)}, f32[6,1,16,128]{3,2,1,0:T(8,128)S(1)}, u32[]{:S(2)}, u32[]{:S(2)}) collective-permute-start(f32[6,1,16,128]{3,2,1,0:T(8,128)} %get-tuple-element.47), channel_id=1, source_target_pairs={{64,0},{128,64},{192,128},{65,1},{129,65},{193,129},{66,2},{130,66... | collective-permute-start | bytes 147464 | tf_op jit(solution)/shard_map/ppermute | solution.py:203
  89.0 25.6 %all-to-all-start.2 = ((f32[16,1,384]{2,1,0:T(1,128)}), f32[16,1,384]{2,1,0:T(1,128)S(1)}, u32[]{:S(2)}, u32[]{:S(2)}) async-start(f32[16,1,384]{2,1,0:T(1,128)} %get-tuple-element.52), calls=%async_computation.2 | async-start | bytes 49152 | tf_op jit(solution)/shard_map/all_to_all | solution.py:256
  97.0 17.6 %collective-permute-start.14 = (f32[6,8,128]{2,1,0:T(8,128)S(1)}, f32[6,8,128]{2,1,0:T(8,128)S(1)}, u32[]{:S(2)}, u32[]{:S(2)}) collective-permute-start(f32[6,8,128]{2,1,0:T(8,128)S(1)} %copy-done.24), channel_id=1, source_target_pairs={{0,4},{4,8},{8,12},{12,16},{16,20},{20,24},{24,28},{28,32},{32,36}... | collective-permute-start | bytes 73736 | tf_op jit(solution)/shard_map/ppermute | solution.py:202
  100.1 14.5 %collective-permute-start.15 = (f32[6,8,128]{2,1,0:T(8,128)S(1)}, f32[6,8,128]{2,1,0:T(8,128)S(1)}, u32[]{:S(2)}, u32[]{:S(2)}) collective-permute-start(f32[6,8,128]{2,1,0:T(8,128)S(1)} %copy-done.22), channel_id=1, source_target_pairs={{4,0},{8,4},{12,8},{16,12},{20,16},{24,20},{28,24},{32,28},{36,32}... | collective-permute-start | bytes 73736 | tf_op jit(solution)/shard_map/ppermute | solution.py:203
  103.2 4.4 %collective-permute-start.16 = (f32[6,128]{1,0:T(8,128)S(1)}, f32[6,128]{1,0:T(8,128)S(1)}, u32[]{:S(2)}, u32[]{:S(2)}) collective-permute-start(f32[6,128]{1,0:T(8,128)S(1)} %copy-done.29), channel_id=1, source_target_pairs={{0,1},{1,2},{2,3},{4,5},{5,6},{6,7},{8,9},{9,10},{10,11},{12,13},{... | collective-permute-start | bytes 9224 | tf_op jit(solution)/shard_map/ppermute | solution.py:202
  107.6 7.0 %collective-permute-start.17 = (f32[6,128]{1,0:T(8,128)S(1)}, f32[6,128]{1,0:T(8,128)S(1)}, u32[]{:S(2)}, u32[]{:S(2)}) collective-permute-start(f32[6,128]{1,0:T(8,128)S(1)} %copy-done.27), channel_id=1, source_target_pairs={{1,0},{2,1},{3,2},{5,4},{6,5},{7,6},{9,8},{10,9},{11,10},{13,12},{... | collective-permute-start | bytes 9224 | tf_op jit(solution)/shard_map/ppermute | solution.py:203
  (29 other events, 119.9 us)

commit v6 on v5

--- a/solution.py
+++ b/solution.py
@@ -72,7 +72,7 @@
 
 
 def write_faces(adj, faces):
-    c_lo, c_hi, s_lo, s_hi, w_lo, w_hi = faces
+    c_lo, c_hi, s_lo, s_hi, w_buf, wall_me = faces
     nx, ny, nz = adj.shape[1], adj.shape[2], adj.shape[3]
     j_idx = lax.broadcasted_iota(jnp.int32, adj.shape, 2)
     c_lo[...] = adj[:, 0:1]
@@ -80,19 +80,38 @@
     s_lo[...] = jnp.sum(jnp.where(j_idx == 0, adj, 0.0), axis=2)
     s_hi[...] = jnp.sum(jnp.where(j_idx == ny - 1, adj, 0.0), axis=2)
     lo, hi = wall_columns(adj)
-    w_lo[...] = lo
-    w_hi[...] = hi
-
-
-def init_kernel(ub_ref, lb_ref, ib_ref, sens_ref, diag_ref, send_ref, orient_ref, weight_ref, tgt_ref,
-                adj_ref, rows_ref, c_lo, c_hi, s_lo, s_hi, w_lo, w_hi):
+    me = wall_me[0]
+    n_wall = w_buf.shape[0]
+    lo = jnp.concatenate([lo[v:v + 1] for v in range(lo.shape[0])], axis=1)
+    hi = jnp.concatenate([hi[v:v + 1] for v in range(hi.shape[0])], axis=1)
+    for t in range(n_wall):
+        w_buf[t] = jnp.where(me + 1 == t, hi, jnp.where(me - 1 == t, lo, 0.0))
+
+
+def wall_halos(w_inc, wall_me, n_var):
+    me = wall_me[0]
+    n_wall, _, width = w_inc.shape
+    below = None
+    above = None
+    for t in range(n_wall):
+        b = jnp.where(me - 1 == t, w_inc[t], 0.0)
+        a = jnp.where(me + 1 == t, w_inc[t], 0.0)
+        below = b if below is None else below + b
+        above = a if above is None else above + a
+    rows = width // n_var
+    unflat = lambda x: jnp.concatenate([x[:, v * rows:(v + 1) * rows] for v in range(n_var)], axis=0)
+    return unflat(below), unflat(above)
+
+
+def init_kernel(ub_ref, lb_ref, ib_ref, wall_me, sens_ref, diag_ref, send_ref, orient_ref, weight_ref, tgt_ref,
+                adj_ref, rows_ref, c_lo, c_hi, s_lo, s_hi, w_buf):
     n_var = sens_ref.shape[0]
     lanes = sens_ref.shape[3]
     slots = send_ref.shape[1]
     blk_ref = (ub_ref, lb_ref, ib_ref)
     adj = sens_ref[...] / diag_ref[...]
     adj_ref[...] = adj
-    write_faces(adj, (c_lo, c_hi, s_lo, s_hi, w_lo, w_hi))
+    write_faces(adj, (c_lo, c_hi, s_lo, s_hi, w_buf, wall_me))
     pieces = gather_rows(adj, send_ref, orient_ref, weight_ref, blk_ref, n_var, lanes)
     to_chunks(rows_ref, pieces + [flat_row(tgt_ref[...]).astype(F32)], slots)
 
@@ -142,14 +161,14 @@
     return jnp.stack(new, axis=0)
 
 
-def sweep_kernel(ub_ref, lb_ref, ib_ref, adj_ref, sens_ref, diag_ref, face_ref, hcl, hch, hsl, hsh, hwl, hwh,
+def sweep_kernel(ub_ref, lb_ref, ib_ref, wall_me, adj_ref, sens_ref, diag_ref, face_ref, hcl, hch, hsl, hsh, w_inc,
                  inc_ref, tgt_ref, send_ref, orient_ref, weight_ref,
-                 out_ref, rows_ref, tgt_out, c_lo, c_hi, s_lo, s_hi, w_lo, w_hi):
+                 out_ref, rows_ref, tgt_out, c_lo, c_hi, s_lo, s_hi, w_buf):
     n_var = adj_ref.shape[0]
     lanes = adj_ref.shape[3]
     slots = send_ref.shape[1]
     blk_ref = (ub_ref, lb_ref, ib_ref)
-    halos = (hcl[...], hch[...], hsl[...], hsh[...], hwl[...], hwh[...])
+    halos = (hcl[...], hch[...], hsl[...], hsh[...]) + wall_halos(w_inc[...], wall_me, n_var)
     inc = inc_ref[...]
     if tgt_ref is None:
         got = from_chunks(inc, n_var + 1, slots)
@@ -161,22 +180,22 @@
     new = sweep_body(blk_ref, adj_ref[...], sens_ref[...], diag_ref[...], face_ref[...], halos,
                      jnp.concatenate(got[:n_var], axis=0), cell)
     out_ref[...] = new
-    write_faces(new, (c_lo, c_hi, s_lo, s_hi, w_lo, w_hi))
+    write_faces(new, (c_lo, c_hi, s_lo, s_hi, w_buf, wall_me))
     to_chunks(rows_ref, gather_rows(new, send_ref, orient_ref, weight_ref, blk_ref, n_var, lanes), slots)
 
 
-def first_sweep_kernel(ub_ref, lb_ref, ib_ref, adj_ref, sens_ref, diag_ref, face_ref, hcl, hch, hsl, hsh, hwl, hwh,
-                       inc_ref, send_ref, orient_ref, weight_ref, *outs):
-    sweep_kernel(ub_ref, lb_ref, ib_ref, adj_ref, sens_ref, diag_ref, face_ref, hcl, hch, hsl, hsh, hwl, hwh,
+def first_sweep_kernel(ub_ref, lb_ref, ib_ref, wall_me, adj_ref, sens_ref, diag_ref, face_ref, hcl, hch, hsl, hsh,
+                       w_inc, inc_ref, send_ref, orient_ref, weight_ref, *outs):
+    sweep_kernel(ub_ref, lb_ref, ib_ref, wall_me, adj_ref, sens_ref, diag_ref, face_ref, hcl, hch, hsl, hsh, w_inc,
                  inc_ref, None, send_ref, orient_ref, weight_ref, *outs)
 
 
-def last_kernel(ub_ref, lb_ref, ib_ref, adj_ref, sens_ref, diag_ref, face_ref, hcl, hch, hsl, hsh, hwl, hwh,
+def last_kernel(ub_ref, lb_ref, ib_ref, wall_me, adj_ref, sens_ref, diag_ref, face_ref, hcl, hch, hsl, hsh, w_inc,
                 inc_ref, tgt_ref, prod_ref, out_ref, grad_ref):
     n_var = adj_ref.shape[0]
     slots = inc_ref.shape[2] // n_var
     blk_ref = (ub_ref, lb_ref, ib_ref)
-    halos = (hcl[...], hch[...], hsl[...], hsh[...], hwl[...], hwh[...])
+    halos = (hcl[...], hch[...], hsl[...], hsh[...]) + wall_halos(w_inc[...], wall_me, n_var)
     got = from_chunks(inc_ref[...], n_var, slots)
     new = sweep_body(blk_ref, adj_ref[...], sens_ref[...], diag_ref[...], face_ref[...], halos,
                      jnp.concatenate(got, axis=0), tgt_ref[...])
@@ -184,23 +203,24 @@
     grad_ref[...] = prod_ref[...] * new[n_var - 1]
 
 
-def face_shapes(shape):
+def face_shapes(shape, n_wall):
     n_var, nx, ny, nz = shape
     c = jax.ShapeDtypeStruct((n_var, 1, ny, nz), F32)
     s = jax.ShapeDtypeStruct((n_var, nx, nz), F32)
-    w = jax.ShapeDtypeStruct((n_var, nx * ny), F32)
-    return [c, c, s, s, w, w]
+    w = jax.ShapeDtypeStruct((n_wall, 1, n_var * nx * ny), F32)
+    return [c, c, s, s, w]
 
 
 def exchange(faces):
-    c_lo, c_hi, s_lo, s_hi, w_lo, w_hi = faces
+    c_lo, c_hi, s_lo, s_hi, w_buf = faces
     out = []
-    for axis, lo_face, hi_face in (("chord", c_lo, c_hi), ("span", s_lo, s_hi), ("wall", w_lo, w_hi)):
+    for axis, lo_face, hi_face in (("chord", c_lo, c_hi), ("span", s_lo, s_hi)):
         count = lax.axis_size(axis)
         forward = [(i, i + 1) for i in range(count - 1)]
         backward = [(i + 1, i) for i in range(count - 1)]
         out.append(lax.ppermute(hi_face, axis, forward))
         out.append(lax.ppermute(lo_face, axis, backward))
+    out.append(lax.all_to_all(w_buf, "wall", split_axis=0, concat_axis=0, tiled=True))
     return out
 
 
@@ -211,7 +231,9 @@
     slots = send_cell.shape[-1]
     n_rows = n_span * slots
     shape = sensitivity.shape
-    blk = (upper_blocks, lower_blocks, iface_blocks)
+    n_wall = lax.axis_size("wall")
+    wall_me = lax.axis_index("wall").astype(jnp.int32).reshape(1)
+    blk = (upper_blocks, lower_blocks, iface_blocks, wall_me)
     send_row = send_cell.reshape(n_span, slots)
     orient_row = orient.reshape(n_span, slots)
     weight_row = iface_weight.reshape(n_span, slots)
@@ -226,28 +248,28 @@
 
     init = pl.pallas_call(
         init_kernel,
-        out_shape=[adj_sds, first_rows] + face_shapes(shape),
-        in_specs=[smem] * 3 + [vmem] * 6,
-        out_specs=[vmem] * 8,
+        out_shape=[adj_sds, first_rows] + face_shapes(shape, n_wall),
+        in_specs=[smem] * 4 + [vmem] * 6,
+        out_specs=[vmem] * 7,
     )
     adj, rows, *faces = init(*blk, sensitivity, diagonal, send_row, orient_row, weight_row, target_row)
 
     first = pl.pallas_call(
         first_sweep_kernel,
-        out_shape=[adj_sds, rows_sds, tgt_sds] + face_shapes(shape),
-        in_specs=[smem] * 3 + [vmem] * 14,
-        out_specs=[vmem] * 9,
+        out_shape=[adj_sds, rows_sds, tgt_sds] + face_shapes(shape, n_wall),
+        in_specs=[smem] * 4 + [vmem] * 13,
+        out_specs=[vmem] * 8,
     )
     step = pl.pallas_call(
         sweep_kernel,
-        out_shape=[adj_sds, rows_sds, tgt_sds] + face_shapes(shape),
-        in_specs=[smem] * 3 + [vmem] * 15,
-        out_specs=[vmem] * 9,
+        out_shape=[adj_sds, rows_sds, tgt_sds] + face_shapes(shape, n_wall),
+        in_specs=[smem] * 4 + [vmem] * 14,
+        out_specs=[vmem] * 8,
     )
     last = pl.pallas_call(
         last_kernel,
         out_shape=[adj_sds, jax.ShapeDtypeStruct(production.shape, F32)],
-        in_specs=[smem] * 3 + [vmem] * 13,
+        in_specs=[smem] * 4 + [vmem] * 12,
         out_specs=[vmem] * 2,
     )
     received = None

time: 121 us -> 120 us (level)
  the two profiles are of different devices: /device:TPU:49 before, /device:TPU:118 now
where the time goes in v6:
time: 120 us; the launch traced here: 119 us
  starting transfers between devices  69.5 us (58%)
  Pallas kernels  19.1 us (16%)
  waiting for transfers between devices  17.5 us (15%)
  blocking collectives  7.26 us (6%)
  local copies, waits for them, and re-layouts  4.28 us (4%)
    ppermute x6, starting transfers between devices, exchange(): out.append(lax.ppermute(hi_face, axis, forward))  23.3 us
    all_to_all x3, starting transfers between devices, local(): lax.all_to_all(rows, 'span', split_axis=0, concat_axis=0, tiled=True)  20.7 us
    ppermute x6, waiting for transfers between devices, exchange(): out.append(lax.ppermute(lo_face, axis, backward))  17.5 us
    ppermute x6, starting transfers between devices, exchange(): out.append(lax.ppermute(lo_face, axis, backward))  13.9 us
    all_to_all x2, starting transfers between devices, exchange(): lax.all_to_all(w_buf, 'wall', split_axis=0, concat_axis=0, tiled=True)  11.5 us
    all_to_all x1, blocking collectives, exchange(): lax.all_to_all(w_buf, 'wall', split_axis=0, concat_axis=0, tiled=True)  7.26 us
    pallas_call x1, Pallas kernels, local(): step(*blk, adj, sensitivity, diagonal, face_coef, *halos, incoming, recei...  5.69 us
    pallas_call x1, Pallas kernels, local(): first(*blk, adj, sensitivity, diagonal, face_coef, *halos, incoming, send...  5.53 us
  transfers between devices with their start and end apart: 17, of which 3 were waited for; matrix products, arithmetic and copies ran while one was open for 0% of the time, Pallas kernels for 0%

profile of v6, /device:TPU:118, one launch (start us, length us, event | category | flops | bytes accessed | tf_op | source)
XLA Modules:
  0.0 118.6 jit_solution(1793326733687730937)
XLA Ops:
  1.9 3.2 %shard_map.122 = (f32[6,8,16,128]{3,2,1,0:T(8,128)}, f32[16,1,448]{2,1,0:T(1,128)}, f32[6,1,16,128]{3,2,1,0:T(8,128)}, f32[6,1,16,128]{3,2,1,0:T(8,128)}, f32[6,...) custom-call(f32[3,6,6]{2,1,0:T(8,128)} %ub_ref.7, f32[3,6,6]{2,1,0:T(8,128)} %lb_ref.7, ...), custom_call_target="tpu_custom_call" | custom-call | tf_op jit(solution)/shard_map/pallas_call | solution.py:255
  5.1 7.3 %all_to_all.30.w_inc = f32[4,1,768]{2,1,0:T(1,128)} all-to-all(f32[4,1,768]{2,1,0:T(1,128)} %get-tuple-element.30), channel_id=1, replica_groups=mesh['chord'=4,'span'=16,'wall'=4] {'wall'}, dimensions={0} | all-to-all | bytes 24576 | tf_op jit(solution)/shard_map/all_to_all | solution.py:223
  12.4 8.7 %all-to-all-start.1 = ((f32[16,1,448]{2,1,0:T(1,128)}), f32[16,1,448]{2,1,0:T(1,128)S(1)}, u32[]{:S(2)}, u32[]{:S(2)}) async-start(f32[16,1,448]{2,1,0:T(1,128)} %get-tuple-element.31), calls=%async_computation.1 | async-start | bytes 65536 | tf_op jit(solution)/shard_map/all_to_all | solution.py:278
  21.1 3.2 %collective-permute-start = (f32[6,1,16,128]{3,2,1,0:T(8,128)}, f32[6,1,16,128]{3,2,1,0:T(8,128)S(1)}, u32[]{:S(2)}, u32[]{:S(2)}) collective-permute-start(f32[6,1,16,128]{3,2,1,0:T(8,128)} %get-tuple-element.26), channel_id=1, source_target_pairs={{0,64},{64,128},{128,192},{1,65},{65,129},{129,193},{2,66},{66,130... | collective-permute-start | bytes 147464 | tf_op jit(solution)/shard_map/ppermute | solution.py:221
  24.3 2.7 %collective-permute-start.1 = (f32[6,1,16,128]{3,2,1,0:T(8,128)S(1)}, f32[6,1,16,128]{3,2,1,0:T(8,128)S(1)}, u32[]{:S(2)}, u32[]{:S(2)}) collective-permute-start(f32[6,1,16,128]{3,2,1,0:T(8,128)S(1)} %copy-done.17), channel_id=1, source_target_pairs={{64,0},{128,64},{192,128},{65,1},{129,65},{193,129},{66,2},{130,66... | collective-permute-start | bytes 147464 | tf_op jit(solution)/shard_map/ppermute | solution.py:222
  27.0 4.6 %collective-permute-start.2 = (f32[6,8,128]{2,1,0:T(8,128)S(1)}, f32[6,8,128]{2,1,0:T(8,128)S(1)}, u32[]{:S(2)}, u32[]{:S(2)}) collective-permute-start(f32[6,8,128]{2,1,0:T(8,128)S(1)} %copy-done.23), channel_id=1, source_target_pairs={{0,4},{4,8},{8,12},{12,16},{16,20},{20,24},{24,28},{28,32},{32,36}... | collective-permute-start | bytes 73736 | tf_op jit(solution)/shard_map/ppermute | solution.py:221
  31.6 1.9 %collective-permute-start.3 = (f32[6,8,128]{2,1,0:T(8,128)S(1)}, f32[6,8,128]{2,1,0:T(8,128)S(1)}, u32[]{:S(2)}, u32[]{:S(2)}) collective-permute-start(f32[6,8,128]{2,1,0:T(8,128)S(1)} %copy-done.22), channel_id=1, source_target_pairs={{4,0},{8,4},{12,8},{16,12},{20,16},{24,20},{28,24},{32,28},{36,32}... | collective-permute-start | bytes 73736 | tf_op jit(solution)/shard_map/ppermute | solution.py:222
  33.5 5.9 %collective-permute-done.3.hsh = f32[6,8,128]{2,1,0:T(8,128)S(1)} collective-permute-done((f32[6,8,128]{2,1,0:T(8,128)S(1)}, f32[6,8,128]{2,1,0:T(8,128)S(1)}, u32[]{:S(2)}, u32[]{:S(2)}) %collective-permute-start.3) | collective-permute-done | bytes 24608 | tf_op jit(solution)/shard_map/ppermute | solution.py:222
  40.0 5.5 %shard_map.123 = (f32[6,8,16,128]{3,2,1,0:T(8,128)}, f32[16,1,384]{2,1,0:T(1,128)}, s32[1,1024]{1,0:T(1,128)}, f32[6,1,16,128]{3,2,1,0:T(8,128)}, f32[6,1,16,128...) custom-call(f32[3,6,6]{2,1,0:T(8,128)} %ub_ref.7, f32[3,6,6]{2,1,0:T(8,128)} %lb_ref.7, ...), custom_call_target="tpu_custom_call" | custom-call | tf_op jit(solution)/shard_map/pallas_call | solution.py:280
  45.6 6.7 %all-to-all-start.2 = ((f32[4,1,768]{2,1,0:T(1,128)}), f32[4,1,768]{2,1,0:T(1,128)S(1)}, u32[]{:S(2)}, u32[]{:S(2)}) async-start(f32[4,1,768]{2,1,0:T(1,128)} %get-tuple-element.37), calls=%async_computation.2 | async-start | bytes 24576 | tf_op jit(solution)/shard_map/all_to_all | solution.py:223
  52.3 3.2 %collective-permute-start.4 = (f32[6,1,16,128]{3,2,1,0:T(8,128)}, f32[6,1,16,128]{3,2,1,0:T(8,128)S(1)}, u32[]{:S(2)}, u32[]{:S(2)}) collective-permute-start(f32[6,1,16,128]{3,2,1,0:T(8,128)} %get-tuple-element.33), channel_id=1, source_target_pairs={{0,64},{64,128},{128,192},{1,65},{65,129},{129,193},{2,66},{66,130... | collective-permute-start | bytes 147464 | tf_op jit(solution)/shard_map/ppermute | solution.py:221
  55.5 2.7 %collective-permute-start.5 = (f32[6,1,16,128]{3,2,1,0:T(8,128)}, f32[6,1,16,128]{3,2,1,0:T(8,128)S(1)}, u32[]{:S(2)}, u32[]{:S(2)}) collective-permute-start(f32[6,1,16,128]{3,2,1,0:T(8,128)} %get-tuple-element.34), channel_id=1, source_target_pairs={{64,0},{128,64},{192,128},{65,1},{129,65},{193,129},{66,2},{130,66... | collective-permute-start | bytes 147464 | tf_op jit(solution)/shard_map/ppermute | solution.py:222
  58.8 6.0 %all-to-all-start.3 = ((f32[16,1,384]{2,1,0:T(1,128)}), f32[16,1,384]{2,1,0:T(1,128)S(1)}, u32[]{:S(2)}, u32[]{:S(2)}) async-start(f32[16,1,384]{2,1,0:T(1,128)} %get-tuple-element.38), calls=%async_computation.3 | async-start | bytes 49152 | tf_op jit(solution)/shard_map/all_to_all | solution.py:278
  64.8 4.6 %collective-permute-start.6 = (f32[6,8,128]{2,1,0:T(8,128)S(1)}, f32[6,8,128]{2,1,0:T(8,128)S(1)}, u32[]{:S(2)}, u32[]{:S(2)}) collective-permute-start(f32[6,8,128]{2,1,0:T(8,128)S(1)} %copy-done.21), channel_id=1, source_target_pairs={{0,4},{4,8},{8,12},{12,16},{16,20},{20,24},{24,28},{28,32},{32,36}... | collective-permute-start | bytes 73736 | tf_op jit(solution)/shard_map/ppermute | solution.py:221
  71.3 5.9 %collective-permute-done.7.hsh = f32[6,8,128]{2,1,0:T(8,128)S(1)} collective-permute-done((f32[6,8,128]{2,1,0:T(8,128)S(1)}, f32[6,8,128]{2,1,0:T(8,128)S(1)}, u32[]{:S(2)}, u32[]{:S(2)}) %collective-permute-start.7) | collective-permute-done | bytes 24608 | tf_op jit(solution)/shard_map/ppermute | solution.py:222
  77.9 5.7 %shard_map.124 = (f32[6,8,16,128]{3,2,1,0:T(8,128)}, f32[16,1,384]{2,1,0:T(1,128)}, s32[1,1024]{1,0:T(1,128)}, f32[6,1,16,128]{3,2,1,0:T(8,128)}, f32[6,1,16,128...) custom-call(f32[3,6,6]{2,1,0:T(8,128)} %ub_ref.7, f32[3,6,6]{2,1,0:T(8,128)} %lb_ref.7, ...), custom_call_target="tpu_custom_call" | custom-call | tf_op jit(solution)/shard_map/pallas_call | solution.py:283
  83.6 4.8 %all-to-all-start.4 = ((f32[4,1,768]{2,1,0:T(1,128)}), f32[4,1,768]{2,1,0:T(1,128)S(1)}, u32[]{:S(2)}, u32[]{:S(2)}) async-start(f32[4,1,768]{2,1,0:T(1,128)} %get-tuple-element.45), calls=%async_computation.4 | async-start | bytes 24576 | tf_op jit(solution)/shard_map/all_to_all | solution.py:223
  88.4 3.2 %collective-permute-start.8 = (f32[6,1,16,128]{3,2,1,0:T(8,128)}, f32[6,1,16,128]{3,2,1,0:T(8,128)S(1)}, u32[]{:S(2)}, u32[]{:S(2)}) collective-permute-start(f32[6,1,16,128]{3,2,1,0:T(8,128)} %get-tuple-element.41), channel_id=1, source_target_pairs={{0,64},{64,128},{128,192},{1,65},{65,129},{129,193},{2,66},{66,130... | collective-permute-start | bytes 147464 | tf_op jit(solution)/shard_map/ppermute | solution.py:221
  91.6 2.6 %collective-permute-start.9 = (f32[6,1,16,128]{3,2,1,0:T(8,128)}, f32[6,1,16,128]{3,2,1,0:T(8,128)S(1)}, u32[]{:S(2)}, u32[]{:S(2)}) collective-permute-start(f32[6,1,16,128]{3,2,1,0:T(8,128)} %get-tuple-element.42), channel_id=1, source_target_pairs={{64,0},{128,64},{192,128},{65,1},{129,65},{193,129},{66,2},{130,66... | collective-permute-start | bytes 147464 | tf_op jit(solution)/shard_map/ppermute | solution.py:222
  94.8 6.0 %all-to-all-start.5 = ((f32[16,1,384]{2,1,0:T(1,128)}), f32[16,1,384]{2,1,0:T(1,128)S(1)}, u32[]{:S(2)}, u32[]{:S(2)}) async-start(f32[16,1,384]{2,1,0:T(1,128)} %get-tuple-element.46), calls=%async_computation.5 | async-start | bytes 49152 | tf_op jit(solution)/shard_map/all_to_all | solution.py:278
  100.8 4.6 %collective-permute-start.10 = (f32[6,8,128]{2,1,0:T(8,128)S(1)}, f32[6,8,128]{2,1,0:T(8,128)S(1)}, u32[]{:S(2)}, u32[]{:S(2)}) collective-permute-start(f32[6,8,128]{2,1,0:T(8,128)S(1)} %copy-done.20), channel_id=1, source_target_pairs={{0,4},{4,8},{8,12},{12,16},{16,20},{20,24},{24,28},{28,32},{32,36}... | collective-permute-start | bytes 73736 | tf_op jit(solution)/shard_map/ppermute | solution.py:221
  105.4 2.1 %collective-permute-start.11 = (f32[6,8,128]{2,1,0:T(8,128)S(1)}, f32[6,8,128]{2,1,0:T(8,128)S(1)}, u32[]{:S(2)}, u32[]{:S(2)}) collective-permute-start(f32[6,8,128]{2,1,0:T(8,128)S(1)} %copy-done.18), channel_id=1, source_target_pairs={{4,0},{8,4},{12,8},{16,12},{20,16},{24,20},{28,24},{32,28},{36,32}... | collective-permute-start | bytes 73736 | tf_op jit(solution)/shard_map/ppermute | solution.py:222
  107.6 5.7 %collective-permute-done.11.hsh = f32[6,8,128]{2,1,0:T(8,128)S(1)} collective-permute-done((f32[6,8,128]{2,1,0:T(8,128)S(1)}, f32[6,8,128]{2,1,0:T(8,128)S(1)}, u32[]{:S(2)}, u32[]{:S(2)}) %collective-permute-start.11) | collective-permute-done | bytes 24608 | tf_op jit(solution)/shard_map/ppermute | solution.py:222
  113.9 4.7 %shard_map.125 = (f32[6,8,16,128]{3,2,1,0:T(8,128)}, f32[8,16,128]{2,1,0:T(8,128)}) custom-call(f32[3,6,6]{2,1,0:T(8,128)} %ub_ref.7, f32[3,6,6]{2,1,0:T(8,128)} %lb_ref.7, f32[2,6,6]{2,1,0:T(8,128)} %copy.16.ib_ref, s32[1]{0:T(128)} %bitcast.wall_me, f32[6,8,16,128]{3,2,1,0:T(8,128)} %get-tuple-element.40.adj_ref, f32[6,8,16,128]{3,2,1,0:T(8,128)} %sens_ref.7, ...), custom_call_target="tpu_custom_call" | custom-call | tf_op jit(solution)/shard_map/pallas_call | solution.py:286
  (64 shorter events, 6.2 us)
Async XLA Ops:
  5.1 19.2 %copy-start.17 = (f32[6,1,16,128]{3,2,1,0:T(8,128)S(1)}, f32[6,1,16,128]{3,2,1,0:T(8,128)}, u32[]{:S(2)}) copy-start(f32[6,1,16,128]{3,2,1,0:T(8,128)} %get-tuple-element.27) | copy-start | bytes 147460
  12.4 14.6 %copy-start.23 = (f32[6,8,128]{2,1,0:T(8,128)S(1)}, f32[6,8,128]{2,1,0:T(8,128)}, u32[]{:S(2)}) copy-start(f32[6,8,128]{2,1,0:T(8,128)} %get-tuple-element.28) | copy-start | bytes 73732
  12.4 19.2 %copy-start.22 = (f32[6,8,128]{2,1,0:T(8,128)S(1)}, f32[6,8,128]{2,1,0:T(8,128)}, u32[]{:S(2)}) copy-start(f32[6,8,128]{2,1,0:T(8,128)} %get-tuple-element.29) | copy-start | bytes 73732
  12.4 27.0 %all-to-all-start.1 = ((f32[16,1,448]{2,1,0:T(1,128)}), f32[16,1,448]{2,1,0:T(1,128)S(1)}, u32[]{:S(2)}, u32[]{:S(2)}) async-start(f32[16,1,448]{2,1,0:T(1,128)} %get-tuple-element.31), calls=%async_computation.1 | async-start | bytes 65536 | tf_op jit(solution)/shard_map/all_to_all | solution.py:278
  21.1 18.3 %collective-permute-start = (f32[6,1,16,128]{3,2,1,0:T(8,128)}, f32[6,1,16,128]{3,2,1,0:T(8,128)S(1)}, u32[]{:S(2)}, u32[]{:S(2)}) collective-permute-start(f32[6,1,16,128]{3,2,1,0:T(8,128)} %get-tuple-element.26), channel_id=1, source_target_pairs={{0,64},{64,128},{128,192},{1,65},{65,129},{129,193},{2,66},{66,130... | collective-permute-start | bytes 147464 | tf_op jit(solution)/shard_map/ppermute | solution.py:221
  24.3 15.1 %collective-permute-start.1 = (f32[6,1,16,128]{3,2,1,0:T(8,128)S(1)}, f32[6,1,16,128]{3,2,1,0:T(8,128)S(1)}, u32[]{:S(2)}, u32[]{:S(2)}) collective-permute-start(f32[6,1,16,128]{3,2,1,0:T(8,128)S(1)} %copy-done.17), channel_id=1, source_target_pairs={{64,0},{128,64},{192,128},{65,1},{129,65},{193,129},{66,2},{130,66... | collective-permute-start | bytes 147464 | tf_op jit(solution)/shard_map/ppermute | solution.py:222
  27.0 6.5 %collective-permute-start.2 = (f32[6,8,128]{2,1,0:T(8,128)S(1)}, f32[6,8,128]{2,1,0:T(8,128)S(1)}, u32[]{:S(2)}, u32[]{:S(2)}) collective-permute-start(f32[6,8,128]{2,1,0:T(8,128)S(1)} %copy-done.23), channel_id=1, source_target_pairs={{0,4},{4,8},{8,12},{12,16},{16,20},{20,24},{24,28},{28,32},{32,36}... | collective-permute-start | bytes 73736 | tf_op jit(solution)/shard_map/ppermute | solution.py:221
  31.6 7.8 %collective-permute-start.3 = (f32[6,8,128]{2,1,0:T(8,128)S(1)}, f32[6,8,128]{2,1,0:T(8,128)S(1)}, u32[]{:S(2)}, u32[]{:S(2)}) collective-permute-start(f32[6,8,128]{2,1,0:T(8,128)S(1)} %copy-done.22), channel_id=1, source_target_pairs={{4,0},{8,4},{12,8},{16,12},{20,16},{24,20},{28,24},{32,28},{36,32}... | collective-permute-start | bytes 73736 | tf_op jit(solution)/shard_map/ppermute | solution.py:222
  45.6 12.6 %all-to-all-start.2 = ((f32[4,1,768]{2,1,0:T(1,128)}), f32[4,1,768]{2,1,0:T(1,128)S(1)}, u32[]{:S(2)}, u32[]{:S(2)}) async-start(f32[4,1,768]{2,1,0:T(1,128)} %get-tuple-element.37), calls=%async_computation.2 | async-start | bytes 24576 | tf_op jit(solution)/shard_map/all_to_all | solution.py:223
  52.3 24.9 %collective-permute-start.4 = (f32[6,1,16,128]{3,2,1,0:T(8,128)}, f32[6,1,16,128]{3,2,1,0:T(8,128)S(1)}, u32[]{:S(2)}, u32[]{:S(2)}) collective-permute-start(f32[6,1,16,128]{3,2,1,0:T(8,128)} %get-tuple-element.33), channel_id=1, source_target_pairs={{0,64},{64,128},{128,192},{1,65},{65,129},{129,193},{2,66},{66,130... | collective-permute-start | bytes 147464 | tf_op jit(solution)/shard_map/ppermute | solution.py:221
  55.5 21.7 %collective-permute-start.5 = (f32[6,1,16,128]{3,2,1,0:T(8,128)}, f32[6,1,16,128]{3,2,1,0:T(8,128)S(1)}, u32[]{:S(2)}, u32[]{:S(2)}) collective-permute-start(f32[6,1,16,128]{3,2,1,0:T(8,128)} %get-tuple-element.34), channel_id=1, source_target_pairs={{64,0},{128,64},{192,128},{65,1},{129,65},{193,129},{66,2},{130,66... | collective-permute-start | bytes 147464 | tf_op jit(solution)/shard_map/ppermute | solution.py:222
  58.2 6.6 %copy-start.21 = (f32[6,8,128]{2,1,0:T(8,128)S(1)}, f32[6,8,128]{2,1,0:T(8,128)}, u32[]{:S(2)}) copy-start(f32[6,8,128]{2,1,0:T(8,128)} %get-tuple-element.35) | copy-start | bytes 73732
  58.2 11.2 %copy-start.19 = (f32[6,8,128]{2,1,0:T(8,128)S(1)}, f32[6,8,128]{2,1,0:T(8,128)}, u32[]{:S(2)}) copy-start(f32[6,8,128]{2,1,0:T(8,128)} %get-tuple-element.36) | copy-start | bytes 73732
  58.8 18.5 %all-to-all-start.3 = ((f32[16,1,384]{2,1,0:T(1,128)}), f32[16,1,384]{2,1,0:T(1,128)S(1)}, u32[]{:S(2)}, u32[]{:S(2)}) async-start(f32[16,1,384]{2,1,0:T(1,128)} %get-tuple-element.38), calls=%async_computation.3 | async-start | bytes 49152 | tf_op jit(solution)/shard_map/all_to_all | solution.py:278
  64.8 6.5 %collective-permute-start.6 = (f32[6,8,128]{2,1,0:T(8,128)S(1)}, f32[6,8,128]{2,1,0:T(8,128)S(1)}, u32[]{:S(2)}, u32[]{:S(2)}) collective-permute-start(f32[6,8,128]{2,1,0:T(8,128)S(1)} %copy-done.21), channel_id=1, source_target_pairs={{0,4},{4,8},{8,12},{12,16},{16,20},{20,24},{24,28},{28,32},{32,36}... | collective-permute-start | bytes 73736 | tf_op jit(solution)/shard_map/ppermute | solution.py:221
  69.4 7.8 %collective-permute-start.7 = (f32[6,8,128]{2,1,0:T(8,128)S(1)}, f32[6,8,128]{2,1,0:T(8,128)S(1)}, u32[]{:S(2)}, u32[]{:S(2)}) collective-permute-start(f32[6,8,128]{2,1,0:T(8,128)S(1)} %copy-done.19), channel_id=1, source_target_pairs={{4,0},{8,4},{12,8},{16,12},{20,16},{24,20},{28,24},{32,28},{36,32}... | collective-permute-start | bytes 73736 | tf_op jit(solution)/shard_map/ppermute | solution.py:222
  83.6 10.7 %all-to-all-start.4 = ((f32[4,1,768]{2,1,0:T(1,128)}), f32[4,1,768]{2,1,0:T(1,128)S(1)}, u32[]{:S(2)}, u32[]{:S(2)}) async-start(f32[4,1,768]{2,1,0:T(1,128)} %get-tuple-element.45), calls=%async_computation.4 | async-start | bytes 24576 | tf_op jit(solution)/shard_map/all_to_all | solution.py:223
  88.4 24.9 %collective-permute-start.8 = (f32[6,1,16,128]{3,2,1,0:T(8,128)}, f32[6,1,16,128]{3,2,1,0:T(8,128)S(1)}, u32[]{:S(2)}, u32[]{:S(2)}) collective-permute-start(f32[6,1,16,128]{3,2,1,0:T(8,128)} %get-tuple-element.41), channel_id=1, source_target_pairs={{0,64},{64,128},{128,192},{1,65},{65,129},{129,193},{2,66},{66,130... | collective-permute-start | bytes 147464 | tf_op jit(solution)/shard_map/ppermute | solution.py:221
  91.6 21.7 %collective-permute-start.9 = (f32[6,1,16,128]{3,2,1,0:T(8,128)}, f32[6,1,16,128]{3,2,1,0:T(8,128)S(1)}, u32[]{:S(2)}, u32[]{:S(2)}) collective-permute-start(f32[6,1,16,128]{3,2,1,0:T(8,128)} %get-tuple-element.42), channel_id=1, source_target_pairs={{64,0},{128,64},{192,128},{65,1},{129,65},{193,129},{66,2},{130,66... | collective-permute-start | bytes 147464 | tf_op jit(solution)/shard_map/ppermute | solution.py:222
  94.2 6.6 %copy-start.20 = (f32[6,8,128]{2,1,0:T(8,128)S(1)}, f32[6,8,128]{2,1,0:T(8,128)}, u32[]{:S(2)}) copy-start(f32[6,8,128]{2,1,0:T(8,128)} %get-tuple-element.43) | copy-start | bytes 73732
  94.2 11.2 %copy-start.18 = (f32[6,8,128]{2,1,0:T(8,128)S(1)}, f32[6,8,128]{2,1,0:T(8,128)}, u32[]{:S(2)}) copy-start(f32[6,8,128]{2,1,0:T(8,128)} %get-tuple-element.44) | copy-start | bytes 73732
  94.8 18.5 %all-to-all-start.5 = ((f32[16,1,384]{2,1,0:T(1,128)}), f32[16,1,384]{2,1,0:T(1,128)S(1)}, u32[]{:S(2)}, u32[]{:S(2)}) async-start(f32[16,1,384]{2,1,0:T(1,128)} %get-tuple-element.46), calls=%async_computation.5 | async-start | bytes 49152 | tf_op jit(solution)/shard_map/all_to_all | solution.py:278
  100.8 6.7 %collective-permute-start.10 = (f32[6,8,128]{2,1,0:T(8,128)S(1)}, f32[6,8,128]{2,1,0:T(8,128)S(1)}, u32[]{:S(2)}, u32[]{:S(2)}) collective-permute-start(f32[6,8,128]{2,1,0:T(8,128)S(1)} %copy-done.20), channel_id=1, source_target_pairs={{0,4},{4,8},{8,12},{12,16},{16,20},{20,24},{24,28},{28,32},{32,36}... | collective-permute-start | bytes 73736 | tf_op jit(solution)/shard_map/ppermute | solution.py:221
  105.4 7.8 %collective-permute-start.11 = (f32[6,8,128]{2,1,0:T(8,128)S(1)}, f32[6,8,128]{2,1,0:T(8,128)S(1)}, u32[]{:S(2)}, u32[]{:S(2)}) collective-permute-start(f32[6,8,128]{2,1,0:T(8,128)S(1)} %copy-done.18), channel_id=1, source_target_pairs={{4,0},{8,4},{12,8},{16,12},{20,16},{24,20},{28,24},{32,28},{36,32}... | collective-permute-start | bytes 73736 | tf_op jit(solution)/shard_map/ppermute | solution.py:222
  (17 other events, 26.2 us)

commit v7 on v6

--- a/solution.py
+++ b/solution.py
@@ -275,6 +275,7 @@
     received = None
     for sweep in range(SWEEPS):
         halos = exchange(faces)
+        rows, halos[2], halos[3] = lax.optimization_barrier((rows, halos[2], halos[3]))
         incoming = lax.all_to_all(rows, "span", split_axis=0, concat_axis=0, tiled=True)
         if sweep == 0:
             adj, rows, received, *faces = first(*blk, adj, sensitivity, diagonal, face_coef, *halos,

time: 120 us -> 124 us (1.033)
  the two profiles are of different devices: /device:TPU:118 before, /device:TPU:12 now
where the time goes in v7:
time: 124 us; the launch traced here: 123 us
  starting transfers between devices  75.8 us (61%)
  waiting for transfers between devices  22.6 us (18%)
  Pallas kernels  19.1 us (15%)
  local copies, waits for them, and re-layouts  4.92 us (4%)
    all_to_all x3, starting transfers between devices, local(): lax.all_to_all(rows, 'span', split_axis=0, concat_axis=0, tiled=True)  28.4 us
    ppermute x6, starting transfers between devices, exchange(): out.append(lax.ppermute(hi_face, axis, forward))  19.5 us
    all_to_all x3, waiting for transfers between devices, local(): lax.all_to_all(rows, 'span', split_axis=0, concat_axis=0, tiled=True)  17.1 us
    all_to_all x3, starting transfers between devices, exchange(): lax.all_to_all(w_buf, 'wall', split_axis=0, concat_axis=0, tiled=True)  16.4 us
    ppermute x6, starting transfers between devices, exchange(): out.append(lax.ppermute(lo_face, axis, backward))  11.7 us
    pallas_call x1, Pallas kernels, local(): step(*blk, adj, sensitivity, diagonal, face_coef, *halos, incoming, recei...  5.7 us
    pallas_call x1, Pallas kernels, local(): first(*blk, adj, sensitivity, diagonal, face_coef, *halos, incoming, send...  5.55 us
    unnamed x41, local copies, waits for them, and re-layouts  4.92 us
  transfers between devices with their start and end apart: 18, of which 5 were waited for; matrix products, arithmetic and copies ran while one was open for 0% of the time, Pallas kernels for 0%

profile of v7, /device:TPU:12, one launch (start us, length us, event | category | flops | bytes accessed | tf_op | source)
XLA Modules:
  0.0 123.4 jit_solution(1336297852499753976)
XLA Ops:
  1.9 3.2 %shard_map.122 = (f32[6,8,16,128]{3,2,1,0:T(8,128)}, f32[16,1,448]{2,1,0:T(1,128)}, f32[6,1,16,128]{3,2,1,0:T(8,128)}, f32[6,1,16,128]{3,2,1,0:T(8,128)}, f32[6,...) custom-call(f32[3,6,6]{2,1,0:T(8,128)} %ub_ref.7, f32[3,6,6]{2,1,0:T(8,128)} %lb_ref.7, ...), custom_call_target="tpu_custom_call" | custom-call | tf_op jit(solution)/shard_map/pallas_call | solution.py:255
  5.1 3.2 %collective-permute-start.2 = (f32[6,8,128]{2,1,0:T(8,128)}, f32[6,8,128]{2,1,0:T(8,128)S(1)}, u32[]{:S(2)}, u32[]{:S(2)}) collective-permute-start(f32[6,8,128]{2,1,0:T(8,128)} %get-tuple-element.38), channel_id=1, source_target_pairs={{0,4},{4,8},{8,12},{12,16},{16,20},{20,24},{24,28},{28,32},{32,36}... | collective-permute-start | bytes 73736 | tf_op jit(solution)/shard_map/ppermute | solution.py:221
  8.4 1.4 %collective-permute-start.3 = (f32[6,8,128]{2,1,0:T(8,128)}, f32[6,8,128]{2,1,0:T(8,128)S(1)}, u32[]{:S(2)}, u32[]{:S(2)}) collective-permute-start(f32[6,8,128]{2,1,0:T(8,128)} %get-tuple-element.39), channel_id=1, source_target_pairs={{4,0},{8,4},{12,8},{16,12},{20,16},{24,20},{28,24},{32,28},{36,32}... | collective-permute-start | bytes 73736 | tf_op jit(solution)/shard_map/ppermute | solution.py:222
  9.8 4.8 %all-to-all-start = ((f32[4,1,768]{2,1,0:T(1,128)}), f32[4,1,768]{2,1,0:T(1,128)S(1)}, u32[]{:S(2)}, u32[]{:S(2)}) async-start(f32[4,1,768]{2,1,0:T(1,128)} %get-tuple-element.42), calls=%async_computation | async-start | bytes 24576 | tf_op jit(solution)/shard_map/all_to_all | solution.py:223
  14.6 1.8 %all-to-all-done.w_inc = f32[4,1,768]{2,1,0:T(1,128)S(1)} async-done(((f32[4,1,768]{2,1,0:T(1,128)}), f32[4,1,768]{2,1,0:T(1,128)S(1)}, u32[]{:S(2)}, u32[]{:S(2)}) %all-to-all-start) | async-done | bytes 12320 | tf_op jit(solution)/shard_map/all_to_all | solution.py:223
  17.0 12.1 %all-to-all-start.1 = ((f32[16,1,448]{2,1,0:T(1,128)}), f32[16,1,448]{2,1,0:T(1,128)S(1)}, u32[]{:S(2)}, u32[]{:S(2)}) async-start(f32[16,1,448]{2,1,0:T(1,128)} %get-tuple-element.43), calls=%async_computation.1 | async-start | bytes 65536 | tf_op jit(solution)/shard_map/all_to_all | solution.py:279
  29.2 3.5 %collective-permute-start = (f32[6,1,16,128]{3,2,1,0:T(8,128)S(1)}, f32[6,1,16,128]{3,2,1,0:T(8,128)S(1)}, u32[]{:S(2)}, u32[]{:S(2)}) collective-permute-start(f32[6,1,16,128]{3,2,1,0:T(8,128)S(1)} %copy-done.19), channel_id=1, source_target_pairs={{0,64},{64,128},{128,192},{1,65},{65,129},{129,193},{2,66},{66,130... | collective-permute-start | bytes 147464 | tf_op jit(solution)/shard_map/ppermute | solution.py:221
  32.7 2.4 %collective-permute-start.1 = (f32[6,1,16,128]{3,2,1,0:T(8,128)S(1)}, f32[6,1,16,128]{3,2,1,0:T(8,128)S(1)}, u32[]{:S(2)}, u32[]{:S(2)}) collective-permute-start(f32[6,1,16,128]{3,2,1,0:T(8,128)S(1)} %copy-done.18), channel_id=1, source_target_pairs={{64,0},{128,64},{192,128},{65,1},{129,65},{193,129},{66,2},{130,66... | collective-permute-start | bytes 147464 | tf_op jit(solution)/shard_map/ppermute | solution.py:222
  35.2 3.5 %collective-permute-done.1.hch = f32[6,1,16,128]{3,2,1,0:T(8,128)S(1)} collective-permute-done((f32[6,1,16,128]{3,2,1,0:T(8,128)S(1)}, f32[6,1,16,128]{3,2,1,0:T(8,128)S(1)}, u32[]{:S(2)}, u32[]{:S(2)}) %collective-permute-start.1) | collective-permute-done | bytes 49184 | tf_op jit(solution)/shard_map/ppermute | solution.py:222
  39.3 5.5 %shard_map.123 = (f32[6,8,16,128]{3,2,1,0:T(8,128)}, f32[16,1,384]{2,1,0:T(1,128)}, s32[1,1024]{1,0:T(1,128)}, f32[6,1,16,128]{3,2,1,0:T(8,128)}, f32[6,1,16,128...) custom-call(f32[3,6,6]{2,1,0:T(8,128)} %ub_ref.7, f32[3,6,6]{2,1,0:T(8,128)} %lb_ref.7, ...), custom_call_target="tpu_custom_call" | custom-call | tf_op jit(solution)/shard_map/pallas_call | solution.py:281
  44.8 3.8 %collective-permute-start.6 = (f32[6,8,128]{2,1,0:T(8,128)}, f32[6,8,128]{2,1,0:T(8,128)S(1)}, u32[]{:S(2)}, u32[]{:S(2)}) collective-permute-start(f32[6,8,128]{2,1,0:T(8,128)} %get-tuple-element.48), channel_id=1, source_target_pairs={{0,4},{4,8},{8,12},{12,16},{16,20},{20,24},{24,28},{28,32},{32,36}... | collective-permute-start | bytes 73736 | tf_op jit(solution)/shard_map/ppermute | solution.py:221
  50.0 6.7 %all-to-all-start.2 = ((f32[4,1,768]{2,1,0:T(1,128)}), f32[4,1,768]{2,1,0:T(1,128)S(1)}, u32[]{:S(2)}, u32[]{:S(2)}) async-start(f32[4,1,768]{2,1,0:T(1,128)} %get-tuple-element.52), calls=%async_computation.2 | async-start | bytes 24576 | tf_op jit(solution)/shard_map/all_to_all | solution.py:223
  56.7 3.2 %collective-permute-start.4 = (f32[6,1,16,128]{3,2,1,0:T(8,128)}, f32[6,1,16,128]{3,2,1,0:T(8,128)S(1)}, u32[]{:S(2)}, u32[]{:S(2)}) collective-permute-start(f32[6,1,16,128]{3,2,1,0:T(8,128)} %get-tuple-element.45), channel_id=1, source_target_pairs={{0,64},{64,128},{128,192},{1,65},{65,129},{129,193},{2,66},{66,130... | collective-permute-start | bytes 147464 | tf_op jit(solution)/shard_map/ppermute | solution.py:221
  59.9 2.6 %collective-permute-start.5 = (f32[6,1,16,128]{3,2,1,0:T(8,128)}, f32[6,1,16,128]{3,2,1,0:T(8,128)S(1)}, u32[]{:S(2)}, u32[]{:S(2)}) collective-permute-start(f32[6,1,16,128]{3,2,1,0:T(8,128)} %get-tuple-element.46), channel_id=1, source_target_pairs={{64,0},{128,64},{192,128},{65,1},{129,65},{193,129},{66,2},{130,66... | collective-permute-start | bytes 147464 | tf_op jit(solution)/shard_map/ppermute | solution.py:222
  63.2 10.0 %all-to-all-start.3 = ((f32[16,1,384]{2,1,0:T(1,128)}), f32[16,1,384]{2,1,0:T(1,128)S(1)}, u32[]{:S(2)}, u32[]{:S(2)}) async-start(f32[16,1,384]{2,1,0:T(1,128)} %get-tuple-element.53), calls=%async_computation.3 | async-start | bytes 49152 | tf_op jit(solution)/shard_map/all_to_all | solution.py:279
  73.3 8.6 %all-to-all-done.3.inc_ref = f32[16,1,384]{2,1,0:T(1,128)S(1)} async-done(((f32[16,1,384]{2,1,0:T(1,128)}), f32[16,1,384]{2,1,0:T(1,128)S(1)}, u32[]{:S(2)}, u32[]{:S(2)}) %all-to-all-start.3) | async-done | bytes 24608 | tf_op jit(solution)/shard_map/all_to_all | solution.py:279
  82.5 5.7 %shard_map.124 = (f32[6,8,16,128]{3,2,1,0:T(8,128)}, f32[16,1,384]{2,1,0:T(1,128)}, s32[1,1024]{1,0:T(1,128)}, f32[6,1,16,128]{3,2,1,0:T(8,128)}, f32[6,1,16,128...) custom-call(f32[3,6,6]{2,1,0:T(8,128)} %ub_ref.7, f32[3,6,6]{2,1,0:T(8,128)} %lb_ref.7, ...), custom_call_target="tpu_custom_call" | custom-call | tf_op jit(solution)/shard_map/pallas_call | solution.py:284
  88.2 2.6 %collective-permute-start.10 = (f32[6,8,128]{2,1,0:T(8,128)}, f32[6,8,128]{2,1,0:T(8,128)S(1)}, u32[]{:S(2)}, u32[]{:S(2)}) collective-permute-start(f32[6,8,128]{2,1,0:T(8,128)} %get-tuple-element.59), channel_id=1, source_target_pairs={{0,4},{4,8},{8,12},{12,16},{16,20},{20,24},{24,28},{28,32},{32,36}... | collective-permute-start | bytes 73736 | tf_op jit(solution)/shard_map/ppermute | solution.py:221
  92.1 4.8 %all-to-all-start.4 = ((f32[4,1,768]{2,1,0:T(1,128)}), f32[4,1,768]{2,1,0:T(1,128)S(1)}, u32[]{:S(2)}, u32[]{:S(2)}) async-start(f32[4,1,768]{2,1,0:T(1,128)} %get-tuple-element.63), calls=%async_computation.4 | async-start | bytes 24576 | tf_op jit(solution)/shard_map/all_to_all | solution.py:223
  96.9 3.2 %collective-permute-start.8 = (f32[6,1,16,128]{3,2,1,0:T(8,128)}, f32[6,1,16,128]{3,2,1,0:T(8,128)S(1)}, u32[]{:S(2)}, u32[]{:S(2)}) collective-permute-start(f32[6,1,16,128]{3,2,1,0:T(8,128)} %get-tuple-element.56), channel_id=1, source_target_pairs={{0,64},{64,128},{128,192},{1,65},{65,129},{129,193},{2,66},{66,130... | collective-permute-start | bytes 147464 | tf_op jit(solution)/shard_map/ppermute | solution.py:221
  100.1 2.6 %collective-permute-start.9 = (f32[6,1,16,128]{3,2,1,0:T(8,128)}, f32[6,1,16,128]{3,2,1,0:T(8,128)S(1)}, u32[]{:S(2)}, u32[]{:S(2)}) collective-permute-start(f32[6,1,16,128]{3,2,1,0:T(8,128)} %get-tuple-element.57), channel_id=1, source_target_pairs={{64,0},{128,64},{192,128},{65,1},{129,65},{193,129},{66,2},{130,66... | collective-permute-start | bytes 147464 | tf_op jit(solution)/shard_map/ppermute | solution.py:222
  103.4 6.2 %all-to-all-start.5 = ((f32[16,1,384]{2,1,0:T(1,128)}), f32[16,1,384]{2,1,0:T(1,128)S(1)}, u32[]{:S(2)}, u32[]{:S(2)}) async-start(f32[16,1,384]{2,1,0:T(1,128)} %get-tuple-element.64), calls=%async_computation.5 | async-start | bytes 49152 | tf_op jit(solution)/shard_map/all_to_all | solution.py:279
  109.6 8.6 %all-to-all-done.5.inc_ref = f32[16,1,384]{2,1,0:T(1,128)S(1)} async-done(((f32[16,1,384]{2,1,0:T(1,128)}), f32[16,1,384]{2,1,0:T(1,128)S(1)}, u32[]{:S(2)}, u32[]{:S(2)}) %all-to-all-start.5) | async-done | bytes 24608 | tf_op jit(solution)/shard_map/all_to_all | solution.py:279
  118.8 4.7 %shard_map.125 = (f32[6,8,16,128]{3,2,1,0:T(8,128)}, f32[8,16,128]{2,1,0:T(8,128)}) custom-call(f32[3,6,6]{2,1,0:T(8,128)} %ub_ref.7, f32[3,6,6]{2,1,0:T(8,128)} %lb_ref.7, f32[2,6,6]{2,1,0:T(8,128)} %copy.16.ib_ref, s32[1]{0:T(128)} %bitcast.wall_me, f32[6,8,16,128]{3,2,1,0:T(8,128)} %get-tuple-element.55.adj_ref, f32[6,8,16,128]{3,2,1,0:T(8,128)} %sens_ref.7, ...), custom_call_target="tpu_custom_call" | custom-call | tf_op jit(solution)/shard_map/pallas_call | solution.py:287
  (57 shorter events, 7.7 us)
Async XLA Ops:
  5.1 24.0 %copy-start.19 = (f32[6,1,16,128]{3,2,1,0:T(8,128)S(1)}, f32[6,1,16,128]{3,2,1,0:T(8,128)}, u32[]{:S(2)}) copy-start(f32[6,1,16,128]{3,2,1,0:T(8,128)} %get-tuple-element.35) | copy-start | bytes 147460
  5.1 9.5 %collective-permute-start.2 = (f32[6,8,128]{2,1,0:T(8,128)}, f32[6,8,128]{2,1,0:T(8,128)S(1)}, u32[]{:S(2)}, u32[]{:S(2)}) collective-permute-start(f32[6,8,128]{2,1,0:T(8,128)} %get-tuple-element.38), channel_id=1, source_target_pairs={{0,4},{4,8},{8,12},{12,16},{16,20},{20,24},{24,28},{28,32},{32,36}... | collective-permute-start | bytes 73736 | tf_op jit(solution)/shard_map/ppermute | solution.py:221
  8.4 24.3 %copy-start.18 = (f32[6,1,16,128]{3,2,1,0:T(8,128)S(1)}, f32[6,1,16,128]{3,2,1,0:T(8,128)}, u32[]{:S(2)}) copy-start(f32[6,1,16,128]{3,2,1,0:T(8,128)} %get-tuple-element.36) | copy-start | bytes 147460
  8.4 6.2 %collective-permute-start.3 = (f32[6,8,128]{2,1,0:T(8,128)}, f32[6,8,128]{2,1,0:T(8,128)S(1)}, u32[]{:S(2)}, u32[]{:S(2)}) collective-permute-start(f32[6,8,128]{2,1,0:T(8,128)} %get-tuple-element.39), channel_id=1, source_target_pairs={{4,0},{8,4},{12,8},{16,12},{20,16},{24,20},{28,24},{32,28},{36,32}... | collective-permute-start | bytes 73736 | tf_op jit(solution)/shard_map/ppermute | solution.py:222
  9.8 6.6 %all-to-all-start = ((f32[4,1,768]{2,1,0:T(1,128)}), f32[4,1,768]{2,1,0:T(1,128)S(1)}, u32[]{:S(2)}, u32[]{:S(2)}) async-start(f32[4,1,768]{2,1,0:T(1,128)} %get-tuple-element.42), calls=%async_computation | async-start | bytes 24576 | tf_op jit(solution)/shard_map/all_to_all | solution.py:223
  17.0 21.6 %all-to-all-start.1 = ((f32[16,1,448]{2,1,0:T(1,128)}), f32[16,1,448]{2,1,0:T(1,128)S(1)}, u32[]{:S(2)}, u32[]{:S(2)}) async-start(f32[16,1,448]{2,1,0:T(1,128)} %get-tuple-element.43), calls=%async_computation.1 | async-start | bytes 65536 | tf_op jit(solution)/shard_map/all_to_all | solution.py:279
  29.2 6.0 %collective-permute-start = (f32[6,1,16,128]{3,2,1,0:T(8,128)S(1)}, f32[6,1,16,128]{3,2,1,0:T(8,128)S(1)}, u32[]{:S(2)}, u32[]{:S(2)}) collective-permute-start(f32[6,1,16,128]{3,2,1,0:T(8,128)S(1)} %copy-done.19), channel_id=1, source_target_pairs={{0,64},{64,128},{128,192},{1,65},{65,129},{129,193},{2,66},{66,130... | collective-permute-start | bytes 147464 | tf_op jit(solution)/shard_map/ppermute | solution.py:221
  32.7 6.0 %collective-permute-start.1 = (f32[6,1,16,128]{3,2,1,0:T(8,128)S(1)}, f32[6,1,16,128]{3,2,1,0:T(8,128)S(1)}, u32[]{:S(2)}, u32[]{:S(2)}) collective-permute-start(f32[6,1,16,128]{3,2,1,0:T(8,128)S(1)} %copy-done.18), channel_id=1, source_target_pairs={{64,0},{128,64},{192,128},{65,1},{129,65},{193,129},{66,2},{130,66... | collective-permute-start | bytes 147464 | tf_op jit(solution)/shard_map/ppermute | solution.py:222
  44.8 17.7 %collective-permute-start.6 = (f32[6,8,128]{2,1,0:T(8,128)}, f32[6,8,128]{2,1,0:T(8,128)S(1)}, u32[]{:S(2)}, u32[]{:S(2)}) collective-permute-start(f32[6,8,128]{2,1,0:T(8,128)} %get-tuple-element.48), channel_id=1, source_target_pairs={{0,4},{4,8},{8,12},{12,16},{16,20},{20,24},{24,28},{28,32},{32,36}... | collective-permute-start | bytes 73736 | tf_op jit(solution)/shard_map/ppermute | solution.py:221
  48.7 13.9 %collective-permute-start.7 = (f32[6,8,128]{2,1,0:T(8,128)}, f32[6,8,128]{2,1,0:T(8,128)S(1)}, u32[]{:S(2)}, u32[]{:S(2)}) collective-permute-start(f32[6,8,128]{2,1,0:T(8,128)} %get-tuple-element.49), channel_id=1, source_target_pairs={{4,0},{8,4},{12,8},{16,12},{20,16},{24,20},{28,24},{32,28},{36,32}... | collective-permute-start | bytes 73736 | tf_op jit(solution)/shard_map/ppermute | solution.py:222
  50.0 12.6 %all-to-all-start.2 = ((f32[4,1,768]{2,1,0:T(1,128)}), f32[4,1,768]{2,1,0:T(1,128)S(1)}, u32[]{:S(2)}, u32[]{:S(2)}) async-start(f32[4,1,768]{2,1,0:T(1,128)} %get-tuple-element.52), calls=%async_computation.2 | async-start | bytes 24576 | tf_op jit(solution)/shard_map/all_to_all | solution.py:223
  56.7 16.5 %collective-permute-start.4 = (f32[6,1,16,128]{3,2,1,0:T(8,128)}, f32[6,1,16,128]{3,2,1,0:T(8,128)S(1)}, u32[]{:S(2)}, u32[]{:S(2)}) collective-permute-start(f32[6,1,16,128]{3,2,1,0:T(8,128)} %get-tuple-element.45), channel_id=1, source_target_pairs={{0,64},{64,128},{128,192},{1,65},{65,129},{129,193},{2,66},{66,130... | collective-permute-start | bytes 147464 | tf_op jit(solution)/shard_map/ppermute | solution.py:221
  59.9 13.4 %collective-permute-start.5 = (f32[6,1,16,128]{3,2,1,0:T(8,128)}, f32[6,1,16,128]{3,2,1,0:T(8,128)S(1)}, u32[]{:S(2)}, u32[]{:S(2)}) collective-permute-start(f32[6,1,16,128]{3,2,1,0:T(8,128)} %get-tuple-element.46), channel_id=1, source_target_pairs={{64,0},{128,64},{192,128},{65,1},{129,65},{193,129},{66,2},{130,66... | collective-permute-start | bytes 147464 | tf_op jit(solution)/shard_map/ppermute | solution.py:222
  62.6 19.3 %copy-start.14 = (f32[6,8,128]{2,1,0:T(8,128)}, f32[6,8,128]{2,1,0:T(8,128)S(1)}, u32[]{:S(2)}) copy-start(f32[6,8,128]{2,1,0:T(8,128)S(1)} %collective-permute-done.7.hsh) | copy-start | bytes 73732
  63.2 18.7 %all-to-all-start.3 = ((f32[16,1,384]{2,1,0:T(1,128)}), f32[16,1,384]{2,1,0:T(1,128)S(1)}, u32[]{:S(2)}, u32[]{:S(2)}) async-start(f32[16,1,384]{2,1,0:T(1,128)} %get-tuple-element.53), calls=%async_computation.3 | async-start | bytes 49152 | tf_op jit(solution)/shard_map/all_to_all | solution.py:279
  73.3 8.6 %copy-start.6 = (f32[6,1,16,128]{3,2,1,0:T(8,128)}, f32[6,1,16,128]{3,2,1,0:T(8,128)S(1)}, u32[]{:S(2)}) copy-start(f32[6,1,16,128]{3,2,1,0:T(8,128)S(1)} %collective-permute-done.4.hcl) | copy-start | bytes 147460
  88.2 14.5 %collective-permute-start.10 = (f32[6,8,128]{2,1,0:T(8,128)}, f32[6,8,128]{2,1,0:T(8,128)S(1)}, u32[]{:S(2)}, u32[]{:S(2)}) collective-permute-start(f32[6,8,128]{2,1,0:T(8,128)} %get-tuple-element.59), channel_id=1, source_target_pairs={{0,4},{4,8},{8,12},{12,16},{16,20},{20,24},{24,28},{28,32},{32,36}... | collective-permute-start | bytes 73736 | tf_op jit(solution)/shard_map/ppermute | solution.py:221
  90.8 12.0 %collective-permute-start.11 = (f32[6,8,128]{2,1,0:T(8,128)}, f32[6,8,128]{2,1,0:T(8,128)S(1)}, u32[]{:S(2)}, u32[]{:S(2)}) collective-permute-start(f32[6,8,128]{2,1,0:T(8,128)} %get-tuple-element.60), channel_id=1, source_target_pairs={{4,0},{8,4},{12,8},{16,12},{20,16},{24,20},{28,24},{32,28},{36,32}... | collective-permute-start | bytes 73736 | tf_op jit(solution)/shard_map/ppermute | solution.py:222
  92.1 10.7 %all-to-all-start.4 = ((f32[4,1,768]{2,1,0:T(1,128)}), f32[4,1,768]{2,1,0:T(1,128)S(1)}, u32[]{:S(2)}, u32[]{:S(2)}) async-start(f32[4,1,768]{2,1,0:T(1,128)} %get-tuple-element.63), calls=%async_computation.4 | async-start | bytes 24576 | tf_op jit(solution)/shard_map/all_to_all | solution.py:223
  96.9 12.7 %collective-permute-start.8 = (f32[6,1,16,128]{3,2,1,0:T(8,128)}, f32[6,1,16,128]{3,2,1,0:T(8,128)S(1)}, u32[]{:S(2)}, u32[]{:S(2)}) collective-permute-start(f32[6,1,16,128]{3,2,1,0:T(8,128)} %get-tuple-element.56), channel_id=1, source_target_pairs={{0,64},{64,128},{128,192},{1,65},{65,129},{129,193},{2,66},{66,130... | collective-permute-start | bytes 147464 | tf_op jit(solution)/shard_map/ppermute | solution.py:221
  100.1 9.5 %collective-permute-start.9 = (f32[6,1,16,128]{3,2,1,0:T(8,128)}, f32[6,1,16,128]{3,2,1,0:T(8,128)S(1)}, u32[]{:S(2)}, u32[]{:S(2)}) collective-permute-start(f32[6,1,16,128]{3,2,1,0:T(8,128)} %get-tuple-element.57), channel_id=1, source_target_pairs={{64,0},{128,64},{192,128},{65,1},{129,65},{193,129},{66,2},{130,66... | collective-permute-start | bytes 147464 | tf_op jit(solution)/shard_map/ppermute | solution.py:222
  102.8 15.4 %copy-start.17 = (f32[6,8,128]{2,1,0:T(8,128)}, f32[6,8,128]{2,1,0:T(8,128)S(1)}, u32[]{:S(2)}) copy-start(f32[6,8,128]{2,1,0:T(8,128)S(1)} %collective-permute-done.11.hsh) | copy-start | bytes 73732
  103.4 14.8 %all-to-all-start.5 = ((f32[16,1,384]{2,1,0:T(1,128)}), f32[16,1,384]{2,1,0:T(1,128)S(1)}, u32[]{:S(2)}, u32[]{:S(2)}) async-start(f32[16,1,384]{2,1,0:T(1,128)} %get-tuple-element.64), calls=%async_computation.5 | async-start | bytes 49152 | tf_op jit(solution)/shard_map/all_to_all | solution.py:279
  109.6 8.6 %copy-start.8 = (f32[6,1,16,128]{3,2,1,0:T(8,128)}, f32[6,1,16,128]{3,2,1,0:T(8,128)S(1)}, u32[]{:S(2)}) copy-start(f32[6,1,16,128]{3,2,1,0:T(8,128)S(1)} %collective-permute-done.8.hcl) | copy-start | bytes 147460
  (14 other events, 29.8 us)

commit v8 on v6

--- a/solution.py
+++ b/solution.py
@@ -12,10 +12,8 @@
 
 def split3(x):
     p1 = x.astype(BF16)
-    r1 = x - p1.astype(F32)
-    p2 = r1.astype(BF16)
-    p3 = (r1 - p2.astype(F32)).astype(BF16)
-    return p1, p2, p3
+    p2 = (x - p1.astype(F32)).astype(BF16)
+    return p1, p2
 
 
 def gather_rows(adj, send_ref, orient_ref, weight_ref, blk, n_var, lanes):
@@ -28,7 +26,7 @@
     row_hot = (lax.broadcasted_iota(jnp.int32, (rows, n_rows), 0) == row_of).astype(F32)
     flat = adj.reshape(n_var * rows, lanes)
     picked = jnp.dot(jnp.concatenate(split3(flat), axis=1),
-                     jnp.concatenate([lane_hot] * 3, axis=0), preferred_element_type=F32)
+                     jnp.concatenate([lane_hot] * 2, axis=0), preferred_element_type=F32)
     src = jnp.sum(picked.reshape(n_var, rows, n_rows) * row_hot[None], axis=1)
     orient = flat_row(orient_ref[...])
     weight = flat_row(weight_ref[...])
@@ -145,7 +143,7 @@
     lane_hot = (lax.broadcasted_iota(jnp.int32, (nz, n_rows), 0) == lane_of).astype(BF16)
     lhs = jnp.concatenate([(row_hot[None] * part[:, None, :]).reshape(n_var * rows, n_rows)
                            for part in split3(incoming)], axis=1)
-    coupled = lax.dot_general(lhs, jnp.concatenate([lane_hot] * 3, axis=1), (((1,), (1,)), ((), ())),
+    coupled = lax.dot_general(lhs, jnp.concatenate([lane_hot] * 2, axis=1), (((1,), (1,)), ((), ())),
                               preferred_element_type=F32)
     coupled = coupled.reshape(n_var, nx, ny, nz)
     new = []

time: 120 us -> 117 us (0.975)
  Pallas kernels: 19.1 us -> 16.8 us
where the time goes in v8:
time: 117 us; the launch traced here: 116 us
  starting transfers between devices  69.3 us (59%)
  waiting for transfers between devices  17.7 us (15%)
  Pallas kernels  16.8 us (14%)
  blocking collectives  7.26 us (6%)
  local copies, waits for them, and re-layouts  4.28 us (4%)
    ppermute x6, starting transfers between devices, exchange(): out.append(lax.ppermute(hi_face, axis, forward))  23.3 us
    all_to_all x3, starting transfers between devices, local(): lax.all_to_all(rows, 'span', split_axis=0, concat_axis=0, tiled=True)  20.7 us
    ppermute x6, waiting for transfers between devices, exchange(): out.append(lax.ppermute(lo_face, axis, backward))  17.7 us
    ppermute x6, starting transfers between devices, exchange(): out.append(lax.ppermute(lo_face, axis, backward))  13.7 us
    all_to_all x2, starting transfers between devices, exchange(): lax.all_to_all(w_buf, 'wall', split_axis=0, concat_axis=0, tiled=True)  11.5 us
    all_to_all x1, blocking collectives, exchange(): lax.all_to_all(w_buf, 'wall', split_axis=0, concat_axis=0, tiled=True)  7.26 us
    pallas_call x1, Pallas kernels, local(): step(*blk, adj, sensitivity, diagonal, face_coef, *halos, incoming, recei...  4.92 us
    pallas_call x1, Pallas kernels, local(): first(*blk, adj, sensitivity, diagonal, face_coef, *halos, incoming, send...  4.86 us
  transfers between devices with their start and end apart: 17, of which 3 were waited for; matrix products, arithmetic and copies ran while one was open for 0% of the time, Pallas kernels for 0%

profile of v8, /device:TPU:118, one launch (start us, length us, event | category | flops | bytes accessed | tf_op | source)
XLA Modules:
  0.0 116.3 jit_solution(10203482527964597718)
XLA Ops:
  1.9 2.8 %shard_map.122 = (f32[6,8,16,128]{3,2,1,0:T(8,128)}, f32[16,1,448]{2,1,0:T(1,128)}, f32[6,1,16,128]{3,2,1,0:T(8,128)}, f32[6,1,16,128]{3,2,1,0:T(8,128)}, f32[6,...) custom-call(f32[3,6,6]{2,1,0:T(8,128)} %ub_ref.7, f32[3,6,6]{2,1,0:T(8,128)} %lb_ref.7, ...), custom_call_target="tpu_custom_call" | custom-call | tf_op jit(solution)/shard_map/pallas_call | solution.py:253
  4.8 7.3 %all_to_all.30.w_inc = f32[4,1,768]{2,1,0:T(1,128)} all-to-all(f32[4,1,768]{2,1,0:T(1,128)} %get-tuple-element.30), channel_id=1, replica_groups=mesh['chord'=4,'span'=16,'wall'=4] {'wall'}, dimensions={0} | all-to-all | bytes 24576 | tf_op jit(solution)/shard_map/all_to_all | solution.py:221
  12.0 8.7 %all-to-all-start.1 = ((f32[16,1,448]{2,1,0:T(1,128)}), f32[16,1,448]{2,1,0:T(1,128)S(1)}, u32[]{:S(2)}, u32[]{:S(2)}) async-start(f32[16,1,448]{2,1,0:T(1,128)} %get-tuple-element.31), calls=%async_computation.1 | async-start | bytes 65536 | tf_op jit(solution)/shard_map/all_to_all | solution.py:276
  20.7 3.2 %collective-permute-start = (f32[6,1,16,128]{3,2,1,0:T(8,128)}, f32[6,1,16,128]{3,2,1,0:T(8,128)S(1)}, u32[]{:S(2)}, u32[]{:S(2)}) collective-permute-start(f32[6,1,16,128]{3,2,1,0:T(8,128)} %get-tuple-element.26), channel_id=1, source_target_pairs={{0,64},{64,128},{128,192},{1,65},{65,129},{129,193},{2,66},{66,130... | collective-permute-start | bytes 147464 | tf_op jit(solution)/shard_map/ppermute | solution.py:219
  23.9 2.7 %collective-permute-start.1 = (f32[6,1,16,128]{3,2,1,0:T(8,128)S(1)}, f32[6,1,16,128]{3,2,1,0:T(8,128)S(1)}, u32[]{:S(2)}, u32[]{:S(2)}) collective-permute-start(f32[6,1,16,128]{3,2,1,0:T(8,128)S(1)} %copy-done.17), channel_id=1, source_target_pairs={{64,0},{128,64},{192,128},{65,1},{129,65},{193,129},{66,2},{130,66... | collective-permute-start | bytes 147464 | tf_op jit(solution)/shard_map/ppermute | solution.py:220
  26.6 4.6 %collective-permute-start.2 = (f32[6,8,128]{2,1,0:T(8,128)S(1)}, f32[6,8,128]{2,1,0:T(8,128)S(1)}, u32[]{:S(2)}, u32[]{:S(2)}) collective-permute-start(f32[6,8,128]{2,1,0:T(8,128)S(1)} %copy-done.23), channel_id=1, source_target_pairs={{0,4},{4,8},{8,12},{12,16},{16,20},{20,24},{24,28},{28,32},{32,36}... | collective-permute-start | bytes 73736 | tf_op jit(solution)/shard_map/ppermute | solution.py:219
  31.2 1.9 %collective-permute-start.3 = (f32[6,8,128]{2,1,0:T(8,128)S(1)}, f32[6,8,128]{2,1,0:T(8,128)S(1)}, u32[]{:S(2)}, u32[]{:S(2)}) collective-permute-start(f32[6,8,128]{2,1,0:T(8,128)S(1)} %copy-done.22), channel_id=1, source_target_pairs={{4,0},{8,4},{12,8},{16,12},{20,16},{24,20},{28,24},{32,28},{36,32}... | collective-permute-start | bytes 73736 | tf_op jit(solution)/shard_map/ppermute | solution.py:220
  33.1 5.9 %collective-permute-done.3.hsh = f32[6,8,128]{2,1,0:T(8,128)S(1)} collective-permute-done((f32[6,8,128]{2,1,0:T(8,128)S(1)}, f32[6,8,128]{2,1,0:T(8,128)S(1)}, u32[]{:S(2)}, u32[]{:S(2)}) %collective-permute-start.3) | collective-permute-done | bytes 24608 | tf_op jit(solution)/shard_map/ppermute | solution.py:220
  39.7 4.9 %shard_map.123 = (f32[6,8,16,128]{3,2,1,0:T(8,128)}, f32[16,1,384]{2,1,0:T(1,128)}, s32[1,1024]{1,0:T(1,128)}, f32[6,1,16,128]{3,2,1,0:T(8,128)}, f32[6,1,16,128...) custom-call(f32[3,6,6]{2,1,0:T(8,128)} %ub_ref.7, f32[3,6,6]{2,1,0:T(8,128)} %lb_ref.7, ...), custom_call_target="tpu_custom_call" | custom-call | tf_op jit(solution)/shard_map/pallas_call | solution.py:278
  44.5 6.7 %all-to-all-start.2 = ((f32[4,1,768]{2,1,0:T(1,128)}), f32[4,1,768]{2,1,0:T(1,128)S(1)}, u32[]{:S(2)}, u32[]{:S(2)}) async-start(f32[4,1,768]{2,1,0:T(1,128)} %get-tuple-element.37), calls=%async_computation.2 | async-start | bytes 24576 | tf_op jit(solution)/shard_map/all_to_all | solution.py:221
  51.3 3.2 %collective-permute-start.4 = (f32[6,1,16,128]{3,2,1,0:T(8,128)}, f32[6,1,16,128]{3,2,1,0:T(8,128)S(1)}, u32[]{:S(2)}, u32[]{:S(2)}) collective-permute-start(f32[6,1,16,128]{3,2,1,0:T(8,128)} %get-tuple-element.33), channel_id=1, source_target_pairs={{0,64},{64,128},{128,192},{1,65},{65,129},{129,193},{2,66},{66,130... | collective-permute-start | bytes 147464 | tf_op jit(solution)/shard_map/ppermute | solution.py:219
  54.4 2.7 %collective-permute-start.5 = (f32[6,1,16,128]{3,2,1,0:T(8,128)}, f32[6,1,16,128]{3,2,1,0:T(8,128)S(1)}, u32[]{:S(2)}, u32[]{:S(2)}) collective-permute-start(f32[6,1,16,128]{3,2,1,0:T(8,128)} %get-tuple-element.34), channel_id=1, source_target_pairs={{64,0},{128,64},{192,128},{65,1},{129,65},{193,129},{66,2},{130,66... | collective-permute-start | bytes 147464 | tf_op jit(solution)/shard_map/ppermute | solution.py:220
  57.7 6.0 %all-to-all-start.3 = ((f32[16,1,384]{2,1,0:T(1,128)}), f32[16,1,384]{2,1,0:T(1,128)S(1)}, u32[]{:S(2)}, u32[]{:S(2)}) async-start(f32[16,1,384]{2,1,0:T(1,128)} %get-tuple-element.38), calls=%async_computation.3 | async-start | bytes 49152 | tf_op jit(solution)/shard_map/all_to_all | solution.py:276
  63.7 4.6 %collective-permute-start.6 = (f32[6,8,128]{2,1,0:T(8,128)S(1)}, f32[6,8,128]{2,1,0:T(8,128)S(1)}, u32[]{:S(2)}, u32[]{:S(2)}) collective-permute-start(f32[6,8,128]{2,1,0:T(8,128)S(1)} %copy-done.21), channel_id=1, source_target_pairs={{0,4},{4,8},{8,12},{12,16},{16,20},{20,24},{24,28},{28,32},{32,36}... | collective-permute-start | bytes 73736 | tf_op jit(solution)/shard_map/ppermute | solution.py:219
  68.3 1.9 %collective-permute-start.7 = (f32[6,8,128]{2,1,0:T(8,128)S(1)}, f32[6,8,128]{2,1,0:T(8,128)S(1)}, u32[]{:S(2)}, u32[]{:S(2)}) collective-permute-start(f32[6,8,128]{2,1,0:T(8,128)S(1)} %copy-done.19), channel_id=1, source_target_pairs={{4,0},{8,4},{12,8},{16,12},{20,16},{24,20},{28,24},{32,28},{36,32}... | collective-permute-start | bytes 73736 | tf_op jit(solution)/shard_map/ppermute | solution.py:220
  70.3 5.9 %collective-permute-done.7.hsh = f32[6,8,128]{2,1,0:T(8,128)S(1)} collective-permute-done((f32[6,8,128]{2,1,0:T(8,128)S(1)}, f32[6,8,128]{2,1,0:T(8,128)S(1)}, u32[]{:S(2)}, u32[]{:S(2)}) %collective-permute-start.7) | collective-permute-done | bytes 24608 | tf_op jit(solution)/shard_map/ppermute | solution.py:220
  76.8 4.9 %shard_map.124 = (f32[6,8,16,128]{3,2,1,0:T(8,128)}, f32[16,1,384]{2,1,0:T(1,128)}, s32[1,1024]{1,0:T(1,128)}, f32[6,1,16,128]{3,2,1,0:T(8,128)}, f32[6,1,16,128...) custom-call(f32[3,6,6]{2,1,0:T(8,128)} %ub_ref.7, f32[3,6,6]{2,1,0:T(8,128)} %lb_ref.7, ...), custom_call_target="tpu_custom_call" | custom-call | tf_op jit(solution)/shard_map/pallas_call | solution.py:281
  81.7 4.8 %all-to-all-start.4 = ((f32[4,1,768]{2,1,0:T(1,128)}), f32[4,1,768]{2,1,0:T(1,128)S(1)}, u32[]{:S(2)}, u32[]{:S(2)}) async-start(f32[4,1,768]{2,1,0:T(1,128)} %get-tuple-element.45), calls=%async_computation.4 | async-start | bytes 24576 | tf_op jit(solution)/shard_map/all_to_all | solution.py:221
  86.6 3.2 %collective-permute-start.8 = (f32[6,1,16,128]{3,2,1,0:T(8,128)}, f32[6,1,16,128]{3,2,1,0:T(8,128)S(1)}, u32[]{:S(2)}, u32[]{:S(2)}) collective-permute-start(f32[6,1,16,128]{3,2,1,0:T(8,128)} %get-tuple-element.41), channel_id=1, source_target_pairs={{0,64},{64,128},{128,192},{1,65},{65,129},{129,193},{2,66},{66,130... | collective-permute-start | bytes 147464 | tf_op jit(solution)/shard_map/ppermute | solution.py:219
  89.7 2.7 %collective-permute-start.9 = (f32[6,1,16,128]{3,2,1,0:T(8,128)}, f32[6,1,16,128]{3,2,1,0:T(8,128)S(1)}, u32[]{:S(2)}, u32[]{:S(2)}) collective-permute-start(f32[6,1,16,128]{3,2,1,0:T(8,128)} %get-tuple-element.42), channel_id=1, source_target_pairs={{64,0},{128,64},{192,128},{65,1},{129,65},{193,129},{66,2},{130,66... | collective-permute-start | bytes 147464 | tf_op jit(solution)/shard_map/ppermute | solution.py:220
  93.0 6.0 %all-to-all-start.5 = ((f32[16,1,384]{2,1,0:T(1,128)}), f32[16,1,384]{2,1,0:T(1,128)S(1)}, u32[]{:S(2)}, u32[]{:S(2)}) async-start(f32[16,1,384]{2,1,0:T(1,128)} %get-tuple-element.46), calls=%async_computation.5 | async-start | bytes 49152 | tf_op jit(solution)/shard_map/all_to_all | solution.py:276
  99.0 4.6 %collective-permute-start.10 = (f32[6,8,128]{2,1,0:T(8,128)S(1)}, f32[6,8,128]{2,1,0:T(8,128)S(1)}, u32[]{:S(2)}, u32[]{:S(2)}) collective-permute-start(f32[6,8,128]{2,1,0:T(8,128)S(1)} %copy-done.20), channel_id=1, source_target_pairs={{0,4},{4,8},{8,12},{12,16},{16,20},{20,24},{24,28},{28,32},{32,36}... | collective-permute-start | bytes 73736 | tf_op jit(solution)/shard_map/ppermute | solution.py:219
  105.6 5.9 %collective-permute-done.11.hsh = f32[6,8,128]{2,1,0:T(8,128)S(1)} collective-permute-done((f32[6,8,128]{2,1,0:T(8,128)S(1)}, f32[6,8,128]{2,1,0:T(8,128)S(1)}, u32[]{:S(2)}, u32[]{:S(2)}) %collective-permute-start.11) | collective-permute-done | bytes 24608 | tf_op jit(solution)/shard_map/ppermute | solution.py:220
  112.1 4.2 %shard_map.125 = (f32[6,8,16,128]{3,2,1,0:T(8,128)}, f32[8,16,128]{2,1,0:T(8,128)}) custom-call(f32[3,6,6]{2,1,0:T(8,128)} %ub_ref.7, f32[3,6,6]{2,1,0:T(8,128)} %lb_ref.7, f32[2,6,6]{2,1,0:T(8,128)} %copy.16.ib_ref, s32[1]{0:T(128)} %bitcast.wall_me, f32[6,8,16,128]{3,2,1,0:T(8,128)} %get-tuple-element.40.adj_ref, f32[6,8,16,128]{3,2,1,0:T(8,128)} %sens_ref.7, ...), custom_call_target="tpu_custom_call" | custom-call | tf_op jit(solution)/shard_map/pallas_call | solution.py:284
  (64 shorter events, 6.2 us)
Async XLA Ops:
  4.8 19.2 %copy-start.17 = (f32[6,1,16,128]{3,2,1,0:T(8,128)S(1)}, f32[6,1,16,128]{3,2,1,0:T(8,128)}, u32[]{:S(2)}) copy-start(f32[6,1,16,128]{3,2,1,0:T(8,128)} %get-tuple-element.27) | copy-start | bytes 147460
  12.0 14.6 %copy-start.23 = (f32[6,8,128]{2,1,0:T(8,128)S(1)}, f32[6,8,128]{2,1,0:T(8,128)}, u32[]{:S(2)}) copy-start(f32[6,8,128]{2,1,0:T(8,128)} %get-tuple-element.28) | copy-start | bytes 73732
  12.0 19.2 %copy-start.22 = (f32[6,8,128]{2,1,0:T(8,128)S(1)}, f32[6,8,128]{2,1,0:T(8,128)}, u32[]{:S(2)}) copy-start(f32[6,8,128]{2,1,0:T(8,128)} %get-tuple-element.29) | copy-start | bytes 73732
  12.0 27.0 %all-to-all-start.1 = ((f32[16,1,448]{2,1,0:T(1,128)}), f32[16,1,448]{2,1,0:T(1,128)S(1)}, u32[]{:S(2)}, u32[]{:S(2)}) async-start(f32[16,1,448]{2,1,0:T(1,128)} %get-tuple-element.31), calls=%async_computation.1 | async-start | bytes 65536 | tf_op jit(solution)/shard_map/all_to_all | solution.py:276
  20.7 18.3 %collective-permute-start = (f32[6,1,16,128]{3,2,1,0:T(8,128)}, f32[6,1,16,128]{3,2,1,0:T(8,128)S(1)}, u32[]{:S(2)}, u32[]{:S(2)}) collective-permute-start(f32[6,1,16,128]{3,2,1,0:T(8,128)} %get-tuple-element.26), channel_id=1, source_target_pairs={{0,64},{64,128},{128,192},{1,65},{65,129},{129,193},{2,66},{66,130... | collective-permute-start | bytes 147464 | tf_op jit(solution)/shard_map/ppermute | solution.py:219
  23.9 15.1 %collective-permute-start.1 = (f32[6,1,16,128]{3,2,1,0:T(8,128)S(1)}, f32[6,1,16,128]{3,2,1,0:T(8,128)S(1)}, u32[]{:S(2)}, u32[]{:S(2)}) collective-permute-start(f32[6,1,16,128]{3,2,1,0:T(8,128)S(1)} %copy-done.17), channel_id=1, source_target_pairs={{64,0},{128,64},{192,128},{65,1},{129,65},{193,129},{66,2},{130,66... | collective-permute-start | bytes 147464 | tf_op jit(solution)/shard_map/ppermute | solution.py:220
  26.6 6.5 %collective-permute-start.2 = (f32[6,8,128]{2,1,0:T(8,128)S(1)}, f32[6,8,128]{2,1,0:T(8,128)S(1)}, u32[]{:S(2)}, u32[]{:S(2)}) collective-permute-start(f32[6,8,128]{2,1,0:T(8,128)S(1)} %copy-done.23), channel_id=1, source_target_pairs={{0,4},{4,8},{8,12},{12,16},{16,20},{20,24},{24,28},{28,32},{32,36}... | collective-permute-start | bytes 73736 | tf_op jit(solution)/shard_map/ppermute | solution.py:219
  31.2 7.8 %collective-permute-start.3 = (f32[6,8,128]{2,1,0:T(8,128)S(1)}, f32[6,8,128]{2,1,0:T(8,128)S(1)}, u32[]{:S(2)}, u32[]{:S(2)}) collective-permute-start(f32[6,8,128]{2,1,0:T(8,128)S(1)} %copy-done.22), channel_id=1, source_target_pairs={{4,0},{8,4},{12,8},{16,12},{20,16},{24,20},{28,24},{32,28},{36,32}... | collective-permute-start | bytes 73736 | tf_op jit(solution)/shard_map/ppermute | solution.py:220
  44.5 12.6 %all-to-all-start.2 = ((f32[4,1,768]{2,1,0:T(1,128)}), f32[4,1,768]{2,1,0:T(1,128)S(1)}, u32[]{:S(2)}, u32[]{:S(2)}) async-start(f32[4,1,768]{2,1,0:T(1,128)} %get-tuple-element.37), calls=%async_computation.2 | async-start | bytes 24576 | tf_op jit(solution)/shard_map/all_to_all | solution.py:221
  51.3 24.9 %collective-permute-start.4 = (f32[6,1,16,128]{3,2,1,0:T(8,128)}, f32[6,1,16,128]{3,2,1,0:T(8,128)S(1)}, u32[]{:S(2)}, u32[]{:S(2)}) collective-permute-start(f32[6,1,16,128]{3,2,1,0:T(8,128)} %get-tuple-element.33), channel_id=1, source_target_pairs={{0,64},{64,128},{128,192},{1,65},{65,129},{129,193},{2,66},{66,130... | collective-permute-start | bytes 147464 | tf_op jit(solution)/shard_map/ppermute | solution.py:219
  54.4 21.7 %collective-permute-start.5 = (f32[6,1,16,128]{3,2,1,0:T(8,128)}, f32[6,1,16,128]{3,2,1,0:T(8,128)S(1)}, u32[]{:S(2)}, u32[]{:S(2)}) collective-permute-start(f32[6,1,16,128]{3,2,1,0:T(8,128)} %get-tuple-element.34), channel_id=1, source_target_pairs={{64,0},{128,64},{192,128},{65,1},{129,65},{193,129},{66,2},{130,66... | collective-permute-start | bytes 147464 | tf_op jit(solution)/shard_map/ppermute | solution.py:220
  57.1 6.6 %copy-start.21 = (f32[6,8,128]{2,1,0:T(8,128)S(1)}, f32[6,8,128]{2,1,0:T(8,128)}, u32[]{:S(2)}) copy-start(f32[6,8,128]{2,1,0:T(8,128)} %get-tuple-element.35) | copy-start | bytes 73732
  57.1 11.2 %copy-start.19 = (f32[6,8,128]{2,1,0:T(8,128)S(1)}, f32[6,8,128]{2,1,0:T(8,128)}, u32[]{:S(2)}) copy-start(f32[6,8,128]{2,1,0:T(8,128)} %get-tuple-element.36) | copy-start | bytes 73732
  57.7 18.5 %all-to-all-start.3 = ((f32[16,1,384]{2,1,0:T(1,128)}), f32[16,1,384]{2,1,0:T(1,128)S(1)}, u32[]{:S(2)}, u32[]{:S(2)}) async-start(f32[16,1,384]{2,1,0:T(1,128)} %get-tuple-element.38), calls=%async_computation.3 | async-start | bytes 49152 | tf_op jit(solution)/shard_map/all_to_all | solution.py:276
  63.7 6.5 %collective-permute-start.6 = (f32[6,8,128]{2,1,0:T(8,128)S(1)}, f32[6,8,128]{2,1,0:T(8,128)S(1)}, u32[]{:S(2)}, u32[]{:S(2)}) collective-permute-start(f32[6,8,128]{2,1,0:T(8,128)S(1)} %copy-done.21), channel_id=1, source_target_pairs={{0,4},{4,8},{8,12},{12,16},{16,20},{20,24},{24,28},{28,32},{32,36}... | collective-permute-start | bytes 73736 | tf_op jit(solution)/shard_map/ppermute | solution.py:219
  68.3 7.8 %collective-permute-start.7 = (f32[6,8,128]{2,1,0:T(8,128)S(1)}, f32[6,8,128]{2,1,0:T(8,128)S(1)}, u32[]{:S(2)}, u32[]{:S(2)}) collective-permute-start(f32[6,8,128]{2,1,0:T(8,128)S(1)} %copy-done.19), channel_id=1, source_target_pairs={{4,0},{8,4},{12,8},{16,12},{20,16},{24,20},{28,24},{32,28},{36,32}... | collective-permute-start | bytes 73736 | tf_op jit(solution)/shard_map/ppermute | solution.py:220
  81.7 10.7 %all-to-all-start.4 = ((f32[4,1,768]{2,1,0:T(1,128)}), f32[4,1,768]{2,1,0:T(1,128)S(1)}, u32[]{:S(2)}, u32[]{:S(2)}) async-start(f32[4,1,768]{2,1,0:T(1,128)} %get-tuple-element.45), calls=%async_computation.4 | async-start | bytes 24576 | tf_op jit(solution)/shard_map/all_to_all | solution.py:221
  86.6 24.9 %collective-permute-start.8 = (f32[6,1,16,128]{3,2,1,0:T(8,128)}, f32[6,1,16,128]{3,2,1,0:T(8,128)S(1)}, u32[]{:S(2)}, u32[]{:S(2)}) collective-permute-start(f32[6,1,16,128]{3,2,1,0:T(8,128)} %get-tuple-element.41), channel_id=1, source_target_pairs={{0,64},{64,128},{128,192},{1,65},{65,129},{129,193},{2,66},{66,130... | collective-permute-start | bytes 147464 | tf_op jit(solution)/shard_map/ppermute | solution.py:219
  89.7 21.8 %collective-permute-start.9 = (f32[6,1,16,128]{3,2,1,0:T(8,128)}, f32[6,1,16,128]{3,2,1,0:T(8,128)S(1)}, u32[]{:S(2)}, u32[]{:S(2)}) collective-permute-start(f32[6,1,16,128]{3,2,1,0:T(8,128)} %get-tuple-element.42), channel_id=1, source_target_pairs={{64,0},{128,64},{192,128},{65,1},{129,65},{193,129},{66,2},{130,66... | collective-permute-start | bytes 147464 | tf_op jit(solution)/shard_map/ppermute | solution.py:220
  92.4 6.6 %copy-start.20 = (f32[6,8,128]{2,1,0:T(8,128)S(1)}, f32[6,8,128]{2,1,0:T(8,128)}, u32[]{:S(2)}) copy-start(f32[6,8,128]{2,1,0:T(8,128)} %get-tuple-element.43) | copy-start | bytes 73732
  92.4 11.2 %copy-start.18 = (f32[6,8,128]{2,1,0:T(8,128)S(1)}, f32[6,8,128]{2,1,0:T(8,128)}, u32[]{:S(2)}) copy-start(f32[6,8,128]{2,1,0:T(8,128)} %get-tuple-element.44) | copy-start | bytes 73732
  93.0 18.5 %all-to-all-start.5 = ((f32[16,1,384]{2,1,0:T(1,128)}), f32[16,1,384]{2,1,0:T(1,128)S(1)}, u32[]{:S(2)}, u32[]{:S(2)}) async-start(f32[16,1,384]{2,1,0:T(1,128)} %get-tuple-element.46), calls=%async_computation.5 | async-start | bytes 49152 | tf_op jit(solution)/shard_map/all_to_all | solution.py:276
  99.0 6.5 %collective-permute-start.10 = (f32[6,8,128]{2,1,0:T(8,128)S(1)}, f32[6,8,128]{2,1,0:T(8,128)S(1)}, u32[]{:S(2)}, u32[]{:S(2)}) collective-permute-start(f32[6,8,128]{2,1,0:T(8,128)S(1)} %copy-done.20), channel_id=1, source_target_pairs={{0,4},{4,8},{8,12},{12,16},{16,20},{20,24},{24,28},{28,32},{32,36}... | collective-permute-start | bytes 73736 | tf_op jit(solution)/shard_map/ppermute | solution.py:219
  103.6 7.8 %collective-permute-start.11 = (f32[6,8,128]{2,1,0:T(8,128)S(1)}, f32[6,8,128]{2,1,0:T(8,128)S(1)}, u32[]{:S(2)}, u32[]{:S(2)}) collective-permute-start(f32[6,8,128]{2,1,0:T(8,128)S(1)} %copy-done.18), channel_id=1, source_target_pairs={{4,0},{8,4},{12,8},{16,12},{20,16},{24,20},{28,24},{32,28},{36,32}... | collective-permute-start | bytes 73736 | tf_op jit(solution)/shard_map/ppermute | solution.py:220
  (17 other events, 26.4 us)

commit v9 on v8

--- a/solution.py
+++ b/solution.py
@@ -159,46 +159,63 @@
     return jnp.stack(new, axis=0)
 
 
-def sweep_kernel(ub_ref, lb_ref, ib_ref, wall_me, adj_ref, sens_ref, diag_ref, face_ref, hcl, hch, hsl, hsh, w_inc,
-                 inc_ref, tgt_ref, send_ref, orient_ref, weight_ref,
-                 out_ref, rows_ref, tgt_out, c_lo, c_hi, s_lo, s_hi, w_buf):
-    n_var = adj_ref.shape[0]
-    lanes = adj_ref.shape[3]
-    slots = send_ref.shape[1]
-    blk_ref = (ub_ref, lb_ref, ib_ref)
-    halos = (hcl[...], hch[...], hsl[...], hsh[...]) + wall_halos(w_inc[...], wall_me, n_var)
-    inc = inc_ref[...]
-    if tgt_ref is None:
-        got = from_chunks(inc, n_var + 1, slots)
-        cell = got[n_var].astype(jnp.int32)
-    else:
-        got = from_chunks(inc, n_var, slots)
-        cell = tgt_ref[...]
-    tgt_out[...] = cell
-    new = sweep_body(blk_ref, adj_ref[...], sens_ref[...], diag_ref[...], face_ref[...], halos,
-                     jnp.concatenate(got[:n_var], axis=0), cell)
-    out_ref[...] = new
-    write_faces(new, (c_lo, c_hi, s_lo, s_hi, w_buf, wall_me))
-    to_chunks(rows_ref, gather_rows(new, send_ref, orient_ref, weight_ref, blk_ref, n_var, lanes), slots)
-
-
-def first_sweep_kernel(ub_ref, lb_ref, ib_ref, wall_me, adj_ref, sens_ref, diag_ref, face_ref, hcl, hch, hsl, hsh,
-                       w_inc, inc_ref, send_ref, orient_ref, weight_ref, *outs):
-    sweep_kernel(ub_ref, lb_ref, ib_ref, wall_me, adj_ref, sens_ref, diag_ref, face_ref, hcl, hch, hsl, hsh, w_inc,
-                 inc_ref, None, send_ref, orient_ref, weight_ref, *outs)
-
-
-def last_kernel(ub_ref, lb_ref, ib_ref, wall_me, adj_ref, sens_ref, diag_ref, face_ref, hcl, hch, hsl, hsh, w_inc,
-                inc_ref, tgt_ref, prod_ref, out_ref, grad_ref):
-    n_var = adj_ref.shape[0]
-    slots = inc_ref.shape[2] // n_var
-    blk_ref = (ub_ref, lb_ref, ib_ref)
-    halos = (hcl[...], hch[...], hsl[...], hsh[...]) + wall_halos(w_inc[...], wall_me, n_var)
-    got = from_chunks(inc_ref[...], n_var, slots)
-    new = sweep_body(blk_ref, adj_ref[...], sens_ref[...], diag_ref[...], face_ref[...], halos,
-                     jnp.concatenate(got, axis=0), tgt_ref[...])
-    out_ref[...] = new
-    grad_ref[...] = prod_ref[...] * new[n_var - 1]
+def make_part_a(first, slots):
+    def kernel(ub_ref, lb_ref, ib_ref, wall_me, adj_ref, sens_ref, diag_ref, face_ref, hcl, hch, w_inc,
+               inc_ref, *rest):
+        if first:
+            out_ref, tgt_out = rest
+        else:
+            tgt_ref, out_ref = rest
+        n_var, nx, ny, nz = adj_ref.shape
+        blk_ref = (ub_ref, lb_ref, ib_ref)
+        inc = inc_ref[...]
+        if first:
+            got = from_chunks(inc, n_var + 1, slots)
+            cell = got[n_var].astype(jnp.int32)
+            tgt_out[...] = cell
+        else:
+            got = from_chunks(inc, n_var, slots)
+            cell = tgt_ref[...]
+        none = jnp.zeros((n_var, nx, nz), F32)
+        halos = (hcl[...], hch[...], none, none) + wall_halos(w_inc[...], wall_me, n_var)
+        out_ref[...] = sweep_body(blk_ref, adj_ref[...], sens_ref[...], diag_ref[...], face_ref[...], halos,
+                                  jnp.concatenate(got[:n_var], axis=0), cell)
+    return kernel
+
+
+def make_part_b(last, slots):
+    def kernel(ub_ref, lb_ref, ib_ref, part_ref, diag_ref, face_ref, hsl, hsh, *rest):
+        n_var, nx, ny, nz = part_ref.shape
+        part = part_ref[...]
+        diag = diag_ref[...]
+        face_y = face_ref[1]
+        h_lo = hsl[...]
+        h_hi = hsh[...]
+        j_idx = lax.broadcasted_iota(jnp.int32, (nx, ny, nz), 1)
+        new = []
+        for i in range(n_var):
+            above = None
+            below = None
+            for j in range(n_var):
+                a = ub_ref[1, j, i] * h_hi[j]
+                b = lb_ref[1, j, i] * h_lo[j]
+                above = a if above is None else above + a
+                below = b if below is None else below + b
+            edge = (jnp.where(j_idx == ny - 1, above[:, None, :], 0.0)
+                    + jnp.where(j_idx == 0, below[:, None, :], 0.0))
+            new.append(part[i] - face_y * edge / diag[i])
+        new = jnp.stack(new, axis=0)
+        if last:
+            prod_ref, out_ref, grad_ref = rest
+            out_ref[...] = new
+            grad_ref[...] = prod_ref[...] * new[n_var - 1]
+        else:
+            send_ref, orient_ref, weight_ref, wall_me, out_ref, rows_ref, c_lo, c_hi, s_lo, s_hi, w_buf = rest
+            out_ref[...] = new
+            write_faces(new, (c_lo, c_hi, s_lo, s_hi, w_buf, wall_me))
+            blk_ref = (ub_ref, lb_ref, ib_ref)
+            to_chunks(rows_ref, gather_rows(new, send_ref, orient_ref, weight_ref, blk_ref, n_var, nz), slots)
+    return kernel
 
 
 def face_shapes(shape, n_wall):
@@ -252,37 +269,44 @@
     )
     adj, rows, *faces = init(*blk, sensitivity, diagonal, send_row, orient_row, weight_row, target_row)
 
-    first = pl.pallas_call(
-        first_sweep_kernel,
-        out_shape=[adj_sds, rows_sds, tgt_sds] + face_shapes(shape, n_wall),
-        in_specs=[smem] * 4 + [vmem] * 13,
-        out_specs=[vmem] * 8,
-    )
-    step = pl.pallas_call(
-        sweep_kernel,
-        out_shape=[adj_sds, rows_sds, tgt_sds] + face_shapes(shape, n_wall),
-        in_specs=[smem] * 4 + [vmem] * 14,
-        out_specs=[vmem] * 8,
-    )
-    last = pl.pallas_call(
-        last_kernel,
+    part_a_first = pl.pallas_call(
+        make_part_a(True, slots),
+        out_shape=[adj_sds, tgt_sds],
+        in_specs=[smem] * 4 + [vmem] * 8,
+        out_specs=[vmem] * 2,
+    )
+    part_a = pl.pallas_call(
+        make_part_a(False, slots),
+        out_shape=adj_sds,
+        in_specs=[smem] * 4 + [vmem] * 9,
+        out_specs=vmem,
+    )
+    part_b = pl.pallas_call(
+        make_part_b(False, slots),
+        out_shape=[adj_sds, rows_sds] + face_shapes(shape, n_wall),
+        in_specs=[smem] * 3 + [vmem] * 8 + [smem],
+        out_specs=[vmem] * 7,
+    )
+    part_b_last = pl.pallas_call(
+        make_part_b(True, slots),
         out_shape=[adj_sds, jax.ShapeDtypeStruct(production.shape, F32)],
-        in_specs=[smem] * 4 + [vmem] * 12,
+        in_specs=[smem] * 3 + [vmem] * 6,
         out_specs=[vmem] * 2,
     )
+    ub, lb, ib, _ = blk
     received = None
     for sweep in range(SWEEPS):
-        halos = exchange(faces)
+        hcl, hch, hsl, hsh, w_inc = exchange(faces)
         incoming = lax.all_to_all(rows, "span", split_axis=0, concat_axis=0, tiled=True)
         if sweep == 0:
-            adj, rows, received, *faces = first(*blk, adj, sensitivity, diagonal, face_coef, *halos,
-                                                incoming, send_row, orient_row, weight_row)
-        elif sweep < SWEEPS - 1:
-            adj, rows, received, *faces = step(*blk, adj, sensitivity, diagonal, face_coef, *halos,
-                                               incoming, received, send_row, orient_row, weight_row)
-        else:
-            adj, gradient = last(*blk, adj, sensitivity, diagonal, face_coef, *halos, incoming,
-                                 received, production)
+            partial, received = part_a_first(*blk, adj, sensitivity, diagonal, face_coef, hcl, hch, w_inc, incoming)
+        else:
+            partial = part_a(*blk, adj, sensitivity, diagonal, face_coef, hcl, hch, w_inc, incoming, received)
+        if sweep < SWEEPS - 1:
+            adj, rows, *faces = part_b(ub, lb, ib, partial, diagonal, face_coef, hsl, hsh,
+                                       send_row, orient_row, weight_row, wall_me)
+        else:
+            adj, gradient = part_b_last(ub, lb, ib, partial, diagonal, face_coef, hsl, hsh, production)
     return (adj, gradient)
 
 

time: 117 us -> 117 us (level)
  the two profiles are of different devices: /device:TPU:118 before, /device:TPU:12 now
where the time goes in v9:
time: 117 us; the launch traced here: 116 us
  starting transfers between devices  70.2 us (60%)
  Pallas kernels  23.4 us (20%)
  local copies, waits for them, and re-layouts  7.3 us (6%)
  waiting for transfers between devices  6.94 us (6%)
  blocking collectives  6.86 us (6%)
    all_to_all x3, starting transfers between devices, local(): lax.all_to_all(rows, 'span', split_axis=0, concat_axis=0, tiled=True)  26.5 us
    ppermute x6, starting transfers between devices, exchange(): out.append(lax.ppermute(hi_face, axis, forward))  21.9 us
    ppermute x6, starting transfers between devices, exchange(): out.append(lax.ppermute(lo_face, axis, backward))  10.9 us
    all_to_all x2, starting transfers between devices, exchange(): lax.all_to_all(w_buf, 'wall', split_axis=0, concat_axis=0, tiled=True)  10.9 us
    pallas_call x2, Pallas kernels, local(): part_a(*blk, adj, sensitivity, diagonal, face_coef, hcl, hch, w_inc, inco...  8.24 us
    unnamed x49, local copies, waits for them, and re-layouts  7.3 us
    all_to_all x3, waiting for transfers between devices, local(): lax.all_to_all(rows, 'span', split_axis=0, concat_axis=0, tiled=True)  6.9 us
    all_to_all x1, blocking collectives, exchange(): lax.all_to_all(w_buf, 'wall', split_axis=0, concat_axis=0, tiled=True)  6.86 us
  transfers between devices with their start and end apart: 17, of which 2 were waited for; matrix products, arithmetic and copies ran while one was open for 0% of the time, Pallas kernels for 11%

profile of v9, /device:TPU:12, one launch (start us, length us, event | category | flops | bytes accessed | tf_op | source)
XLA Modules:
  0.0 115.7 jit_solution(15440246661248829327)
XLA Ops:
  1.9 2.8 %shard_map.122 = (f32[6,8,16,128]{3,2,1,0:T(8,128)}, f32[16,1,448]{2,1,0:T(1,128)}, f32[6,1,16,128]{3,2,1,0:T(8,128)}, f32[6,1,16,128]{3,2,1,0:T(8,128)}, f32[6,...) custom-call(f32[3,6,6]{2,1,0:T(8,128)} %ub_ref.13, f32[3,6,6]{2,1,0:T(8,128)} %lb_ref.13, ...), custom_call_target="tpu_custom_call" | custom-call | tf_op jit(solution)/shard_map/pallas_call | solution.py:270
  4.8 6.9 %all_to_all.30.w_inc = f32[4,1,768]{2,1,0:T(1,128)} all-to-all(f32[4,1,768]{2,1,0:T(1,128)} %get-tuple-element.28), channel_id=1, replica_groups=mesh['chord'=4,'span'=16,'wall'=4] {'wall'}, dimensions={0} | all-to-all | bytes 24576 | tf_op jit(solution)/shard_map/all_to_all | solution.py:238
  11.6 9.8 %all-to-all-start.1 = ((f32[16,1,448]{2,1,0:T(1,128)}), f32[16,1,448]{2,1,0:T(1,128)S(1)}, u32[]{:S(2)}, u32[]{:S(2)}) async-start(f32[16,1,448]{2,1,0:T(1,128)} %get-tuple-element.29), calls=%async_computation.1 | async-start | bytes 65536 | tf_op jit(solution)/shard_map/all_to_all | solution.py:300
  21.4 3.5 %collective-permute-start = (f32[6,1,16,128]{3,2,1,0:T(8,128)}, f32[6,1,16,128]{3,2,1,0:T(8,128)S(1)}, u32[]{:S(2)}, u32[]{:S(2)}) collective-permute-start(f32[6,1,16,128]{3,2,1,0:T(8,128)} %get-tuple-element.26), channel_id=1, source_target_pairs={{0,64},{64,128},{128,192},{1,65},{65,129},{129,193},{2,66},{66,130... | collective-permute-start | bytes 147464 | tf_op jit(solution)/shard_map/ppermute | solution.py:236
  24.9 2.4 %collective-permute-start.1 = (f32[6,1,16,128]{3,2,1,0:T(8,128)S(1)}, f32[6,1,16,128]{3,2,1,0:T(8,128)S(1)}, u32[]{:S(2)}, u32[]{:S(2)}) collective-permute-start(f32[6,1,16,128]{3,2,1,0:T(8,128)S(1)} %copy-done.17), channel_id=1, source_target_pairs={{64,0},{128,64},{192,128},{65,1},{129,65},{193,129},{66,2},{130,66... | collective-permute-start | bytes 147464 | tf_op jit(solution)/shard_map/ppermute | solution.py:237
  27.3 3.8 %collective-permute-start.2 = (f32[6,8,128]{2,1,0:T(8,128)S(1)}, f32[6,8,128]{2,1,0:T(8,128)S(1)}, u32[]{:S(2)}, u32[]{:S(2)}) collective-permute-start(f32[6,8,128]{2,1,0:T(8,128)S(1)} %copy-done.23), channel_id=1, source_target_pairs={{0,4},{4,8},{8,12},{12,16},{16,20},{20,24},{24,28},{28,32},{32,36}... | collective-permute-start | bytes 73736 | tf_op jit(solution)/shard_map/ppermute | solution.py:236
  33.1 4.1 %shard_map.123 = (f32[6,8,16,128]{3,2,1,0:T(8,128)}, s32[1,1024]{1,0:T(1,128)}) custom-call(f32[3,6,6]{2,1,0:T(8,128)} %ub_ref.13, f32[3,6,6]{2,1,0:T(8,128)} %lb_ref.13, f32[2,6,6]{2,1,0:T(8,128)} %copy.19.ib_ref, s32[1]{0:T(128)} %bitcast.wall_me.rest_3_, f32[6,8,16,128]{3,2,1,0:T(8,128)} %get-tuple-element.25.adj_ref, f32[6,8,16,128]{3,2,1,0:T(8,128)} %sens_ref.7, ...), custom_call_target="tpu_custom_call" | custom-call | tf_op jit(solution)/shard_map/pallas_call | solution.py:302
  37.9 3.0 %shard_map.124 = (f32[6,8,16,128]{3,2,1,0:T(8,128)}, f32[16,1,384]{2,1,0:T(1,128)}, f32[6,1,16,128]{3,2,1,0:T(8,128)}, f32[6,1,16,128]{3,2,1,0:T(8,128)}, f32[6,...) custom-call(f32[3,6,6]{2,1,0:T(8,128)} %ub_ref.13, f32[3,6,6]{2,1,0:T(8,128)} %lb_ref.13, ...), custom_call_target="tpu_custom_call" | custom-call | tf_op jit(solution)/shard_map/pallas_call | solution.py:306
  40.9 6.1 %all-to-all-start.2 = ((f32[4,1,768]{2,1,0:T(1,128)}), f32[4,1,768]{2,1,0:T(1,128)S(1)}, u32[]{:S(2)}, u32[]{:S(2)}) async-start(f32[4,1,768]{2,1,0:T(1,128)} %get-tuple-element.36), calls=%async_computation.2 | async-start | bytes 24576 | tf_op jit(solution)/shard_map/all_to_all | solution.py:238
  47.0 3.5 %collective-permute-start.4 = (f32[6,1,16,128]{3,2,1,0:T(8,128)}, f32[6,1,16,128]{3,2,1,0:T(8,128)S(1)}, u32[]{:S(2)}, u32[]{:S(2)}) collective-permute-start(f32[6,1,16,128]{3,2,1,0:T(8,128)} %get-tuple-element.34), channel_id=1, source_target_pairs={{0,64},{64,128},{128,192},{1,65},{65,129},{129,193},{2,66},{66,130... | collective-permute-start | bytes 147464 | tf_op jit(solution)/shard_map/ppermute | solution.py:236
  50.4 2.4 %collective-permute-start.5 = (f32[6,1,16,128]{3,2,1,0:T(8,128)}, f32[6,1,16,128]{3,2,1,0:T(8,128)S(1)}, u32[]{:S(2)}, u32[]{:S(2)}) collective-permute-start(f32[6,1,16,128]{3,2,1,0:T(8,128)} %get-tuple-element.35), channel_id=1, source_target_pairs={{64,0},{128,64},{192,128},{65,1},{129,65},{193,129},{66,2},{130,66... | collective-permute-start | bytes 147464 | tf_op jit(solution)/shard_map/ppermute | solution.py:237
  53.4 10.0 %all-to-all-start.3 = ((f32[16,1,384]{2,1,0:T(1,128)}), f32[16,1,384]{2,1,0:T(1,128)S(1)}, u32[]{:S(2)}, u32[]{:S(2)}) async-start(f32[16,1,384]{2,1,0:T(1,128)} %get-tuple-element.37), calls=%async_computation.3 | async-start | bytes 49152 | tf_op jit(solution)/shard_map/all_to_all | solution.py:300
  63.5 3.8 %collective-permute-start.6 = (f32[6,8,128]{2,1,0:T(8,128)S(1)}, f32[6,8,128]{2,1,0:T(8,128)S(1)}, u32[]{:S(2)}, u32[]{:S(2)}) collective-permute-start(f32[6,8,128]{2,1,0:T(8,128)S(1)} %copy-done.21), channel_id=1, source_target_pairs={{0,4},{4,8},{8,12},{12,16},{16,20},{20,24},{24,28},{28,32},{32,36}... | collective-permute-start | bytes 73736 | tf_op jit(solution)/shard_map/ppermute | solution.py:236
  68.6 3.4 %all-to-all-done.3.inc_ref = f32[16,1,384]{2,1,0:T(1,128)S(1)} async-done(((f32[16,1,384]{2,1,0:T(1,128)}), f32[16,1,384]{2,1,0:T(1,128)S(1)}, u32[]{:S(2)}, u32[]{:S(2)}) %all-to-all-start.3) | async-done | bytes 24608 | tf_op jit(solution)/shard_map/all_to_all | solution.py:300
  72.7 4.1 %shard_map.125.part_ref = f32[6,8,16,128]{3,2,1,0:T(8,128)} custom-call(f32[3,6,6]{2,1,0:T(8,128)} %ub_ref.13, f32[3,6,6]{2,1,0:T(8,128)} %lb_ref.13, f32[2,6,6]{2,1,0:T(8,128)} %copy.19.ib_ref, s32[1]{0:T(128)} %bitcast.wall_me.rest_3_, f32[6,8,16,128]{3,2,1,0:T(8,128)} %get-tuple-element.33.adj_ref, f32[6,8,16,128]{3,2,1,0:T(8,128)} %sens_ref.7, ...), custom_call_target="tpu_custom_call" | custom-call | tf_op jit(solution)/shard_map/pallas_call | solution.py:304
  78.1 3.0 %shard_map.126 = (f32[6,8,16,128]{3,2,1,0:T(8,128)}, f32[16,1,384]{2,1,0:T(1,128)}, f32[6,1,16,128]{3,2,1,0:T(8,128)}, f32[6,1,16,128]{3,2,1,0:T(8,128)}, f32[6,...) custom-call(f32[3,6,6]{2,1,0:T(8,128)} %ub_ref.13, f32[3,6,6]{2,1,0:T(8,128)} %lb_ref.13, ...), custom_call_target="tpu_custom_call" | custom-call | tf_op jit(solution)/shard_map/pallas_call | solution.py:306
  81.0 4.8 %all-to-all-start.4 = ((f32[4,1,768]{2,1,0:T(1,128)}), f32[4,1,768]{2,1,0:T(1,128)S(1)}, u32[]{:S(2)}, u32[]{:S(2)}) async-start(f32[4,1,768]{2,1,0:T(1,128)} %get-tuple-element.44), calls=%async_computation.4 | async-start | bytes 24576 | tf_op jit(solution)/shard_map/all_to_all | solution.py:238
  85.9 3.5 %collective-permute-start.8 = (f32[6,1,16,128]{3,2,1,0:T(8,128)}, f32[6,1,16,128]{3,2,1,0:T(8,128)S(1)}, u32[]{:S(2)}, u32[]{:S(2)}) collective-permute-start(f32[6,1,16,128]{3,2,1,0:T(8,128)} %get-tuple-element.42), channel_id=1, source_target_pairs={{0,64},{64,128},{128,192},{1,65},{65,129},{129,193},{2,66},{66,130... | collective-permute-start | bytes 147464 | tf_op jit(solution)/shard_map/ppermute | solution.py:236
  89.3 2.3 %collective-permute-start.9 = (f32[6,1,16,128]{3,2,1,0:T(8,128)}, f32[6,1,16,128]{3,2,1,0:T(8,128)S(1)}, u32[]{:S(2)}, u32[]{:S(2)}) collective-permute-start(f32[6,1,16,128]{3,2,1,0:T(8,128)} %get-tuple-element.43), channel_id=1, source_target_pairs={{64,0},{128,64},{192,128},{65,1},{129,65},{193,129},{66,2},{130,66... | collective-permute-start | bytes 147464 | tf_op jit(solution)/shard_map/ppermute | solution.py:237
  92.3 6.6 %all-to-all-start.5 = ((f32[16,1,384]{2,1,0:T(1,128)}), f32[16,1,384]{2,1,0:T(1,128)S(1)}, u32[]{:S(2)}, u32[]{:S(2)}) async-start(f32[16,1,384]{2,1,0:T(1,128)} %get-tuple-element.45), calls=%async_computation.5 | async-start | bytes 49152 | tf_op jit(solution)/shard_map/all_to_all | solution.py:300
  99.0 3.8 %collective-permute-start.10 = (f32[6,8,128]{2,1,0:T(8,128)S(1)}, f32[6,8,128]{2,1,0:T(8,128)S(1)}, u32[]{:S(2)}, u32[]{:S(2)}) collective-permute-start(f32[6,8,128]{2,1,0:T(8,128)S(1)} %copy-done.20), channel_id=1, source_target_pairs={{0,4},{4,8},{8,12},{12,16},{16,20},{20,24},{24,28},{28,32},{32,36}... | collective-permute-start | bytes 73736 | tf_op jit(solution)/shard_map/ppermute | solution.py:236
  104.1 3.4 %all-to-all-done.5.inc_ref = f32[16,1,384]{2,1,0:T(1,128)S(1)} async-done(((f32[16,1,384]{2,1,0:T(1,128)}), f32[16,1,384]{2,1,0:T(1,128)S(1)}, u32[]{:S(2)}, u32[]{:S(2)}) %all-to-all-start.5) | async-done | bytes 24608 | tf_op jit(solution)/shard_map/all_to_all | solution.py:300
  108.2 4.1 %shard_map.127.part_ref = f32[6,8,16,128]{3,2,1,0:T(8,128)} custom-call(f32[3,6,6]{2,1,0:T(8,128)} %ub_ref.13, f32[3,6,6]{2,1,0:T(8,128)} %lb_ref.13, f32[2,6,6]{2,1,0:T(8,128)} %copy.19.ib_ref, s32[1]{0:T(128)} %bitcast.wall_me.rest_3_, f32[6,8,16,128]{3,2,1,0:T(8,128)} %get-tuple-element.41.adj_ref, f32[6,8,16,128]{3,2,1,0:T(8,128)} %sens_ref.7, ...), custom_call_target="tpu_custom_call" | custom-call | tf_op jit(solution)/shard_map/pallas_call | solution.py:304
  113.5 2.2 %shard_map.128 = (f32[6,8,16,128]{3,2,1,0:T(8,128)}, f32[8,16,128]{2,1,0:T(8,128)}) custom-call(f32[3,6,6]{2,1,0:T(8,128)} %ub_ref.13, f32[3,6,6]{2,1,0:T(8,128)} %lb_ref.13, f32[2,6,6]{2,1,0:T(8,128)} %copy.19.ib_ref, f32[6,8,16,128]{3,2,1,0:T(8,128)} %shard_map.127.part_ref, f32[6,8,16,128]{3,2,1,0:T(8,128)} %diag_ref.13, f32[3,8,16,128]{3,2,1,0:T(8,128)} %face_ref.11, ...), custom_call_target="tpu_custom_call" | custom-call | tf_op jit(solution)/shard_map/pallas_call | solution.py:309
  (67 shorter events, 11.2 us)
Async XLA Ops:
  4.8 20.1 %copy-start.17 = (f32[6,1,16,128]{3,2,1,0:T(8,128)S(1)}, f32[6,1,16,128]{3,2,1,0:T(8,128)}, u32[]{:S(2)}) copy-start(f32[6,1,16,128]{3,2,1,0:T(8,128)} %get-tuple-element.27) | copy-start | bytes 147460
  11.6 15.6 %copy-start.23 = (f32[6,8,128]{2,1,0:T(8,128)S(1)}, f32[6,8,128]{2,1,0:T(8,128)}, u32[]{:S(2)}) copy-start(f32[6,8,128]{2,1,0:T(8,128)} %get-tuple-element.31) | copy-start | bytes 73732
  11.6 19.5 %copy-start.22 = (f32[6,8,128]{2,1,0:T(8,128)S(1)}, f32[6,8,128]{2,1,0:T(8,128)}, u32[]{:S(2)}) copy-start(f32[6,8,128]{2,1,0:T(8,128)} %get-tuple-element.32) | copy-start | bytes 73732
  11.6 20.8 %all-to-all-start.1 = ((f32[16,1,448]{2,1,0:T(1,128)}), f32[16,1,448]{2,1,0:T(1,128)S(1)}, u32[]{:S(2)}, u32[]{:S(2)}) async-start(f32[16,1,448]{2,1,0:T(1,128)} %get-tuple-element.29), calls=%async_computation.1 | async-start | bytes 65536 | tf_op jit(solution)/shard_map/all_to_all | solution.py:300
  21.4 11.0 %collective-permute-start = (f32[6,1,16,128]{3,2,1,0:T(8,128)}, f32[6,1,16,128]{3,2,1,0:T(8,128)S(1)}, u32[]{:S(2)}, u32[]{:S(2)}) collective-permute-start(f32[6,1,16,128]{3,2,1,0:T(8,128)} %get-tuple-element.26), channel_id=1, source_target_pairs={{0,64},{64,128},{128,192},{1,65},{65,129},{129,193},{2,66},{66,130... | collective-permute-start | bytes 147464 | tf_op jit(solution)/shard_map/ppermute | solution.py:236
  24.9 7.5 %collective-permute-start.1 = (f32[6,1,16,128]{3,2,1,0:T(8,128)S(1)}, f32[6,1,16,128]{3,2,1,0:T(8,128)S(1)}, u32[]{:S(2)}, u32[]{:S(2)}) collective-permute-start(f32[6,1,16,128]{3,2,1,0:T(8,128)S(1)} %copy-done.17), channel_id=1, source_target_pairs={{64,0},{128,64},{192,128},{65,1},{129,65},{193,129},{66,2},{130,66... | collective-permute-start | bytes 147464 | tf_op jit(solution)/shard_map/ppermute | solution.py:237
  27.3 9.9 %collective-permute-start.2 = (f32[6,8,128]{2,1,0:T(8,128)S(1)}, f32[6,8,128]{2,1,0:T(8,128)S(1)}, u32[]{:S(2)}, u32[]{:S(2)}) collective-permute-start(f32[6,8,128]{2,1,0:T(8,128)S(1)} %copy-done.23), channel_id=1, source_target_pairs={{0,4},{4,8},{8,12},{12,16},{16,20},{20,24},{24,28},{28,32},{32,36}... | collective-permute-start | bytes 73736 | tf_op jit(solution)/shard_map/ppermute | solution.py:236
  31.1 6.1 %collective-permute-start.3 = (f32[6,8,128]{2,1,0:T(8,128)S(1)}, f32[6,8,128]{2,1,0:T(8,128)S(1)}, u32[]{:S(2)}, u32[]{:S(2)}) collective-permute-start(f32[6,8,128]{2,1,0:T(8,128)S(1)} %copy-done.22), channel_id=1, source_target_pairs={{4,0},{8,4},{12,8},{16,12},{20,16},{24,20},{28,24},{32,28},{36,32}... | collective-permute-start | bytes 73736 | tf_op jit(solution)/shard_map/ppermute | solution.py:237
  40.9 12.0 %all-to-all-start.2 = ((f32[4,1,768]{2,1,0:T(1,128)}), f32[4,1,768]{2,1,0:T(1,128)S(1)}, u32[]{:S(2)}, u32[]{:S(2)}) async-start(f32[4,1,768]{2,1,0:T(1,128)} %get-tuple-element.36), calls=%async_computation.2 | async-start | bytes 24576 | tf_op jit(solution)/shard_map/all_to_all | solution.py:238
  47.0 25.1 %collective-permute-start.4 = (f32[6,1,16,128]{3,2,1,0:T(8,128)}, f32[6,1,16,128]{3,2,1,0:T(8,128)S(1)}, u32[]{:S(2)}, u32[]{:S(2)}) collective-permute-start(f32[6,1,16,128]{3,2,1,0:T(8,128)} %get-tuple-element.34), channel_id=1, source_target_pairs={{0,64},{64,128},{128,192},{1,65},{65,129},{129,193},{2,66},{66,130... | collective-permute-start | bytes 147464 | tf_op jit(solution)/shard_map/ppermute | solution.py:236
  50.4 21.6 %collective-permute-start.5 = (f32[6,1,16,128]{3,2,1,0:T(8,128)}, f32[6,1,16,128]{3,2,1,0:T(8,128)S(1)}, u32[]{:S(2)}, u32[]{:S(2)}) collective-permute-start(f32[6,1,16,128]{3,2,1,0:T(8,128)} %get-tuple-element.35), channel_id=1, source_target_pairs={{64,0},{128,64},{192,128},{65,1},{129,65},{193,129},{66,2},{130,66... | collective-permute-start | bytes 147464 | tf_op jit(solution)/shard_map/ppermute | solution.py:237
  52.8 10.6 %copy-start.21 = (f32[6,8,128]{2,1,0:T(8,128)S(1)}, f32[6,8,128]{2,1,0:T(8,128)}, u32[]{:S(2)}) copy-start(f32[6,8,128]{2,1,0:T(8,128)} %get-tuple-element.39) | copy-start | bytes 73732
  52.8 14.5 %copy-start.19 = (f32[6,8,128]{2,1,0:T(8,128)S(1)}, f32[6,8,128]{2,1,0:T(8,128)}, u32[]{:S(2)}) copy-start(f32[6,8,128]{2,1,0:T(8,128)} %get-tuple-element.40) | copy-start | bytes 73732
  53.4 18.7 %all-to-all-start.3 = ((f32[16,1,384]{2,1,0:T(1,128)}), f32[16,1,384]{2,1,0:T(1,128)S(1)}, u32[]{:S(2)}, u32[]{:S(2)}) async-start(f32[16,1,384]{2,1,0:T(1,128)} %get-tuple-element.37), calls=%async_computation.3 | async-start | bytes 49152 | tf_op jit(solution)/shard_map/all_to_all | solution.py:300
  63.5 13.4 %collective-permute-start.6 = (f32[6,8,128]{2,1,0:T(8,128)S(1)}, f32[6,8,128]{2,1,0:T(8,128)S(1)}, u32[]{:S(2)}, u32[]{:S(2)}) collective-permute-start(f32[6,8,128]{2,1,0:T(8,128)S(1)} %copy-done.21), channel_id=1, source_target_pairs={{0,4},{4,8},{8,12},{12,16},{16,20},{20,24},{24,28},{28,32},{32,36}... | collective-permute-start | bytes 73736 | tf_op jit(solution)/shard_map/ppermute | solution.py:236
  67.3 9.5 %collective-permute-start.7 = (f32[6,8,128]{2,1,0:T(8,128)S(1)}, f32[6,8,128]{2,1,0:T(8,128)S(1)}, u32[]{:S(2)}, u32[]{:S(2)}) collective-permute-start(f32[6,8,128]{2,1,0:T(8,128)S(1)} %copy-done.19), channel_id=1, source_target_pairs={{4,0},{8,4},{12,8},{16,12},{20,16},{24,20},{28,24},{32,28},{36,32}... | collective-permute-start | bytes 73736 | tf_op jit(solution)/shard_map/ppermute | solution.py:237
  81.0 10.6 %all-to-all-start.4 = ((f32[4,1,768]{2,1,0:T(1,128)}), f32[4,1,768]{2,1,0:T(1,128)S(1)}, u32[]{:S(2)}, u32[]{:S(2)}) async-start(f32[4,1,768]{2,1,0:T(1,128)} %get-tuple-element.44), calls=%async_computation.4 | async-start | bytes 24576 | tf_op jit(solution)/shard_map/all_to_all | solution.py:238
  85.9 21.7 %collective-permute-start.8 = (f32[6,1,16,128]{3,2,1,0:T(8,128)}, f32[6,1,16,128]{3,2,1,0:T(8,128)S(1)}, u32[]{:S(2)}, u32[]{:S(2)}) collective-permute-start(f32[6,1,16,128]{3,2,1,0:T(8,128)} %get-tuple-element.42), channel_id=1, source_target_pairs={{0,64},{64,128},{128,192},{1,65},{65,129},{129,193},{2,66},{66,130... | collective-permute-start | bytes 147464 | tf_op jit(solution)/shard_map/ppermute | solution.py:236
  89.3 18.2 %collective-permute-start.9 = (f32[6,1,16,128]{3,2,1,0:T(8,128)}, f32[6,1,16,128]{3,2,1,0:T(8,128)S(1)}, u32[]{:S(2)}, u32[]{:S(2)}) collective-permute-start(f32[6,1,16,128]{3,2,1,0:T(8,128)} %get-tuple-element.43), channel_id=1, source_target_pairs={{64,0},{128,64},{192,128},{65,1},{129,65},{193,129},{66,2},{130,66... | collective-permute-start | bytes 147464 | tf_op jit(solution)/shard_map/ppermute | solution.py:237
  91.7 7.2 %copy-start.20 = (f32[6,8,128]{2,1,0:T(8,128)S(1)}, f32[6,8,128]{2,1,0:T(8,128)}, u32[]{:S(2)}) copy-start(f32[6,8,128]{2,1,0:T(8,128)} %get-tuple-element.46) | copy-start | bytes 73732
  91.7 11.1 %copy-start.18 = (f32[6,8,128]{2,1,0:T(8,128)S(1)}, f32[6,8,128]{2,1,0:T(8,128)}, u32[]{:S(2)}) copy-start(f32[6,8,128]{2,1,0:T(8,128)} %get-tuple-element.47) | copy-start | bytes 73732
  92.3 15.3 %all-to-all-start.5 = ((f32[16,1,384]{2,1,0:T(1,128)}), f32[16,1,384]{2,1,0:T(1,128)S(1)}, u32[]{:S(2)}, u32[]{:S(2)}) async-start(f32[16,1,384]{2,1,0:T(1,128)} %get-tuple-element.45), calls=%async_computation.5 | async-start | bytes 49152 | tf_op jit(solution)/shard_map/all_to_all | solution.py:300
  99.0 13.4 %collective-permute-start.10 = (f32[6,8,128]{2,1,0:T(8,128)S(1)}, f32[6,8,128]{2,1,0:T(8,128)S(1)}, u32[]{:S(2)}, u32[]{:S(2)}) collective-permute-start(f32[6,8,128]{2,1,0:T(8,128)S(1)} %copy-done.20), channel_id=1, source_target_pairs={{0,4},{4,8},{8,12},{12,16},{16,20},{20,24},{24,28},{28,32},{32,36}... | collective-permute-start | bytes 73736 | tf_op jit(solution)/shard_map/ppermute | solution.py:236
  102.8 9.5 %collective-permute-start.11 = (f32[6,8,128]{2,1,0:T(8,128)S(1)}, f32[6,8,128]{2,1,0:T(8,128)S(1)}, u32[]{:S(2)}, u32[]{:S(2)}) collective-permute-start(f32[6,8,128]{2,1,0:T(8,128)S(1)} %copy-done.18), channel_id=1, source_target_pairs={{4,0},{8,4},{12,8},{16,12},{20,16},{24,20},{28,24},{32,28},{36,32}... | collective-permute-start | bytes 73736 | tf_op jit(solution)/shard_map/ppermute | solution.py:237
  (17 other events, 10.4 us)

commit v10 on v9

--- a/solution.py
+++ b/solution.py
@@ -45,6 +45,11 @@
 
 def flat_row(x):
     return jnp.concatenate([x[t:t + 1] for t in range(x.shape[0])], axis=1)
+
+
+def own_rows(g_ref, me):
+    n_src, _, _, width = g_ref.shape
+    return g_ref[:, pl.ds(me, 1)].reshape(n_src, 1, width)
 
 
 def to_chunks(rows_ref, pieces, slots):
@@ -160,7 +165,7 @@
 
 
 def make_part_a(first, slots):
-    def kernel(ub_ref, lb_ref, ib_ref, wall_me, adj_ref, sens_ref, diag_ref, face_ref, hcl, hch, w_inc,
+    def kernel(ub_ref, lb_ref, ib_ref, wall_me, span_me, adj_ref, sens_ref, diag_ref, face_ref, hcl, hch, w_inc,
                inc_ref, *rest):
         if first:
             out_ref, tgt_out = rest
@@ -168,7 +173,7 @@
             tgt_ref, out_ref = rest
         n_var, nx, ny, nz = adj_ref.shape
         blk_ref = (ub_ref, lb_ref, ib_ref)
-        inc = inc_ref[...]
+        inc = own_rows(inc_ref, span_me[0])
         if first:
             got = from_chunks(inc, n_var + 1, slots)
             cell = got[n_var].astype(jnp.int32)
@@ -272,13 +277,13 @@
     part_a_first = pl.pallas_call(
         make_part_a(True, slots),
         out_shape=[adj_sds, tgt_sds],
-        in_specs=[smem] * 4 + [vmem] * 8,
+        in_specs=[smem] * 5 + [vmem] * 8,
         out_specs=[vmem] * 2,
     )
     part_a = pl.pallas_call(
         make_part_a(False, slots),
         out_shape=adj_sds,
-        in_specs=[smem] * 4 + [vmem] * 9,
+        in_specs=[smem] * 5 + [vmem] * 9,
         out_specs=vmem,
     )
     part_b = pl.pallas_call(
@@ -294,14 +299,15 @@
         out_specs=[vmem] * 2,
     )
     ub, lb, ib, _ = blk
+    span_me = lax.axis_index("span").astype(jnp.int32).reshape(1)
     received = None
     for sweep in range(SWEEPS):
         hcl, hch, hsl, hsh, w_inc = exchange(faces)
-        incoming = lax.all_to_all(rows, "span", split_axis=0, concat_axis=0, tiled=True)
+        incoming = lax.all_gather(rows, "span", axis=0)
         if sweep == 0:
-            partial, received = part_a_first(*blk, adj, sensitivity, diagonal, face_coef, hcl, hch, w_inc, incoming)
-        else:
-            partial = part_a(*blk, adj, sensitivity, diagonal, face_coef, hcl, hch, w_inc, incoming, received)
+            partial, received = part_a_first(*blk, span_me, adj, sensitivity, diagonal, face_coef, hcl, hch, w_inc, incoming)
+        else:
+            partial = part_a(*blk, span_me, adj, sensitivity, diagonal, face_coef, hcl, hch, w_inc, incoming, received)
         if sweep < SWEEPS - 1:
             adj, rows, *faces = part_b(ub, lb, ib, partial, diagonal, face_coef, hsl, hsh,
                                        send_row, orient_row, weight_row, wall_me)

time: 117 us -> 192 us (1.64)
  the two profiles are of different devices: /device:TPU:12 before, /device:TPU:118 now
where the time goes in v10:
time: 192 us; the launch traced here: 191 us
  blocking collectives  109 us (57%)
  starting transfers between devices  51.4 us (27%)
  Pallas kernels  23.9 us (12%)
  local copies, waits for them, and re-layouts  6.13 us (3%)
    all_gather x3, blocking collectives, local(): incoming = lax.all_gather(rows, 'span', axis=0)  109 us
    ppermute x6, starting transfers between devices, exchange(): out.append(lax.ppermute(hi_face, axis, forward))  23.1 us
    all_to_all x3, starting transfers between devices, exchange(): lax.all_to_all(w_buf, 'wall', split_axis=0, concat_axis=0, tiled=True)  14.5 us
    ppermute x6, starting transfers between devices, exchange(): out.append(lax.ppermute(lo_face, axis, backward))  13.7 us
    pallas_call x2, Pallas kernels, local(): part_a(*blk, span_me, adj, sensitivity, diagonal, face_coef, hcl, hch, w_...  8.48 us
    unnamed x37, local copies, waits for them, and re-layouts  6.13 us
    pallas_call x2, Pallas kernels, local(): part_b(ub, lb, ib, partial, diagonal, face_coef, hsl, hsh, send_row, orie...  6.01 us
    pallas_call x1, Pallas kernels, local(): part_a_first(*blk, span_me, adj, sensitivity, diagonal, face_coef, hcl, h...  4.37 us
  transfers between devices with their start and end apart: 15, of which 0 were waited for; matrix products, arithmetic and copies ran while one was open for 0% of the time, Pallas kernels for 7%

profile of v10, /device:TPU:118, one launch (start us, length us, event | category | flops | bytes accessed | tf_op | source)
XLA Modules:
  0.0 191.4 jit_solution(2927215680541440813)
XLA Ops:
  1.9 2.8 %shard_map.122 = (f32[6,8,16,128]{3,2,1,0:T(8,128)}, f32[16,1,448]{2,1,0:T(1,128)}, f32[6,1,16,128]{3,2,1,0:T(8,128)}, f32[6,1,16,128]{3,2,1,0:T(8,128)}, f32[6,...) custom-call(f32[3,6,6]{2,1,0:T(8,128)} %ub_ref.13, f32[3,6,6]{2,1,0:T(8,128)} %lb_ref.13, ...), custom_call_target="tpu_custom_call" | custom-call | tf_op jit(solution)/shard_map/pallas_call | solution.py:275
  4.8 4.9 %all-to-all-start = ((f32[4,1,768]{2,1,0:T(1,128)}), f32[4,1,768]{2,1,0:T(1,128)S(1)}, u32[]{:S(2)}, u32[]{:S(2)}) async-start(f32[4,1,768]{2,1,0:T(1,128)} %get-tuple-element.28), calls=%async_computation | async-start | bytes 24576 | tf_op jit(solution)/shard_map/all_to_all | solution.py:243
  9.7 5.3 %collective-permute-start.2 = (f32[6,8,128]{2,1,0:T(8,128)}, f32[6,8,128]{2,1,0:T(8,128)S(1)}, u32[]{:S(2)}, u32[]{:S(2)}) collective-permute-start(f32[6,8,128]{2,1,0:T(8,128)} %get-tuple-element.31), channel_id=1, source_target_pairs={{0,4},{4,8},{8,12},{12,16},{16,20},{20,24},{24,28},{28,32},{32,36}... | collective-permute-start | bytes 73736 | tf_op jit(solution)/shard_map/ppermute | solution.py:241
  15.0 1.9 %collective-permute-start.3 = (f32[6,8,128]{2,1,0:T(8,128)}, f32[6,8,128]{2,1,0:T(8,128)S(1)}, u32[]{:S(2)}, u32[]{:S(2)}) collective-permute-start(f32[6,8,128]{2,1,0:T(8,128)} %get-tuple-element.32), channel_id=1, source_target_pairs={{4,0},{8,4},{12,8},{16,12},{20,16},{24,20},{28,24},{32,28},{36,32}... | collective-permute-start | bytes 73736 | tf_op jit(solution)/shard_map/ppermute | solution.py:242
  16.9 3.2 %collective-permute-start = (f32[6,1,16,128]{3,2,1,0:T(8,128)}, f32[6,1,16,128]{3,2,1,0:T(8,128)S(1)}, u32[]{:S(2)}, u32[]{:S(2)}) collective-permute-start(f32[6,1,16,128]{3,2,1,0:T(8,128)} %get-tuple-element.26), channel_id=1, source_target_pairs={{0,64},{64,128},{128,192},{1,65},{65,129},{129,193},{2,66},{66,130... | collective-permute-start | bytes 147464 | tf_op jit(solution)/shard_map/ppermute | solution.py:241
  20.1 2.7 %collective-permute-start.1 = (f32[6,1,16,128]{3,2,1,0:T(8,128)}, f32[6,1,16,128]{3,2,1,0:T(8,128)S(1)}, u32[]{:S(2)}, u32[]{:S(2)}) collective-permute-start(f32[6,1,16,128]{3,2,1,0:T(8,128)} %get-tuple-element.27), channel_id=1, source_target_pairs={{64,0},{128,64},{192,128},{65,1},{129,65},{193,129},{66,2},{130,66... | collective-permute-start | bytes 147464 | tf_op jit(solution)/shard_map/ppermute | solution.py:242
  22.8 36.8 %all-gather = f32[256,1,448]{2,1,0:T(1,128)} all-gather(f32[16,1,448]{2,1,0:T(1,128)S(1)} %copy-done.9), channel_id=2, replica_groups=mesh['chord'=4,'span'=16,'wall'=4] {'span'}, dimensions={0}, use_global_device_ids=true | all-gather | bytes 487424 | tf_op jit(solution)/shard_map/all_gather | solution.py:306
  60.2 4.4 %shard_map.123 = (f32[6,8,16,128]{3,2,1,0:T(8,128)}, s32[1,1024]{1,0:T(1,128)}) custom-call(f32[3,6,6]{2,1,0:T(8,128)} %ub_ref.13, f32[3,6,6]{2,1,0:T(8,128)} %lb_ref.13, f32[2,6,6]{2,1,0:T(8,128)} %copy.26.ib_ref, s32[1]{0:T(128)} %bitcast.wall_me.rest_3_, s32[1]{0:T(128)} %bitcast.1.span_me, f32[6,8,16,128]{3,2,1,0:T(8,128)} %get-tuple-element.25.adj_ref, ...), custom_call_target="tpu_custom_call" | custom-call | tf_op jit(solution)/shard_map/pallas_call | solution.py:308
  65.2 3.0 %shard_map.124 = (f32[6,8,16,128]{3,2,1,0:T(8,128)}, f32[16,1,384]{2,1,0:T(1,128)}, f32[6,1,16,128]{3,2,1,0:T(8,128)}, f32[6,1,16,128]{3,2,1,0:T(8,128)}, f32[6,...) custom-call(f32[3,6,6]{2,1,0:T(8,128)} %ub_ref.13, f32[3,6,6]{2,1,0:T(8,128)} %lb_ref.13, ...), custom_call_target="tpu_custom_call" | custom-call | tf_op jit(solution)/shard_map/pallas_call | solution.py:312
  68.2 4.8 %all-to-all-start.1 = ((f32[4,1,768]{2,1,0:T(1,128)}), f32[4,1,768]{2,1,0:T(1,128)S(1)}, u32[]{:S(2)}, u32[]{:S(2)}) async-start(f32[4,1,768]{2,1,0:T(1,128)} %get-tuple-element.36), calls=%async_computation.1 | async-start | bytes 24576 | tf_op jit(solution)/shard_map/all_to_all | solution.py:243
  73.0 4.2 %collective-permute-start.6 = (f32[6,8,128]{2,1,0:T(8,128)}, f32[6,8,128]{2,1,0:T(8,128)S(1)}, u32[]{:S(2)}, u32[]{:S(2)}) collective-permute-start(f32[6,8,128]{2,1,0:T(8,128)} %get-tuple-element.39), channel_id=1, source_target_pairs={{0,4},{4,8},{8,12},{12,16},{16,20},{20,24},{24,28},{28,32},{32,36}... | collective-permute-start | bytes 73736 | tf_op jit(solution)/shard_map/ppermute | solution.py:241
  77.3 1.9 %collective-permute-start.7 = (f32[6,8,128]{2,1,0:T(8,128)}, f32[6,8,128]{2,1,0:T(8,128)S(1)}, u32[]{:S(2)}, u32[]{:S(2)}) collective-permute-start(f32[6,8,128]{2,1,0:T(8,128)} %get-tuple-element.40), channel_id=1, source_target_pairs={{4,0},{8,4},{12,8},{16,12},{20,16},{24,20},{28,24},{32,28},{36,32}... | collective-permute-start | bytes 73736 | tf_op jit(solution)/shard_map/ppermute | solution.py:242
  79.2 3.2 %collective-permute-start.4 = (f32[6,1,16,128]{3,2,1,0:T(8,128)}, f32[6,1,16,128]{3,2,1,0:T(8,128)S(1)}, u32[]{:S(2)}, u32[]{:S(2)}) collective-permute-start(f32[6,1,16,128]{3,2,1,0:T(8,128)} %get-tuple-element.34), channel_id=1, source_target_pairs={{0,64},{64,128},{128,192},{1,65},{65,129},{129,193},{2,66},{66,130... | collective-permute-start | bytes 147464 | tf_op jit(solution)/shard_map/ppermute | solution.py:241
  82.4 2.6 %collective-permute-start.5 = (f32[6,1,16,128]{3,2,1,0:T(8,128)}, f32[6,1,16,128]{3,2,1,0:T(8,128)S(1)}, u32[]{:S(2)}, u32[]{:S(2)}) collective-permute-start(f32[6,1,16,128]{3,2,1,0:T(8,128)} %get-tuple-element.35), channel_id=1, source_target_pairs={{64,0},{128,64},{192,128},{65,1},{129,65},{193,129},{66,2},{130,66... | collective-permute-start | bytes 147464 | tf_op jit(solution)/shard_map/ppermute | solution.py:242
  85.1 36.1 %all-gather.1 = f32[256,1,384]{2,1,0:T(1,128)} all-gather(f32[16,1,384]{2,1,0:T(1,128)S(1)} %copy-done.10), channel_id=3, replica_groups=mesh['chord'=4,'span'=16,'wall'=4] {'span'}, dimensions={0}, use_global_device_ids=true | all-gather | bytes 417792 | tf_op jit(solution)/shard_map/all_gather | solution.py:306
  121.8 4.2 %shard_map.125.part_ref = f32[6,8,16,128]{3,2,1,0:T(8,128)} custom-call(f32[3,6,6]{2,1,0:T(8,128)} %ub_ref.13, f32[3,6,6]{2,1,0:T(8,128)} %lb_ref.13, f32[2,6,6]{2,1,0:T(8,128)} %copy.26.ib_ref, s32[1]{0:T(128)} %bitcast.wall_me.rest_3_, s32[1]{0:T(128)} %bitcast.1.span_me, f32[6,8,16,128]{3,2,1,0:T(8,128)} %get-tuple-element.33.adj_ref, ...), custom_call_target="tpu_custom_call" | custom-call | tf_op jit(solution)/shard_map/pallas_call | solution.py:310
  127.3 3.0 %shard_map.126 = (f32[6,8,16,128]{3,2,1,0:T(8,128)}, f32[16,1,384]{2,1,0:T(1,128)}, f32[6,1,16,128]{3,2,1,0:T(8,128)}, f32[6,1,16,128]{3,2,1,0:T(8,128)}, f32[6,...) custom-call(f32[3,6,6]{2,1,0:T(8,128)} %ub_ref.13, f32[3,6,6]{2,1,0:T(8,128)} %lb_ref.13, ...), custom_call_target="tpu_custom_call" | custom-call | tf_op jit(solution)/shard_map/pallas_call | solution.py:312
  130.3 4.8 %all-to-all-start.2 = ((f32[4,1,768]{2,1,0:T(1,128)}), f32[4,1,768]{2,1,0:T(1,128)S(1)}, u32[]{:S(2)}, u32[]{:S(2)}) async-start(f32[4,1,768]{2,1,0:T(1,128)} %get-tuple-element.44), calls=%async_computation.2 | async-start | bytes 24576 | tf_op jit(solution)/shard_map/all_to_all | solution.py:243
  135.1 4.0 %collective-permute-start.10 = (f32[6,8,128]{2,1,0:T(8,128)}, f32[6,8,128]{2,1,0:T(8,128)S(1)}, u32[]{:S(2)}, u32[]{:S(2)}) collective-permute-start(f32[6,8,128]{2,1,0:T(8,128)} %get-tuple-element.46), channel_id=1, source_target_pairs={{0,4},{4,8},{8,12},{12,16},{16,20},{20,24},{24,28},{28,32},{32,36}... | collective-permute-start | bytes 73736 | tf_op jit(solution)/shard_map/ppermute | solution.py:241
  141.1 3.2 %collective-permute-start.8 = (f32[6,1,16,128]{3,2,1,0:T(8,128)}, f32[6,1,16,128]{3,2,1,0:T(8,128)S(1)}, u32[]{:S(2)}, u32[]{:S(2)}) collective-permute-start(f32[6,1,16,128]{3,2,1,0:T(8,128)} %get-tuple-element.42), channel_id=1, source_target_pairs={{0,64},{64,128},{128,192},{1,65},{65,129},{129,193},{2,66},{66,130... | collective-permute-start | bytes 147464 | tf_op jit(solution)/shard_map/ppermute | solution.py:241
  144.3 2.6 %collective-permute-start.9 = (f32[6,1,16,128]{3,2,1,0:T(8,128)}, f32[6,1,16,128]{3,2,1,0:T(8,128)S(1)}, u32[]{:S(2)}, u32[]{:S(2)}) collective-permute-start(f32[6,1,16,128]{3,2,1,0:T(8,128)} %get-tuple-element.43), channel_id=1, source_target_pairs={{64,0},{128,64},{192,128},{65,1},{129,65},{193,129},{66,2},{130,66... | collective-permute-start | bytes 147464 | tf_op jit(solution)/shard_map/ppermute | solution.py:242
  146.9 36.1 %all-gather.2 = f32[256,1,384]{2,1,0:T(1,128)} all-gather(f32[16,1,384]{2,1,0:T(1,128)S(1)} %copy-done.11), channel_id=4, replica_groups=mesh['chord'=4,'span'=16,'wall'=4] {'span'}, dimensions={0}, use_global_device_ids=true | all-gather | bytes 417792 | tf_op jit(solution)/shard_map/all_gather | solution.py:306
  183.7 4.2 %shard_map.127.part_ref = f32[6,8,16,128]{3,2,1,0:T(8,128)} custom-call(f32[3,6,6]{2,1,0:T(8,128)} %ub_ref.13, f32[3,6,6]{2,1,0:T(8,128)} %lb_ref.13, f32[2,6,6]{2,1,0:T(8,128)} %copy.26.ib_ref, s32[1]{0:T(128)} %bitcast.wall_me.rest_3_, s32[1]{0:T(128)} %bitcast.1.span_me, f32[6,8,16,128]{3,2,1,0:T(8,128)} %get-tuple-element.41.adj_ref, ...), custom_call_target="tpu_custom_call" | custom-call | tf_op jit(solution)/shard_map/pallas_call | solution.py:310
  189.2 2.2 %shard_map.128 = (f32[6,8,16,128]{3,2,1,0:T(8,128)}, f32[8,16,128]{2,1,0:T(8,128)}) custom-call(f32[3,6,6]{2,1,0:T(8,128)} %ub_ref.13, f32[3,6,6]{2,1,0:T(8,128)} %lb_ref.13, f32[2,6,6]{2,1,0:T(8,128)} %copy.26.ib_ref, f32[6,8,16,128]{3,2,1,0:T(8,128)} %shard_map.127.part_ref, f32[6,8,16,128]{3,2,1,0:T(8,128)} %diag_ref.13, f32[3,8,16,128]{3,2,1,0:T(8,128)} %face_ref.11, ...), custom_call_target="tpu_custom_call" | custom-call | tf_op jit(solution)/shard_map/pallas_call | solution.py:315
  (53 shorter events, 8.1 us)
Async XLA Ops:
  4.8 18.0 %copy-start.9 = (f32[16,1,448]{2,1,0:T(1,128)S(1)}, f32[16,1,448]{2,1,0:T(1,128)}, u32[]{:S(2)}) copy-start(f32[16,1,448]{2,1,0:T(1,128)} %get-tuple-element.29) | copy-start | bytes 86020
  4.8 54.8 %all-to-all-start = ((f32[4,1,768]{2,1,0:T(1,128)}), f32[4,1,768]{2,1,0:T(1,128)S(1)}, u32[]{:S(2)}, u32[]{:S(2)}) async-start(f32[4,1,768]{2,1,0:T(1,128)} %get-tuple-element.28), calls=%async_computation | async-start | bytes 24576 | tf_op jit(solution)/shard_map/all_to_all | solution.py:243
  9.7 54.9 %collective-permute-start.2 = (f32[6,8,128]{2,1,0:T(8,128)}, f32[6,8,128]{2,1,0:T(8,128)S(1)}, u32[]{:S(2)}, u32[]{:S(2)}) collective-permute-start(f32[6,8,128]{2,1,0:T(8,128)} %get-tuple-element.31), channel_id=1, source_target_pairs={{0,4},{4,8},{8,12},{12,16},{16,20},{20,24},{24,28},{28,32},{32,36}... | collective-permute-start | bytes 73736 | tf_op jit(solution)/shard_map/ppermute | solution.py:241
  15.0 49.6 %collective-permute-start.3 = (f32[6,8,128]{2,1,0:T(8,128)}, f32[6,8,128]{2,1,0:T(8,128)S(1)}, u32[]{:S(2)}, u32[]{:S(2)}) collective-permute-start(f32[6,8,128]{2,1,0:T(8,128)} %get-tuple-element.32), channel_id=1, source_target_pairs={{4,0},{8,4},{12,8},{16,12},{20,16},{24,20},{28,24},{32,28},{36,32}... | collective-permute-start | bytes 73736 | tf_op jit(solution)/shard_map/ppermute | solution.py:242
  16.9 42.7 %collective-permute-start = (f32[6,1,16,128]{3,2,1,0:T(8,128)}, f32[6,1,16,128]{3,2,1,0:T(8,128)S(1)}, u32[]{:S(2)}, u32[]{:S(2)}) collective-permute-start(f32[6,1,16,128]{3,2,1,0:T(8,128)} %get-tuple-element.26), channel_id=1, source_target_pairs={{0,64},{64,128},{128,192},{1,65},{65,129},{129,193},{2,66},{66,130... | collective-permute-start | bytes 147464 | tf_op jit(solution)/shard_map/ppermute | solution.py:241
  20.1 39.5 %collective-permute-start.1 = (f32[6,1,16,128]{3,2,1,0:T(8,128)}, f32[6,1,16,128]{3,2,1,0:T(8,128)S(1)}, u32[]{:S(2)}, u32[]{:S(2)}) collective-permute-start(f32[6,1,16,128]{3,2,1,0:T(8,128)} %get-tuple-element.27), channel_id=1, source_target_pairs={{64,0},{128,64},{192,128},{65,1},{129,65},{193,129},{66,2},{130,66... | collective-permute-start | bytes 147464 | tf_op jit(solution)/shard_map/ppermute | solution.py:242
  59.6 0.6 copy-start.3
  59.6 0.6 copy-start.4
  68.2 16.8 %copy-start.10 = (f32[16,1,384]{2,1,0:T(1,128)S(1)}, f32[16,1,384]{2,1,0:T(1,128)}, u32[]{:S(2)}) copy-start(f32[16,1,384]{2,1,0:T(1,128)} %get-tuple-element.37) | copy-start | bytes 73732
  68.2 53.0 %all-to-all-start.1 = ((f32[4,1,768]{2,1,0:T(1,128)}), f32[4,1,768]{2,1,0:T(1,128)S(1)}, u32[]{:S(2)}, u32[]{:S(2)}) async-start(f32[4,1,768]{2,1,0:T(1,128)} %get-tuple-element.36), calls=%async_computation.1 | async-start | bytes 24576 | tf_op jit(solution)/shard_map/all_to_all | solution.py:243
  73.0 53.0 %collective-permute-start.6 = (f32[6,8,128]{2,1,0:T(8,128)}, f32[6,8,128]{2,1,0:T(8,128)S(1)}, u32[]{:S(2)}, u32[]{:S(2)}) collective-permute-start(f32[6,8,128]{2,1,0:T(8,128)} %get-tuple-element.39), channel_id=1, source_target_pairs={{0,4},{4,8},{8,12},{12,16},{16,20},{20,24},{24,28},{28,32},{32,36}... | collective-permute-start | bytes 73736 | tf_op jit(solution)/shard_map/ppermute | solution.py:241
  77.3 48.8 %collective-permute-start.7 = (f32[6,8,128]{2,1,0:T(8,128)}, f32[6,8,128]{2,1,0:T(8,128)S(1)}, u32[]{:S(2)}, u32[]{:S(2)}) collective-permute-start(f32[6,8,128]{2,1,0:T(8,128)} %get-tuple-element.40), channel_id=1, source_target_pairs={{4,0},{8,4},{12,8},{16,12},{20,16},{24,20},{28,24},{32,28},{36,32}... | collective-permute-start | bytes 73736 | tf_op jit(solution)/shard_map/ppermute | solution.py:242
  79.2 42.0 %collective-permute-start.4 = (f32[6,1,16,128]{3,2,1,0:T(8,128)}, f32[6,1,16,128]{3,2,1,0:T(8,128)S(1)}, u32[]{:S(2)}, u32[]{:S(2)}) collective-permute-start(f32[6,1,16,128]{3,2,1,0:T(8,128)} %get-tuple-element.34), channel_id=1, source_target_pairs={{0,64},{64,128},{128,192},{1,65},{65,129},{129,193},{2,66},{66,130... | collective-permute-start | bytes 147464 | tf_op jit(solution)/shard_map/ppermute | solution.py:241
  82.4 38.8 %collective-permute-start.5 = (f32[6,1,16,128]{3,2,1,0:T(8,128)}, f32[6,1,16,128]{3,2,1,0:T(8,128)S(1)}, u32[]{:S(2)}, u32[]{:S(2)}) collective-permute-start(f32[6,1,16,128]{3,2,1,0:T(8,128)} %get-tuple-element.35), channel_id=1, source_target_pairs={{64,0},{128,64},{192,128},{65,1},{129,65},{193,129},{66,2},{130,66... | collective-permute-start | bytes 147464 | tf_op jit(solution)/shard_map/ppermute | solution.py:242
  121.2 0.6 copy-start.6
  121.2 0.6 copy-start.8
  130.3 16.6 %copy-start.11 = (f32[16,1,384]{2,1,0:T(1,128)S(1)}, f32[16,1,384]{2,1,0:T(1,128)}, u32[]{:S(2)}) copy-start(f32[16,1,384]{2,1,0:T(1,128)} %get-tuple-element.45) | copy-start | bytes 73732
  130.3 52.8 %all-to-all-start.2 = ((f32[4,1,768]{2,1,0:T(1,128)}), f32[4,1,768]{2,1,0:T(1,128)S(1)}, u32[]{:S(2)}, u32[]{:S(2)}) async-start(f32[4,1,768]{2,1,0:T(1,128)} %get-tuple-element.44), calls=%async_computation.2 | async-start | bytes 24576 | tf_op jit(solution)/shard_map/all_to_all | solution.py:243
  135.1 52.9 %collective-permute-start.10 = (f32[6,8,128]{2,1,0:T(8,128)}, f32[6,8,128]{2,1,0:T(8,128)S(1)}, u32[]{:S(2)}, u32[]{:S(2)}) collective-permute-start(f32[6,8,128]{2,1,0:T(8,128)} %get-tuple-element.46), channel_id=1, source_target_pairs={{0,4},{4,8},{8,12},{12,16},{16,20},{20,24},{24,28},{28,32},{32,36}... | collective-permute-start | bytes 73736 | tf_op jit(solution)/shard_map/ppermute | solution.py:241
  139.1 48.8 %collective-permute-start.11 = (f32[6,8,128]{2,1,0:T(8,128)}, f32[6,8,128]{2,1,0:T(8,128)S(1)}, u32[]{:S(2)}, u32[]{:S(2)}) collective-permute-start(f32[6,8,128]{2,1,0:T(8,128)} %get-tuple-element.47), channel_id=1, source_target_pairs={{4,0},{8,4},{12,8},{16,12},{20,16},{24,20},{28,24},{32,28},{36,32}... | collective-permute-start | bytes 73736 | tf_op jit(solution)/shard_map/ppermute | solution.py:242
  141.1 42.0 %collective-permute-start.8 = (f32[6,1,16,128]{3,2,1,0:T(8,128)}, f32[6,1,16,128]{3,2,1,0:T(8,128)S(1)}, u32[]{:S(2)}, u32[]{:S(2)}) collective-permute-start(f32[6,1,16,128]{3,2,1,0:T(8,128)} %get-tuple-element.42), channel_id=1, source_target_pairs={{0,64},{64,128},{128,192},{1,65},{65,129},{129,193},{2,66},{66,130... | collective-permute-start | bytes 147464 | tf_op jit(solution)/shard_map/ppermute | solution.py:241
  144.3 38.8 %collective-permute-start.9 = (f32[6,1,16,128]{3,2,1,0:T(8,128)}, f32[6,1,16,128]{3,2,1,0:T(8,128)S(1)}, u32[]{:S(2)}, u32[]{:S(2)}) collective-permute-start(f32[6,1,16,128]{3,2,1,0:T(8,128)} %get-tuple-element.43), channel_id=1, source_target_pairs={{64,0},{128,64},{192,128},{65,1},{129,65},{193,129},{66,2},{130,66... | collective-permute-start | bytes 147464 | tf_op jit(solution)/shard_map/ppermute | solution.py:242
  183.1 0.6 copy-start.5
  183.1 0.6 copy-start.7
  (9 other events, 5.4 us)

commit v11 on v9

--- a/solution.py
+++ b/solution.py
@@ -210,11 +210,17 @@
             out_ref[...] = new
             grad_ref[...] = prod_ref[...] * new[n_var - 1]
         else:
-            send_ref, orient_ref, weight_ref, wall_me, out_ref, rows_ref, c_lo, c_hi, s_lo, s_hi, w_buf = rest
+            wall_me, out_ref, c_lo, c_hi, s_lo, s_hi, w_buf = rest
             out_ref[...] = new
             write_faces(new, (c_lo, c_hi, s_lo, s_hi, w_buf, wall_me))
-            blk_ref = (ub_ref, lb_ref, ib_ref)
-            to_chunks(rows_ref, gather_rows(new, send_ref, orient_ref, weight_ref, blk_ref, n_var, nz), slots)
+    return kernel
+
+
+def make_rows(slots):
+    def kernel(ub_ref, lb_ref, ib_ref, adj_ref, send_ref, orient_ref, weight_ref, rows_ref):
+        n_var, nx, ny, nz = adj_ref.shape
+        blk_ref = (ub_ref, lb_ref, ib_ref)
+        to_chunks(rows_ref, gather_rows(adj_ref[...], send_ref, orient_ref, weight_ref, blk_ref, n_var, nz), slots)
     return kernel
 
 
@@ -283,9 +289,15 @@
     )
     part_b = pl.pallas_call(
         make_part_b(False, slots),
-        out_shape=[adj_sds, rows_sds] + face_shapes(shape, n_wall),
-        in_specs=[smem] * 3 + [vmem] * 8 + [smem],
-        out_specs=[vmem] * 7,
+        out_shape=[adj_sds] + face_shapes(shape, n_wall),
+        in_specs=[smem] * 3 + [vmem] * 5 + [smem],
+        out_specs=[vmem] * 6,
+    )
+    next_rows = pl.pallas_call(
+        make_rows(slots),
+        out_shape=rows_sds,
+        in_specs=[smem] * 3 + [vmem] * 4,
+        out_specs=vmem,
     )
     part_b_last = pl.pallas_call(
         make_part_b(True, slots),
@@ -303,8 +315,8 @@
         else:
             partial = part_a(*blk, adj, sensitivity, diagonal, face_coef, hcl, hch, w_inc, incoming, received)
         if sweep < SWEEPS - 1:
-            adj, rows, *faces = part_b(ub, lb, ib, partial, diagonal, face_coef, hsl, hsh,
-                                       send_row, orient_row, weight_row, wall_me)
+            adj, *faces = part_b(ub, lb, ib, partial, diagonal, face_coef, hsl, hsh, wall_me)
+            rows = next_rows(ub, lb, ib, adj, send_row, orient_row, weight_row)
         else:
             adj, gradient = part_b_last(ub, lb, ib, partial, diagonal, face_coef, hsl, hsh, production)
     return (adj, gradient)

time: 117 us -> 122 us (1.043)
  the two profiles are of different devices: /device:TPU:12 before, /device:TPU:20 now
where the time goes in v11:
time: 122 us; the launch traced here: 120 us
  starting transfers between devices  70.2 us (58%)
  Pallas kernels  27.6 us (23%)
  local copies, waits for them, and re-layouts  7.94 us (7%)
  waiting for transfers between devices  6.94 us (6%)
  blocking collectives  6.86 us (6%)
    all_to_all x3, starting transfers between devices, local(): lax.all_to_all(rows, 'span', split_axis=0, concat_axis=0, tiled=True)  26.4 us
    ppermute x6, starting transfers between devices, exchange(): out.append(lax.ppermute(hi_face, axis, forward))  21 us
    ppermute x6, starting transfers between devices, exchange(): out.append(lax.ppermute(lo_face, axis, backward))  11.8 us
    all_to_all x2, starting transfers between devices, exchange(): lax.all_to_all(w_buf, 'wall', split_axis=0, concat_axis=0, tiled=True)  10.9 us
    pallas_call x2, Pallas kernels, local(): part_a(*blk, adj, sensitivity, diagonal, face_coef, hcl, hch, w_inc, inco...  8.23 us
    unnamed x49, local copies, waits for them, and re-layouts  7.94 us
    all_to_all x3, waiting for transfers between devices, local(): lax.all_to_all(rows, 'span', split_axis=0, concat_axis=0, tiled=True)  6.9 us
    all_to_all x1, blocking collectives, exchange(): lax.all_to_all(w_buf, 'wall', split_axis=0, concat_axis=0, tiled=True)  6.86 us
  transfers between devices with their start and end apart: 17, of which 2 were waited for; matrix products, arithmetic and copies ran while one was open for 0% of the time, Pallas kernels for 15%

profile of v11, /device:TPU:20, one launch (start us, length us, event | category | flops | bytes accessed | tf_op | source)
XLA Modules:
  0.0 120.5 jit_solution(11741869722377943053)
XLA Ops:
  1.9 2.8 %shard_map.122 = (f32[6,8,16,128]{3,2,1,0:T(8,128)}, f32[16,1,448]{2,1,0:T(1,128)}, f32[6,1,16,128]{3,2,1,0:T(8,128)}, f32[6,1,16,128]{3,2,1,0:T(8,128)}, f32[6,...) custom-call(f32[3,6,6]{2,1,0:T(8,128)} %ub_ref.17, f32[3,6,6]{2,1,0:T(8,128)} %lb_ref.17, ...), custom_call_target="tpu_custom_call" | custom-call | tf_op jit(solution)/shard_map/pallas_call | solution.py:276
  4.8 6.9 %all_to_all.30.w_inc = f32[4,1,768]{2,1,0:T(1,128)} all-to-all(f32[4,1,768]{2,1,0:T(1,128)} %get-tuple-element.26), channel_id=1, replica_groups=mesh['chord'=4,'span'=16,'wall'=4] {'wall'}, dimensions={0} | all-to-all | bytes 24576 | tf_op jit(solution)/shard_map/all_to_all | solution.py:244
  11.6 9.8 %all-to-all-start.1 = ((f32[16,1,448]{2,1,0:T(1,128)}), f32[16,1,448]{2,1,0:T(1,128)S(1)}, u32[]{:S(2)}, u32[]{:S(2)}) async-start(f32[16,1,448]{2,1,0:T(1,128)} %get-tuple-element.27), calls=%async_computation.1 | async-start | bytes 65536 | tf_op jit(solution)/shard_map/all_to_all | solution.py:312
  21.4 3.2 %collective-permute-start = (f32[6,1,16,128]{3,2,1,0:T(8,128)}, f32[6,1,16,128]{3,2,1,0:T(8,128)S(1)}, u32[]{:S(2)}, u32[]{:S(2)}) collective-permute-start(f32[6,1,16,128]{3,2,1,0:T(8,128)} %get-tuple-element.24), channel_id=1, source_target_pairs={{0,64},{64,128},{128,192},{1,65},{65,129},{129,193},{2,66},{66,130... | collective-permute-start | bytes 147464 | tf_op jit(solution)/shard_map/ppermute | solution.py:242
  24.6 2.7 %collective-permute-start.1 = (f32[6,1,16,128]{3,2,1,0:T(8,128)S(1)}, f32[6,1,16,128]{3,2,1,0:T(8,128)S(1)}, u32[]{:S(2)}, u32[]{:S(2)}) collective-permute-start(f32[6,1,16,128]{3,2,1,0:T(8,128)S(1)} %copy-done.17), channel_id=1, source_target_pairs={{64,0},{128,64},{192,128},{65,1},{129,65},{193,129},{66,2},{130,66... | collective-permute-start | bytes 147464 | tf_op jit(solution)/shard_map/ppermute | solution.py:243
  27.3 3.8 %collective-permute-start.2 = (f32[6,8,128]{2,1,0:T(8,128)S(1)}, f32[6,8,128]{2,1,0:T(8,128)S(1)}, u32[]{:S(2)}, u32[]{:S(2)}) collective-permute-start(f32[6,8,128]{2,1,0:T(8,128)S(1)} %copy-done.23), channel_id=1, source_target_pairs={{0,4},{4,8},{8,12},{12,16},{16,20},{20,24},{24,28},{28,32},{32,36}... | collective-permute-start | bytes 73736 | tf_op jit(solution)/shard_map/ppermute | solution.py:242
  33.1 4.1 %shard_map.123 = (f32[6,8,16,128]{3,2,1,0:T(8,128)}, s32[1,1024]{1,0:T(1,128)}) custom-call(f32[3,6,6]{2,1,0:T(8,128)} %ub_ref.17, f32[3,6,6]{2,1,0:T(8,128)} %lb_ref.17, f32[2,6,6]{2,1,0:T(8,128)} %copy.21.ib_ref, s32[1]{0:T(128)} %bitcast.wall_me.rest_0_, f32[6,8,16,128]{3,2,1,0:T(8,128)} %get-tuple-element.23.adj_ref, f32[6,8,16,128]{3,2,1,0:T(8,128)} %sens_ref.7, ...), custom_call_target="tpu_custom_call" | custom-call | tf_op jit(solution)/shard_map/pallas_call | solution.py:314
  37.9 2.3 %shard_map.124 = (f32[6,8,16,128]{3,2,1,0:T(8,128)}, f32[6,1,16,128]{3,2,1,0:T(8,128)}, f32[6,1,16,128]{3,2,1,0:T(8,128)}, f32[6,8,128]{2,1,0:T(8,128)}, f32[6,8,128]{2,1,0:T(8,128)}, /*index=5*/f32[4,1,768]{2,1,0:T(1,128)}) custom-call(f32[3,6,6]{2,1,0:T(8,128)} %ub_ref.17, f32[3,6,6]{2,1,0:T(8,128)} %lb_ref.17, f32[2,6,6]{2,1,0:T(8,128)} %copy.21.ib_ref, ...), custom_call_target="tpu_custom_call" | custom-call | tf_op jit(solution)/shard_map/pallas_call | solution.py:318
  40.2 6.1 %all-to-all-start.2 = ((f32[4,1,768]{2,1,0:T(1,128)}), f32[4,1,768]{2,1,0:T(1,128)S(1)}, u32[]{:S(2)}, u32[]{:S(2)}) async-start(f32[4,1,768]{2,1,0:T(1,128)} %get-tuple-element.34), calls=%async_computation.2 | async-start | bytes 24576 | tf_op jit(solution)/shard_map/all_to_all | solution.py:244
  46.3 3.2 %collective-permute-start.4 = (f32[6,1,16,128]{3,2,1,0:T(8,128)}, f32[6,1,16,128]{3,2,1,0:T(8,128)S(1)}, u32[]{:S(2)}, u32[]{:S(2)}) collective-permute-start(f32[6,1,16,128]{3,2,1,0:T(8,128)} %get-tuple-element.32), channel_id=1, source_target_pairs={{0,64},{64,128},{128,192},{1,65},{65,129},{129,193},{2,66},{66,130... | collective-permute-start | bytes 147464 | tf_op jit(solution)/shard_map/ppermute | solution.py:242
  49.5 2.7 %collective-permute-start.5 = (f32[6,1,16,128]{3,2,1,0:T(8,128)}, f32[6,1,16,128]{3,2,1,0:T(8,128)S(1)}, u32[]{:S(2)}, u32[]{:S(2)}) collective-permute-start(f32[6,1,16,128]{3,2,1,0:T(8,128)} %get-tuple-element.33), channel_id=1, source_target_pairs={{64,0},{128,64},{192,128},{65,1},{129,65},{193,129},{66,2},{130,66... | collective-permute-start | bytes 147464 | tf_op jit(solution)/shard_map/ppermute | solution.py:243
  52.1 2.8 %shard_map.125 = f32[16,1,384]{2,1,0:T(1,128)} custom-call(f32[3,6,6]{2,1,0:T(8,128)} %ub_ref.17, f32[3,6,6]{2,1,0:T(8,128)} %lb_ref.17, f32[2,6,6]{2,1,0:T(8,128)} %copy.21.ib_ref, f32[6,8,16,128]{3,2,1,0:T(8,128)} %get-tuple-element.31.adj_ref, s32[16,64]{1,0:T(8,128)} %bitcast.6, s32[16,64]{1,0:T(8,128)} %bitcast.9, f32[16,64]{1,0:T(8,128)} %bitcast.12), custom_call_target="tpu_custom_call" | custom-call | tf_op jit(solution)/shard_map/pallas_call | solution.py:319
  55.5 10.0 %all-to-all-start.3 = ((f32[16,1,384]{2,1,0:T(1,128)}), f32[16,1,384]{2,1,0:T(1,128)S(1)}, u32[]{:S(2)}, u32[]{:S(2)}) async-start(f32[16,1,384]{2,1,0:T(1,128)} %shard_map.125), calls=%async_computation.3 | async-start | bytes 49152 | tf_op jit(solution)/shard_map/all_to_all | solution.py:312
  65.6 3.8 %collective-permute-start.6 = (f32[6,8,128]{2,1,0:T(8,128)S(1)}, f32[6,8,128]{2,1,0:T(8,128)S(1)}, u32[]{:S(2)}, u32[]{:S(2)}) collective-permute-start(f32[6,8,128]{2,1,0:T(8,128)S(1)} %copy-done.21), channel_id=1, source_target_pairs={{0,4},{4,8},{8,12},{12,16},{16,20},{20,24},{24,28},{28,32},{32,36}... | collective-permute-start | bytes 73736 | tf_op jit(solution)/shard_map/ppermute | solution.py:242
  70.7 3.4 %all-to-all-done.3.inc_ref = f32[16,1,384]{2,1,0:T(1,128)S(1)} async-done(((f32[16,1,384]{2,1,0:T(1,128)}), f32[16,1,384]{2,1,0:T(1,128)S(1)}, u32[]{:S(2)}, u32[]{:S(2)}) %all-to-all-start.3) | async-done | bytes 24608 | tf_op jit(solution)/shard_map/all_to_all | solution.py:312
  74.8 4.1 %shard_map.126.part_ref = f32[6,8,16,128]{3,2,1,0:T(8,128)} custom-call(f32[3,6,6]{2,1,0:T(8,128)} %ub_ref.17, f32[3,6,6]{2,1,0:T(8,128)} %lb_ref.17, f32[2,6,6]{2,1,0:T(8,128)} %copy.21.ib_ref, s32[1]{0:T(128)} %bitcast.wall_me.rest_0_, f32[6,8,16,128]{3,2,1,0:T(8,128)} %get-tuple-element.31.adj_ref, f32[6,8,16,128]{3,2,1,0:T(8,128)} %sens_ref.7, ...), custom_call_target="tpu_custom_call" | custom-call | tf_op jit(solution)/shard_map/pallas_call | solution.py:316
  82.4 4.8 %all-to-all-start.4 = ((f32[4,1,768]{2,1,0:T(1,128)}), f32[4,1,768]{2,1,0:T(1,128)S(1)}, u32[]{:S(2)}, u32[]{:S(2)}) async-start(f32[4,1,768]{2,1,0:T(1,128)} %get-tuple-element.41), calls=%async_computation.4 | async-start | bytes 24576 | tf_op jit(solution)/shard_map/all_to_all | solution.py:244
  87.2 3.2 %collective-permute-start.8 = (f32[6,1,16,128]{3,2,1,0:T(8,128)}, f32[6,1,16,128]{3,2,1,0:T(8,128)S(1)}, u32[]{:S(2)}, u32[]{:S(2)}) collective-permute-start(f32[6,1,16,128]{3,2,1,0:T(8,128)} %get-tuple-element.39), channel_id=1, source_target_pairs={{0,64},{64,128},{128,192},{1,65},{65,129},{129,193},{2,66},{66,130... | collective-permute-start | bytes 147464 | tf_op jit(solution)/shard_map/ppermute | solution.py:242
  90.4 2.7 %collective-permute-start.9 = (f32[6,1,16,128]{3,2,1,0:T(8,128)}, f32[6,1,16,128]{3,2,1,0:T(8,128)S(1)}, u32[]{:S(2)}, u32[]{:S(2)}) collective-permute-start(f32[6,1,16,128]{3,2,1,0:T(8,128)} %get-tuple-element.40), channel_id=1, source_target_pairs={{64,0},{128,64},{192,128},{65,1},{129,65},{193,129},{66,2},{130,66... | collective-permute-start | bytes 147464 | tf_op jit(solution)/shard_map/ppermute | solution.py:243
  93.1 2.8 %shard_map.128 = f32[16,1,384]{2,1,0:T(1,128)} custom-call(f32[3,6,6]{2,1,0:T(8,128)} %ub_ref.17, f32[3,6,6]{2,1,0:T(8,128)} %lb_ref.17, f32[2,6,6]{2,1,0:T(8,128)} %copy.21.ib_ref, f32[6,8,16,128]{3,2,1,0:T(8,128)} %get-tuple-element.38.adj_ref, s32[16,64]{1,0:T(8,128)} %bitcast.7, s32[16,64]{1,0:T(8,128)} %bitcast.10, f32[16,64]{1,0:T(8,128)} %bitcast.13), custom_call_target="tpu_custom_call" | custom-call | tf_op jit(solution)/shard_map/pallas_call | solution.py:319
  96.5 6.6 %all-to-all-start.5 = ((f32[16,1,384]{2,1,0:T(1,128)}), f32[16,1,384]{2,1,0:T(1,128)S(1)}, u32[]{:S(2)}, u32[]{:S(2)}) async-start(f32[16,1,384]{2,1,0:T(1,128)} %shard_map.128), calls=%async_computation.5 | async-start | bytes 49152 | tf_op jit(solution)/shard_map/all_to_all | solution.py:312
  103.1 3.8 %collective-permute-start.10 = (f32[6,8,128]{2,1,0:T(8,128)S(1)}, f32[6,8,128]{2,1,0:T(8,128)S(1)}, u32[]{:S(2)}, u32[]{:S(2)}) collective-permute-start(f32[6,8,128]{2,1,0:T(8,128)S(1)} %copy-done.20), channel_id=1, source_target_pairs={{0,4},{4,8},{8,12},{12,16},{16,20},{20,24},{24,28},{28,32},{32,36}... | collective-permute-start | bytes 73736 | tf_op jit(solution)/shard_map/ppermute | solution.py:242
  108.3 3.4 %all-to-all-done.5.inc_ref = f32[16,1,384]{2,1,0:T(1,128)S(1)} async-done(((f32[16,1,384]{2,1,0:T(1,128)}), f32[16,1,384]{2,1,0:T(1,128)S(1)}, u32[]{:S(2)}, u32[]{:S(2)}) %all-to-all-start.5) | async-done | bytes 24608 | tf_op jit(solution)/shard_map/all_to_all | solution.py:312
  113.0 4.1 %shard_map.129.part_ref = f32[6,8,16,128]{3,2,1,0:T(8,128)} custom-call(f32[3,6,6]{2,1,0:T(8,128)} %ub_ref.17, f32[3,6,6]{2,1,0:T(8,128)} %lb_ref.17, f32[2,6,6]{2,1,0:T(8,128)} %copy.21.ib_ref, s32[1]{0:T(128)} %bitcast.wall_me.rest_0_, f32[6,8,16,128]{3,2,1,0:T(8,128)} %get-tuple-element.38.adj_ref, f32[6,8,16,128]{3,2,1,0:T(8,128)} %sens_ref.7, ...), custom_call_target="tpu_custom_call" | custom-call | tf_op jit(solution)/shard_map/pallas_call | solution.py:316
  (69 shorter events, 16.4 us)
Async XLA Ops:
  4.8 19.8 %copy-start.17 = (f32[6,1,16,128]{3,2,1,0:T(8,128)S(1)}, f32[6,1,16,128]{3,2,1,0:T(8,128)}, u32[]{:S(2)}) copy-start(f32[6,1,16,128]{3,2,1,0:T(8,128)} %get-tuple-element.25) | copy-start | bytes 147460
  11.6 15.6 %copy-start.23 = (f32[6,8,128]{2,1,0:T(8,128)S(1)}, f32[6,8,128]{2,1,0:T(8,128)}, u32[]{:S(2)}) copy-start(f32[6,8,128]{2,1,0:T(8,128)} %get-tuple-element.29) | copy-start | bytes 73732
  11.6 19.5 %copy-start.22 = (f32[6,8,128]{2,1,0:T(8,128)S(1)}, f32[6,8,128]{2,1,0:T(8,128)}, u32[]{:S(2)}) copy-start(f32[6,8,128]{2,1,0:T(8,128)} %get-tuple-element.30) | copy-start | bytes 73732
  11.6 20.8 %all-to-all-start.1 = ((f32[16,1,448]{2,1,0:T(1,128)}), f32[16,1,448]{2,1,0:T(1,128)S(1)}, u32[]{:S(2)}, u32[]{:S(2)}) async-start(f32[16,1,448]{2,1,0:T(1,128)} %get-tuple-element.27), calls=%async_computation.1 | async-start | bytes 65536 | tf_op jit(solution)/shard_map/all_to_all | solution.py:312
  21.4 11.0 %collective-permute-start = (f32[6,1,16,128]{3,2,1,0:T(8,128)}, f32[6,1,16,128]{3,2,1,0:T(8,128)S(1)}, u32[]{:S(2)}, u32[]{:S(2)}) collective-permute-start(f32[6,1,16,128]{3,2,1,0:T(8,128)} %get-tuple-element.24), channel_id=1, source_target_pairs={{0,64},{64,128},{128,192},{1,65},{65,129},{129,193},{2,66},{66,130... | collective-permute-start | bytes 147464 | tf_op jit(solution)/shard_map/ppermute | solution.py:242
  24.6 7.8 %collective-permute-start.1 = (f32[6,1,16,128]{3,2,1,0:T(8,128)S(1)}, f32[6,1,16,128]{3,2,1,0:T(8,128)S(1)}, u32[]{:S(2)}, u32[]{:S(2)}) collective-permute-start(f32[6,1,16,128]{3,2,1,0:T(8,128)S(1)} %copy-done.17), channel_id=1, source_target_pairs={{64,0},{128,64},{192,128},{65,1},{129,65},{193,129},{66,2},{130,66... | collective-permute-start | bytes 147464 | tf_op jit(solution)/shard_map/ppermute | solution.py:243
  27.3 9.9 %collective-permute-start.2 = (f32[6,8,128]{2,1,0:T(8,128)S(1)}, f32[6,8,128]{2,1,0:T(8,128)S(1)}, u32[]{:S(2)}, u32[]{:S(2)}) collective-permute-start(f32[6,8,128]{2,1,0:T(8,128)S(1)} %copy-done.23), channel_id=1, source_target_pairs={{0,4},{4,8},{8,12},{12,16},{16,20},{20,24},{24,28},{28,32},{32,36}... | collective-permute-start | bytes 73736 | tf_op jit(solution)/shard_map/ppermute | solution.py:242
  31.1 6.1 %collective-permute-start.3 = (f32[6,8,128]{2,1,0:T(8,128)S(1)}, f32[6,8,128]{2,1,0:T(8,128)S(1)}, u32[]{:S(2)}, u32[]{:S(2)}) collective-permute-start(f32[6,8,128]{2,1,0:T(8,128)S(1)} %copy-done.22), channel_id=1, source_target_pairs={{4,0},{8,4},{12,8},{16,12},{20,16},{24,20},{28,24},{32,28},{36,32}... | collective-permute-start | bytes 73736 | tf_op jit(solution)/shard_map/ppermute | solution.py:243
  40.2 14.7 %all-to-all-start.2 = ((f32[4,1,768]{2,1,0:T(1,128)}), f32[4,1,768]{2,1,0:T(1,128)S(1)}, u32[]{:S(2)}, u32[]{:S(2)}) async-start(f32[4,1,768]{2,1,0:T(1,128)} %get-tuple-element.34), calls=%async_computation.2 | async-start | bytes 24576 | tf_op jit(solution)/shard_map/all_to_all | solution.py:244
  46.3 27.9 %collective-permute-start.4 = (f32[6,1,16,128]{3,2,1,0:T(8,128)}, f32[6,1,16,128]{3,2,1,0:T(8,128)S(1)}, u32[]{:S(2)}, u32[]{:S(2)}) collective-permute-start(f32[6,1,16,128]{3,2,1,0:T(8,128)} %get-tuple-element.32), channel_id=1, source_target_pairs={{0,64},{64,128},{128,192},{1,65},{65,129},{129,193},{2,66},{66,130... | collective-permute-start | bytes 147464 | tf_op jit(solution)/shard_map/ppermute | solution.py:242
  49.5 24.7 %collective-permute-start.5 = (f32[6,1,16,128]{3,2,1,0:T(8,128)}, f32[6,1,16,128]{3,2,1,0:T(8,128)S(1)}, u32[]{:S(2)}, u32[]{:S(2)}) collective-permute-start(f32[6,1,16,128]{3,2,1,0:T(8,128)} %get-tuple-element.33), channel_id=1, source_target_pairs={{64,0},{128,64},{192,128},{65,1},{129,65},{193,129},{66,2},{130,66... | collective-permute-start | bytes 147464 | tf_op jit(solution)/shard_map/ppermute | solution.py:243
  54.9 10.7 %copy-start.21 = (f32[6,8,128]{2,1,0:T(8,128)S(1)}, f32[6,8,128]{2,1,0:T(8,128)}, u32[]{:S(2)}) copy-start(f32[6,8,128]{2,1,0:T(8,128)} %get-tuple-element.36) | copy-start | bytes 73732
  54.9 14.5 %copy-start.19 = (f32[6,8,128]{2,1,0:T(8,128)S(1)}, f32[6,8,128]{2,1,0:T(8,128)}, u32[]{:S(2)}) copy-start(f32[6,8,128]{2,1,0:T(8,128)} %get-tuple-element.37) | copy-start | bytes 73732
  55.5 18.7 %all-to-all-start.3 = ((f32[16,1,384]{2,1,0:T(1,128)}), f32[16,1,384]{2,1,0:T(1,128)S(1)}, u32[]{:S(2)}, u32[]{:S(2)}) async-start(f32[16,1,384]{2,1,0:T(1,128)} %shard_map.125), calls=%async_computation.3 | async-start | bytes 49152 | tf_op jit(solution)/shard_map/all_to_all | solution.py:312
  65.6 13.4 %collective-permute-start.6 = (f32[6,8,128]{2,1,0:T(8,128)S(1)}, f32[6,8,128]{2,1,0:T(8,128)S(1)}, u32[]{:S(2)}, u32[]{:S(2)}) collective-permute-start(f32[6,8,128]{2,1,0:T(8,128)S(1)} %copy-done.21), channel_id=1, source_target_pairs={{0,4},{4,8},{8,12},{12,16},{16,20},{20,24},{24,28},{28,32},{32,36}... | collective-permute-start | bytes 73736 | tf_op jit(solution)/shard_map/ppermute | solution.py:242
  69.4 9.5 %collective-permute-start.7 = (f32[6,8,128]{2,1,0:T(8,128)S(1)}, f32[6,8,128]{2,1,0:T(8,128)S(1)}, u32[]{:S(2)}, u32[]{:S(2)}) collective-permute-start(f32[6,8,128]{2,1,0:T(8,128)S(1)} %copy-done.19), channel_id=1, source_target_pairs={{4,0},{8,4},{12,8},{16,12},{20,16},{24,20},{28,24},{32,28},{36,32}... | collective-permute-start | bytes 73736 | tf_op jit(solution)/shard_map/ppermute | solution.py:243
  82.4 13.4 %all-to-all-start.4 = ((f32[4,1,768]{2,1,0:T(1,128)}), f32[4,1,768]{2,1,0:T(1,128)S(1)}, u32[]{:S(2)}, u32[]{:S(2)}) async-start(f32[4,1,768]{2,1,0:T(1,128)} %get-tuple-element.41), calls=%async_computation.4 | async-start | bytes 24576 | tf_op jit(solution)/shard_map/all_to_all | solution.py:244
  87.2 24.5 %collective-permute-start.8 = (f32[6,1,16,128]{3,2,1,0:T(8,128)}, f32[6,1,16,128]{3,2,1,0:T(8,128)S(1)}, u32[]{:S(2)}, u32[]{:S(2)}) collective-permute-start(f32[6,1,16,128]{3,2,1,0:T(8,128)} %get-tuple-element.39), channel_id=1, source_target_pairs={{0,64},{64,128},{128,192},{1,65},{65,129},{129,193},{2,66},{66,130... | collective-permute-start | bytes 147464 | tf_op jit(solution)/shard_map/ppermute | solution.py:242
  90.4 21.3 %collective-permute-start.9 = (f32[6,1,16,128]{3,2,1,0:T(8,128)}, f32[6,1,16,128]{3,2,1,0:T(8,128)S(1)}, u32[]{:S(2)}, u32[]{:S(2)}) collective-permute-start(f32[6,1,16,128]{3,2,1,0:T(8,128)} %get-tuple-element.40), channel_id=1, source_target_pairs={{64,0},{128,64},{192,128},{65,1},{129,65},{193,129},{66,2},{130,66... | collective-permute-start | bytes 147464 | tf_op jit(solution)/shard_map/ppermute | solution.py:243
  95.9 7.2 %copy-start.20 = (f32[6,8,128]{2,1,0:T(8,128)S(1)}, f32[6,8,128]{2,1,0:T(8,128)}, u32[]{:S(2)}) copy-start(f32[6,8,128]{2,1,0:T(8,128)} %get-tuple-element.42) | copy-start | bytes 73732
  95.9 11.1 %copy-start.18 = (f32[6,8,128]{2,1,0:T(8,128)S(1)}, f32[6,8,128]{2,1,0:T(8,128)}, u32[]{:S(2)}) copy-start(f32[6,8,128]{2,1,0:T(8,128)} %get-tuple-element.43) | copy-start | bytes 73732
  96.5 15.2 %all-to-all-start.5 = ((f32[16,1,384]{2,1,0:T(1,128)}), f32[16,1,384]{2,1,0:T(1,128)S(1)}, u32[]{:S(2)}, u32[]{:S(2)}) async-start(f32[16,1,384]{2,1,0:T(1,128)} %shard_map.128), calls=%async_computation.5 | async-start | bytes 49152 | tf_op jit(solution)/shard_map/all_to_all | solution.py:312
  103.1 14.0 %collective-permute-start.10 = (f32[6,8,128]{2,1,0:T(8,128)S(1)}, f32[6,8,128]{2,1,0:T(8,128)S(1)}, u32[]{:S(2)}, u32[]{:S(2)}) collective-permute-start(f32[6,8,128]{2,1,0:T(8,128)S(1)} %copy-done.20), channel_id=1, source_target_pairs={{0,4},{4,8},{8,12},{12,16},{16,20},{20,24},{24,28},{28,32},{32,36}... | collective-permute-start | bytes 73736 | tf_op jit(solution)/shard_map/ppermute | solution.py:242
  107.0 10.1 %collective-permute-start.11 = (f32[6,8,128]{2,1,0:T(8,128)S(1)}, f32[6,8,128]{2,1,0:T(8,128)S(1)}, u32[]{:S(2)}, u32[]{:S(2)}) collective-permute-start(f32[6,8,128]{2,1,0:T(8,128)S(1)} %copy-done.18), channel_id=1, source_target_pairs={{4,0},{8,4},{12,8},{16,12},{20,16},{24,20},{28,24},{32,28},{36,32}... | collective-permute-start | bytes 73736 | tf_op jit(solution)/shard_map/ppermute | solution.py:243
  (17 other events, 10.4 us)

commit v12 on v9

--- a/solution.py
+++ b/solution.py
@@ -70,11 +70,14 @@
 
 
 def write_faces(adj, faces):
-    c_lo, c_hi, s_lo, s_hi, w_buf, wall_me = faces
+    c_buf, chord_me, s_lo, s_hi, w_buf, wall_me = faces
     nx, ny, nz = adj.shape[1], adj.shape[2], adj.shape[3]
     j_idx = lax.broadcasted_iota(jnp.int32, adj.shape, 2)
-    c_lo[...] = adj[:, 0:1]
-    c_hi[...] = adj[:, nx - 1:nx]
+    cm = chord_me[0]
+    c_lo = adj[:, 0]
+    c_hi = adj[:, nx - 1]
+    for t in range(c_buf.shape[0]):
+        c_buf[t] = jnp.where(cm + 1 == t, c_hi, jnp.where(cm - 1 == t, c_lo, 0.0))
     s_lo[...] = jnp.sum(jnp.where(j_idx == 0, adj, 0.0), axis=2)
     s_hi[...] = jnp.sum(jnp.where(j_idx == ny - 1, adj, 0.0), axis=2)
     lo, hi = wall_columns(adj)
@@ -84,6 +87,18 @@
     hi = jnp.concatenate([hi[v:v + 1] for v in range(hi.shape[0])], axis=1)
     for t in range(n_wall):
         w_buf[t] = jnp.where(me + 1 == t, hi, jnp.where(me - 1 == t, lo, 0.0))
+
+
+def chord_halos(c_inc, chord_me):
+    me = chord_me[0]
+    below = None
+    above = None
+    for t in range(c_inc.shape[0]):
+        b = jnp.where(me - 1 == t, c_inc[t], 0.0)
+        a = jnp.where(me + 1 == t, c_inc[t], 0.0)
+        below = b if below is None else below + b
+        above = a if above is None else above + a
+    return below[:, None], above[:, None]
 
 
 def wall_halos(w_inc, wall_me, n_var):
@@ -101,15 +116,15 @@
     return unflat(below), unflat(above)
 
 
-def init_kernel(ub_ref, lb_ref, ib_ref, wall_me, sens_ref, diag_ref, send_ref, orient_ref, weight_ref, tgt_ref,
-                adj_ref, rows_ref, c_lo, c_hi, s_lo, s_hi, w_buf):
+def init_kernel(ub_ref, lb_ref, ib_ref, wall_me, chord_me, sens_ref, diag_ref, send_ref, orient_ref, weight_ref,
+                tgt_ref, adj_ref, rows_ref, c_buf, s_lo, s_hi, w_buf):
     n_var = sens_ref.shape[0]
     lanes = sens_ref.shape[3]
     slots = send_ref.shape[1]
     blk_ref = (ub_ref, lb_ref, ib_ref)
     adj = sens_ref[...] / diag_ref[...]
     adj_ref[...] = adj
-    write_faces(adj, (c_lo, c_hi, s_lo, s_hi, w_buf, wall_me))
+    write_faces(adj, (c_buf, chord_me, s_lo, s_hi, w_buf, wall_me))
     pieces = gather_rows(adj, send_ref, orient_ref, weight_ref, blk_ref, n_var, lanes)
     to_chunks(rows_ref, pieces + [flat_row(tgt_ref[...]).astype(F32)], slots)
 
@@ -160,7 +175,7 @@
 
 
 def make_part_a(first, slots):
-    def kernel(ub_ref, lb_ref, ib_ref, wall_me, adj_ref, sens_ref, diag_ref, face_ref, hcl, hch, w_inc,
+    def kernel(ub_ref, lb_ref, ib_ref, wall_me, chord_me, adj_ref, sens_ref, diag_ref, face_ref, c_inc, w_inc,
                inc_ref, *rest):
         if first:
             out_ref, tgt_out = rest
@@ -177,7 +192,7 @@
             got = from_chunks(inc, n_var, slots)
             cell = tgt_ref[...]
         none = jnp.zeros((n_var, nx, nz), F32)
-        halos = (hcl[...], hch[...], none, none) + wall_halos(w_inc[...], wall_me, n_var)
+        halos = chord_halos(c_inc[...], chord_me) + (none, none) + wall_halos(w_inc[...], wall_me, n_var)
         out_ref[...] = sweep_body(blk_ref, adj_ref[...], sens_ref[...], diag_ref[...], face_ref[...], halos,
                                   jnp.concatenate(got[:n_var], axis=0), cell)
     return kernel
@@ -210,26 +225,26 @@
             out_ref[...] = new
             grad_ref[...] = prod_ref[...] * new[n_var - 1]
         else:
-            send_ref, orient_ref, weight_ref, wall_me, out_ref, rows_ref, c_lo, c_hi, s_lo, s_hi, w_buf = rest
+            send_ref, orient_ref, weight_ref, wall_me, chord_me, out_ref, rows_ref, c_buf, s_lo, s_hi, w_buf = rest
             out_ref[...] = new
-            write_faces(new, (c_lo, c_hi, s_lo, s_hi, w_buf, wall_me))
+            write_faces(new, (c_buf, chord_me, s_lo, s_hi, w_buf, wall_me))
             blk_ref = (ub_ref, lb_ref, ib_ref)
             to_chunks(rows_ref, gather_rows(new, send_ref, orient_ref, weight_ref, blk_ref, n_var, nz), slots)
     return kernel
 
 
-def face_shapes(shape, n_wall):
+def face_shapes(shape, n_wall, n_chord):
     n_var, nx, ny, nz = shape
-    c = jax.ShapeDtypeStruct((n_var, 1, ny, nz), F32)
+    c = jax.ShapeDtypeStruct((n_chord, n_var, ny, nz), F32)
     s = jax.ShapeDtypeStruct((n_var, nx, nz), F32)
     w = jax.ShapeDtypeStruct((n_wall, 1, n_var * nx * ny), F32)
-    return [c, c, s, s, w]
+    return [c, s, s, w]
 
 
 def exchange(faces):
-    c_lo, c_hi, s_lo, s_hi, w_buf = faces
-    out = []
-    for axis, lo_face, hi_face in (("chord", c_lo, c_hi), ("span", s_lo, s_hi)):
+    c_buf, s_lo, s_hi, w_buf = faces
+    out = [lax.all_to_all(c_buf, "chord", split_axis=0, concat_axis=0, tiled=True)]
+    for axis, lo_face, hi_face in (("span", s_lo, s_hi),):
         count = lax.axis_size(axis)
         forward = [(i, i + 1) for i in range(count - 1)]
         backward = [(i + 1, i) for i in range(count - 1)]
@@ -247,8 +262,10 @@
     n_rows = n_span * slots
     shape = sensitivity.shape
     n_wall = lax.axis_size("wall")
+    n_chord = lax.axis_size("chord")
     wall_me = lax.axis_index("wall").astype(jnp.int32).reshape(1)
-    blk = (upper_blocks, lower_blocks, iface_blocks, wall_me)
+    chord_me = lax.axis_index("chord").astype(jnp.int32).reshape(1)
+    blk = (upper_blocks, lower_blocks, iface_blocks, wall_me, chord_me)
     send_row = send_cell.reshape(n_span, slots)
     orient_row = orient.reshape(n_span, slots)
     weight_row = iface_weight.reshape(n_span, slots)
@@ -263,29 +280,29 @@
 
     init = pl.pallas_call(
         init_kernel,
-        out_shape=[adj_sds, first_rows] + face_shapes(shape, n_wall),
-        in_specs=[smem] * 4 + [vmem] * 6,
-        out_specs=[vmem] * 7,
+        out_shape=[adj_sds, first_rows] + face_shapes(shape, n_wall, n_chord),
+        in_specs=[smem] * 5 + [vmem] * 6,
+        out_specs=[vmem] * 6,
     )
     adj, rows, *faces = init(*blk, sensitivity, diagonal, send_row, orient_row, weight_row, target_row)
 
     part_a_first = pl.pallas_call(
         make_part_a(True, slots),
         out_shape=[adj_sds, tgt_sds],
-        in_specs=[smem] * 4 + [vmem] * 8,
+        in_specs=[smem] * 5 + [vmem] * 7,
         out_specs=[vmem] * 2,
     )
     part_a = pl.pallas_call(
         make_part_a(False, slots),
         out_shape=adj_sds,
-        in_specs=[smem] * 4 + [vmem] * 9,
+        in_specs=[smem] * 5 + [vmem] * 8,
         out_specs=vmem,
     )
     part_b = pl.pallas_call(
         make_part_b(False, slots),
-        out_shape=[adj_sds, rows_sds] + face_shapes(shape, n_wall),
-        in_specs=[smem] * 3 + [vmem] * 8 + [smem],
-        out_specs=[vmem] * 7,
+        out_shape=[adj_sds, rows_sds] + face_shapes(shape, n_wall, n_chord),
+        in_specs=[smem] * 3 + [vmem] * 8 + [smem] * 2,
+        out_specs=[vmem] * 6,
     )
     part_b_last = pl.pallas_call(
         make_part_b(True, slots),
@@ -293,18 +310,18 @@
         in_specs=[smem] * 3 + [vmem] * 6,
         out_specs=[vmem] * 2,
     )
-    ub, lb, ib, _ = blk
+    ub, lb, ib, _, _ = blk
     received = None
     for sweep in range(SWEEPS):
-        hcl, hch, hsl, hsh, w_inc = exchange(faces)
+        c_inc, hsl, hsh, w_inc = exchange(faces)
         incoming = lax.all_to_all(rows, "span", split_axis=0, concat_axis=0, tiled=True)
         if sweep == 0:
-            partial, received = part_a_first(*blk, adj, sensitivity, diagonal, face_coef, hcl, hch, w_inc, incoming)
-        else:
-            partial = part_a(*blk, adj, sensitivity, diagonal, face_coef, hcl, hch, w_inc, incoming, received)
+            partial, received = part_a_first(*blk, adj, sensitivity, diagonal, face_coef, c_inc, w_inc, incoming)
+        else:
+            partial = part_a(*blk, adj, sensitivity, diagonal, face_coef, c_inc, w_inc, incoming, received)
         if sweep < SWEEPS - 1:
             adj, rows, *faces = part_b(ub, lb, ib, partial, diagonal, face_coef, hsl, hsh,
-                                       send_row, orient_row, weight_row, wall_me)
+                                       send_row, orient_row, weight_row, wall_me, chord_me)
         else:
             adj, gradient = part_b_last(ub, lb, ib, partial, diagonal, face_coef, hsl, hsh, production)
     return (adj, gradient)

time: 117 us -> 136 us (1.16)
  the two profiles are of different devices: /device:TPU:12 before, /device:TPU:40 now
where the time goes in v12:
time: 136 us; the launch traced here: 134 us
  blocking collectives  68.4 us (50%)
  starting transfers between devices  35.1 us (26%)
  Pallas kernels  23.8 us (18%)
  local copies, waits for them, and re-layouts  6.29 us (5%)
    all_to_all x3, blocking collectives, local(): lax.all_to_all(rows, 'span', split_axis=0, concat_axis=0, tiled=True)  40.1 us
    all_to_all x3, blocking collectives, exchange(): lax.all_to_all(w_buf, 'wall', split_axis=0, concat_axis=0, tiled=True)  28.3 us
    all_to_all x3, starting transfers between devices, exchange(): lax.all_to_all(c_buf, 'chord', split_axis=0, concat_axis=0, tiled=True)  14.9 us
    ppermute x3, starting transfers between devices, exchange(): out.append(lax.ppermute(lo_face, axis, backward))  12.8 us
    pallas_call x2, Pallas kernels, local(): part_a(*blk, adj, sensitivity, diagonal, face_coef, c_inc, w_inc, incomin...  8.37 us
    ppermute x3, starting transfers between devices, exchange(): out.append(lax.ppermute(hi_face, axis, forward))  7.43 us
    unnamed x37, local copies, waits for them, and re-layouts  6.29 us
    pallas_call x2, Pallas kernels, local(): part_b(ub, lb, ib, partial, diagonal, face_coef, hsl, hsh, send_row, orie...  6.12 us
  transfers between devices with their start and end apart: 9, of which 0 were waited for; matrix products, arithmetic and copies ran while one was open for 0% of the time, Pallas kernels for 9%

profile of v12, /device:TPU:40, one launch (start us, length us, event | category | flops | bytes accessed | tf_op | source)
XLA Modules:
  0.0 134.4 jit_solution(6786696137176253290)
XLA Ops:
  0.6 0.7 copy-done.11
  1.9 2.9 %shard_map.122 = (f32[6,8,16,128]{3,2,1,0:T(8,128)}, f32[16,1,448]{2,1,0:T(1,128)}, f32[4,6,16,128]{3,2,1,0:T(8,128)}, f32[6,8,128]{2,1,0:T(8,128)}, f32[6,8,128]{2,1,0:T(8,128)}, /*index=5*/f32[4,1,768]{2,1,0:T(1,128)}) custom-call(f32[3,6,6]{2,1,0:T(8,128)} %ub_ref.13, f32[3,6,6]{2,1,0:T(8,128)} %lb_ref.13, f32[2,6,6]{2,1,0:T(8,128)} %copy.19.ib_ref, ...), custom_call_target="tpu_custom_call" | custom-call | tf_op jit(solution)/shard_map/pallas_call | solution.py:287
  4.8 9.7 %all_to_all.45.w_inc = f32[4,1,768]{2,1,0:T(1,128)} all-to-all(f32[4,1,768]{2,1,0:T(1,128)} %get-tuple-element.24), channel_id=1, replica_groups=mesh['chord'=4,'span'=16,'wall'=4] {'wall'}, dimensions={0} | all-to-all | bytes 24576 | tf_op jit(solution)/shard_map/all_to_all | solution.py:253
  14.6 16.4 %all_to_all.46.inc_ref = f32[16,1,448]{2,1,0:T(1,128)} all-to-all(f32[16,1,448]{2,1,0:T(1,128)} %get-tuple-element.25), channel_id=1, replica_groups=mesh['chord'=4,'span'=16,'wall'=4] {'span'}, dimensions={0} | all-to-all | bytes 57344 | tf_op jit(solution)/shard_map/all_to_all | solution.py:317
  31.0 5.0 %all-to-all-start = ((f32[4,6,16,128]{3,2,1,0:T(8,128)}), f32[4,6,16,128]{3,2,1,0:T(8,128)S(1)}, u32[]{:S(2)}, u32[]{:S(2)}) async-start(f32[4,6,16,128]{3,2,1,0:T(8,128)} %get-tuple-element.23), calls=%async_computation | async-start | bytes 393216 | tf_op jit(solution)/shard_map/all_to_all | solution.py:246
  36.1 2.5 %collective-permute-start = (f32[6,8,128]{2,1,0:T(8,128)S(1)}, f32[6,8,128]{2,1,0:T(8,128)S(1)}, u32[]{:S(2)}, u32[]{:S(2)}) collective-permute-start(f32[6,8,128]{2,1,0:T(8,128)S(1)} %copy-done.17), channel_id=1, source_target_pairs={{0,4},{4,8},{8,12},{12,16},{16,20},{20,24},{24,28},{28,32},{32,36}... | collective-permute-start | bytes 73736 | tf_op jit(solution)/shard_map/ppermute | solution.py:251
  38.6 4.2 %collective-permute-start.1 = (f32[6,8,128]{2,1,0:T(8,128)S(1)}, f32[6,8,128]{2,1,0:T(8,128)S(1)}, u32[]{:S(2)}, u32[]{:S(2)}) collective-permute-start(f32[6,8,128]{2,1,0:T(8,128)S(1)} %copy-done.15), channel_id=1, source_target_pairs={{4,0},{8,4},{12,8},{16,12},{20,16},{24,20},{28,24},{32,28},{36,32}... | collective-permute-start | bytes 73736 | tf_op jit(solution)/shard_map/ppermute | solution.py:252
  43.5 4.2 %shard_map.123 = (f32[6,8,16,128]{3,2,1,0:T(8,128)}, s32[1,1024]{1,0:T(1,128)}) custom-call(f32[3,6,6]{2,1,0:T(8,128)} %ub_ref.13, f32[3,6,6]{2,1,0:T(8,128)} %lb_ref.13, f32[2,6,6]{2,1,0:T(8,128)} %copy.19.ib_ref, s32[1]{0:T(128)} %bitcast.wall_me.rest_3_, s32[1]{0:T(128)} %bitcast.1.chord_me.rest_4_, f32[6,8,16,128]{3,2,1,0:T(8,128)} %get-tuple-element.22.adj_ref, ...), custom_call_target="tpu_custom_call" | custom-call | tf_op jit(solution)/shard_map/pallas_call | solution.py:319
  48.3 3.1 %shard_map.124 = (f32[6,8,16,128]{3,2,1,0:T(8,128)}, f32[16,1,384]{2,1,0:T(1,128)}, f32[4,6,16,128]{3,2,1,0:T(8,128)}, f32[6,8,128]{2,1,0:T(8,128)}, f32[6,8,128]{2,1,0:T(8,128)}, /*index=5*/f32[4,1,768]{2,1,0:T(1,128)}) custom-call(f32[3,6,6]{2,1,0:T(8,128)} %ub_ref.13, f32[3,6,6]{2,1,0:T(8,128)} %lb_ref.13, f32[2,6,6]{2,1,0:T(8,128)} %copy.19.ib_ref, ...), custom_call_target="tpu_custom_call" | custom-call | tf_op jit(solution)/shard_map/pallas_call | solution.py:323
  51.4 9.3 %all_to_all.47.w_inc = f32[4,1,768]{2,1,0:T(1,128)} all-to-all(f32[4,1,768]{2,1,0:T(1,128)} %get-tuple-element.31), channel_id=1, replica_groups=mesh['chord'=4,'span'=16,'wall'=4] {'wall'}, dimensions={0} | all-to-all | bytes 24576 | tf_op jit(solution)/shard_map/all_to_all | solution.py:253
  60.7 11.8 %all_to_all.48.inc_ref = f32[16,1,384]{2,1,0:T(1,128)} all-to-all(f32[16,1,384]{2,1,0:T(1,128)S(1)} %copy-done.3), channel_id=1, replica_groups=mesh['chord'=4,'span'=16,'wall'=4] {'span'}, dimensions={0} | all-to-all | bytes 49152 | tf_op jit(solution)/shard_map/all_to_all | solution.py:317
  72.5 4.9 %all-to-all-start.3 = ((f32[4,6,16,128]{3,2,1,0:T(8,128)}), f32[4,6,16,128]{3,2,1,0:T(8,128)S(1)}, u32[]{:S(2)}, u32[]{:S(2)}) async-start(f32[4,6,16,128]{3,2,1,0:T(8,128)} %get-tuple-element.30), calls=%async_computation.3 | async-start | bytes 393216 | tf_op jit(solution)/shard_map/all_to_all | solution.py:246
  77.5 2.5 %collective-permute-start.2 = (f32[6,8,128]{2,1,0:T(8,128)S(1)}, f32[6,8,128]{2,1,0:T(8,128)S(1)}, u32[]{:S(2)}, u32[]{:S(2)}) collective-permute-start(f32[6,8,128]{2,1,0:T(8,128)S(1)} %copy-done.16), channel_id=1, source_target_pairs={{0,4},{4,8},{8,12},{12,16},{16,20},{20,24},{24,28},{28,32},{32,36}... | collective-permute-start | bytes 73736 | tf_op jit(solution)/shard_map/ppermute | solution.py:251
  79.9 4.3 %collective-permute-start.3 = (f32[6,8,128]{2,1,0:T(8,128)S(1)}, f32[6,8,128]{2,1,0:T(8,128)S(1)}, u32[]{:S(2)}, u32[]{:S(2)}) collective-permute-start(f32[6,8,128]{2,1,0:T(8,128)S(1)} %copy-done.13), channel_id=1, source_target_pairs={{4,0},{8,4},{12,8},{16,12},{20,16},{24,20},{28,24},{32,28},{36,32}... | collective-permute-start | bytes 73736 | tf_op jit(solution)/shard_map/ppermute | solution.py:252
  84.9 4.2 %shard_map.125.part_ref = f32[6,8,16,128]{3,2,1,0:T(8,128)} custom-call(f32[3,6,6]{2,1,0:T(8,128)} %ub_ref.13, f32[3,6,6]{2,1,0:T(8,128)} %lb_ref.13, f32[2,6,6]{2,1,0:T(8,128)} %copy.19.ib_ref, s32[1]{0:T(128)} %bitcast.wall_me.rest_3_, s32[1]{0:T(128)} %bitcast.1.chord_me.rest_4_, f32[6,8,16,128]{3,2,1,0:T(8,128)} %get-tuple-element.29.adj_ref, ...), custom_call_target="tpu_custom_call" | custom-call | tf_op jit(solution)/shard_map/pallas_call | solution.py:321
  90.3 3.1 %shard_map.126 = (f32[6,8,16,128]{3,2,1,0:T(8,128)}, f32[16,1,384]{2,1,0:T(1,128)}, f32[4,6,16,128]{3,2,1,0:T(8,128)}, f32[6,8,128]{2,1,0:T(8,128)}, f32[6,8,128]{2,1,0:T(8,128)}, /*index=5*/f32[4,1,768]{2,1,0:T(1,128)}) custom-call(f32[3,6,6]{2,1,0:T(8,128)} %ub_ref.13, f32[3,6,6]{2,1,0:T(8,128)} %lb_ref.13, f32[2,6,6]{2,1,0:T(8,128)} %copy.19.ib_ref, ...), custom_call_target="tpu_custom_call" | custom-call | tf_op jit(solution)/shard_map/pallas_call | solution.py:323
  93.4 9.3 %all_to_all.49.w_inc = f32[4,1,768]{2,1,0:T(1,128)} all-to-all(f32[4,1,768]{2,1,0:T(1,128)} %get-tuple-element.38), channel_id=1, replica_groups=mesh['chord'=4,'span'=16,'wall'=4] {'wall'}, dimensions={0} | all-to-all | bytes 24576 | tf_op jit(solution)/shard_map/all_to_all | solution.py:253
  102.6 11.8 %all_to_all.50.inc_ref = f32[16,1,384]{2,1,0:T(1,128)} all-to-all(f32[16,1,384]{2,1,0:T(1,128)S(1)} %copy-done.4), channel_id=1, replica_groups=mesh['chord'=4,'span'=16,'wall'=4] {'span'}, dimensions={0} | all-to-all | bytes 49152 | tf_op jit(solution)/shard_map/all_to_all | solution.py:317
  114.4 4.9 %all-to-all-start.6 = ((f32[4,6,16,128]{3,2,1,0:T(8,128)}), f32[4,6,16,128]{3,2,1,0:T(8,128)S(1)}, u32[]{:S(2)}, u32[]{:S(2)}) async-start(f32[4,6,16,128]{3,2,1,0:T(8,128)} %get-tuple-element.37), calls=%async_computation.6 | async-start | bytes 393216 | tf_op jit(solution)/shard_map/all_to_all | solution.py:246
  119.4 2.5 %collective-permute-start.4 = (f32[6,8,128]{2,1,0:T(8,128)S(1)}, f32[6,8,128]{2,1,0:T(8,128)S(1)}, u32[]{:S(2)}, u32[]{:S(2)}) collective-permute-start(f32[6,8,128]{2,1,0:T(8,128)S(1)} %copy-done.14), channel_id=1, source_target_pairs={{0,4},{4,8},{8,12},{12,16},{16,20},{20,24},{24,28},{28,32},{32,36}... | collective-permute-start | bytes 73736 | tf_op jit(solution)/shard_map/ppermute | solution.py:251
  121.9 4.3 %collective-permute-start.5 = (f32[6,8,128]{2,1,0:T(8,128)S(1)}, f32[6,8,128]{2,1,0:T(8,128)S(1)}, u32[]{:S(2)}, u32[]{:S(2)}) collective-permute-start(f32[6,8,128]{2,1,0:T(8,128)S(1)} %copy-done.12), channel_id=1, source_target_pairs={{4,0},{8,4},{12,8},{16,12},{20,16},{24,20},{28,24},{32,28},{36,32}... | collective-permute-start | bytes 73736 | tf_op jit(solution)/shard_map/ppermute | solution.py:252
  126.1 0.7 copy-done
  126.8 4.2 %shard_map.127.part_ref = f32[6,8,16,128]{3,2,1,0:T(8,128)} custom-call(f32[3,6,6]{2,1,0:T(8,128)} %ub_ref.13, f32[3,6,6]{2,1,0:T(8,128)} %lb_ref.13, f32[2,6,6]{2,1,0:T(8,128)} %copy.19.ib_ref, s32[1]{0:T(128)} %bitcast.wall_me.rest_3_, s32[1]{0:T(128)} %bitcast.1.chord_me.rest_4_, f32[6,8,16,128]{3,2,1,0:T(8,128)} %get-tuple-element.36.adj_ref, ...), custom_call_target="tpu_custom_call" | custom-call | tf_op jit(solution)/shard_map/pallas_call | solution.py:321
  132.2 2.2 %shard_map.128 = (f32[6,8,16,128]{3,2,1,0:T(8,128)}, f32[8,16,128]{2,1,0:T(8,128)}) custom-call(f32[3,6,6]{2,1,0:T(8,128)} %ub_ref.13, f32[3,6,6]{2,1,0:T(8,128)} %lb_ref.13, f32[2,6,6]{2,1,0:T(8,128)} %copy.19.ib_ref, f32[6,8,16,128]{3,2,1,0:T(8,128)} %shard_map.127.part_ref, f32[6,8,16,128]{3,2,1,0:T(8,128)} %diag_ref.13, f32[3,8,16,128]{3,2,1,0:T(8,128)} %face_ref.11, ...), custom_call_target="tpu_custom_call" | custom-call | tf_op jit(solution)/shard_map/pallas_call | solution.py:326
  (44 shorter events, 5.0 us)
Async XLA Ops:
  0.6 0.7 copy-start.11
  31.0 5.0 %copy-start.17 = (f32[6,8,128]{2,1,0:T(8,128)S(1)}, f32[6,8,128]{2,1,0:T(8,128)}, u32[]{:S(2)}) copy-start(f32[6,8,128]{2,1,0:T(8,128)} %get-tuple-element.27) | copy-start | bytes 73732
  31.0 7.6 %copy-start.15 = (f32[6,8,128]{2,1,0:T(8,128)S(1)}, f32[6,8,128]{2,1,0:T(8,128)}, u32[]{:S(2)}) copy-start(f32[6,8,128]{2,1,0:T(8,128)} %get-tuple-element.28) | copy-start | bytes 73732
  31.0 11.8 %all-to-all-start = ((f32[4,6,16,128]{3,2,1,0:T(8,128)}), f32[4,6,16,128]{3,2,1,0:T(8,128)S(1)}, u32[]{:S(2)}, u32[]{:S(2)}) async-start(f32[4,6,16,128]{3,2,1,0:T(8,128)} %get-tuple-element.23), calls=%async_computation | async-start | bytes 393216 | tf_op jit(solution)/shard_map/all_to_all | solution.py:246
  36.1 11.7 %collective-permute-start = (f32[6,8,128]{2,1,0:T(8,128)S(1)}, f32[6,8,128]{2,1,0:T(8,128)S(1)}, u32[]{:S(2)}, u32[]{:S(2)}) collective-permute-start(f32[6,8,128]{2,1,0:T(8,128)S(1)} %copy-done.17), channel_id=1, source_target_pairs={{0,4},{4,8},{8,12},{12,16},{16,20},{20,24},{24,28},{28,32},{32,36}... | collective-permute-start | bytes 73736 | tf_op jit(solution)/shard_map/ppermute | solution.py:251
  38.6 9.2 %collective-permute-start.1 = (f32[6,8,128]{2,1,0:T(8,128)S(1)}, f32[6,8,128]{2,1,0:T(8,128)S(1)}, u32[]{:S(2)}, u32[]{:S(2)}) collective-permute-start(f32[6,8,128]{2,1,0:T(8,128)S(1)} %copy-done.15), channel_id=1, source_target_pairs={{4,0},{8,4},{12,8},{16,12},{20,16},{24,20},{28,24},{32,28},{36,32}... | collective-permute-start | bytes 73736 | tf_op jit(solution)/shard_map/ppermute | solution.py:252
  42.8 0.7 copy-start.2
  47.7 0.6 copy-start.5
  51.4 9.3 %copy-start.3 = (f32[16,1,384]{2,1,0:T(1,128)S(1)}, f32[16,1,384]{2,1,0:T(1,128)}, u32[]{:S(2)}) copy-start(f32[16,1,384]{2,1,0:T(1,128)} %get-tuple-element.32) | copy-start | bytes 73732
  72.5 4.9 %copy-start.16 = (f32[6,8,128]{2,1,0:T(8,128)S(1)}, f32[6,8,128]{2,1,0:T(8,128)}, u32[]{:S(2)}) copy-start(f32[6,8,128]{2,1,0:T(8,128)} %get-tuple-element.34) | copy-start | bytes 73732
  72.5 7.4 %copy-start.13 = (f32[6,8,128]{2,1,0:T(8,128)S(1)}, f32[6,8,128]{2,1,0:T(8,128)}, u32[]{:S(2)}) copy-start(f32[6,8,128]{2,1,0:T(8,128)} %get-tuple-element.35) | copy-start | bytes 73732
  72.5 11.7 %all-to-all-start.3 = ((f32[4,6,16,128]{3,2,1,0:T(8,128)}), f32[4,6,16,128]{3,2,1,0:T(8,128)S(1)}, u32[]{:S(2)}, u32[]{:S(2)}) async-start(f32[4,6,16,128]{3,2,1,0:T(8,128)} %get-tuple-element.30), calls=%async_computation.3 | async-start | bytes 393216 | tf_op jit(solution)/shard_map/all_to_all | solution.py:246
  77.5 11.6 %collective-permute-start.2 = (f32[6,8,128]{2,1,0:T(8,128)S(1)}, f32[6,8,128]{2,1,0:T(8,128)S(1)}, u32[]{:S(2)}, u32[]{:S(2)}) collective-permute-start(f32[6,8,128]{2,1,0:T(8,128)S(1)} %copy-done.16), channel_id=1, source_target_pairs={{0,4},{4,8},{8,12},{12,16},{16,20},{20,24},{24,28},{28,32},{32,36}... | collective-permute-start | bytes 73736 | tf_op jit(solution)/shard_map/ppermute | solution.py:251
  79.9 9.2 %collective-permute-start.3 = (f32[6,8,128]{2,1,0:T(8,128)S(1)}, f32[6,8,128]{2,1,0:T(8,128)S(1)}, u32[]{:S(2)}, u32[]{:S(2)}) collective-permute-start(f32[6,8,128]{2,1,0:T(8,128)S(1)} %copy-done.13), channel_id=1, source_target_pairs={{4,0},{8,4},{12,8},{16,12},{20,16},{24,20},{28,24},{32,28},{36,32}... | collective-permute-start | bytes 73736 | tf_op jit(solution)/shard_map/ppermute | solution.py:252
  84.2 0.7 copy-start.1
  89.1 0.6 copy-start.6
  93.4 9.3 %copy-start.4 = (f32[16,1,384]{2,1,0:T(1,128)S(1)}, f32[16,1,384]{2,1,0:T(1,128)}, u32[]{:S(2)}) copy-start(f32[16,1,384]{2,1,0:T(1,128)} %get-tuple-element.39) | copy-start | bytes 73732
  114.4 4.9 %copy-start.14 = (f32[6,8,128]{2,1,0:T(8,128)S(1)}, f32[6,8,128]{2,1,0:T(8,128)}, u32[]{:S(2)}) copy-start(f32[6,8,128]{2,1,0:T(8,128)} %get-tuple-element.40) | copy-start | bytes 73732
  114.4 7.4 %copy-start.12 = (f32[6,8,128]{2,1,0:T(8,128)S(1)}, f32[6,8,128]{2,1,0:T(8,128)}, u32[]{:S(2)}) copy-start(f32[6,8,128]{2,1,0:T(8,128)} %get-tuple-element.41) | copy-start | bytes 73732
  114.4 11.7 %all-to-all-start.6 = ((f32[4,6,16,128]{3,2,1,0:T(8,128)}), f32[4,6,16,128]{3,2,1,0:T(8,128)S(1)}, u32[]{:S(2)}, u32[]{:S(2)}) async-start(f32[4,6,16,128]{3,2,1,0:T(8,128)} %get-tuple-element.37), calls=%async_computation.6 | async-start | bytes 393216 | tf_op jit(solution)/shard_map/all_to_all | solution.py:246
  119.4 11.6 %collective-permute-start.4 = (f32[6,8,128]{2,1,0:T(8,128)S(1)}, f32[6,8,128]{2,1,0:T(8,128)S(1)}, u32[]{:S(2)}, u32[]{:S(2)}) collective-permute-start(f32[6,8,128]{2,1,0:T(8,128)S(1)} %copy-done.14), channel_id=1, source_target_pairs={{0,4},{4,8},{8,12},{12,16},{16,20},{20,24},{24,28},{28,32},{32,36}... | collective-permute-start | bytes 73736 | tf_op jit(solution)/shard_map/ppermute | solution.py:251
  121.9 9.2 %collective-permute-start.5 = (f32[6,8,128]{2,1,0:T(8,128)S(1)}, f32[6,8,128]{2,1,0:T(8,128)S(1)}, u32[]{:S(2)}, u32[]{:S(2)}) collective-permute-start(f32[6,8,128]{2,1,0:T(8,128)S(1)} %copy-done.12), channel_id=1, source_target_pairs={{4,0},{8,4},{12,8},{16,12},{20,16},{24,20},{28,24},{32,28},{36,32}... | collective-permute-start | bytes 73736 | tf_op jit(solution)/shard_map/ppermute | solution.py:252
  126.1 0.7 copy-start
  131.6 0.6 copy-start.10
  (3 other events, 1.8 us)

commit v13 on v9

--- a/solution.py
+++ b/solution.py
@@ -114,7 +114,22 @@
     to_chunks(rows_ref, pieces + [flat_row(tgt_ref[...]).astype(F32)], slots)
 
 
-def sweep_body(blk, adj, sens, diag, face, halos, incoming, cell):
+def scatter_rows(incoming, cell, shape):
+    n_var, nx, ny, nz = shape
+    rows = nx * ny
+    n_rows = incoming.shape[1]
+    row_of = cell // nz
+    lane_of = cell % nz
+    row_hot = (lax.broadcasted_iota(jnp.int32, (rows, n_rows), 0) == row_of).astype(BF16)
+    lane_hot = (lax.broadcasted_iota(jnp.int32, (nz, n_rows), 0) == lane_of).astype(BF16)
+    lhs = jnp.concatenate([(row_hot[None] * part[:, None, :]).reshape(n_var * rows, n_rows)
+                           for part in split3(incoming)], axis=1)
+    coupled = lax.dot_general(lhs, jnp.concatenate([lane_hot] * 2, axis=1), (((1,), (1,)), ((), ())),
+                              preferred_element_type=F32)
+    return coupled.reshape(n_var, nx, ny, nz)
+
+
+def sweep_body(blk, adj, sens, diag, face, halos):
     n_var, nx, ny, nz = adj.shape
     rows = nx * ny
     h_c_lo, h_c_hi, h_s_lo, h_s_hi, h_w_lo, h_w_hi = halos
@@ -136,19 +151,9 @@
         jnp.where(j_idx == 0, h_s_lo[:, :, None, :], pltpu.roll(adj, 1, 2)),
         jnp.where(k_idx == 0, wall, pltpu.roll(adj, 1, 3)),
     ]
-    n_rows = incoming.shape[1]
-    row_of = cell // nz
-    lane_of = cell % nz
-    row_hot = (lax.broadcasted_iota(jnp.int32, (rows, n_rows), 0) == row_of).astype(BF16)
-    lane_hot = (lax.broadcasted_iota(jnp.int32, (nz, n_rows), 0) == lane_of).astype(BF16)
-    lhs = jnp.concatenate([(row_hot[None] * part[:, None, :]).reshape(n_var * rows, n_rows)
-                           for part in split3(incoming)], axis=1)
-    coupled = lax.dot_general(lhs, jnp.concatenate([lane_hot] * 2, axis=1), (((1,), (1,)), ((), ())),
-                              preferred_element_type=F32)
-    coupled = coupled.reshape(n_var, nx, ny, nz)
     new = []
     for i in range(n_var):
-        applied = diag[i] * adj[i] + coupled[i]
+        applied = diag[i] * adj[i]
         for d in range(3):
             acc = None
             for j in range(n_var):
@@ -159,33 +164,30 @@
     return jnp.stack(new, axis=0)
 
 
-def make_part_a(first, slots):
-    def kernel(ub_ref, lb_ref, ib_ref, wall_me, adj_ref, sens_ref, diag_ref, face_ref, hcl, hch, w_inc,
-               inc_ref, *rest):
-        if first:
-            out_ref, tgt_out = rest
-        else:
-            tgt_ref, out_ref = rest
+def make_part_a(slots):
+    def kernel(ub_ref, lb_ref, ib_ref, wall_me, adj_ref, sens_ref, diag_ref, face_ref, hcl, hch, w_inc, out_ref):
         n_var, nx, ny, nz = adj_ref.shape
         blk_ref = (ub_ref, lb_ref, ib_ref)
+        none = jnp.zeros((n_var, nx, nz), F32)
+        halos = (hcl[...], hch[...], none, none) + wall_halos(w_inc[...], wall_me, n_var)
+        out_ref[...] = sweep_body(blk_ref, adj_ref[...], sens_ref[...], diag_ref[...], face_ref[...], halos)
+    return kernel
+
+
+def make_part_b(first, last, slots):
+    def kernel(ub_ref, lb_ref, ib_ref, part_ref, diag_ref, face_ref, hsl, hsh, inc_ref, *rest):
+        n_var, nx, ny, nz = part_ref.shape
         inc = inc_ref[...]
         if first:
+            tgt_out, rest = rest[-1], rest[:-1]
             got = from_chunks(inc, n_var + 1, slots)
             cell = got[n_var].astype(jnp.int32)
             tgt_out[...] = cell
         else:
+            tgt_ref, rest = rest[0], rest[1:]
             got = from_chunks(inc, n_var, slots)
             cell = tgt_ref[...]
-        none = jnp.zeros((n_var, nx, nz), F32)
-        halos = (hcl[...], hch[...], none, none) + wall_halos(w_inc[...], wall_me, n_var)
-        out_ref[...] = sweep_body(blk_ref, adj_ref[...], sens_ref[...], diag_ref[...], face_ref[...], halos,
-                                  jnp.concatenate(got[:n_var], axis=0), cell)
-    return kernel
-
-
-def make_part_b(last, slots):
-    def kernel(ub_ref, lb_ref, ib_ref, part_ref, diag_ref, face_ref, hsl, hsh, *rest):
-        n_var, nx, ny, nz = part_ref.shape
+        coupled = scatter_rows(jnp.concatenate(got[:n_var], axis=0), cell, part_ref.shape)
         part = part_ref[...]
         diag = diag_ref[...]
         face_y = face_ref[1]
@@ -203,7 +205,7 @@
                 below = b if below is None else below + b
             edge = (jnp.where(j_idx == ny - 1, above[:, None, :], 0.0)
                     + jnp.where(j_idx == 0, below[:, None, :], 0.0))
-            new.append(part[i] - face_y * edge / diag[i])
+            new.append(part[i] - (face_y * edge + coupled[i]) / diag[i])
         new = jnp.stack(new, axis=0)
         if last:
             prod_ref, out_ref, grad_ref = rest
@@ -269,28 +271,28 @@
     )
     adj, rows, *faces = init(*blk, sensitivity, diagonal, send_row, orient_row, weight_row, target_row)
 
-    part_a_first = pl.pallas_call(
-        make_part_a(True, slots),
-        out_shape=[adj_sds, tgt_sds],
-        in_specs=[smem] * 4 + [vmem] * 8,
-        out_specs=[vmem] * 2,
-    )
     part_a = pl.pallas_call(
-        make_part_a(False, slots),
+        make_part_a(slots),
         out_shape=adj_sds,
-        in_specs=[smem] * 4 + [vmem] * 9,
+        in_specs=[smem] * 4 + [vmem] * 7,
         out_specs=vmem,
     )
-    part_b = pl.pallas_call(
-        make_part_b(False, slots),
+    b_first = pl.pallas_call(
+        make_part_b(True, False, slots),
+        out_shape=[adj_sds, rows_sds] + face_shapes(shape, n_wall) + [tgt_sds],
+        in_specs=[smem] * 3 + [vmem] * 9 + [smem],
+        out_specs=[vmem] * 8,
+    )
+    b_step = pl.pallas_call(
+        make_part_b(False, False, slots),
         out_shape=[adj_sds, rows_sds] + face_shapes(shape, n_wall),
-        in_specs=[smem] * 3 + [vmem] * 8 + [smem],
+        in_specs=[smem] * 3 + [vmem] * 10 + [smem],
         out_specs=[vmem] * 7,
     )
-    part_b_last = pl.pallas_call(
-        make_part_b(True, slots),
+    b_last = pl.pallas_call(
+        make_part_b(False, True, slots),
         out_shape=[adj_sds, jax.ShapeDtypeStruct(production.shape, F32)],
-        in_specs=[smem] * 3 + [vmem] * 6,
+        in_specs=[smem] * 3 + [vmem] * 8,
         out_specs=[vmem] * 2,
     )
     ub, lb, ib, _ = blk
@@ -298,15 +300,14 @@
     for sweep in range(SWEEPS):
         hcl, hch, hsl, hsh, w_inc = exchange(faces)
         incoming = lax.all_to_all(rows, "span", split_axis=0, concat_axis=0, tiled=True)
+        partial = part_a(*blk, adj, sensitivity, diagonal, face_coef, hcl, hch, w_inc)
+        common = (ub, lb, ib, partial, diagonal, face_coef, hsl, hsh, incoming)
         if sweep == 0:
-            partial, received = part_a_first(*blk, adj, sensitivity, diagonal, face_coef, hcl, hch, w_inc, incoming)
+            adj, rows, *faces, received = b_first(*common, send_row, orient_row, weight_row, wall_me)
+        elif sweep < SWEEPS - 1:
+            adj, rows, *faces = b_step(*common, received, send_row, orient_row, weight_row, wall_me)
         else:
-            partial = part_a(*blk, adj, sensitivity, diagonal, face_coef, hcl, hch, w_inc, incoming, received)
-        if sweep < SWEEPS - 1:
-            adj, rows, *faces = part_b(ub, lb, ib, partial, diagonal, face_coef, hsl, hsh,
-                                       send_row, orient_row, weight_row, wall_me)
-        else:
-            adj, gradient = part_b_last(ub, lb, ib, partial, diagonal, face_coef, hsl, hsh, production)
+            adj, gradient = b_last(*common, received, production)
     return (adj, gradient)
 
 

time: 117 us -> 117 us (level)
  the two profiles are of different devices: /device:TPU:12 before, /device:TPU:118 now
where the time goes in v13:
time: 117 us; the launch traced here: 116 us
  starting transfers between devices  70.8 us (61%)
  Pallas kernels  24.5 us (21%)
  local copies, waits for them, and re-layouts  7.32 us (6%)
  blocking collectives  7.28 us (6%)
  waiting for transfers between devices  4.9 us (4%)
    ppermute x6, starting transfers between devices, exchange(): out.append(lax.ppermute(hi_face, axis, forward))  23.3 us
    all_to_all x3, starting transfers between devices, local(): lax.all_to_all(rows, 'span', split_axis=0, concat_axis=0, tiled=True)  22.1 us
    ppermute x6, starting transfers between devices, exchange(): out.append(lax.ppermute(lo_face, axis, backward))  13.9 us
    all_to_all x2, starting transfers between devices, exchange(): lax.all_to_all(w_buf, 'wall', split_axis=0, concat_axis=0, tiled=True)  11.5 us
    pallas_call x3, Pallas kernels, local(): part_a(*blk, adj, sensitivity, diagonal, face_coef, hcl, hch, w_inc)  10.7 us
    unnamed x49, local copies, waits for them, and re-layouts  7.32 us
    all_to_all x1, blocking collectives, exchange(): lax.all_to_all(w_buf, 'wall', split_axis=0, concat_axis=0, tiled=True)  7.28 us
    ppermute x6, waiting for transfers between devices, exchange(): out.append(lax.ppermute(lo_face, axis, backward))  4.87 us
  transfers between devices with their start and end apart: 17, of which 3 were waited for; matrix products, arithmetic and copies ran while one was open for 0% of the time, Pallas kernels for 9%

profile of v13, /device:TPU:118, one launch (start us, length us, event | category | flops | bytes accessed | tf_op | source)
XLA Modules:
  0.0 115.8 jit_solution(8003965148460796277)
XLA Ops:
  1.9 2.8 %shard_map.122 = (f32[6,8,16,128]{3,2,1,0:T(8,128)}, f32[16,1,448]{2,1,0:T(1,128)}, f32[6,1,16,128]{3,2,1,0:T(8,128)}, f32[6,1,16,128]{3,2,1,0:T(8,128)}, f32[6,...) custom-call(f32[3,6,6]{2,1,0:T(8,128)} %ub_ref.13, f32[3,6,6]{2,1,0:T(8,128)} %lb_ref.13, ...), custom_call_target="tpu_custom_call" | custom-call | tf_op jit(solution)/shard_map/pallas_call | solution.py:272
  4.8 7.3 %all_to_all.30.w_inc = f32[4,1,768]{2,1,0:T(1,128)} all-to-all(f32[4,1,768]{2,1,0:T(1,128)} %get-tuple-element.27), channel_id=1, replica_groups=mesh['chord'=4,'span'=16,'wall'=4] {'wall'}, dimensions={0} | all-to-all | bytes 24576 | tf_op jit(solution)/shard_map/all_to_all | solution.py:240
  12.0 8.7 %all-to-all-start.1 = ((f32[16,1,448]{2,1,0:T(1,128)}), f32[16,1,448]{2,1,0:T(1,128)S(1)}, u32[]{:S(2)}, u32[]{:S(2)}) async-start(f32[16,1,448]{2,1,0:T(1,128)} %get-tuple-element.30), calls=%async_computation.1 | async-start | bytes 65536 | tf_op jit(solution)/shard_map/all_to_all | solution.py:302
  20.8 3.2 %collective-permute-start = (f32[6,1,16,128]{3,2,1,0:T(8,128)}, f32[6,1,16,128]{3,2,1,0:T(8,128)S(1)}, u32[]{:S(2)}, u32[]{:S(2)}) collective-permute-start(f32[6,1,16,128]{3,2,1,0:T(8,128)} %get-tuple-element.25), channel_id=1, source_target_pairs={{0,64},{64,128},{128,192},{1,65},{65,129},{129,193},{2,66},{66,130... | collective-permute-start | bytes 147464 | tf_op jit(solution)/shard_map/ppermute | solution.py:238
  24.0 2.7 %collective-permute-start.1 = (f32[6,1,16,128]{3,2,1,0:T(8,128)S(1)}, f32[6,1,16,128]{3,2,1,0:T(8,128)S(1)}, u32[]{:S(2)}, u32[]{:S(2)}) collective-permute-start(f32[6,1,16,128]{3,2,1,0:T(8,128)S(1)} %copy-done.17), channel_id=1, source_target_pairs={{64,0},{128,64},{192,128},{65,1},{129,65},{193,129},{66,2},{130,66... | collective-permute-start | bytes 147464 | tf_op jit(solution)/shard_map/ppermute | solution.py:239
  26.6 4.6 %collective-permute-start.2 = (f32[6,8,128]{2,1,0:T(8,128)S(1)}, f32[6,8,128]{2,1,0:T(8,128)S(1)}, u32[]{:S(2)}, u32[]{:S(2)}) collective-permute-start(f32[6,8,128]{2,1,0:T(8,128)S(1)} %copy-done.23), channel_id=1, source_target_pairs={{0,4},{4,8},{8,12},{12,16},{16,20},{20,24},{24,28},{28,32},{32,36}... | collective-permute-start | bytes 73736 | tf_op jit(solution)/shard_map/ppermute | solution.py:238
  33.8 3.6 %shard_map.123.part_ref = f32[6,8,16,128]{3,2,1,0:T(8,128)} custom-call(f32[3,6,6]{2,1,0:T(8,128)} %ub_ref.13, f32[3,6,6]{2,1,0:T(8,128)} %lb_ref.13, f32[2,6,6]{2,1,0:T(8,128)} %copy.19.ib_ref, s32[1]{0:T(128)} %bitcast.wall_me.rest_3_.rest_4_, f32[6,8,16,128]{3,2,1,0:T(8,128)} %get-tuple-element.24.adj_ref, f32[6,8,16,128]{3,2,1,0:T(8,128)} %sens_ref.7, ...), custom_call_target="tpu_custom_call" | custom-call | tf_op jit(solution)/shard_map/pallas_call | solution.py:303
  40.2 3.9 %shard_map.124 = (f32[6,8,16,128]{3,2,1,0:T(8,128)}, f32[16,1,384]{2,1,0:T(1,128)}, f32[6,1,16,128]{3,2,1,0:T(8,128)}, f32[6,1,16,128]{3,2,1,0:T(8,128)}, f32[6,...) custom-call(f32[3,6,6]{2,1,0:T(8,128)} %ub_ref.13, f32[3,6,6]{2,1,0:T(8,128)} %lb_ref.13, ...), custom_call_target="tpu_custom_call" | custom-call | tf_op jit(solution)/shard_map/pallas_call | solution.py:306
  44.2 6.7 %all-to-all-start.2 = ((f32[4,1,768]{2,1,0:T(1,128)}), f32[4,1,768]{2,1,0:T(1,128)S(1)}, u32[]{:S(2)}, u32[]{:S(2)}) async-start(f32[4,1,768]{2,1,0:T(1,128)} %get-tuple-element.34), calls=%async_computation.2 | async-start | bytes 24576 | tf_op jit(solution)/shard_map/all_to_all | solution.py:240
  50.9 3.2 %collective-permute-start.4 = (f32[6,1,16,128]{3,2,1,0:T(8,128)}, f32[6,1,16,128]{3,2,1,0:T(8,128)S(1)}, u32[]{:S(2)}, u32[]{:S(2)}) collective-permute-start(f32[6,1,16,128]{3,2,1,0:T(8,128)} %get-tuple-element.32), channel_id=1, source_target_pairs={{0,64},{64,128},{128,192},{1,65},{65,129},{129,193},{2,66},{66,130... | collective-permute-start | bytes 147464 | tf_op jit(solution)/shard_map/ppermute | solution.py:238
  54.1 2.7 %collective-permute-start.5 = (f32[6,1,16,128]{3,2,1,0:T(8,128)}, f32[6,1,16,128]{3,2,1,0:T(8,128)S(1)}, u32[]{:S(2)}, u32[]{:S(2)}) collective-permute-start(f32[6,1,16,128]{3,2,1,0:T(8,128)} %get-tuple-element.33), channel_id=1, source_target_pairs={{64,0},{128,64},{192,128},{65,1},{129,65},{193,129},{66,2},{130,66... | collective-permute-start | bytes 147464 | tf_op jit(solution)/shard_map/ppermute | solution.py:239
  57.3 6.4 %all-to-all-start.3 = ((f32[16,1,384]{2,1,0:T(1,128)}), f32[16,1,384]{2,1,0:T(1,128)S(1)}, u32[]{:S(2)}, u32[]{:S(2)}) async-start(f32[16,1,384]{2,1,0:T(1,128)} %get-tuple-element.37), calls=%async_computation.3 | async-start | bytes 49152 | tf_op jit(solution)/shard_map/all_to_all | solution.py:302
  63.7 4.6 %collective-permute-start.6 = (f32[6,8,128]{2,1,0:T(8,128)S(1)}, f32[6,8,128]{2,1,0:T(8,128)S(1)}, u32[]{:S(2)}, u32[]{:S(2)}) collective-permute-start(f32[6,8,128]{2,1,0:T(8,128)S(1)} %copy-done.20), channel_id=1, source_target_pairs={{0,4},{4,8},{8,12},{12,16},{16,20},{20,24},{24,28},{28,32},{32,36}... | collective-permute-start | bytes 73736 | tf_op jit(solution)/shard_map/ppermute | solution.py:238
  68.3 1.9 %collective-permute-start.7 = (f32[6,8,128]{2,1,0:T(8,128)S(1)}, f32[6,8,128]{2,1,0:T(8,128)S(1)}, u32[]{:S(2)}, u32[]{:S(2)}) collective-permute-start(f32[6,8,128]{2,1,0:T(8,128)S(1)} %copy-done.18), channel_id=1, source_target_pairs={{4,0},{8,4},{12,8},{16,12},{20,16},{24,20},{28,24},{32,28},{36,32}... | collective-permute-start | bytes 73736 | tf_op jit(solution)/shard_map/ppermute | solution.py:239
  70.9 3.6 %shard_map.125.part_ref = f32[6,8,16,128]{3,2,1,0:T(8,128)} custom-call(f32[3,6,6]{2,1,0:T(8,128)} %ub_ref.13, f32[3,6,6]{2,1,0:T(8,128)} %lb_ref.13, f32[2,6,6]{2,1,0:T(8,128)} %copy.19.ib_ref, s32[1]{0:T(128)} %bitcast.wall_me.rest_3_.rest_4_, f32[6,8,16,128]{3,2,1,0:T(8,128)} %get-tuple-element.31.adj_ref, f32[6,8,16,128]{3,2,1,0:T(8,128)} %sens_ref.7, ...), custom_call_target="tpu_custom_call" | custom-call | tf_op jit(solution)/shard_map/pallas_call | solution.py:303
  76.8 3.9 %shard_map.126 = (f32[6,8,16,128]{3,2,1,0:T(8,128)}, f32[16,1,384]{2,1,0:T(1,128)}, f32[6,1,16,128]{3,2,1,0:T(8,128)}, f32[6,1,16,128]{3,2,1,0:T(8,128)}, f32[6,...) custom-call(f32[3,6,6]{2,1,0:T(8,128)} %ub_ref.13, f32[3,6,6]{2,1,0:T(8,128)} %lb_ref.13, ...), custom_call_target="tpu_custom_call" | custom-call | tf_op jit(solution)/shard_map/pallas_call | solution.py:308
  80.7 4.8 %all-to-all-start.4 = ((f32[4,1,768]{2,1,0:T(1,128)}), f32[4,1,768]{2,1,0:T(1,128)S(1)}, u32[]{:S(2)}, u32[]{:S(2)}) async-start(f32[4,1,768]{2,1,0:T(1,128)} %get-tuple-element.42), calls=%async_computation.4 | async-start | bytes 24576 | tf_op jit(solution)/shard_map/all_to_all | solution.py:240
  85.5 3.2 %collective-permute-start.8 = (f32[6,1,16,128]{3,2,1,0:T(8,128)}, f32[6,1,16,128]{3,2,1,0:T(8,128)S(1)}, u32[]{:S(2)}, u32[]{:S(2)}) collective-permute-start(f32[6,1,16,128]{3,2,1,0:T(8,128)} %get-tuple-element.40), channel_id=1, source_target_pairs={{0,64},{64,128},{128,192},{1,65},{65,129},{129,193},{2,66},{66,130... | collective-permute-start | bytes 147464 | tf_op jit(solution)/shard_map/ppermute | solution.py:238
  88.7 2.7 %collective-permute-start.9 = (f32[6,1,16,128]{3,2,1,0:T(8,128)}, f32[6,1,16,128]{3,2,1,0:T(8,128)S(1)}, u32[]{:S(2)}, u32[]{:S(2)}) collective-permute-start(f32[6,1,16,128]{3,2,1,0:T(8,128)} %get-tuple-element.41), channel_id=1, source_target_pairs={{64,0},{128,64},{192,128},{65,1},{129,65},{193,129},{66,2},{130,66... | collective-permute-start | bytes 147464 | tf_op jit(solution)/shard_map/ppermute | solution.py:239
  91.9 7.0 %all-to-all-start.5 = ((f32[16,1,384]{2,1,0:T(1,128)}), f32[16,1,384]{2,1,0:T(1,128)S(1)}, u32[]{:S(2)}, u32[]{:S(2)}) async-start(f32[16,1,384]{2,1,0:T(1,128)} %get-tuple-element.45), calls=%async_computation.5 | async-start | bytes 49152 | tf_op jit(solution)/shard_map/all_to_all | solution.py:302
  99.0 4.6 %collective-permute-start.10 = (f32[6,8,128]{2,1,0:T(8,128)S(1)}, f32[6,8,128]{2,1,0:T(8,128)S(1)}, u32[]{:S(2)}, u32[]{:S(2)}) collective-permute-start(f32[6,8,128]{2,1,0:T(8,128)S(1)} %copy-done.21), channel_id=1, source_target_pairs={{0,4},{4,8},{8,12},{12,16},{16,20},{20,24},{24,28},{28,32},{32,36}... | collective-permute-start | bytes 73736 | tf_op jit(solution)/shard_map/ppermute | solution.py:238
  103.6 2.1 %collective-permute-start.11 = (f32[6,8,128]{2,1,0:T(8,128)S(1)}, f32[6,8,128]{2,1,0:T(8,128)S(1)}, u32[]{:S(2)}, u32[]{:S(2)}) collective-permute-start(f32[6,8,128]{2,1,0:T(8,128)S(1)} %copy-done.19), channel_id=1, source_target_pairs={{4,0},{8,4},{12,8},{16,12},{20,16},{24,20},{28,24},{32,28},{36,32}... | collective-permute-start | bytes 73736 | tf_op jit(solution)/shard_map/ppermute | solution.py:239
  106.3 3.6 %shard_map.127.part_ref = f32[6,8,16,128]{3,2,1,0:T(8,128)} custom-call(f32[3,6,6]{2,1,0:T(8,128)} %ub_ref.13, f32[3,6,6]{2,1,0:T(8,128)} %lb_ref.13, f32[2,6,6]{2,1,0:T(8,128)} %copy.19.ib_ref, s32[1]{0:T(128)} %bitcast.wall_me.rest_3_.rest_4_, f32[6,8,16,128]{3,2,1,0:T(8,128)} %get-tuple-element.39.adj_ref, f32[6,8,16,128]{3,2,1,0:T(8,128)} %sens_ref.7, ...), custom_call_target="tpu_custom_call" | custom-call | tf_op jit(solution)/shard_map/pallas_call | solution.py:303
  112.6 3.2 %shard_map.128 = (f32[6,8,16,128]{3,2,1,0:T(8,128)}, f32[8,16,128]{2,1,0:T(8,128)}) custom-call(f32[3,6,6]{2,1,0:T(8,128)} %ub_ref.13, f32[3,6,6]{2,1,0:T(8,128)} %lb_ref.13, f32[2,6,6]{2,1,0:T(8,128)} %copy.19.ib_ref, f32[6,8,16,128]{3,2,1,0:T(8,128)} %shard_map.127.part_ref, f32[6,8,16,128]{3,2,1,0:T(8,128)} %diag_ref.13, f32[3,8,16,128]{3,2,1,0:T(8,128)} %face_ref.11, ...), custom_call_target="tpu_custom_call" | custom-call | tf_op jit(solution)/shard_map/pallas_call | solution.py:310
  (67 shorter events, 14.1 us)
Async XLA Ops:
  4.8 19.2 %copy-start.17 = (f32[6,1,16,128]{3,2,1,0:T(8,128)S(1)}, f32[6,1,16,128]{3,2,1,0:T(8,128)}, u32[]{:S(2)}) copy-start(f32[6,1,16,128]{3,2,1,0:T(8,128)} %get-tuple-element.26) | copy-start | bytes 147460
  12.0 14.6 %copy-start.23 = (f32[6,8,128]{2,1,0:T(8,128)S(1)}, f32[6,8,128]{2,1,0:T(8,128)}, u32[]{:S(2)}) copy-start(f32[6,8,128]{2,1,0:T(8,128)} %get-tuple-element.28) | copy-start | bytes 73732
  12.0 19.2 %copy-start.22 = (f32[6,8,128]{2,1,0:T(8,128)S(1)}, f32[6,8,128]{2,1,0:T(8,128)}, u32[]{:S(2)}) copy-start(f32[6,8,128]{2,1,0:T(8,128)} %get-tuple-element.29) | copy-start | bytes 73732
  12.0 27.0 %all-to-all-start.1 = ((f32[16,1,448]{2,1,0:T(1,128)}), f32[16,1,448]{2,1,0:T(1,128)S(1)}, u32[]{:S(2)}, u32[]{:S(2)}) async-start(f32[16,1,448]{2,1,0:T(1,128)} %get-tuple-element.30), calls=%async_computation.1 | async-start | bytes 65536 | tf_op jit(solution)/shard_map/all_to_all | solution.py:302
  20.8 12.4 %collective-permute-start = (f32[6,1,16,128]{3,2,1,0:T(8,128)}, f32[6,1,16,128]{3,2,1,0:T(8,128)S(1)}, u32[]{:S(2)}, u32[]{:S(2)}) collective-permute-start(f32[6,1,16,128]{3,2,1,0:T(8,128)} %get-tuple-element.25), channel_id=1, source_target_pairs={{0,64},{64,128},{128,192},{1,65},{65,129},{129,193},{2,66},{66,130... | collective-permute-start | bytes 147464 | tf_op jit(solution)/shard_map/ppermute | solution.py:238
  24.0 9.2 %collective-permute-start.1 = (f32[6,1,16,128]{3,2,1,0:T(8,128)S(1)}, f32[6,1,16,128]{3,2,1,0:T(8,128)S(1)}, u32[]{:S(2)}, u32[]{:S(2)}) collective-permute-start(f32[6,1,16,128]{3,2,1,0:T(8,128)S(1)} %copy-done.17), channel_id=1, source_target_pairs={{64,0},{128,64},{192,128},{65,1},{129,65},{193,129},{66,2},{130,66... | collective-permute-start | bytes 147464 | tf_op jit(solution)/shard_map/ppermute | solution.py:239
  26.6 10.7 %collective-permute-start.2 = (f32[6,8,128]{2,1,0:T(8,128)S(1)}, f32[6,8,128]{2,1,0:T(8,128)S(1)}, u32[]{:S(2)}, u32[]{:S(2)}) collective-permute-start(f32[6,8,128]{2,1,0:T(8,128)S(1)} %copy-done.23), channel_id=1, source_target_pairs={{0,4},{4,8},{8,12},{12,16},{16,20},{20,24},{24,28},{28,32},{32,36}... | collective-permute-start | bytes 73736 | tf_op jit(solution)/shard_map/ppermute | solution.py:238
  31.2 7.8 %collective-permute-start.3 = (f32[6,8,128]{2,1,0:T(8,128)S(1)}, f32[6,8,128]{2,1,0:T(8,128)S(1)}, u32[]{:S(2)}, u32[]{:S(2)}) collective-permute-start(f32[6,8,128]{2,1,0:T(8,128)S(1)} %copy-done.22), channel_id=1, source_target_pairs={{4,0},{8,4},{12,8},{16,12},{20,16},{24,20},{28,24},{32,28},{36,32}... | collective-permute-start | bytes 73736 | tf_op jit(solution)/shard_map/ppermute | solution.py:239
  44.2 12.6 %all-to-all-start.2 = ((f32[4,1,768]{2,1,0:T(1,128)}), f32[4,1,768]{2,1,0:T(1,128)S(1)}, u32[]{:S(2)}, u32[]{:S(2)}) async-start(f32[4,1,768]{2,1,0:T(1,128)} %get-tuple-element.34), calls=%async_computation.2 | async-start | bytes 24576 | tf_op jit(solution)/shard_map/all_to_all | solution.py:240
  50.9 19.4 %collective-permute-start.4 = (f32[6,1,16,128]{3,2,1,0:T(8,128)}, f32[6,1,16,128]{3,2,1,0:T(8,128)S(1)}, u32[]{:S(2)}, u32[]{:S(2)}) collective-permute-start(f32[6,1,16,128]{3,2,1,0:T(8,128)} %get-tuple-element.32), channel_id=1, source_target_pairs={{0,64},{64,128},{128,192},{1,65},{65,129},{129,193},{2,66},{66,130... | collective-permute-start | bytes 147464 | tf_op jit(solution)/shard_map/ppermute | solution.py:238
  54.1 16.2 %collective-permute-start.5 = (f32[6,1,16,128]{3,2,1,0:T(8,128)}, f32[6,1,16,128]{3,2,1,0:T(8,128)S(1)}, u32[]{:S(2)}, u32[]{:S(2)}) collective-permute-start(f32[6,1,16,128]{3,2,1,0:T(8,128)} %get-tuple-element.33), channel_id=1, source_target_pairs={{64,0},{128,64},{192,128},{65,1},{129,65},{193,129},{66,2},{130,66... | collective-permute-start | bytes 147464 | tf_op jit(solution)/shard_map/ppermute | solution.py:239
  56.8 7.0 %copy-start.20 = (f32[6,8,128]{2,1,0:T(8,128)S(1)}, f32[6,8,128]{2,1,0:T(8,128)}, u32[]{:S(2)}) copy-start(f32[6,8,128]{2,1,0:T(8,128)} %get-tuple-element.35) | copy-start | bytes 73732
  56.8 11.6 %copy-start.18 = (f32[6,8,128]{2,1,0:T(8,128)S(1)}, f32[6,8,128]{2,1,0:T(8,128)}, u32[]{:S(2)}) copy-start(f32[6,8,128]{2,1,0:T(8,128)} %get-tuple-element.36) | copy-start | bytes 73732
  57.3 18.8 %all-to-all-start.3 = ((f32[16,1,384]{2,1,0:T(1,128)}), f32[16,1,384]{2,1,0:T(1,128)S(1)}, u32[]{:S(2)}, u32[]{:S(2)}) async-start(f32[16,1,384]{2,1,0:T(1,128)} %get-tuple-element.37), calls=%async_computation.3 | async-start | bytes 49152 | tf_op jit(solution)/shard_map/all_to_all | solution.py:302
  63.7 10.7 %collective-permute-start.6 = (f32[6,8,128]{2,1,0:T(8,128)S(1)}, f32[6,8,128]{2,1,0:T(8,128)S(1)}, u32[]{:S(2)}, u32[]{:S(2)}) collective-permute-start(f32[6,8,128]{2,1,0:T(8,128)S(1)} %copy-done.20), channel_id=1, source_target_pairs={{0,4},{4,8},{8,12},{12,16},{16,20},{20,24},{24,28},{28,32},{32,36}... | collective-permute-start | bytes 73736 | tf_op jit(solution)/shard_map/ppermute | solution.py:238
  68.3 7.8 %collective-permute-start.7 = (f32[6,8,128]{2,1,0:T(8,128)S(1)}, f32[6,8,128]{2,1,0:T(8,128)S(1)}, u32[]{:S(2)}, u32[]{:S(2)}) collective-permute-start(f32[6,8,128]{2,1,0:T(8,128)S(1)} %copy-done.18), channel_id=1, source_target_pairs={{4,0},{8,4},{12,8},{16,12},{20,16},{24,20},{28,24},{32,28},{36,32}... | collective-permute-start | bytes 73736 | tf_op jit(solution)/shard_map/ppermute | solution.py:239
  80.7 10.7 %all-to-all-start.4 = ((f32[4,1,768]{2,1,0:T(1,128)}), f32[4,1,768]{2,1,0:T(1,128)S(1)}, u32[]{:S(2)}, u32[]{:S(2)}) async-start(f32[4,1,768]{2,1,0:T(1,128)} %get-tuple-element.42), calls=%async_computation.4 | async-start | bytes 24576 | tf_op jit(solution)/shard_map/all_to_all | solution.py:240
  85.5 20.2 %collective-permute-start.8 = (f32[6,1,16,128]{3,2,1,0:T(8,128)}, f32[6,1,16,128]{3,2,1,0:T(8,128)S(1)}, u32[]{:S(2)}, u32[]{:S(2)}) collective-permute-start(f32[6,1,16,128]{3,2,1,0:T(8,128)} %get-tuple-element.40), channel_id=1, source_target_pairs={{0,64},{64,128},{128,192},{1,65},{65,129},{129,193},{2,66},{66,130... | collective-permute-start | bytes 147464 | tf_op jit(solution)/shard_map/ppermute | solution.py:238
  88.7 17.0 %collective-permute-start.9 = (f32[6,1,16,128]{3,2,1,0:T(8,128)}, f32[6,1,16,128]{3,2,1,0:T(8,128)S(1)}, u32[]{:S(2)}, u32[]{:S(2)}) collective-permute-start(f32[6,1,16,128]{3,2,1,0:T(8,128)} %get-tuple-element.41), channel_id=1, source_target_pairs={{64,0},{128,64},{192,128},{65,1},{129,65},{193,129},{66,2},{130,66... | collective-permute-start | bytes 147464 | tf_op jit(solution)/shard_map/ppermute | solution.py:239
  91.3 7.6 %copy-start.21 = (f32[6,8,128]{2,1,0:T(8,128)S(1)}, f32[6,8,128]{2,1,0:T(8,128)}, u32[]{:S(2)}) copy-start(f32[6,8,128]{2,1,0:T(8,128)} %get-tuple-element.43) | copy-start | bytes 73732
  91.4 12.2 %copy-start.19 = (f32[6,8,128]{2,1,0:T(8,128)S(1)}, f32[6,8,128]{2,1,0:T(8,128)}, u32[]{:S(2)}) copy-start(f32[6,8,128]{2,1,0:T(8,128)} %get-tuple-element.44) | copy-start | bytes 73732
  91.9 19.5 %all-to-all-start.5 = ((f32[16,1,384]{2,1,0:T(1,128)}), f32[16,1,384]{2,1,0:T(1,128)S(1)}, u32[]{:S(2)}, u32[]{:S(2)}) async-start(f32[16,1,384]{2,1,0:T(1,128)} %get-tuple-element.45), calls=%async_computation.5 | async-start | bytes 49152 | tf_op jit(solution)/shard_map/all_to_all | solution.py:302
  99.0 10.9 %collective-permute-start.10 = (f32[6,8,128]{2,1,0:T(8,128)S(1)}, f32[6,8,128]{2,1,0:T(8,128)S(1)}, u32[]{:S(2)}, u32[]{:S(2)}) collective-permute-start(f32[6,8,128]{2,1,0:T(8,128)S(1)} %copy-done.21), channel_id=1, source_target_pairs={{0,4},{4,8},{8,12},{12,16},{16,20},{20,24},{24,28},{28,32},{32,36}... | collective-permute-start | bytes 73736 | tf_op jit(solution)/shard_map/ppermute | solution.py:238
  103.6 7.8 %collective-permute-start.11 = (f32[6,8,128]{2,1,0:T(8,128)S(1)}, f32[6,8,128]{2,1,0:T(8,128)S(1)}, u32[]{:S(2)}, u32[]{:S(2)}) collective-permute-start(f32[6,8,128]{2,1,0:T(8,128)S(1)} %copy-done.19), channel_id=1, source_target_pairs={{4,0},{8,4},{12,8},{16,12},{20,16},{24,20},{28,24},{32,28},{36,32}... | collective-permute-start | bytes 73736 | tf_op jit(solution)/shard_map/ppermute | solution.py:239
  (17 other events, 13.4 us)

commit v14 on v13

--- a/solution.py
+++ b/solution.py
@@ -35,8 +35,8 @@
         first = None
         second = None
         for j in range(n_var):
-            a = blk[2][0, j, i] * src[j:j + 1]
-            b = blk[2][1, j, i] * src[j:j + 1]
+            a = blk[2][j, 0, i] * src[j:j + 1]
+            b = blk[2][j, 1, i] * src[j:j + 1]
             first = a if first is None else first + a
             second = b if second is None else second + b
         out.append(jnp.where(orient == 1, second, first) * weight)
@@ -250,7 +250,7 @@
     shape = sensitivity.shape
     n_wall = lax.axis_size("wall")
     wall_me = lax.axis_index("wall").astype(jnp.int32).reshape(1)
-    blk = (upper_blocks, lower_blocks, iface_blocks, wall_me)
+    blk = (upper_blocks, lower_blocks, jnp.transpose(iface_blocks, (1, 0, 2)), wall_me)
     send_row = send_cell.reshape(n_span, slots)
     orient_row = orient.reshape(n_span, slots)
     weight_row = iface_weight.reshape(n_span, slots)

time: 117 us -> 115 us (0.983)
  local copies, waits for them, and re-layouts: 7.32 us -> 6.03 us
    unnamed x49 -> x48, local copies, waits for them, and re-layouts: 7.32 us -> 6.03 us
where the time goes in v14:
time: 115 us; the launch traced here: 114 us
  starting transfers between devices  70.8 us (62%)
  Pallas kernels  24.4 us (21%)
  blocking collectives  7.28 us (6%)
  local copies, waits for them, and re-layouts  6.03 us (5%)
  waiting for transfers between devices  4.9 us (4%)
    ppermute x6, starting transfers between devices, exchange(): out.append(lax.ppermute(hi_face, axis, forward))  23.3 us
    all_to_all x3, starting transfers between devices, local(): lax.all_to_all(rows, 'span', split_axis=0, concat_axis=0, tiled=True)  22.1 us
    ppermute x6, starting transfers between devices, exchange(): out.append(lax.ppermute(lo_face, axis, backward))  13.9 us
    all_to_all x2, starting transfers between devices, exchange(): lax.all_to_all(w_buf, 'wall', split_axis=0, concat_axis=0, tiled=True)  11.5 us
    pallas_call x3, Pallas kernels, local(): part_a(*blk, adj, sensitivity, diagonal, face_coef, hcl, hch, w_inc)  10.7 us
    all_to_all x1, blocking collectives, exchange(): lax.all_to_all(w_buf, 'wall', split_axis=0, concat_axis=0, tiled=True)  7.28 us
    unnamed x48, local copies, waits for them, and re-layouts  6.03 us
    ppermute x6, waiting for transfers between devices, exchange(): out.append(lax.ppermute(lo_face, axis, backward))  4.87 us
  transfers between devices with their start and end apart: 17, of which 3 were waited for; matrix products, arithmetic and copies ran while one was open for 0% of the time, Pallas kernels for 9%

profile of v14, /device:TPU:118, one launch (start us, length us, event | category | flops | bytes accessed | tf_op | source)
XLA Modules:
  0.0 114.4 jit_solution(16353634930467038865)
XLA Ops:
  0.6 2.8 %shard_map.122 = (f32[6,8,16,128]{3,2,1,0:T(8,128)}, f32[16,1,448]{2,1,0:T(1,128)}, f32[6,1,16,128]{3,2,1,0:T(8,128)}, f32[6,1,16,128]{3,2,1,0:T(8,128)}, f32[6,...) custom-call(f32[3,6,6]{2,1,0:T(8,128)} %ub_ref.13, f32[3,6,6]{2,1,0:T(8,128)} %lb_ref.13, ...), custom_call_target="tpu_custom_call" | custom-call | tf_op jit(solution)/shard_map/pallas_call | solution.py:272
  3.4 7.3 %all_to_all.30.w_inc = f32[4,1,768]{2,1,0:T(1,128)} all-to-all(f32[4,1,768]{2,1,0:T(1,128)} %get-tuple-element.27), channel_id=1, replica_groups=mesh['chord'=4,'span'=16,'wall'=4] {'wall'}, dimensions={0} | all-to-all | bytes 24576 | tf_op jit(solution)/shard_map/all_to_all | solution.py:240
  10.7 8.7 %all-to-all-start.1 = ((f32[16,1,448]{2,1,0:T(1,128)}), f32[16,1,448]{2,1,0:T(1,128)S(1)}, u32[]{:S(2)}, u32[]{:S(2)}) async-start(f32[16,1,448]{2,1,0:T(1,128)} %get-tuple-element.30), calls=%async_computation.1 | async-start | bytes 65536 | tf_op jit(solution)/shard_map/all_to_all | solution.py:302
  19.4 3.2 %collective-permute-start = (f32[6,1,16,128]{3,2,1,0:T(8,128)}, f32[6,1,16,128]{3,2,1,0:T(8,128)S(1)}, u32[]{:S(2)}, u32[]{:S(2)}) collective-permute-start(f32[6,1,16,128]{3,2,1,0:T(8,128)} %get-tuple-element.25), channel_id=1, source_target_pairs={{0,64},{64,128},{128,192},{1,65},{65,129},{129,193},{2,66},{66,130... | collective-permute-start | bytes 147464 | tf_op jit(solution)/shard_map/ppermute | solution.py:238
  22.6 2.7 %collective-permute-start.1 = (f32[6,1,16,128]{3,2,1,0:T(8,128)S(1)}, f32[6,1,16,128]{3,2,1,0:T(8,128)S(1)}, u32[]{:S(2)}, u32[]{:S(2)}) collective-permute-start(f32[6,1,16,128]{3,2,1,0:T(8,128)S(1)} %copy-done.17), channel_id=1, source_target_pairs={{64,0},{128,64},{192,128},{65,1},{129,65},{193,129},{66,2},{130,66... | collective-permute-start | bytes 147464 | tf_op jit(solution)/shard_map/ppermute | solution.py:239
  25.3 4.6 %collective-permute-start.2 = (f32[6,8,128]{2,1,0:T(8,128)S(1)}, f32[6,8,128]{2,1,0:T(8,128)S(1)}, u32[]{:S(2)}, u32[]{:S(2)}) collective-permute-start(f32[6,8,128]{2,1,0:T(8,128)S(1)} %copy-done.23), channel_id=1, source_target_pairs={{0,4},{4,8},{8,12},{12,16},{16,20},{20,24},{24,28},{28,32},{32,36}... | collective-permute-start | bytes 73736 | tf_op jit(solution)/shard_map/ppermute | solution.py:238
  29.9 1.9 %collective-permute-start.3 = (f32[6,8,128]{2,1,0:T(8,128)S(1)}, f32[6,8,128]{2,1,0:T(8,128)S(1)}, u32[]{:S(2)}, u32[]{:S(2)}) collective-permute-start(f32[6,8,128]{2,1,0:T(8,128)S(1)} %copy-done.22), channel_id=1, source_target_pairs={{4,0},{8,4},{12,8},{16,12},{20,16},{24,20},{28,24},{32,28},{36,32}... | collective-permute-start | bytes 73736 | tf_op jit(solution)/shard_map/ppermute | solution.py:239
  32.5 3.6 %shard_map.123.part_ref = f32[6,8,16,128]{3,2,1,0:T(8,128)} custom-call(f32[3,6,6]{2,1,0:T(8,128)} %ub_ref.13, f32[3,6,6]{2,1,0:T(8,128)} %lb_ref.13, f32[6,2,6]{2,1,0:T(2,128)} %bitcast.7, s32[1]{0:T(128)} %bitcast.1.wall_me.rest_3_.rest_4_, f32[6,8,16,128]{3,2,1,0:T(8,128)} %get-tuple-element.24.adj_ref, f32[6,8,16,128]{3,2,1,0:T(8,128)} %sens_ref.7, ...), custom_call_target="tpu_custom_call" | custom-call | tf_op jit(solution)/shard_map/pallas_call | solution.py:303
  38.9 3.9 %shard_map.124 = (f32[6,8,16,128]{3,2,1,0:T(8,128)}, f32[16,1,384]{2,1,0:T(1,128)}, f32[6,1,16,128]{3,2,1,0:T(8,128)}, f32[6,1,16,128]{3,2,1,0:T(8,128)}, f32[6,...) custom-call(f32[3,6,6]{2,1,0:T(8,128)} %ub_ref.13, f32[3,6,6]{2,1,0:T(8,128)} %lb_ref.13, ...), custom_call_target="tpu_custom_call" | custom-call | tf_op jit(solution)/shard_map/pallas_call | solution.py:306
  42.8 6.7 %all-to-all-start.2 = ((f32[4,1,768]{2,1,0:T(1,128)}), f32[4,1,768]{2,1,0:T(1,128)S(1)}, u32[]{:S(2)}, u32[]{:S(2)}) async-start(f32[4,1,768]{2,1,0:T(1,128)} %get-tuple-element.34), calls=%async_computation.2 | async-start | bytes 24576 | tf_op jit(solution)/shard_map/all_to_all | solution.py:240
  49.5 3.2 %collective-permute-start.4 = (f32[6,1,16,128]{3,2,1,0:T(8,128)}, f32[6,1,16,128]{3,2,1,0:T(8,128)S(1)}, u32[]{:S(2)}, u32[]{:S(2)}) collective-permute-start(f32[6,1,16,128]{3,2,1,0:T(8,128)} %get-tuple-element.32), channel_id=1, source_target_pairs={{0,64},{64,128},{128,192},{1,65},{65,129},{129,193},{2,66},{66,130... | collective-permute-start | bytes 147464 | tf_op jit(solution)/shard_map/ppermute | solution.py:238
  52.7 2.7 %collective-permute-start.5 = (f32[6,1,16,128]{3,2,1,0:T(8,128)}, f32[6,1,16,128]{3,2,1,0:T(8,128)S(1)}, u32[]{:S(2)}, u32[]{:S(2)}) collective-permute-start(f32[6,1,16,128]{3,2,1,0:T(8,128)} %get-tuple-element.33), channel_id=1, source_target_pairs={{64,0},{128,64},{192,128},{65,1},{129,65},{193,129},{66,2},{130,66... | collective-permute-start | bytes 147464 | tf_op jit(solution)/shard_map/ppermute | solution.py:239
  56.0 6.4 %all-to-all-start.3 = ((f32[16,1,384]{2,1,0:T(1,128)}), f32[16,1,384]{2,1,0:T(1,128)S(1)}, u32[]{:S(2)}, u32[]{:S(2)}) async-start(f32[16,1,384]{2,1,0:T(1,128)} %get-tuple-element.37), calls=%async_computation.3 | async-start | bytes 49152 | tf_op jit(solution)/shard_map/all_to_all | solution.py:302
  62.4 4.6 %collective-permute-start.6 = (f32[6,8,128]{2,1,0:T(8,128)S(1)}, f32[6,8,128]{2,1,0:T(8,128)S(1)}, u32[]{:S(2)}, u32[]{:S(2)}) collective-permute-start(f32[6,8,128]{2,1,0:T(8,128)S(1)} %copy-done.20), channel_id=1, source_target_pairs={{0,4},{4,8},{8,12},{12,16},{16,20},{20,24},{24,28},{28,32},{32,36}... | collective-permute-start | bytes 73736 | tf_op jit(solution)/shard_map/ppermute | solution.py:238
  69.6 3.6 %shard_map.125.part_ref = f32[6,8,16,128]{3,2,1,0:T(8,128)} custom-call(f32[3,6,6]{2,1,0:T(8,128)} %ub_ref.13, f32[3,6,6]{2,1,0:T(8,128)} %lb_ref.13, f32[6,2,6]{2,1,0:T(2,128)} %bitcast.9, s32[1]{0:T(128)} %bitcast.1.wall_me.rest_3_.rest_4_, f32[6,8,16,128]{3,2,1,0:T(8,128)} %get-tuple-element.31.adj_ref, f32[6,8,16,128]{3,2,1,0:T(8,128)} %sens_ref.7, ...), custom_call_target="tpu_custom_call" | custom-call | tf_op jit(solution)/shard_map/pallas_call | solution.py:303
  75.4 3.8 %shard_map.126 = (f32[6,8,16,128]{3,2,1,0:T(8,128)}, f32[16,1,384]{2,1,0:T(1,128)}, f32[6,1,16,128]{3,2,1,0:T(8,128)}, f32[6,1,16,128]{3,2,1,0:T(8,128)}, f32[6,...) custom-call(f32[3,6,6]{2,1,0:T(8,128)} %ub_ref.13, f32[3,6,6]{2,1,0:T(8,128)} %lb_ref.13, ...), custom_call_target="tpu_custom_call" | custom-call | tf_op jit(solution)/shard_map/pallas_call | solution.py:308
  79.3 4.8 %all-to-all-start.4 = ((f32[4,1,768]{2,1,0:T(1,128)}), f32[4,1,768]{2,1,0:T(1,128)S(1)}, u32[]{:S(2)}, u32[]{:S(2)}) async-start(f32[4,1,768]{2,1,0:T(1,128)} %get-tuple-element.42), calls=%async_computation.4 | async-start | bytes 24576 | tf_op jit(solution)/shard_map/all_to_all | solution.py:240
  84.1 3.2 %collective-permute-start.8 = (f32[6,1,16,128]{3,2,1,0:T(8,128)}, f32[6,1,16,128]{3,2,1,0:T(8,128)S(1)}, u32[]{:S(2)}, u32[]{:S(2)}) collective-permute-start(f32[6,1,16,128]{3,2,1,0:T(8,128)} %get-tuple-element.40), channel_id=1, source_target_pairs={{0,64},{64,128},{128,192},{1,65},{65,129},{129,193},{2,66},{66,130... | collective-permute-start | bytes 147464 | tf_op jit(solution)/shard_map/ppermute | solution.py:238
  87.3 2.7 %collective-permute-start.9 = (f32[6,1,16,128]{3,2,1,0:T(8,128)}, f32[6,1,16,128]{3,2,1,0:T(8,128)S(1)}, u32[]{:S(2)}, u32[]{:S(2)}) collective-permute-start(f32[6,1,16,128]{3,2,1,0:T(8,128)} %get-tuple-element.41), channel_id=1, source_target_pairs={{64,0},{128,64},{192,128},{65,1},{129,65},{193,129},{66,2},{130,66... | collective-permute-start | bytes 147464 | tf_op jit(solution)/shard_map/ppermute | solution.py:239
  90.6 7.0 %all-to-all-start.5 = ((f32[16,1,384]{2,1,0:T(1,128)}), f32[16,1,384]{2,1,0:T(1,128)S(1)}, u32[]{:S(2)}, u32[]{:S(2)}) async-start(f32[16,1,384]{2,1,0:T(1,128)} %get-tuple-element.45), calls=%async_computation.5 | async-start | bytes 49152 | tf_op jit(solution)/shard_map/all_to_all | solution.py:302
  97.6 4.6 %collective-permute-start.10 = (f32[6,8,128]{2,1,0:T(8,128)S(1)}, f32[6,8,128]{2,1,0:T(8,128)S(1)}, u32[]{:S(2)}, u32[]{:S(2)}) collective-permute-start(f32[6,8,128]{2,1,0:T(8,128)S(1)} %copy-done.21), channel_id=1, source_target_pairs={{0,4},{4,8},{8,12},{12,16},{16,20},{20,24},{24,28},{28,32},{32,36}... | collective-permute-start | bytes 73736 | tf_op jit(solution)/shard_map/ppermute | solution.py:238
  102.2 2.1 %collective-permute-start.11 = (f32[6,8,128]{2,1,0:T(8,128)S(1)}, f32[6,8,128]{2,1,0:T(8,128)S(1)}, u32[]{:S(2)}, u32[]{:S(2)}) collective-permute-start(f32[6,8,128]{2,1,0:T(8,128)S(1)} %copy-done.19), channel_id=1, source_target_pairs={{4,0},{8,4},{12,8},{16,12},{20,16},{24,20},{28,24},{32,28},{36,32}... | collective-permute-start | bytes 73736 | tf_op jit(solution)/shard_map/ppermute | solution.py:239
  104.9 3.6 %shard_map.127.part_ref = f32[6,8,16,128]{3,2,1,0:T(8,128)} custom-call(f32[3,6,6]{2,1,0:T(8,128)} %ub_ref.13, f32[3,6,6]{2,1,0:T(8,128)} %lb_ref.13, f32[6,2,6]{2,1,0:T(2,128)} %bitcast.11, s32[1]{0:T(128)} %bitcast.1.wall_me.rest_3_.rest_4_, f32[6,8,16,128]{3,2,1,0:T(8,128)} %get-tuple-element.39.adj_ref, f32[6,8,16,128]{3,2,1,0:T(8,128)} %sens_ref.7, ...), custom_call_target="tpu_custom_call" | custom-call | tf_op jit(solution)/shard_map/pallas_call | solution.py:303
  111.2 3.2 %shard_map.128 = (f32[6,8,16,128]{3,2,1,0:T(8,128)}, f32[8,16,128]{2,1,0:T(8,128)}) custom-call(f32[3,6,6]{2,1,0:T(8,128)} %ub_ref.13, f32[3,6,6]{2,1,0:T(8,128)} %lb_ref.13, f32[6,2,6]{2,1,0:T(2,128)} %bitcast.12, f32[6,8,16,128]{3,2,1,0:T(8,128)} %shard_map.127.part_ref, f32[6,8,16,128]{3,2,1,0:T(8,128)} %diag_ref.13, f32[3,8,16,128]{3,2,1,0:T(8,128)} %face_ref.11, ...), custom_call_target="tpu_custom_call" | custom-call | tf_op jit(solution)/shard_map/pallas_call | solution.py:310
  (66 shorter events, 12.8 us)
Async XLA Ops:
  3.4 19.2 %copy-start.17 = (f32[6,1,16,128]{3,2,1,0:T(8,128)S(1)}, f32[6,1,16,128]{3,2,1,0:T(8,128)}, u32[]{:S(2)}) copy-start(f32[6,1,16,128]{3,2,1,0:T(8,128)} %get-tuple-element.26) | copy-start | bytes 147460
  10.7 14.6 %copy-start.23 = (f32[6,8,128]{2,1,0:T(8,128)S(1)}, f32[6,8,128]{2,1,0:T(8,128)}, u32[]{:S(2)}) copy-start(f32[6,8,128]{2,1,0:T(8,128)} %get-tuple-element.28) | copy-start | bytes 73732
  10.7 19.2 %copy-start.22 = (f32[6,8,128]{2,1,0:T(8,128)S(1)}, f32[6,8,128]{2,1,0:T(8,128)}, u32[]{:S(2)}) copy-start(f32[6,8,128]{2,1,0:T(8,128)} %get-tuple-element.29) | copy-start | bytes 73732
  10.7 27.0 %all-to-all-start.1 = ((f32[16,1,448]{2,1,0:T(1,128)}), f32[16,1,448]{2,1,0:T(1,128)S(1)}, u32[]{:S(2)}, u32[]{:S(2)}) async-start(f32[16,1,448]{2,1,0:T(1,128)} %get-tuple-element.30), calls=%async_computation.1 | async-start | bytes 65536 | tf_op jit(solution)/shard_map/all_to_all | solution.py:302
  19.4 12.4 %collective-permute-start = (f32[6,1,16,128]{3,2,1,0:T(8,128)}, f32[6,1,16,128]{3,2,1,0:T(8,128)S(1)}, u32[]{:S(2)}, u32[]{:S(2)}) collective-permute-start(f32[6,1,16,128]{3,2,1,0:T(8,128)} %get-tuple-element.25), channel_id=1, source_target_pairs={{0,64},{64,128},{128,192},{1,65},{65,129},{129,193},{2,66},{66,130... | collective-permute-start | bytes 147464 | tf_op jit(solution)/shard_map/ppermute | solution.py:238
  22.6 9.2 %collective-permute-start.1 = (f32[6,1,16,128]{3,2,1,0:T(8,128)S(1)}, f32[6,1,16,128]{3,2,1,0:T(8,128)S(1)}, u32[]{:S(2)}, u32[]{:S(2)}) collective-permute-start(f32[6,1,16,128]{3,2,1,0:T(8,128)S(1)} %copy-done.17), channel_id=1, source_target_pairs={{64,0},{128,64},{192,128},{65,1},{129,65},{193,129},{66,2},{130,66... | collective-permute-start | bytes 147464 | tf_op jit(solution)/shard_map/ppermute | solution.py:239
  25.3 10.7 %collective-permute-start.2 = (f32[6,8,128]{2,1,0:T(8,128)S(1)}, f32[6,8,128]{2,1,0:T(8,128)S(1)}, u32[]{:S(2)}, u32[]{:S(2)}) collective-permute-start(f32[6,8,128]{2,1,0:T(8,128)S(1)} %copy-done.23), channel_id=1, source_target_pairs={{0,4},{4,8},{8,12},{12,16},{16,20},{20,24},{24,28},{28,32},{32,36}... | collective-permute-start | bytes 73736 | tf_op jit(solution)/shard_map/ppermute | solution.py:238
  29.9 7.8 %collective-permute-start.3 = (f32[6,8,128]{2,1,0:T(8,128)S(1)}, f32[6,8,128]{2,1,0:T(8,128)S(1)}, u32[]{:S(2)}, u32[]{:S(2)}) collective-permute-start(f32[6,8,128]{2,1,0:T(8,128)S(1)} %copy-done.22), channel_id=1, source_target_pairs={{4,0},{8,4},{12,8},{16,12},{20,16},{24,20},{28,24},{32,28},{36,32}... | collective-permute-start | bytes 73736 | tf_op jit(solution)/shard_map/ppermute | solution.py:239
  42.8 12.6 %all-to-all-start.2 = ((f32[4,1,768]{2,1,0:T(1,128)}), f32[4,1,768]{2,1,0:T(1,128)S(1)}, u32[]{:S(2)}, u32[]{:S(2)}) async-start(f32[4,1,768]{2,1,0:T(1,128)} %get-tuple-element.34), calls=%async_computation.2 | async-start | bytes 24576 | tf_op jit(solution)/shard_map/all_to_all | solution.py:240
  49.5 19.4 %collective-permute-start.4 = (f32[6,1,16,128]{3,2,1,0:T(8,128)}, f32[6,1,16,128]{3,2,1,0:T(8,128)S(1)}, u32[]{:S(2)}, u32[]{:S(2)}) collective-permute-start(f32[6,1,16,128]{3,2,1,0:T(8,128)} %get-tuple-element.32), channel_id=1, source_target_pairs={{0,64},{64,128},{128,192},{1,65},{65,129},{129,193},{2,66},{66,130... | collective-permute-start | bytes 147464 | tf_op jit(solution)/shard_map/ppermute | solution.py:238
  52.7 16.2 %collective-permute-start.5 = (f32[6,1,16,128]{3,2,1,0:T(8,128)}, f32[6,1,16,128]{3,2,1,0:T(8,128)S(1)}, u32[]{:S(2)}, u32[]{:S(2)}) collective-permute-start(f32[6,1,16,128]{3,2,1,0:T(8,128)} %get-tuple-element.33), channel_id=1, source_target_pairs={{64,0},{128,64},{192,128},{65,1},{129,65},{193,129},{66,2},{130,66... | collective-permute-start | bytes 147464 | tf_op jit(solution)/shard_map/ppermute | solution.py:239
  55.4 7.0 %copy-start.20 = (f32[6,8,128]{2,1,0:T(8,128)S(1)}, f32[6,8,128]{2,1,0:T(8,128)}, u32[]{:S(2)}) copy-start(f32[6,8,128]{2,1,0:T(8,128)} %get-tuple-element.35) | copy-start | bytes 73732
  55.4 11.6 %copy-start.18 = (f32[6,8,128]{2,1,0:T(8,128)S(1)}, f32[6,8,128]{2,1,0:T(8,128)}, u32[]{:S(2)}) copy-start(f32[6,8,128]{2,1,0:T(8,128)} %get-tuple-element.36) | copy-start | bytes 73732
  56.0 18.8 %all-to-all-start.3 = ((f32[16,1,384]{2,1,0:T(1,128)}), f32[16,1,384]{2,1,0:T(1,128)S(1)}, u32[]{:S(2)}, u32[]{:S(2)}) async-start(f32[16,1,384]{2,1,0:T(1,128)} %get-tuple-element.37), calls=%async_computation.3 | async-start | bytes 49152 | tf_op jit(solution)/shard_map/all_to_all | solution.py:302
  62.4 10.7 %collective-permute-start.6 = (f32[6,8,128]{2,1,0:T(8,128)S(1)}, f32[6,8,128]{2,1,0:T(8,128)S(1)}, u32[]{:S(2)}, u32[]{:S(2)}) collective-permute-start(f32[6,8,128]{2,1,0:T(8,128)S(1)} %copy-done.20), channel_id=1, source_target_pairs={{0,4},{4,8},{8,12},{12,16},{16,20},{20,24},{24,28},{28,32},{32,36}... | collective-permute-start | bytes 73736 | tf_op jit(solution)/shard_map/ppermute | solution.py:238
  67.0 7.8 %collective-permute-start.7 = (f32[6,8,128]{2,1,0:T(8,128)S(1)}, f32[6,8,128]{2,1,0:T(8,128)S(1)}, u32[]{:S(2)}, u32[]{:S(2)}) collective-permute-start(f32[6,8,128]{2,1,0:T(8,128)S(1)} %copy-done.18), channel_id=1, source_target_pairs={{4,0},{8,4},{12,8},{16,12},{20,16},{24,20},{28,24},{32,28},{36,32}... | collective-permute-start | bytes 73736 | tf_op jit(solution)/shard_map/ppermute | solution.py:239
  79.3 10.7 %all-to-all-start.4 = ((f32[4,1,768]{2,1,0:T(1,128)}), f32[4,1,768]{2,1,0:T(1,128)S(1)}, u32[]{:S(2)}, u32[]{:S(2)}) async-start(f32[4,1,768]{2,1,0:T(1,128)} %get-tuple-element.42), calls=%async_computation.4 | async-start | bytes 24576 | tf_op jit(solution)/shard_map/all_to_all | solution.py:240
  84.1 20.2 %collective-permute-start.8 = (f32[6,1,16,128]{3,2,1,0:T(8,128)}, f32[6,1,16,128]{3,2,1,0:T(8,128)S(1)}, u32[]{:S(2)}, u32[]{:S(2)}) collective-permute-start(f32[6,1,16,128]{3,2,1,0:T(8,128)} %get-tuple-element.40), channel_id=1, source_target_pairs={{0,64},{64,128},{128,192},{1,65},{65,129},{129,193},{2,66},{66,130... | collective-permute-start | bytes 147464 | tf_op jit(solution)/shard_map/ppermute | solution.py:238
  87.3 17.0 %collective-permute-start.9 = (f32[6,1,16,128]{3,2,1,0:T(8,128)}, f32[6,1,16,128]{3,2,1,0:T(8,128)S(1)}, u32[]{:S(2)}, u32[]{:S(2)}) collective-permute-start(f32[6,1,16,128]{3,2,1,0:T(8,128)} %get-tuple-element.41), channel_id=1, source_target_pairs={{64,0},{128,64},{192,128},{65,1},{129,65},{193,129},{66,2},{130,66... | collective-permute-start | bytes 147464 | tf_op jit(solution)/shard_map/ppermute | solution.py:239
  90.0 7.6 %copy-start.21 = (f32[6,8,128]{2,1,0:T(8,128)S(1)}, f32[6,8,128]{2,1,0:T(8,128)}, u32[]{:S(2)}) copy-start(f32[6,8,128]{2,1,0:T(8,128)} %get-tuple-element.43) | copy-start | bytes 73732
  90.0 12.2 %copy-start.19 = (f32[6,8,128]{2,1,0:T(8,128)S(1)}, f32[6,8,128]{2,1,0:T(8,128)}, u32[]{:S(2)}) copy-start(f32[6,8,128]{2,1,0:T(8,128)} %get-tuple-element.44) | copy-start | bytes 73732
  90.6 19.4 %all-to-all-start.5 = ((f32[16,1,384]{2,1,0:T(1,128)}), f32[16,1,384]{2,1,0:T(1,128)S(1)}, u32[]{:S(2)}, u32[]{:S(2)}) async-start(f32[16,1,384]{2,1,0:T(1,128)} %get-tuple-element.45), calls=%async_computation.5 | async-start | bytes 49152 | tf_op jit(solution)/shard_map/all_to_all | solution.py:302
  97.6 10.9 %collective-permute-start.10 = (f32[6,8,128]{2,1,0:T(8,128)S(1)}, f32[6,8,128]{2,1,0:T(8,128)S(1)}, u32[]{:S(2)}, u32[]{:S(2)}) collective-permute-start(f32[6,8,128]{2,1,0:T(8,128)S(1)} %copy-done.21), channel_id=1, source_target_pairs={{0,4},{4,8},{8,12},{12,16},{16,20},{20,24},{24,28},{28,32},{32,36}... | collective-permute-start | bytes 73736 | tf_op jit(solution)/shard_map/ppermute | solution.py:238
  102.2 7.8 %collective-permute-start.11 = (f32[6,8,128]{2,1,0:T(8,128)S(1)}, f32[6,8,128]{2,1,0:T(8,128)S(1)}, u32[]{:S(2)}, u32[]{:S(2)}) collective-permute-start(f32[6,8,128]{2,1,0:T(8,128)S(1)} %copy-done.19), channel_id=1, source_target_pairs={{4,0},{8,4},{12,8},{16,12},{20,16},{24,20},{28,24},{32,28},{36,32}... | collective-permute-start | bytes 73736 | tf_op jit(solution)/shard_map/ppermute | solution.py:239
  (17 other events, 13.4 us)

commit v15 on v14

--- a/solution.py
+++ b/solution.py
@@ -48,15 +48,23 @@
 
 
 def to_chunks(rows_ref, pieces, slots):
-    n_dest = rows_ref.shape[0]
+    n_dest, n_sub, lanes = rows_ref.shape
+    pad = n_sub * lanes - len(pieces) * slots
     for t in range(n_dest):
-        rows_ref[t] = jnp.concatenate([p[:, t * slots:(t + 1) * slots] for p in pieces], axis=1)
+        flat = [p[:, t * slots:(t + 1) * slots] for p in pieces]
+        if pad:
+            flat.append(jnp.zeros((1, pad), F32))
+        flat = jnp.concatenate(flat, axis=1)
+        rows_ref[t] = jnp.concatenate([flat[:, r * lanes:(r + 1) * lanes] for r in range(n_sub)], axis=0)
 
 
 def from_chunks(inc, count, slots):
-    n_src = inc.shape[0]
-    return [jnp.concatenate([inc[s][:, v * slots:(v + 1) * slots] for s in range(n_src)], axis=1)
-            for v in range(count)]
+    n_src, _, lanes = inc.shape
+
+    def piece(s, v):
+        r, c = divmod(v * slots, lanes)
+        return inc[s][r:r + 1, c:c + slots]
+    return [jnp.concatenate([piece(s, v) for s in range(n_src)], axis=1) for v in range(count)]
 
 
 def wall_columns(adj):
@@ -260,8 +268,9 @@
     smem = pl.BlockSpec(memory_space=pltpu.SMEM)
     adj_sds = jax.ShapeDtypeStruct(shape, F32)
     tgt_sds = jax.ShapeDtypeStruct((1, n_rows), jnp.int32)
-    first_rows = jax.ShapeDtypeStruct((n_span, 1, (n_var + 1) * slots), F32)
-    rows_sds = jax.ShapeDtypeStruct((n_span, 1, n_var * slots), F32)
+    lanes = shape[3]
+    first_rows = jax.ShapeDtypeStruct((n_span, -(-(n_var + 1) * slots // lanes), lanes), F32)
+    rows_sds = jax.ShapeDtypeStruct((n_span, -(-n_var * slots // lanes), lanes), F32)
 
     init = pl.pallas_call(
         init_kernel,

time: 115 us -> 115 us (level)
  no operation moved by 1% of the time
where the time goes in v15:
time: 115 us; the launch traced here: 114 us
  starting transfers between devices  70.8 us (62%)
  Pallas kernels  24.2 us (21%)
  blocking collectives  7.28 us (6%)
  local copies, waits for them, and re-layouts  6.02 us (5%)
  waiting for transfers between devices  4.9 us (4%)
    ppermute x6, starting transfers between devices, exchange(): out.append(lax.ppermute(hi_face, axis, forward))  23.3 us
    all_to_all x3, starting transfers between devices, local(): lax.all_to_all(rows, 'span', split_axis=0, concat_axis=0, tiled=True)  22.1 us
    ppermute x6, starting transfers between devices, exchange(): out.append(lax.ppermute(lo_face, axis, backward))  13.9 us
    all_to_all x2, starting transfers between devices, exchange(): lax.all_to_all(w_buf, 'wall', split_axis=0, concat_axis=0, tiled=True)  11.5 us
    pallas_call x3, Pallas kernels, local(): part_a(*blk, adj, sensitivity, diagonal, face_coef, hcl, hch, w_inc)  10.7 us
    all_to_all x1, blocking collectives, exchange(): lax.all_to_all(w_buf, 'wall', split_axis=0, concat_axis=0, tiled=True)  7.28 us
    unnamed x48, local copies, waits for them, and re-layouts  6.02 us
    ppermute x6, waiting for transfers between devices, exchange(): out.append(lax.ppermute(lo_face, axis, backward))  4.87 us
  transfers between devices with their start and end apart: 17, of which 3 were waited for; matrix products, arithmetic and copies ran while one was open for 0% of the time, Pallas kernels for 9%

profile of v15, /device:TPU:118, one launch (start us, length us, event | category | flops | bytes accessed | tf_op | source)
XLA Modules:
  0.0 114.2 jit_solution(3984894309360889288)
XLA Ops:
  0.6 2.8 %shard_map.122 = (f32[6,8,16,128]{3,2,1,0:T(8,128)}, f32[16,4,128]{2,1,0:T(4,128)}, f32[6,1,16,128]{3,2,1,0:T(8,128)}, f32[6,1,16,128]{3,2,1,0:T(8,128)}, f32[6,...) custom-call(f32[3,6,6]{2,1,0:T(8,128)} %ub_ref.13, f32[3,6,6]{2,1,0:T(8,128)} %lb_ref.13, ...), custom_call_target="tpu_custom_call" | custom-call | tf_op jit(solution)/shard_map/pallas_call | solution.py:281
  3.5 7.3 %all_to_all.30.w_inc = f32[4,1,768]{2,1,0:T(1,128)} all-to-all(f32[4,1,768]{2,1,0:T(1,128)} %get-tuple-element.27), channel_id=1, replica_groups=mesh['chord'=4,'span'=16,'wall'=4] {'wall'}, dimensions={0} | all-to-all | bytes 24576 | tf_op jit(solution)/shard_map/all_to_all | solution.py:248
  10.7 8.7 %all-to-all-start.1 = ((f32[16,4,128]{2,1,0:T(4,128)}), f32[16,4,128]{2,1,0:T(4,128)S(1)}, u32[]{:S(2)}, u32[]{:S(2)}) async-start(f32[16,4,128]{2,1,0:T(4,128)} %get-tuple-element.30), calls=%async_computation.1 | async-start | bytes 65536 | tf_op jit(solution)/shard_map/all_to_all | solution.py:311
  19.5 3.2 %collective-permute-start = (f32[6,1,16,128]{3,2,1,0:T(8,128)}, f32[6,1,16,128]{3,2,1,0:T(8,128)S(1)}, u32[]{:S(2)}, u32[]{:S(2)}) collective-permute-start(f32[6,1,16,128]{3,2,1,0:T(8,128)} %get-tuple-element.25), channel_id=1, source_target_pairs={{0,64},{64,128},{128,192},{1,65},{65,129},{129,193},{2,66},{66,130... | collective-permute-start | bytes 147464 | tf_op jit(solution)/shard_map/ppermute | solution.py:246
  22.7 2.7 %collective-permute-start.1 = (f32[6,1,16,128]{3,2,1,0:T(8,128)S(1)}, f32[6,1,16,128]{3,2,1,0:T(8,128)S(1)}, u32[]{:S(2)}, u32[]{:S(2)}) collective-permute-start(f32[6,1,16,128]{3,2,1,0:T(8,128)S(1)} %copy-done.17), channel_id=1, source_target_pairs={{64,0},{128,64},{192,128},{65,1},{129,65},{193,129},{66,2},{130,66... | collective-permute-start | bytes 147464 | tf_op jit(solution)/shard_map/ppermute | solution.py:247
  25.3 4.6 %collective-permute-start.2 = (f32[6,8,128]{2,1,0:T(8,128)S(1)}, f32[6,8,128]{2,1,0:T(8,128)S(1)}, u32[]{:S(2)}, u32[]{:S(2)}) collective-permute-start(f32[6,8,128]{2,1,0:T(8,128)S(1)} %copy-done.23), channel_id=1, source_target_pairs={{0,4},{4,8},{8,12},{12,16},{16,20},{20,24},{24,28},{28,32},{32,36}... | collective-permute-start | bytes 73736 | tf_op jit(solution)/shard_map/ppermute | solution.py:246
  29.9 1.9 %collective-permute-start.3 = (f32[6,8,128]{2,1,0:T(8,128)S(1)}, f32[6,8,128]{2,1,0:T(8,128)S(1)}, u32[]{:S(2)}, u32[]{:S(2)}) collective-permute-start(f32[6,8,128]{2,1,0:T(8,128)S(1)} %copy-done.22), channel_id=1, source_target_pairs={{4,0},{8,4},{12,8},{16,12},{20,16},{24,20},{28,24},{32,28},{36,32}... | collective-permute-start | bytes 73736 | tf_op jit(solution)/shard_map/ppermute | solution.py:247
  32.5 3.6 %shard_map.123.part_ref = f32[6,8,16,128]{3,2,1,0:T(8,128)} custom-call(f32[3,6,6]{2,1,0:T(8,128)} %ub_ref.13, f32[3,6,6]{2,1,0:T(8,128)} %lb_ref.13, f32[6,2,6]{2,1,0:T(2,128)} %bitcast.7, s32[1]{0:T(128)} %bitcast.1.wall_me.rest_3_.rest_4_, f32[6,8,16,128]{3,2,1,0:T(8,128)} %get-tuple-element.24.adj_ref, f32[6,8,16,128]{3,2,1,0:T(8,128)} %sens_ref.7, ...), custom_call_target="tpu_custom_call" | custom-call | tf_op jit(solution)/shard_map/pallas_call | solution.py:312
  39.0 3.8 %shard_map.124 = (f32[6,8,16,128]{3,2,1,0:T(8,128)}, f32[16,3,128]{2,1,0:T(4,128)}, f32[6,1,16,128]{3,2,1,0:T(8,128)}, f32[6,1,16,128]{3,2,1,0:T(8,128)}, f32[6,...) custom-call(f32[3,6,6]{2,1,0:T(8,128)} %ub_ref.13, f32[3,6,6]{2,1,0:T(8,128)} %lb_ref.13, ...), custom_call_target="tpu_custom_call" | custom-call | tf_op jit(solution)/shard_map/pallas_call | solution.py:315
  42.7 6.7 %all-to-all-start.2 = ((f32[4,1,768]{2,1,0:T(1,128)}), f32[4,1,768]{2,1,0:T(1,128)S(1)}, u32[]{:S(2)}, u32[]{:S(2)}) async-start(f32[4,1,768]{2,1,0:T(1,128)} %get-tuple-element.34), calls=%async_computation.2 | async-start | bytes 24576 | tf_op jit(solution)/shard_map/all_to_all | solution.py:248
  49.5 3.2 %collective-permute-start.4 = (f32[6,1,16,128]{3,2,1,0:T(8,128)}, f32[6,1,16,128]{3,2,1,0:T(8,128)S(1)}, u32[]{:S(2)}, u32[]{:S(2)}) collective-permute-start(f32[6,1,16,128]{3,2,1,0:T(8,128)} %get-tuple-element.32), channel_id=1, source_target_pairs={{0,64},{64,128},{128,192},{1,65},{65,129},{129,193},{2,66},{66,130... | collective-permute-start | bytes 147464 | tf_op jit(solution)/shard_map/ppermute | solution.py:246
  52.6 2.7 %collective-permute-start.5 = (f32[6,1,16,128]{3,2,1,0:T(8,128)}, f32[6,1,16,128]{3,2,1,0:T(8,128)S(1)}, u32[]{:S(2)}, u32[]{:S(2)}) collective-permute-start(f32[6,1,16,128]{3,2,1,0:T(8,128)} %get-tuple-element.33), channel_id=1, source_target_pairs={{64,0},{128,64},{192,128},{65,1},{129,65},{193,129},{66,2},{130,66... | collective-permute-start | bytes 147464 | tf_op jit(solution)/shard_map/ppermute | solution.py:247
  55.9 6.4 %all-to-all-start.3 = ((f32[16,3,128]{2,1,0:T(4,128)}), f32[16,3,128]{2,1,0:T(4,128)S(1)}, u32[]{:S(2)}, u32[]{:S(2)}) async-start(f32[16,3,128]{2,1,0:T(4,128)} %get-tuple-element.37), calls=%async_computation.3 | async-start | bytes 65536 | tf_op jit(solution)/shard_map/all_to_all | solution.py:311
  62.3 4.6 %collective-permute-start.6 = (f32[6,8,128]{2,1,0:T(8,128)S(1)}, f32[6,8,128]{2,1,0:T(8,128)S(1)}, u32[]{:S(2)}, u32[]{:S(2)}) collective-permute-start(f32[6,8,128]{2,1,0:T(8,128)S(1)} %copy-done.20), channel_id=1, source_target_pairs={{0,4},{4,8},{8,12},{12,16},{16,20},{20,24},{24,28},{28,32},{32,36}... | collective-permute-start | bytes 73736 | tf_op jit(solution)/shard_map/ppermute | solution.py:246
  69.5 3.6 %shard_map.125.part_ref = f32[6,8,16,128]{3,2,1,0:T(8,128)} custom-call(f32[3,6,6]{2,1,0:T(8,128)} %ub_ref.13, f32[3,6,6]{2,1,0:T(8,128)} %lb_ref.13, f32[6,2,6]{2,1,0:T(2,128)} %bitcast.9, s32[1]{0:T(128)} %bitcast.1.wall_me.rest_3_.rest_4_, f32[6,8,16,128]{3,2,1,0:T(8,128)} %get-tuple-element.31.adj_ref, f32[6,8,16,128]{3,2,1,0:T(8,128)} %sens_ref.7, ...), custom_call_target="tpu_custom_call" | custom-call | tf_op jit(solution)/shard_map/pallas_call | solution.py:312
  75.4 3.7 %shard_map.126 = (f32[6,8,16,128]{3,2,1,0:T(8,128)}, f32[16,3,128]{2,1,0:T(4,128)}, f32[6,1,16,128]{3,2,1,0:T(8,128)}, f32[6,1,16,128]{3,2,1,0:T(8,128)}, f32[6,...) custom-call(f32[3,6,6]{2,1,0:T(8,128)} %ub_ref.13, f32[3,6,6]{2,1,0:T(8,128)} %lb_ref.13, ...), custom_call_target="tpu_custom_call" | custom-call | tf_op jit(solution)/shard_map/pallas_call | solution.py:317
  79.1 4.8 %all-to-all-start.4 = ((f32[4,1,768]{2,1,0:T(1,128)}), f32[4,1,768]{2,1,0:T(1,128)S(1)}, u32[]{:S(2)}, u32[]{:S(2)}) async-start(f32[4,1,768]{2,1,0:T(1,128)} %get-tuple-element.42), calls=%async_computation.4 | async-start | bytes 24576 | tf_op jit(solution)/shard_map/all_to_all | solution.py:248
  83.9 3.2 %collective-permute-start.8 = (f32[6,1,16,128]{3,2,1,0:T(8,128)}, f32[6,1,16,128]{3,2,1,0:T(8,128)S(1)}, u32[]{:S(2)}, u32[]{:S(2)}) collective-permute-start(f32[6,1,16,128]{3,2,1,0:T(8,128)} %get-tuple-element.40), channel_id=1, source_target_pairs={{0,64},{64,128},{128,192},{1,65},{65,129},{129,193},{2,66},{66,130... | collective-permute-start | bytes 147464 | tf_op jit(solution)/shard_map/ppermute | solution.py:246
  87.1 2.6 %collective-permute-start.9 = (f32[6,1,16,128]{3,2,1,0:T(8,128)}, f32[6,1,16,128]{3,2,1,0:T(8,128)S(1)}, u32[]{:S(2)}, u32[]{:S(2)}) collective-permute-start(f32[6,1,16,128]{3,2,1,0:T(8,128)} %get-tuple-element.41), channel_id=1, source_target_pairs={{64,0},{128,64},{192,128},{65,1},{129,65},{193,129},{66,2},{130,66... | collective-permute-start | bytes 147464 | tf_op jit(solution)/shard_map/ppermute | solution.py:247
  90.4 7.0 %all-to-all-start.5 = ((f32[16,3,128]{2,1,0:T(4,128)}), f32[16,3,128]{2,1,0:T(4,128)S(1)}, u32[]{:S(2)}, u32[]{:S(2)}) async-start(f32[16,3,128]{2,1,0:T(4,128)} %get-tuple-element.45), calls=%async_computation.5 | async-start | bytes 65536 | tf_op jit(solution)/shard_map/all_to_all | solution.py:311
  97.4 4.6 %collective-permute-start.10 = (f32[6,8,128]{2,1,0:T(8,128)S(1)}, f32[6,8,128]{2,1,0:T(8,128)S(1)}, u32[]{:S(2)}, u32[]{:S(2)}) collective-permute-start(f32[6,8,128]{2,1,0:T(8,128)S(1)} %copy-done.21), channel_id=1, source_target_pairs={{0,4},{4,8},{8,12},{12,16},{16,20},{20,24},{24,28},{28,32},{32,36}... | collective-permute-start | bytes 73736 | tf_op jit(solution)/shard_map/ppermute | solution.py:246
  102.0 2.1 %collective-permute-start.11 = (f32[6,8,128]{2,1,0:T(8,128)S(1)}, f32[6,8,128]{2,1,0:T(8,128)S(1)}, u32[]{:S(2)}, u32[]{:S(2)}) collective-permute-start(f32[6,8,128]{2,1,0:T(8,128)S(1)} %copy-done.19), channel_id=1, source_target_pairs={{4,0},{8,4},{12,8},{16,12},{20,16},{24,20},{28,24},{32,28},{36,32}... | collective-permute-start | bytes 73736 | tf_op jit(solution)/shard_map/ppermute | solution.py:247
  104.7 3.6 %shard_map.127.part_ref = f32[6,8,16,128]{3,2,1,0:T(8,128)} custom-call(f32[3,6,6]{2,1,0:T(8,128)} %ub_ref.13, f32[3,6,6]{2,1,0:T(8,128)} %lb_ref.13, f32[6,2,6]{2,1,0:T(2,128)} %bitcast.11, s32[1]{0:T(128)} %bitcast.1.wall_me.rest_3_.rest_4_, f32[6,8,16,128]{3,2,1,0:T(8,128)} %get-tuple-element.39.adj_ref, f32[6,8,16,128]{3,2,1,0:T(8,128)} %sens_ref.7, ...), custom_call_target="tpu_custom_call" | custom-call | tf_op jit(solution)/shard_map/pallas_call | solution.py:312
  111.0 3.2 %shard_map.128 = (f32[6,8,16,128]{3,2,1,0:T(8,128)}, f32[8,16,128]{2,1,0:T(8,128)}) custom-call(f32[3,6,6]{2,1,0:T(8,128)} %ub_ref.13, f32[3,6,6]{2,1,0:T(8,128)} %lb_ref.13, f32[6,2,6]{2,1,0:T(2,128)} %bitcast.12, f32[6,8,16,128]{3,2,1,0:T(8,128)} %shard_map.127.part_ref, f32[6,8,16,128]{3,2,1,0:T(8,128)} %diag_ref.13, f32[3,8,16,128]{3,2,1,0:T(8,128)} %face_ref.11, ...), custom_call_target="tpu_custom_call" | custom-call | tf_op jit(solution)/shard_map/pallas_call | solution.py:319
  (66 shorter events, 12.8 us)
Async XLA Ops:
  3.5 19.2 %copy-start.17 = (f32[6,1,16,128]{3,2,1,0:T(8,128)S(1)}, f32[6,1,16,128]{3,2,1,0:T(8,128)}, u32[]{:S(2)}) copy-start(f32[6,1,16,128]{3,2,1,0:T(8,128)} %get-tuple-element.26) | copy-start | bytes 147460
  10.7 14.6 %copy-start.23 = (f32[6,8,128]{2,1,0:T(8,128)S(1)}, f32[6,8,128]{2,1,0:T(8,128)}, u32[]{:S(2)}) copy-start(f32[6,8,128]{2,1,0:T(8,128)} %get-tuple-element.28) | copy-start | bytes 73732
  10.7 19.2 %copy-start.22 = (f32[6,8,128]{2,1,0:T(8,128)S(1)}, f32[6,8,128]{2,1,0:T(8,128)}, u32[]{:S(2)}) copy-start(f32[6,8,128]{2,1,0:T(8,128)} %get-tuple-element.29) | copy-start | bytes 73732
  10.7 27.0 %all-to-all-start.1 = ((f32[16,4,128]{2,1,0:T(4,128)}), f32[16,4,128]{2,1,0:T(4,128)S(1)}, u32[]{:S(2)}, u32[]{:S(2)}) async-start(f32[16,4,128]{2,1,0:T(4,128)} %get-tuple-element.30), calls=%async_computation.1 | async-start | bytes 65536 | tf_op jit(solution)/shard_map/all_to_all | solution.py:311
  19.5 12.4 %collective-permute-start = (f32[6,1,16,128]{3,2,1,0:T(8,128)}, f32[6,1,16,128]{3,2,1,0:T(8,128)S(1)}, u32[]{:S(2)}, u32[]{:S(2)}) collective-permute-start(f32[6,1,16,128]{3,2,1,0:T(8,128)} %get-tuple-element.25), channel_id=1, source_target_pairs={{0,64},{64,128},{128,192},{1,65},{65,129},{129,193},{2,66},{66,130... | collective-permute-start | bytes 147464 | tf_op jit(solution)/shard_map/ppermute | solution.py:246
  22.7 9.2 %collective-permute-start.1 = (f32[6,1,16,128]{3,2,1,0:T(8,128)S(1)}, f32[6,1,16,128]{3,2,1,0:T(8,128)S(1)}, u32[]{:S(2)}, u32[]{:S(2)}) collective-permute-start(f32[6,1,16,128]{3,2,1,0:T(8,128)S(1)} %copy-done.17), channel_id=1, source_target_pairs={{64,0},{128,64},{192,128},{65,1},{129,65},{193,129},{66,2},{130,66... | collective-permute-start | bytes 147464 | tf_op jit(solution)/shard_map/ppermute | solution.py:247
  25.3 10.7 %collective-permute-start.2 = (f32[6,8,128]{2,1,0:T(8,128)S(1)}, f32[6,8,128]{2,1,0:T(8,128)S(1)}, u32[]{:S(2)}, u32[]{:S(2)}) collective-permute-start(f32[6,8,128]{2,1,0:T(8,128)S(1)} %copy-done.23), channel_id=1, source_target_pairs={{0,4},{4,8},{8,12},{12,16},{16,20},{20,24},{24,28},{28,32},{32,36}... | collective-permute-start | bytes 73736 | tf_op jit(solution)/shard_map/ppermute | solution.py:246
  29.9 7.8 %collective-permute-start.3 = (f32[6,8,128]{2,1,0:T(8,128)S(1)}, f32[6,8,128]{2,1,0:T(8,128)S(1)}, u32[]{:S(2)}, u32[]{:S(2)}) collective-permute-start(f32[6,8,128]{2,1,0:T(8,128)S(1)} %copy-done.22), channel_id=1, source_target_pairs={{4,0},{8,4},{12,8},{16,12},{20,16},{24,20},{28,24},{32,28},{36,32}... | collective-permute-start | bytes 73736 | tf_op jit(solution)/shard_map/ppermute | solution.py:247
  42.7 12.6 %all-to-all-start.2 = ((f32[4,1,768]{2,1,0:T(1,128)}), f32[4,1,768]{2,1,0:T(1,128)S(1)}, u32[]{:S(2)}, u32[]{:S(2)}) async-start(f32[4,1,768]{2,1,0:T(1,128)} %get-tuple-element.34), calls=%async_computation.2 | async-start | bytes 24576 | tf_op jit(solution)/shard_map/all_to_all | solution.py:248
  49.5 19.4 %collective-permute-start.4 = (f32[6,1,16,128]{3,2,1,0:T(8,128)}, f32[6,1,16,128]{3,2,1,0:T(8,128)S(1)}, u32[]{:S(2)}, u32[]{:S(2)}) collective-permute-start(f32[6,1,16,128]{3,2,1,0:T(8,128)} %get-tuple-element.32), channel_id=1, source_target_pairs={{0,64},{64,128},{128,192},{1,65},{65,129},{129,193},{2,66},{66,130... | collective-permute-start | bytes 147464 | tf_op jit(solution)/shard_map/ppermute | solution.py:246
  52.6 16.2 %collective-permute-start.5 = (f32[6,1,16,128]{3,2,1,0:T(8,128)}, f32[6,1,16,128]{3,2,1,0:T(8,128)S(1)}, u32[]{:S(2)}, u32[]{:S(2)}) collective-permute-start(f32[6,1,16,128]{3,2,1,0:T(8,128)} %get-tuple-element.33), channel_id=1, source_target_pairs={{64,0},{128,64},{192,128},{65,1},{129,65},{193,129},{66,2},{130,66... | collective-permute-start | bytes 147464 | tf_op jit(solution)/shard_map/ppermute | solution.py:247
  55.3 7.0 %copy-start.20 = (f32[6,8,128]{2,1,0:T(8,128)S(1)}, f32[6,8,128]{2,1,0:T(8,128)}, u32[]{:S(2)}) copy-start(f32[6,8,128]{2,1,0:T(8,128)} %get-tuple-element.35) | copy-start | bytes 73732
  55.3 11.6 %copy-start.18 = (f32[6,8,128]{2,1,0:T(8,128)S(1)}, f32[6,8,128]{2,1,0:T(8,128)}, u32[]{:S(2)}) copy-start(f32[6,8,128]{2,1,0:T(8,128)} %get-tuple-element.36) | copy-start | bytes 73732
  55.9 18.8 %all-to-all-start.3 = ((f32[16,3,128]{2,1,0:T(4,128)}), f32[16,3,128]{2,1,0:T(4,128)S(1)}, u32[]{:S(2)}, u32[]{:S(2)}) async-start(f32[16,3,128]{2,1,0:T(4,128)} %get-tuple-element.37), calls=%async_computation.3 | async-start | bytes 65536 | tf_op jit(solution)/shard_map/all_to_all | solution.py:311
  62.3 10.7 %collective-permute-start.6 = (f32[6,8,128]{2,1,0:T(8,128)S(1)}, f32[6,8,128]{2,1,0:T(8,128)S(1)}, u32[]{:S(2)}, u32[]{:S(2)}) collective-permute-start(f32[6,8,128]{2,1,0:T(8,128)S(1)} %copy-done.20), channel_id=1, source_target_pairs={{0,4},{4,8},{8,12},{12,16},{16,20},{20,24},{24,28},{28,32},{32,36}... | collective-permute-start | bytes 73736 | tf_op jit(solution)/shard_map/ppermute | solution.py:246
  66.9 7.8 %collective-permute-start.7 = (f32[6,8,128]{2,1,0:T(8,128)S(1)}, f32[6,8,128]{2,1,0:T(8,128)S(1)}, u32[]{:S(2)}, u32[]{:S(2)}) collective-permute-start(f32[6,8,128]{2,1,0:T(8,128)S(1)} %copy-done.18), channel_id=1, source_target_pairs={{4,0},{8,4},{12,8},{16,12},{20,16},{24,20},{28,24},{32,28},{36,32}... | collective-permute-start | bytes 73736 | tf_op jit(solution)/shard_map/ppermute | solution.py:247
  79.1 10.7 %all-to-all-start.4 = ((f32[4,1,768]{2,1,0:T(1,128)}), f32[4,1,768]{2,1,0:T(1,128)S(1)}, u32[]{:S(2)}, u32[]{:S(2)}) async-start(f32[4,1,768]{2,1,0:T(1,128)} %get-tuple-element.42), calls=%async_computation.4 | async-start | bytes 24576 | tf_op jit(solution)/shard_map/all_to_all | solution.py:248
  83.9 20.2 %collective-permute-start.8 = (f32[6,1,16,128]{3,2,1,0:T(8,128)}, f32[6,1,16,128]{3,2,1,0:T(8,128)S(1)}, u32[]{:S(2)}, u32[]{:S(2)}) collective-permute-start(f32[6,1,16,128]{3,2,1,0:T(8,128)} %get-tuple-element.40), channel_id=1, source_target_pairs={{0,64},{64,128},{128,192},{1,65},{65,129},{129,193},{2,66},{66,130... | collective-permute-start | bytes 147464 | tf_op jit(solution)/shard_map/ppermute | solution.py:246
  87.1 17.0 %collective-permute-start.9 = (f32[6,1,16,128]{3,2,1,0:T(8,128)}, f32[6,1,16,128]{3,2,1,0:T(8,128)S(1)}, u32[]{:S(2)}, u32[]{:S(2)}) collective-permute-start(f32[6,1,16,128]{3,2,1,0:T(8,128)} %get-tuple-element.41), channel_id=1, source_target_pairs={{64,0},{128,64},{192,128},{65,1},{129,65},{193,129},{66,2},{130,66... | collective-permute-start | bytes 147464 | tf_op jit(solution)/shard_map/ppermute | solution.py:247
  89.8 7.6 %copy-start.21 = (f32[6,8,128]{2,1,0:T(8,128)S(1)}, f32[6,8,128]{2,1,0:T(8,128)}, u32[]{:S(2)}) copy-start(f32[6,8,128]{2,1,0:T(8,128)} %get-tuple-element.43) | copy-start | bytes 73732
  89.8 12.2 %copy-start.19 = (f32[6,8,128]{2,1,0:T(8,128)S(1)}, f32[6,8,128]{2,1,0:T(8,128)}, u32[]{:S(2)}) copy-start(f32[6,8,128]{2,1,0:T(8,128)} %get-tuple-element.44) | copy-start | bytes 73732
  90.4 19.5 %all-to-all-start.5 = ((f32[16,3,128]{2,1,0:T(4,128)}), f32[16,3,128]{2,1,0:T(4,128)S(1)}, u32[]{:S(2)}, u32[]{:S(2)}) async-start(f32[16,3,128]{2,1,0:T(4,128)} %get-tuple-element.45), calls=%async_computation.5 | async-start | bytes 65536 | tf_op jit(solution)/shard_map/all_to_all | solution.py:311
  97.4 10.9 %collective-permute-start.10 = (f32[6,8,128]{2,1,0:T(8,128)S(1)}, f32[6,8,128]{2,1,0:T(8,128)S(1)}, u32[]{:S(2)}, u32[]{:S(2)}) collective-permute-start(f32[6,8,128]{2,1,0:T(8,128)S(1)} %copy-done.21), channel_id=1, source_target_pairs={{0,4},{4,8},{8,12},{12,16},{16,20},{20,24},{24,28},{28,32},{32,36}... | collective-permute-start | bytes 73736 | tf_op jit(solution)/shard_map/ppermute | solution.py:246
  102.0 7.8 %collective-permute-start.11 = (f32[6,8,128]{2,1,0:T(8,128)S(1)}, f32[6,8,128]{2,1,0:T(8,128)S(1)}, u32[]{:S(2)}, u32[]{:S(2)}) collective-permute-start(f32[6,8,128]{2,1,0:T(8,128)S(1)} %copy-done.19), channel_id=1, source_target_pairs={{4,0},{8,4},{12,8},{16,12},{20,16},{24,20},{28,24},{32,28},{36,32}... | collective-permute-start | bytes 73736 | tf_op jit(solution)/shard_map/ppermute | solution.py:247
  (17 other events, 13.4 us)

commit v16 on v15

--- a/solution.py
+++ b/solution.py
@@ -88,15 +88,13 @@
     lo, hi = wall_columns(adj)
     me = wall_me[0]
     n_wall = w_buf.shape[0]
-    lo = jnp.concatenate([lo[v:v + 1] for v in range(lo.shape[0])], axis=1)
-    hi = jnp.concatenate([hi[v:v + 1] for v in range(hi.shape[0])], axis=1)
     for t in range(n_wall):
         w_buf[t] = jnp.where(me + 1 == t, hi, jnp.where(me - 1 == t, lo, 0.0))
 
 
 def wall_halos(w_inc, wall_me, n_var):
     me = wall_me[0]
-    n_wall, _, width = w_inc.shape
+    n_wall = w_inc.shape[0]
     below = None
     above = None
     for t in range(n_wall):
@@ -104,9 +102,7 @@
         a = jnp.where(me + 1 == t, w_inc[t], 0.0)
         below = b if below is None else below + b
         above = a if above is None else above + a
-    rows = width // n_var
-    unflat = lambda x: jnp.concatenate([x[:, v * rows:(v + 1) * rows] for v in range(n_var)], axis=0)
-    return unflat(below), unflat(above)
+    return below, above
 
 
 def init_kernel(ub_ref, lb_ref, ib_ref, wall_me, sens_ref, diag_ref, send_ref, orient_ref, weight_ref, tgt_ref,
@@ -232,7 +228,7 @@
     n_var, nx, ny, nz = shape
     c = jax.ShapeDtypeStruct((n_var, 1, ny, nz), F32)
     s = jax.ShapeDtypeStruct((n_var, nx, nz), F32)
-    w = jax.ShapeDtypeStruct((n_wall, 1, n_var * nx * ny), F32)
+    w = jax.ShapeDtypeStruct((n_wall, n_var, nx * ny), F32)
     return [c, c, s, s, w]
 
 

time: 115 us -> 115 us (level)
    unnamed x48 -> x46, local copies, waits for them, and re-layouts: 6.02 us -> 6.02 us
where the time goes in v16:
time: 115 us; the launch traced here: 114 us
  starting transfers between devices  70.5 us (61%)
  Pallas kernels  24.2 us (21%)
  blocking collectives  7.31 us (6%)
  local copies, waits for them, and re-layouts  6.02 us (5%)
  waiting for transfers between devices  5.1 us (4%)
    ppermute x6, starting transfers between devices, exchange(): out.append(lax.ppermute(hi_face, axis, forward))  23.3 us
    all_to_all x3, starting transfers between devices, local(): lax.all_to_all(rows, 'span', split_axis=0, concat_axis=0, tiled=True)  21.8 us
    ppermute x6, starting transfers between devices, exchange(): out.append(lax.ppermute(lo_face, axis, backward))  13.9 us
    all_to_all x2, starting transfers between devices, exchange(): lax.all_to_all(w_buf, 'wall', split_axis=0, concat_axis=0, tiled=True)  11.5 us
    pallas_call x3, Pallas kernels, local(): part_a(*blk, adj, sensitivity, diagonal, face_coef, hcl, hch, w_inc)  10.7 us
    all_to_all x1, blocking collectives, exchange(): lax.all_to_all(w_buf, 'wall', split_axis=0, concat_axis=0, tiled=True)  7.31 us
    unnamed x46, local copies, waits for them, and re-layouts  6.02 us
    ppermute x6, waiting for transfers between devices, exchange(): out.append(lax.ppermute(lo_face, axis, backward))  5.07 us
  transfers between devices with their start and end apart: 17, of which 3 were waited for; matrix products, arithmetic and copies ran while one was open for 0% of the time, Pallas kernels for 9%

profile of v16, /device:TPU:118, one launch (start us, length us, event | category | flops | bytes accessed | tf_op | source)
XLA Modules:
  0.0 114.1 jit_solution(17873704930881807329)
XLA Ops:
  0.6 2.8 %shard_map.122 = (f32[6,8,16,128]{3,2,1,0:T(8,128)}, f32[16,4,128]{2,1,0:T(4,128)}, f32[6,1,16,128]{3,2,1,0:T(8,128)}, f32[6,1,16,128]{3,2,1,0:T(8,128)}, f32[6,...) custom-call(f32[3,6,6]{2,1,0:T(8,128)} %ub_ref.13, f32[3,6,6]{2,1,0:T(8,128)} %lb_ref.13, ...), custom_call_target="tpu_custom_call" | custom-call | tf_op jit(solution)/shard_map/pallas_call | solution.py:277
  3.5 7.3 %all_to_all.30.w_inc = f32[4,6,128]{2,1,0:T(8,128)} all-to-all(f32[4,6,128]{2,1,0:T(8,128)} %get-tuple-element.27), channel_id=1, replica_groups=mesh['chord'=4,'span'=16,'wall'=4] {'wall'}, dimensions={0} | all-to-all | bytes 24576 | tf_op jit(solution)/shard_map/all_to_all | solution.py:244
  10.8 8.6 %all-to-all-start.1 = ((f32[16,4,128]{2,1,0:T(4,128)}), f32[16,4,128]{2,1,0:T(4,128)S(1)}, u32[]{:S(2)}, u32[]{:S(2)}) async-start(f32[16,4,128]{2,1,0:T(4,128)} %get-tuple-element.30), calls=%async_computation.1 | async-start | bytes 65536 | tf_op jit(solution)/shard_map/all_to_all | solution.py:307
  19.4 3.2 %collective-permute-start = (f32[6,1,16,128]{3,2,1,0:T(8,128)S(1)}, f32[6,1,16,128]{3,2,1,0:T(8,128)S(1)}, u32[]{:S(2)}, u32[]{:S(2)}) collective-permute-start(f32[6,1,16,128]{3,2,1,0:T(8,128)S(1)} %copy-done.18), channel_id=1, source_target_pairs={{0,64},{64,128},{128,192},{1,65},{65,129},{129,193},{2,66},{66,130... | collective-permute-start | bytes 147464 | tf_op jit(solution)/shard_map/ppermute | solution.py:242
  22.6 2.7 %collective-permute-start.1 = (f32[6,1,16,128]{3,2,1,0:T(8,128)S(1)}, f32[6,1,16,128]{3,2,1,0:T(8,128)S(1)}, u32[]{:S(2)}, u32[]{:S(2)}) collective-permute-start(f32[6,1,16,128]{3,2,1,0:T(8,128)S(1)} %copy-done.17), channel_id=1, source_target_pairs={{64,0},{128,64},{192,128},{65,1},{129,65},{193,129},{66,2},{130,66... | collective-permute-start | bytes 147464 | tf_op jit(solution)/shard_map/ppermute | solution.py:243
  25.2 4.6 %collective-permute-start.2 = (f32[6,8,128]{2,1,0:T(8,128)}, f32[6,8,128]{2,1,0:T(8,128)S(1)}, u32[]{:S(2)}, u32[]{:S(2)}) collective-permute-start(f32[6,8,128]{2,1,0:T(8,128)} %get-tuple-element.28), channel_id=1, source_target_pairs={{0,4},{4,8},{8,12},{12,16},{16,20},{20,24},{24,28},{28,32},{32,36}... | collective-permute-start | bytes 73736 | tf_op jit(solution)/shard_map/ppermute | solution.py:242
  32.4 3.6 %shard_map.123.part_ref = f32[6,8,16,128]{3,2,1,0:T(8,128)} custom-call(f32[3,6,6]{2,1,0:T(8,128)} %ub_ref.13, f32[3,6,6]{2,1,0:T(8,128)} %lb_ref.13, f32[6,2,6]{2,1,0:T(2,128)} %bitcast.7, s32[1]{0:T(128)} %bitcast.1.wall_me.rest_3_.rest_4_, f32[6,8,16,128]{3,2,1,0:T(8,128)} %get-tuple-element.24.adj_ref, f32[6,8,16,128]{3,2,1,0:T(8,128)} %sens_ref.7, ...), custom_call_target="tpu_custom_call" | custom-call | tf_op jit(solution)/shard_map/pallas_call | solution.py:308
  39.1 3.8 %shard_map.124 = (f32[6,8,16,128]{3,2,1,0:T(8,128)}, f32[16,3,128]{2,1,0:T(4,128)}, f32[6,1,16,128]{3,2,1,0:T(8,128)}, f32[6,1,16,128]{3,2,1,0:T(8,128)}, f32[6,...) custom-call(f32[3,6,6]{2,1,0:T(8,128)} %ub_ref.13, f32[3,6,6]{2,1,0:T(8,128)} %lb_ref.13, ...), custom_call_target="tpu_custom_call" | custom-call | tf_op jit(solution)/shard_map/pallas_call | solution.py:311
  42.8 6.7 %all-to-all-start.2 = ((f32[4,6,128]{2,1,0:T(8,128)}), f32[4,6,128]{2,1,0:T(8,128)S(1)}, u32[]{:S(2)}, u32[]{:S(2)}) async-start(f32[4,6,128]{2,1,0:T(8,128)} %get-tuple-element.34), calls=%async_computation.2 | async-start | bytes 32768 | tf_op jit(solution)/shard_map/all_to_all | solution.py:244
  49.6 3.2 %collective-permute-start.4 = (f32[6,1,16,128]{3,2,1,0:T(8,128)}, f32[6,1,16,128]{3,2,1,0:T(8,128)S(1)}, u32[]{:S(2)}, u32[]{:S(2)}) collective-permute-start(f32[6,1,16,128]{3,2,1,0:T(8,128)} %get-tuple-element.32), channel_id=1, source_target_pairs={{0,64},{64,128},{128,192},{1,65},{65,129},{129,193},{2,66},{66,130... | collective-permute-start | bytes 147464 | tf_op jit(solution)/shard_map/ppermute | solution.py:242
  52.8 2.7 %collective-permute-start.5 = (f32[6,1,16,128]{3,2,1,0:T(8,128)}, f32[6,1,16,128]{3,2,1,0:T(8,128)S(1)}, u32[]{:S(2)}, u32[]{:S(2)}) collective-permute-start(f32[6,1,16,128]{3,2,1,0:T(8,128)} %get-tuple-element.33), channel_id=1, source_target_pairs={{64,0},{128,64},{192,128},{65,1},{129,65},{193,129},{66,2},{130,66... | collective-permute-start | bytes 147464 | tf_op jit(solution)/shard_map/ppermute | solution.py:243
  56.0 6.2 %all-to-all-start.3 = ((f32[16,3,128]{2,1,0:T(4,128)}), f32[16,3,128]{2,1,0:T(4,128)S(1)}, u32[]{:S(2)}, u32[]{:S(2)}) async-start(f32[16,3,128]{2,1,0:T(4,128)} %get-tuple-element.37), calls=%async_computation.3 | async-start | bytes 65536 | tf_op jit(solution)/shard_map/all_to_all | solution.py:307
  62.2 4.6 %collective-permute-start.6 = (f32[6,8,128]{2,1,0:T(8,128)S(1)}, f32[6,8,128]{2,1,0:T(8,128)S(1)}, u32[]{:S(2)}, u32[]{:S(2)}) collective-permute-start(f32[6,8,128]{2,1,0:T(8,128)S(1)} %copy-done.21), channel_id=1, source_target_pairs={{0,4},{4,8},{8,12},{12,16},{16,20},{20,24},{24,28},{28,32},{32,36}... | collective-permute-start | bytes 73736 | tf_op jit(solution)/shard_map/ppermute | solution.py:242
  66.8 1.9 %collective-permute-start.7 = (f32[6,8,128]{2,1,0:T(8,128)S(1)}, f32[6,8,128]{2,1,0:T(8,128)S(1)}, u32[]{:S(2)}, u32[]{:S(2)}) collective-permute-start(f32[6,8,128]{2,1,0:T(8,128)S(1)} %copy-done.19), channel_id=1, source_target_pairs={{4,0},{8,4},{12,8},{16,12},{20,16},{24,20},{28,24},{32,28},{36,32}... | collective-permute-start | bytes 73736 | tf_op jit(solution)/shard_map/ppermute | solution.py:243
  69.4 3.6 %shard_map.125.part_ref = f32[6,8,16,128]{3,2,1,0:T(8,128)} custom-call(f32[3,6,6]{2,1,0:T(8,128)} %ub_ref.13, f32[3,6,6]{2,1,0:T(8,128)} %lb_ref.13, f32[6,2,6]{2,1,0:T(2,128)} %bitcast.9, s32[1]{0:T(128)} %bitcast.1.wall_me.rest_3_.rest_4_, f32[6,8,16,128]{3,2,1,0:T(8,128)} %get-tuple-element.31.adj_ref, f32[6,8,16,128]{3,2,1,0:T(8,128)} %sens_ref.7, ...), custom_call_target="tpu_custom_call" | custom-call | tf_op jit(solution)/shard_map/pallas_call | solution.py:308
  75.3 3.8 %shard_map.126 = (f32[6,8,16,128]{3,2,1,0:T(8,128)}, f32[16,3,128]{2,1,0:T(4,128)}, f32[6,1,16,128]{3,2,1,0:T(8,128)}, f32[6,1,16,128]{3,2,1,0:T(8,128)}, f32[6,...) custom-call(f32[3,6,6]{2,1,0:T(8,128)} %ub_ref.13, f32[3,6,6]{2,1,0:T(8,128)} %lb_ref.13, ...), custom_call_target="tpu_custom_call" | custom-call | tf_op jit(solution)/shard_map/pallas_call | solution.py:313
  79.0 4.8 %all-to-all-start.4 = ((f32[4,6,128]{2,1,0:T(8,128)}), f32[4,6,128]{2,1,0:T(8,128)S(1)}, u32[]{:S(2)}, u32[]{:S(2)}) async-start(f32[4,6,128]{2,1,0:T(8,128)} %get-tuple-element.42), calls=%async_computation.4 | async-start | bytes 32768 | tf_op jit(solution)/shard_map/all_to_all | solution.py:244
  83.8 3.2 %collective-permute-start.8 = (f32[6,1,16,128]{3,2,1,0:T(8,128)}, f32[6,1,16,128]{3,2,1,0:T(8,128)S(1)}, u32[]{:S(2)}, u32[]{:S(2)}) collective-permute-start(f32[6,1,16,128]{3,2,1,0:T(8,128)} %get-tuple-element.40), channel_id=1, source_target_pairs={{0,64},{64,128},{128,192},{1,65},{65,129},{129,193},{2,66},{66,130... | collective-permute-start | bytes 147464 | tf_op jit(solution)/shard_map/ppermute | solution.py:242
  87.0 2.6 %collective-permute-start.9 = (f32[6,1,16,128]{3,2,1,0:T(8,128)}, f32[6,1,16,128]{3,2,1,0:T(8,128)S(1)}, u32[]{:S(2)}, u32[]{:S(2)}) collective-permute-start(f32[6,1,16,128]{3,2,1,0:T(8,128)} %get-tuple-element.41), channel_id=1, source_target_pairs={{64,0},{128,64},{192,128},{65,1},{129,65},{193,129},{66,2},{130,66... | collective-permute-start | bytes 147464 | tf_op jit(solution)/shard_map/ppermute | solution.py:243
  90.3 7.0 %all-to-all-start.5 = ((f32[16,3,128]{2,1,0:T(4,128)}), f32[16,3,128]{2,1,0:T(4,128)S(1)}, u32[]{:S(2)}, u32[]{:S(2)}) async-start(f32[16,3,128]{2,1,0:T(4,128)} %get-tuple-element.45), calls=%async_computation.5 | async-start | bytes 65536 | tf_op jit(solution)/shard_map/all_to_all | solution.py:307
  97.3 4.6 %collective-permute-start.10 = (f32[6,8,128]{2,1,0:T(8,128)S(1)}, f32[6,8,128]{2,1,0:T(8,128)S(1)}, u32[]{:S(2)}, u32[]{:S(2)}) collective-permute-start(f32[6,8,128]{2,1,0:T(8,128)S(1)} %copy-done.22), channel_id=1, source_target_pairs={{0,4},{4,8},{8,12},{12,16},{16,20},{20,24},{24,28},{28,32},{32,36}... | collective-permute-start | bytes 73736 | tf_op jit(solution)/shard_map/ppermute | solution.py:242
  101.9 2.1 %collective-permute-start.11 = (f32[6,8,128]{2,1,0:T(8,128)S(1)}, f32[6,8,128]{2,1,0:T(8,128)S(1)}, u32[]{:S(2)}, u32[]{:S(2)}) collective-permute-start(f32[6,8,128]{2,1,0:T(8,128)S(1)} %copy-done.20), channel_id=1, source_target_pairs={{4,0},{8,4},{12,8},{16,12},{20,16},{24,20},{28,24},{32,28},{36,32}... | collective-permute-start | bytes 73736 | tf_op jit(solution)/shard_map/ppermute | solution.py:243
  104.7 3.6 %shard_map.127.part_ref = f32[6,8,16,128]{3,2,1,0:T(8,128)} custom-call(f32[3,6,6]{2,1,0:T(8,128)} %ub_ref.13, f32[3,6,6]{2,1,0:T(8,128)} %lb_ref.13, f32[6,2,6]{2,1,0:T(2,128)} %bitcast.11, s32[1]{0:T(128)} %bitcast.1.wall_me.rest_3_.rest_4_, f32[6,8,16,128]{3,2,1,0:T(8,128)} %get-tuple-element.39.adj_ref, f32[6,8,16,128]{3,2,1,0:T(8,128)} %sens_ref.7, ...), custom_call_target="tpu_custom_call" | custom-call | tf_op jit(solution)/shard_map/pallas_call | solution.py:308
  111.0 3.1 %shard_map.128 = (f32[6,8,16,128]{3,2,1,0:T(8,128)}, f32[8,16,128]{2,1,0:T(8,128)}) custom-call(f32[3,6,6]{2,1,0:T(8,128)} %ub_ref.13, f32[3,6,6]{2,1,0:T(8,128)} %lb_ref.13, f32[6,2,6]{2,1,0:T(2,128)} %bitcast.12, f32[6,8,16,128]{3,2,1,0:T(8,128)} %shard_map.127.part_ref, f32[6,8,16,128]{3,2,1,0:T(8,128)} %diag_ref.13, f32[3,8,16,128]{3,2,1,0:T(8,128)} %face_ref.11, ...), custom_call_target="tpu_custom_call" | custom-call | tf_op jit(solution)/shard_map/pallas_call | solution.py:315
  (64 shorter events, 13.0 us)
Async XLA Ops:
  3.5 15.9 %copy-start.18 = (f32[6,1,16,128]{3,2,1,0:T(8,128)S(1)}, f32[6,1,16,128]{3,2,1,0:T(8,128)}, u32[]{:S(2)}) copy-start(f32[6,1,16,128]{3,2,1,0:T(8,128)} %get-tuple-element.25) | copy-start | bytes 147460
  3.5 19.1 %copy-start.17 = (f32[6,1,16,128]{3,2,1,0:T(8,128)S(1)}, f32[6,1,16,128]{3,2,1,0:T(8,128)}, u32[]{:S(2)}) copy-start(f32[6,1,16,128]{3,2,1,0:T(8,128)} %get-tuple-element.26) | copy-start | bytes 147460
  10.8 27.1 %all-to-all-start.1 = ((f32[16,4,128]{2,1,0:T(4,128)}), f32[16,4,128]{2,1,0:T(4,128)S(1)}, u32[]{:S(2)}, u32[]{:S(2)}) async-start(f32[16,4,128]{2,1,0:T(4,128)} %get-tuple-element.30), calls=%async_computation.1 | async-start | bytes 65536 | tf_op jit(solution)/shard_map/all_to_all | solution.py:307
  19.4 12.4 %collective-permute-start = (f32[6,1,16,128]{3,2,1,0:T(8,128)S(1)}, f32[6,1,16,128]{3,2,1,0:T(8,128)S(1)}, u32[]{:S(2)}, u32[]{:S(2)}) collective-permute-start(f32[6,1,16,128]{3,2,1,0:T(8,128)S(1)} %copy-done.18), channel_id=1, source_target_pairs={{0,64},{64,128},{128,192},{1,65},{65,129},{129,193},{2,66},{66,130... | collective-permute-start | bytes 147464 | tf_op jit(solution)/shard_map/ppermute | solution.py:242
  22.6 9.2 %collective-permute-start.1 = (f32[6,1,16,128]{3,2,1,0:T(8,128)S(1)}, f32[6,1,16,128]{3,2,1,0:T(8,128)S(1)}, u32[]{:S(2)}, u32[]{:S(2)}) collective-permute-start(f32[6,1,16,128]{3,2,1,0:T(8,128)S(1)} %copy-done.17), channel_id=1, source_target_pairs={{64,0},{128,64},{192,128},{65,1},{129,65},{193,129},{66,2},{130,66... | collective-permute-start | bytes 147464 | tf_op jit(solution)/shard_map/ppermute | solution.py:243
  25.2 10.7 %collective-permute-start.2 = (f32[6,8,128]{2,1,0:T(8,128)}, f32[6,8,128]{2,1,0:T(8,128)S(1)}, u32[]{:S(2)}, u32[]{:S(2)}) collective-permute-start(f32[6,8,128]{2,1,0:T(8,128)} %get-tuple-element.28), channel_id=1, source_target_pairs={{0,4},{4,8},{8,12},{12,16},{16,20},{20,24},{24,28},{28,32},{32,36}... | collective-permute-start | bytes 73736 | tf_op jit(solution)/shard_map/ppermute | solution.py:242
  29.8 8.0 %collective-permute-start.3 = (f32[6,8,128]{2,1,0:T(8,128)}, f32[6,8,128]{2,1,0:T(8,128)S(1)}, u32[]{:S(2)}, u32[]{:S(2)}) collective-permute-start(f32[6,8,128]{2,1,0:T(8,128)} %get-tuple-element.29), channel_id=1, source_target_pairs={{4,0},{8,4},{12,8},{16,12},{20,16},{24,20},{28,24},{32,28},{36,32}... | collective-permute-start | bytes 73736 | tf_op jit(solution)/shard_map/ppermute | solution.py:243
  36.0 1.9 %copy-start.11 = (f32[6,8,128]{2,1,0:T(8,128)}, f32[6,8,128]{2,1,0:T(8,128)S(1)}, u32[]{:S(2)}) copy-start(f32[6,8,128]{2,1,0:T(8,128)S(1)} %collective-permute-done.2.hsl) | copy-start | bytes 73732
  42.8 12.6 %all-to-all-start.2 = ((f32[4,6,128]{2,1,0:T(8,128)}), f32[4,6,128]{2,1,0:T(8,128)S(1)}, u32[]{:S(2)}, u32[]{:S(2)}) async-start(f32[4,6,128]{2,1,0:T(8,128)} %get-tuple-element.34), calls=%async_computation.2 | async-start | bytes 32768 | tf_op jit(solution)/shard_map/all_to_all | solution.py:244
  49.6 19.2 %collective-permute-start.4 = (f32[6,1,16,128]{3,2,1,0:T(8,128)}, f32[6,1,16,128]{3,2,1,0:T(8,128)S(1)}, u32[]{:S(2)}, u32[]{:S(2)}) collective-permute-start(f32[6,1,16,128]{3,2,1,0:T(8,128)} %get-tuple-element.32), channel_id=1, source_target_pairs={{0,64},{64,128},{128,192},{1,65},{65,129},{129,193},{2,66},{66,130... | collective-permute-start | bytes 147464 | tf_op jit(solution)/shard_map/ppermute | solution.py:242
  52.8 16.0 %collective-permute-start.5 = (f32[6,1,16,128]{3,2,1,0:T(8,128)}, f32[6,1,16,128]{3,2,1,0:T(8,128)S(1)}, u32[]{:S(2)}, u32[]{:S(2)}) collective-permute-start(f32[6,1,16,128]{3,2,1,0:T(8,128)} %get-tuple-element.33), channel_id=1, source_target_pairs={{64,0},{128,64},{192,128},{65,1},{129,65},{193,129},{66,2},{130,66... | collective-permute-start | bytes 147464 | tf_op jit(solution)/shard_map/ppermute | solution.py:243
  55.4 6.8 %copy-start.21 = (f32[6,8,128]{2,1,0:T(8,128)S(1)}, f32[6,8,128]{2,1,0:T(8,128)}, u32[]{:S(2)}) copy-start(f32[6,8,128]{2,1,0:T(8,128)} %get-tuple-element.35) | copy-start | bytes 73732
  55.4 11.4 %copy-start.19 = (f32[6,8,128]{2,1,0:T(8,128)S(1)}, f32[6,8,128]{2,1,0:T(8,128)}, u32[]{:S(2)}) copy-start(f32[6,8,128]{2,1,0:T(8,128)} %get-tuple-element.36) | copy-start | bytes 73732
  56.0 18.6 %all-to-all-start.3 = ((f32[16,3,128]{2,1,0:T(4,128)}), f32[16,3,128]{2,1,0:T(4,128)S(1)}, u32[]{:S(2)}, u32[]{:S(2)}) async-start(f32[16,3,128]{2,1,0:T(4,128)} %get-tuple-element.37), calls=%async_computation.3 | async-start | bytes 65536 | tf_op jit(solution)/shard_map/all_to_all | solution.py:307
  62.2 10.7 %collective-permute-start.6 = (f32[6,8,128]{2,1,0:T(8,128)S(1)}, f32[6,8,128]{2,1,0:T(8,128)S(1)}, u32[]{:S(2)}, u32[]{:S(2)}) collective-permute-start(f32[6,8,128]{2,1,0:T(8,128)S(1)} %copy-done.21), channel_id=1, source_target_pairs={{0,4},{4,8},{8,12},{12,16},{16,20},{20,24},{24,28},{28,32},{32,36}... | collective-permute-start | bytes 73736 | tf_op jit(solution)/shard_map/ppermute | solution.py:242
  66.8 7.8 %collective-permute-start.7 = (f32[6,8,128]{2,1,0:T(8,128)S(1)}, f32[6,8,128]{2,1,0:T(8,128)S(1)}, u32[]{:S(2)}, u32[]{:S(2)}) collective-permute-start(f32[6,8,128]{2,1,0:T(8,128)S(1)} %copy-done.19), channel_id=1, source_target_pairs={{4,0},{8,4},{12,8},{16,12},{20,16},{24,20},{28,24},{32,28},{36,32}... | collective-permute-start | bytes 73736 | tf_op jit(solution)/shard_map/ppermute | solution.py:243
  79.0 10.7 %all-to-all-start.4 = ((f32[4,6,128]{2,1,0:T(8,128)}), f32[4,6,128]{2,1,0:T(8,128)S(1)}, u32[]{:S(2)}, u32[]{:S(2)}) async-start(f32[4,6,128]{2,1,0:T(8,128)} %get-tuple-element.42), calls=%async_computation.4 | async-start | bytes 32768 | tf_op jit(solution)/shard_map/all_to_all | solution.py:244
  83.8 20.2 %collective-permute-start.8 = (f32[6,1,16,128]{3,2,1,0:T(8,128)}, f32[6,1,16,128]{3,2,1,0:T(8,128)S(1)}, u32[]{:S(2)}, u32[]{:S(2)}) collective-permute-start(f32[6,1,16,128]{3,2,1,0:T(8,128)} %get-tuple-element.40), channel_id=1, source_target_pairs={{0,64},{64,128},{128,192},{1,65},{65,129},{129,193},{2,66},{66,130... | collective-permute-start | bytes 147464 | tf_op jit(solution)/shard_map/ppermute | solution.py:242
  87.0 17.0 %collective-permute-start.9 = (f32[6,1,16,128]{3,2,1,0:T(8,128)}, f32[6,1,16,128]{3,2,1,0:T(8,128)S(1)}, u32[]{:S(2)}, u32[]{:S(2)}) collective-permute-start(f32[6,1,16,128]{3,2,1,0:T(8,128)} %get-tuple-element.41), channel_id=1, source_target_pairs={{64,0},{128,64},{192,128},{65,1},{129,65},{193,129},{66,2},{130,66... | collective-permute-start | bytes 147464 | tf_op jit(solution)/shard_map/ppermute | solution.py:243
  89.7 7.6 %copy-start.22 = (f32[6,8,128]{2,1,0:T(8,128)S(1)}, f32[6,8,128]{2,1,0:T(8,128)}, u32[]{:S(2)}) copy-start(f32[6,8,128]{2,1,0:T(8,128)} %get-tuple-element.43) | copy-start | bytes 73732
  89.7 12.2 %copy-start.20 = (f32[6,8,128]{2,1,0:T(8,128)S(1)}, f32[6,8,128]{2,1,0:T(8,128)}, u32[]{:S(2)}) copy-start(f32[6,8,128]{2,1,0:T(8,128)} %get-tuple-element.44) | copy-start | bytes 73732
  90.3 19.5 %all-to-all-start.5 = ((f32[16,3,128]{2,1,0:T(4,128)}), f32[16,3,128]{2,1,0:T(4,128)S(1)}, u32[]{:S(2)}, u32[]{:S(2)}) async-start(f32[16,3,128]{2,1,0:T(4,128)} %get-tuple-element.45), calls=%async_computation.5 | async-start | bytes 65536 | tf_op jit(solution)/shard_map/all_to_all | solution.py:307
  97.3 10.9 %collective-permute-start.10 = (f32[6,8,128]{2,1,0:T(8,128)S(1)}, f32[6,8,128]{2,1,0:T(8,128)S(1)}, u32[]{:S(2)}, u32[]{:S(2)}) collective-permute-start(f32[6,8,128]{2,1,0:T(8,128)S(1)} %copy-done.22), channel_id=1, source_target_pairs={{0,4},{4,8},{8,12},{12,16},{16,20},{20,24},{24,28},{28,32},{32,36}... | collective-permute-start | bytes 73736 | tf_op jit(solution)/shard_map/ppermute | solution.py:242
  101.9 7.8 %collective-permute-start.11 = (f32[6,8,128]{2,1,0:T(8,128)S(1)}, f32[6,8,128]{2,1,0:T(8,128)S(1)}, u32[]{:S(2)}, u32[]{:S(2)}) collective-permute-start(f32[6,8,128]{2,1,0:T(8,128)S(1)} %copy-done.20), channel_id=1, source_target_pairs={{4,0},{8,4},{12,8},{16,12},{20,16},{24,20},{28,24},{32,28},{36,32}... | collective-permute-start | bytes 73736 | tf_op jit(solution)/shard_map/ppermute | solution.py:243
  (16 other events, 11.7 us)

commit v17 on v15

--- a/solution.py
+++ b/solution.py
@@ -80,11 +80,10 @@
 def write_faces(adj, faces):
     c_lo, c_hi, s_lo, s_hi, w_buf, wall_me = faces
     nx, ny, nz = adj.shape[1], adj.shape[2], adj.shape[3]
-    j_idx = lax.broadcasted_iota(jnp.int32, adj.shape, 2)
     c_lo[...] = adj[:, 0:1]
     c_hi[...] = adj[:, nx - 1:nx]
-    s_lo[...] = jnp.sum(jnp.where(j_idx == 0, adj, 0.0), axis=2)
-    s_hi[...] = jnp.sum(jnp.where(j_idx == ny - 1, adj, 0.0), axis=2)
+    s_lo[...] = adj[:, :, 0, :]
+    s_hi[...] = adj[:, :, ny - 1, :]
     lo, hi = wall_columns(adj)
     me = wall_me[0]
     n_wall = w_buf.shape[0]

time: 115 us -> 115 us (level)
  no operation moved by 1% of the time
where the time goes in v17:
time: 115 us; the launch traced here: 114 us
  starting transfers between devices  70.8 us (62%)
  Pallas kernels  24.1 us (21%)
  blocking collectives  7.29 us (6%)
  local copies, waits for them, and re-layouts  6.02 us (5%)
  waiting for transfers between devices  4.9 us (4%)
    ppermute x6, starting transfers between devices, exchange(): out.append(lax.ppermute(hi_face, axis, forward))  23.3 us
    all_to_all x3, starting transfers between devices, local(): lax.all_to_all(rows, 'span', split_axis=0, concat_axis=0, tiled=True)  22.1 us
    ppermute x6, starting transfers between devices, exchange(): out.append(lax.ppermute(lo_face, axis, backward))  13.9 us
    all_to_all x2, starting transfers between devices, exchange(): lax.all_to_all(w_buf, 'wall', split_axis=0, concat_axis=0, tiled=True)  11.5 us
    pallas_call x3, Pallas kernels, local(): part_a(*blk, adj, sensitivity, diagonal, face_coef, hcl, hch, w_inc)  10.7 us
    all_to_all x1, blocking collectives, exchange(): lax.all_to_all(w_buf, 'wall', split_axis=0, concat_axis=0, tiled=True)  7.29 us
    unnamed x48, local copies, waits for them, and re-layouts  6.02 us
    ppermute x6, waiting for transfers between devices, exchange(): out.append(lax.ppermute(lo_face, axis, backward))  4.87 us
  transfers between devices with their start and end apart: 17, of which 3 were waited for; matrix products, arithmetic and copies ran while one was open for 0% of the time, Pallas kernels for 9%

profile of v17, /device:TPU:118, one launch (start us, length us, event | category | flops | bytes accessed | tf_op | source)
XLA Modules:
  0.0 114.1 jit_solution(1758120792806394677)
XLA Ops:
  0.6 2.8 %shard_map.122 = (f32[6,8,16,128]{3,2,1,0:T(8,128)}, f32[16,4,128]{2,1,0:T(4,128)}, f32[6,1,16,128]{3,2,1,0:T(8,128)}, f32[6,1,16,128]{3,2,1,0:T(8,128)}, f32[6,...) custom-call(f32[3,6,6]{2,1,0:T(8,128)} %ub_ref.13, f32[3,6,6]{2,1,0:T(8,128)} %lb_ref.13, ...), custom_call_target="tpu_custom_call" | custom-call | tf_op jit(solution)/shard_map/pallas_call | solution.py:280
  3.5 7.3 %all_to_all.30.w_inc = f32[4,1,768]{2,1,0:T(1,128)} all-to-all(f32[4,1,768]{2,1,0:T(1,128)} %get-tuple-element.27), channel_id=1, replica_groups=mesh['chord'=4,'span'=16,'wall'=4] {'wall'}, dimensions={0} | all-to-all | bytes 24576 | tf_op jit(solution)/shard_map/all_to_all | solution.py:247
  10.8 8.7 %all-to-all-start.1 = ((f32[16,4,128]{2,1,0:T(4,128)}), f32[16,4,128]{2,1,0:T(4,128)S(1)}, u32[]{:S(2)}, u32[]{:S(2)}) async-start(f32[16,4,128]{2,1,0:T(4,128)} %get-tuple-element.30), calls=%async_computation.1 | async-start | bytes 65536 | tf_op jit(solution)/shard_map/all_to_all | solution.py:310
  19.5 3.2 %collective-permute-start = (f32[6,1,16,128]{3,2,1,0:T(8,128)}, f32[6,1,16,128]{3,2,1,0:T(8,128)S(1)}, u32[]{:S(2)}, u32[]{:S(2)}) collective-permute-start(f32[6,1,16,128]{3,2,1,0:T(8,128)} %get-tuple-element.25), channel_id=1, source_target_pairs={{0,64},{64,128},{128,192},{1,65},{65,129},{129,193},{2,66},{66,130... | collective-permute-start | bytes 147464 | tf_op jit(solution)/shard_map/ppermute | solution.py:245
  22.7 2.7 %collective-permute-start.1 = (f32[6,1,16,128]{3,2,1,0:T(8,128)S(1)}, f32[6,1,16,128]{3,2,1,0:T(8,128)S(1)}, u32[]{:S(2)}, u32[]{:S(2)}) collective-permute-start(f32[6,1,16,128]{3,2,1,0:T(8,128)S(1)} %copy-done.17), channel_id=1, source_target_pairs={{64,0},{128,64},{192,128},{65,1},{129,65},{193,129},{66,2},{130,66... | collective-permute-start | bytes 147464 | tf_op jit(solution)/shard_map/ppermute | solution.py:246
  25.3 4.6 %collective-permute-start.2 = (f32[6,8,128]{2,1,0:T(8,128)S(1)}, f32[6,8,128]{2,1,0:T(8,128)S(1)}, u32[]{:S(2)}, u32[]{:S(2)}) collective-permute-start(f32[6,8,128]{2,1,0:T(8,128)S(1)} %copy-done.23), channel_id=1, source_target_pairs={{0,4},{4,8},{8,12},{12,16},{16,20},{20,24},{24,28},{28,32},{32,36}... | collective-permute-start | bytes 73736 | tf_op jit(solution)/shard_map/ppermute | solution.py:245
  29.9 1.9 %collective-permute-start.3 = (f32[6,8,128]{2,1,0:T(8,128)S(1)}, f32[6,8,128]{2,1,0:T(8,128)S(1)}, u32[]{:S(2)}, u32[]{:S(2)}) collective-permute-start(f32[6,8,128]{2,1,0:T(8,128)S(1)} %copy-done.22), channel_id=1, source_target_pairs={{4,0},{8,4},{12,8},{16,12},{20,16},{24,20},{28,24},{32,28},{36,32}... | collective-permute-start | bytes 73736 | tf_op jit(solution)/shard_map/ppermute | solution.py:246
  32.5 3.6 %shard_map.123.part_ref = f32[6,8,16,128]{3,2,1,0:T(8,128)} custom-call(f32[3,6,6]{2,1,0:T(8,128)} %ub_ref.13, f32[3,6,6]{2,1,0:T(8,128)} %lb_ref.13, f32[6,2,6]{2,1,0:T(2,128)} %bitcast.7, s32[1]{0:T(128)} %bitcast.1.wall_me.rest_3_.rest_4_, f32[6,8,16,128]{3,2,1,0:T(8,128)} %get-tuple-element.24.adj_ref, f32[6,8,16,128]{3,2,1,0:T(8,128)} %sens_ref.7, ...), custom_call_target="tpu_custom_call" | custom-call | tf_op jit(solution)/shard_map/pallas_call | solution.py:311
  39.0 3.8 %shard_map.124 = (f32[6,8,16,128]{3,2,1,0:T(8,128)}, f32[16,3,128]{2,1,0:T(4,128)}, f32[6,1,16,128]{3,2,1,0:T(8,128)}, f32[6,1,16,128]{3,2,1,0:T(8,128)}, f32[6,...) custom-call(f32[3,6,6]{2,1,0:T(8,128)} %ub_ref.13, f32[3,6,6]{2,1,0:T(8,128)} %lb_ref.13, ...), custom_call_target="tpu_custom_call" | custom-call | tf_op jit(solution)/shard_map/pallas_call | solution.py:314
  42.7 6.7 %all-to-all-start.2 = ((f32[4,1,768]{2,1,0:T(1,128)}), f32[4,1,768]{2,1,0:T(1,128)S(1)}, u32[]{:S(2)}, u32[]{:S(2)}) async-start(f32[4,1,768]{2,1,0:T(1,128)} %get-tuple-element.34), calls=%async_computation.2 | async-start | bytes 24576 | tf_op jit(solution)/shard_map/all_to_all | solution.py:247
  49.4 3.2 %collective-permute-start.4 = (f32[6,1,16,128]{3,2,1,0:T(8,128)}, f32[6,1,16,128]{3,2,1,0:T(8,128)S(1)}, u32[]{:S(2)}, u32[]{:S(2)}) collective-permute-start(f32[6,1,16,128]{3,2,1,0:T(8,128)} %get-tuple-element.32), channel_id=1, source_target_pairs={{0,64},{64,128},{128,192},{1,65},{65,129},{129,193},{2,66},{66,130... | collective-permute-start | bytes 147464 | tf_op jit(solution)/shard_map/ppermute | solution.py:245
  52.6 2.7 %collective-permute-start.5 = (f32[6,1,16,128]{3,2,1,0:T(8,128)}, f32[6,1,16,128]{3,2,1,0:T(8,128)S(1)}, u32[]{:S(2)}, u32[]{:S(2)}) collective-permute-start(f32[6,1,16,128]{3,2,1,0:T(8,128)} %get-tuple-element.33), channel_id=1, source_target_pairs={{64,0},{128,64},{192,128},{65,1},{129,65},{193,129},{66,2},{130,66... | collective-permute-start | bytes 147464 | tf_op jit(solution)/shard_map/ppermute | solution.py:246
  55.9 6.4 %all-to-all-start.3 = ((f32[16,3,128]{2,1,0:T(4,128)}), f32[16,3,128]{2,1,0:T(4,128)S(1)}, u32[]{:S(2)}, u32[]{:S(2)}) async-start(f32[16,3,128]{2,1,0:T(4,128)} %get-tuple-element.37), calls=%async_computation.3 | async-start | bytes 65536 | tf_op jit(solution)/shard_map/all_to_all | solution.py:310
  62.3 4.6 %collective-permute-start.6 = (f32[6,8,128]{2,1,0:T(8,128)S(1)}, f32[6,8,128]{2,1,0:T(8,128)S(1)}, u32[]{:S(2)}, u32[]{:S(2)}) collective-permute-start(f32[6,8,128]{2,1,0:T(8,128)S(1)} %copy-done.20), channel_id=1, source_target_pairs={{0,4},{4,8},{8,12},{12,16},{16,20},{20,24},{24,28},{28,32},{32,36}... | collective-permute-start | bytes 73736 | tf_op jit(solution)/shard_map/ppermute | solution.py:245
  69.5 3.6 %shard_map.125.part_ref = f32[6,8,16,128]{3,2,1,0:T(8,128)} custom-call(f32[3,6,6]{2,1,0:T(8,128)} %ub_ref.13, f32[3,6,6]{2,1,0:T(8,128)} %lb_ref.13, f32[6,2,6]{2,1,0:T(2,128)} %bitcast.9, s32[1]{0:T(128)} %bitcast.1.wall_me.rest_3_.rest_4_, f32[6,8,16,128]{3,2,1,0:T(8,128)} %get-tuple-element.31.adj_ref, f32[6,8,16,128]{3,2,1,0:T(8,128)} %sens_ref.7, ...), custom_call_target="tpu_custom_call" | custom-call | tf_op jit(solution)/shard_map/pallas_call | solution.py:311
  75.3 3.7 %shard_map.126 = (f32[6,8,16,128]{3,2,1,0:T(8,128)}, f32[16,3,128]{2,1,0:T(4,128)}, f32[6,1,16,128]{3,2,1,0:T(8,128)}, f32[6,1,16,128]{3,2,1,0:T(8,128)}, f32[6,...) custom-call(f32[3,6,6]{2,1,0:T(8,128)} %ub_ref.13, f32[3,6,6]{2,1,0:T(8,128)} %lb_ref.13, ...), custom_call_target="tpu_custom_call" | custom-call | tf_op jit(solution)/shard_map/pallas_call | solution.py:316
  79.0 4.8 %all-to-all-start.4 = ((f32[4,1,768]{2,1,0:T(1,128)}), f32[4,1,768]{2,1,0:T(1,128)S(1)}, u32[]{:S(2)}, u32[]{:S(2)}) async-start(f32[4,1,768]{2,1,0:T(1,128)} %get-tuple-element.42), calls=%async_computation.4 | async-start | bytes 24576 | tf_op jit(solution)/shard_map/all_to_all | solution.py:247
  83.8 3.2 %collective-permute-start.8 = (f32[6,1,16,128]{3,2,1,0:T(8,128)}, f32[6,1,16,128]{3,2,1,0:T(8,128)S(1)}, u32[]{:S(2)}, u32[]{:S(2)}) collective-permute-start(f32[6,1,16,128]{3,2,1,0:T(8,128)} %get-tuple-element.40), channel_id=1, source_target_pairs={{0,64},{64,128},{128,192},{1,65},{65,129},{129,193},{2,66},{66,130... | collective-permute-start | bytes 147464 | tf_op jit(solution)/shard_map/ppermute | solution.py:245
  87.0 2.7 %collective-permute-start.9 = (f32[6,1,16,128]{3,2,1,0:T(8,128)}, f32[6,1,16,128]{3,2,1,0:T(8,128)S(1)}, u32[]{:S(2)}, u32[]{:S(2)}) collective-permute-start(f32[6,1,16,128]{3,2,1,0:T(8,128)} %get-tuple-element.41), channel_id=1, source_target_pairs={{64,0},{128,64},{192,128},{65,1},{129,65},{193,129},{66,2},{130,66... | collective-permute-start | bytes 147464 | tf_op jit(solution)/shard_map/ppermute | solution.py:246
  90.3 7.0 %all-to-all-start.5 = ((f32[16,3,128]{2,1,0:T(4,128)}), f32[16,3,128]{2,1,0:T(4,128)S(1)}, u32[]{:S(2)}, u32[]{:S(2)}) async-start(f32[16,3,128]{2,1,0:T(4,128)} %get-tuple-element.45), calls=%async_computation.5 | async-start | bytes 65536 | tf_op jit(solution)/shard_map/all_to_all | solution.py:310
  97.3 4.6 %collective-permute-start.10 = (f32[6,8,128]{2,1,0:T(8,128)S(1)}, f32[6,8,128]{2,1,0:T(8,128)S(1)}, u32[]{:S(2)}, u32[]{:S(2)}) collective-permute-start(f32[6,8,128]{2,1,0:T(8,128)S(1)} %copy-done.21), channel_id=1, source_target_pairs={{0,4},{4,8},{8,12},{12,16},{16,20},{20,24},{24,28},{28,32},{32,36}... | collective-permute-start | bytes 73736 | tf_op jit(solution)/shard_map/ppermute | solution.py:245
  101.9 2.1 %collective-permute-start.11 = (f32[6,8,128]{2,1,0:T(8,128)S(1)}, f32[6,8,128]{2,1,0:T(8,128)S(1)}, u32[]{:S(2)}, u32[]{:S(2)}) collective-permute-start(f32[6,8,128]{2,1,0:T(8,128)S(1)} %copy-done.19), channel_id=1, source_target_pairs={{4,0},{8,4},{12,8},{16,12},{20,16},{24,20},{28,24},{32,28},{36,32}... | collective-permute-start | bytes 73736 | tf_op jit(solution)/shard_map/ppermute | solution.py:246
  104.7 3.6 %shard_map.127.part_ref = f32[6,8,16,128]{3,2,1,0:T(8,128)} custom-call(f32[3,6,6]{2,1,0:T(8,128)} %ub_ref.13, f32[3,6,6]{2,1,0:T(8,128)} %lb_ref.13, f32[6,2,6]{2,1,0:T(2,128)} %bitcast.11, s32[1]{0:T(128)} %bitcast.1.wall_me.rest_3_.rest_4_, f32[6,8,16,128]{3,2,1,0:T(8,128)} %get-tuple-element.39.adj_ref, f32[6,8,16,128]{3,2,1,0:T(8,128)} %sens_ref.7, ...), custom_call_target="tpu_custom_call" | custom-call | tf_op jit(solution)/shard_map/pallas_call | solution.py:311
  111.0 3.1 %shard_map.128 = (f32[6,8,16,128]{3,2,1,0:T(8,128)}, f32[8,16,128]{2,1,0:T(8,128)}) custom-call(f32[3,6,6]{2,1,0:T(8,128)} %ub_ref.13, f32[3,6,6]{2,1,0:T(8,128)} %lb_ref.13, f32[6,2,6]{2,1,0:T(2,128)} %bitcast.12, f32[6,8,16,128]{3,2,1,0:T(8,128)} %shard_map.127.part_ref, f32[6,8,16,128]{3,2,1,0:T(8,128)} %diag_ref.13, f32[3,8,16,128]{3,2,1,0:T(8,128)} %face_ref.11, ...), custom_call_target="tpu_custom_call" | custom-call | tf_op jit(solution)/shard_map/pallas_call | solution.py:318
  (66 shorter events, 12.8 us)
Async XLA Ops:
  3.5 19.2 %copy-start.17 = (f32[6,1,16,128]{3,2,1,0:T(8,128)S(1)}, f32[6,1,16,128]{3,2,1,0:T(8,128)}, u32[]{:S(2)}) copy-start(f32[6,1,16,128]{3,2,1,0:T(8,128)} %get-tuple-element.26) | copy-start | bytes 147460
  10.7 14.6 %copy-start.23 = (f32[6,8,128]{2,1,0:T(8,128)S(1)}, f32[6,8,128]{2,1,0:T(8,128)}, u32[]{:S(2)}) copy-start(f32[6,8,128]{2,1,0:T(8,128)} %get-tuple-element.28) | copy-start | bytes 73732
  10.7 19.2 %copy-start.22 = (f32[6,8,128]{2,1,0:T(8,128)S(1)}, f32[6,8,128]{2,1,0:T(8,128)}, u32[]{:S(2)}) copy-start(f32[6,8,128]{2,1,0:T(8,128)} %get-tuple-element.29) | copy-start | bytes 73732
  10.8 27.0 %all-to-all-start.1 = ((f32[16,4,128]{2,1,0:T(4,128)}), f32[16,4,128]{2,1,0:T(4,128)S(1)}, u32[]{:S(2)}, u32[]{:S(2)}) async-start(f32[16,4,128]{2,1,0:T(4,128)} %get-tuple-element.30), calls=%async_computation.1 | async-start | bytes 65536 | tf_op jit(solution)/shard_map/all_to_all | solution.py:310
  19.5 12.4 %collective-permute-start = (f32[6,1,16,128]{3,2,1,0:T(8,128)}, f32[6,1,16,128]{3,2,1,0:T(8,128)S(1)}, u32[]{:S(2)}, u32[]{:S(2)}) collective-permute-start(f32[6,1,16,128]{3,2,1,0:T(8,128)} %get-tuple-element.25), channel_id=1, source_target_pairs={{0,64},{64,128},{128,192},{1,65},{65,129},{129,193},{2,66},{66,130... | collective-permute-start | bytes 147464 | tf_op jit(solution)/shard_map/ppermute | solution.py:245
  22.7 9.2 %collective-permute-start.1 = (f32[6,1,16,128]{3,2,1,0:T(8,128)S(1)}, f32[6,1,16,128]{3,2,1,0:T(8,128)S(1)}, u32[]{:S(2)}, u32[]{:S(2)}) collective-permute-start(f32[6,1,16,128]{3,2,1,0:T(8,128)S(1)} %copy-done.17), channel_id=1, source_target_pairs={{64,0},{128,64},{192,128},{65,1},{129,65},{193,129},{66,2},{130,66... | collective-permute-start | bytes 147464 | tf_op jit(solution)/shard_map/ppermute | solution.py:246
  25.3 10.7 %collective-permute-start.2 = (f32[6,8,128]{2,1,0:T(8,128)S(1)}, f32[6,8,128]{2,1,0:T(8,128)S(1)}, u32[]{:S(2)}, u32[]{:S(2)}) collective-permute-start(f32[6,8,128]{2,1,0:T(8,128)S(1)} %copy-done.23), channel_id=1, source_target_pairs={{0,4},{4,8},{8,12},{12,16},{16,20},{20,24},{24,28},{28,32},{32,36}... | collective-permute-start | bytes 73736 | tf_op jit(solution)/shard_map/ppermute | solution.py:245
  29.9 7.8 %collective-permute-start.3 = (f32[6,8,128]{2,1,0:T(8,128)S(1)}, f32[6,8,128]{2,1,0:T(8,128)S(1)}, u32[]{:S(2)}, u32[]{:S(2)}) collective-permute-start(f32[6,8,128]{2,1,0:T(8,128)S(1)} %copy-done.22), channel_id=1, source_target_pairs={{4,0},{8,4},{12,8},{16,12},{20,16},{24,20},{28,24},{32,28},{36,32}... | collective-permute-start | bytes 73736 | tf_op jit(solution)/shard_map/ppermute | solution.py:246
  42.7 12.6 %all-to-all-start.2 = ((f32[4,1,768]{2,1,0:T(1,128)}), f32[4,1,768]{2,1,0:T(1,128)S(1)}, u32[]{:S(2)}, u32[]{:S(2)}) async-start(f32[4,1,768]{2,1,0:T(1,128)} %get-tuple-element.34), calls=%async_computation.2 | async-start | bytes 24576 | tf_op jit(solution)/shard_map/all_to_all | solution.py:247
  49.4 19.4 %collective-permute-start.4 = (f32[6,1,16,128]{3,2,1,0:T(8,128)}, f32[6,1,16,128]{3,2,1,0:T(8,128)S(1)}, u32[]{:S(2)}, u32[]{:S(2)}) collective-permute-start(f32[6,1,16,128]{3,2,1,0:T(8,128)} %get-tuple-element.32), channel_id=1, source_target_pairs={{0,64},{64,128},{128,192},{1,65},{65,129},{129,193},{2,66},{66,130... | collective-permute-start | bytes 147464 | tf_op jit(solution)/shard_map/ppermute | solution.py:245
  52.6 16.2 %collective-permute-start.5 = (f32[6,1,16,128]{3,2,1,0:T(8,128)}, f32[6,1,16,128]{3,2,1,0:T(8,128)S(1)}, u32[]{:S(2)}, u32[]{:S(2)}) collective-permute-start(f32[6,1,16,128]{3,2,1,0:T(8,128)} %get-tuple-element.33), channel_id=1, source_target_pairs={{64,0},{128,64},{192,128},{65,1},{129,65},{193,129},{66,2},{130,66... | collective-permute-start | bytes 147464 | tf_op jit(solution)/shard_map/ppermute | solution.py:246
  55.3 7.0 %copy-start.20 = (f32[6,8,128]{2,1,0:T(8,128)S(1)}, f32[6,8,128]{2,1,0:T(8,128)}, u32[]{:S(2)}) copy-start(f32[6,8,128]{2,1,0:T(8,128)} %get-tuple-element.35) | copy-start | bytes 73732
  55.3 11.6 %copy-start.18 = (f32[6,8,128]{2,1,0:T(8,128)S(1)}, f32[6,8,128]{2,1,0:T(8,128)}, u32[]{:S(2)}) copy-start(f32[6,8,128]{2,1,0:T(8,128)} %get-tuple-element.36) | copy-start | bytes 73732
  55.9 18.8 %all-to-all-start.3 = ((f32[16,3,128]{2,1,0:T(4,128)}), f32[16,3,128]{2,1,0:T(4,128)S(1)}, u32[]{:S(2)}, u32[]{:S(2)}) async-start(f32[16,3,128]{2,1,0:T(4,128)} %get-tuple-element.37), calls=%async_computation.3 | async-start | bytes 65536 | tf_op jit(solution)/shard_map/all_to_all | solution.py:310
  62.3 10.7 %collective-permute-start.6 = (f32[6,8,128]{2,1,0:T(8,128)S(1)}, f32[6,8,128]{2,1,0:T(8,128)S(1)}, u32[]{:S(2)}, u32[]{:S(2)}) collective-permute-start(f32[6,8,128]{2,1,0:T(8,128)S(1)} %copy-done.20), channel_id=1, source_target_pairs={{0,4},{4,8},{8,12},{12,16},{16,20},{20,24},{24,28},{28,32},{32,36}... | collective-permute-start | bytes 73736 | tf_op jit(solution)/shard_map/ppermute | solution.py:245
  66.9 7.8 %collective-permute-start.7 = (f32[6,8,128]{2,1,0:T(8,128)S(1)}, f32[6,8,128]{2,1,0:T(8,128)S(1)}, u32[]{:S(2)}, u32[]{:S(2)}) collective-permute-start(f32[6,8,128]{2,1,0:T(8,128)S(1)} %copy-done.18), channel_id=1, source_target_pairs={{4,0},{8,4},{12,8},{16,12},{20,16},{24,20},{28,24},{32,28},{36,32}... | collective-permute-start | bytes 73736 | tf_op jit(solution)/shard_map/ppermute | solution.py:246
  79.0 10.7 %all-to-all-start.4 = ((f32[4,1,768]{2,1,0:T(1,128)}), f32[4,1,768]{2,1,0:T(1,128)S(1)}, u32[]{:S(2)}, u32[]{:S(2)}) async-start(f32[4,1,768]{2,1,0:T(1,128)} %get-tuple-element.42), calls=%async_computation.4 | async-start | bytes 24576 | tf_op jit(solution)/shard_map/all_to_all | solution.py:247
  83.8 20.2 %collective-permute-start.8 = (f32[6,1,16,128]{3,2,1,0:T(8,128)}, f32[6,1,16,128]{3,2,1,0:T(8,128)S(1)}, u32[]{:S(2)}, u32[]{:S(2)}) collective-permute-start(f32[6,1,16,128]{3,2,1,0:T(8,128)} %get-tuple-element.40), channel_id=1, source_target_pairs={{0,64},{64,128},{128,192},{1,65},{65,129},{129,193},{2,66},{66,130... | collective-permute-start | bytes 147464 | tf_op jit(solution)/shard_map/ppermute | solution.py:245
  87.0 17.0 %collective-permute-start.9 = (f32[6,1,16,128]{3,2,1,0:T(8,128)}, f32[6,1,16,128]{3,2,1,0:T(8,128)S(1)}, u32[]{:S(2)}, u32[]{:S(2)}) collective-permute-start(f32[6,1,16,128]{3,2,1,0:T(8,128)} %get-tuple-element.41), channel_id=1, source_target_pairs={{64,0},{128,64},{192,128},{65,1},{129,65},{193,129},{66,2},{130,66... | collective-permute-start | bytes 147464 | tf_op jit(solution)/shard_map/ppermute | solution.py:246
  89.7 7.6 %copy-start.21 = (f32[6,8,128]{2,1,0:T(8,128)S(1)}, f32[6,8,128]{2,1,0:T(8,128)}, u32[]{:S(2)}) copy-start(f32[6,8,128]{2,1,0:T(8,128)} %get-tuple-element.43) | copy-start | bytes 73732
  89.7 12.2 %copy-start.19 = (f32[6,8,128]{2,1,0:T(8,128)S(1)}, f32[6,8,128]{2,1,0:T(8,128)}, u32[]{:S(2)}) copy-start(f32[6,8,128]{2,1,0:T(8,128)} %get-tuple-element.44) | copy-start | bytes 73732
  90.3 19.5 %all-to-all-start.5 = ((f32[16,3,128]{2,1,0:T(4,128)}), f32[16,3,128]{2,1,0:T(4,128)S(1)}, u32[]{:S(2)}, u32[]{:S(2)}) async-start(f32[16,3,128]{2,1,0:T(4,128)} %get-tuple-element.45), calls=%async_computation.5 | async-start | bytes 65536 | tf_op jit(solution)/shard_map/all_to_all | solution.py:310
  97.3 10.9 %collective-permute-start.10 = (f32[6,8,128]{2,1,0:T(8,128)S(1)}, f32[6,8,128]{2,1,0:T(8,128)S(1)}, u32[]{:S(2)}, u32[]{:S(2)}) collective-permute-start(f32[6,8,128]{2,1,0:T(8,128)S(1)} %copy-done.21), channel_id=1, source_target_pairs={{0,4},{4,8},{8,12},{12,16},{16,20},{20,24},{24,28},{28,32},{32,36}... | collective-permute-start | bytes 73736 | tf_op jit(solution)/shard_map/ppermute | solution.py:245
  101.9 7.8 %collective-permute-start.11 = (f32[6,8,128]{2,1,0:T(8,128)S(1)}, f32[6,8,128]{2,1,0:T(8,128)S(1)}, u32[]{:S(2)}, u32[]{:S(2)}) collective-permute-start(f32[6,8,128]{2,1,0:T(8,128)S(1)} %copy-done.19), channel_id=1, source_target_pairs={{4,0},{8,4},{12,8},{16,12},{20,16},{24,20},{28,24},{32,28},{36,32}... | collective-permute-start | bytes 73736 | tf_op jit(solution)/shard_map/ppermute | solution.py:246
  (17 other events, 13.4 us)
